TPU v7x, 32 devices: a whole 2x2x4 slice. The times are simulated.
32 devices in a mesh: dp: 2 (over core), lat: 8 (over z, y), lon: 2 (over x).
Axes of the slice: x: 2, y: 2, z: 4, core: 2. Of those that a mesh axis runs over, the one named last changes fastest.
Arguments:
- tokens: bfloat16 [2, 64, 32, 1024], P('dp', 'lat', 'lon'), may hold values from -40 to 40
- cotangent: bfloat16 [2, 64, 32, 1024], P('dp', 'lat', 'lon'), may hold values from -6 to 6
- valid_cells: int32 [64, 32], replicated, may hold values 0 or 1
- w_qkv: bfloat16 [1024, 3072], P('dp'), may hold values from -1 to 1
- w_out: bfloat16 [1024, 1024], P('dp'), may hold values from -0.1875 to 0.1875
Outputs:
- d_input: bfloat16 [2, 64, 32, 1024], P('dp', 'lat', 'lon')
- d_w_out: float32 [1024, 1024], P(('dp', 'lat'), 'lon')
All inputs are finite; a program needn't handle non-finite values.
Results may differ from a plain program's by a relative error of at most 0.015.
The roundings to bfloat16 on the way count: a program that leaves them out, or rounds other values in their place, can miss the bound.
Values may be sent and summed in bfloat16 or wider, within the bound.
No kernel may reach another device: no remote copies, remote signals or barrier semaphores. Data moves between devices by JAX's collectives and lax.ppermute only.
A program may use at most 128 MiB of HBM per device.

v0:
```python
import jax
import jax.numpy as jnp
from jax import lax
from jax.sharding import PartitionSpec as P

HEADS = 16
RADIUS = 6
TILE = 8


def passed_along(value, axis, steps):
    count = lax.axis_size(axis)
    pairs = [(source, (source + steps) % count) for source in range(count)]
    return lax.ppermute(value, axis, pairs)


def shifted(value, axis, by):
    count = lax.axis_size(axis)
    pairs = [(i, i + by) for i in range(count) if 0 <= i + by < count]
    return lax.ppermute(value, axis, pairs)


def extended(block, sides, width, periodic):
    for axis, dim in sides:
        count = lax.axis_size(axis)
        forward = [(i, i + 1) for i in range(count - 1)]
        if periodic:
            forward.append((count - 1, 0))
        backward = [(target, source) for source, target in forward]
        low = lax.ppermute(
            lax.slice_in_dim(block, block.shape[dim] - width, None, axis=dim), axis, forward
        )
        high = lax.ppermute(lax.slice_in_dim(block, 0, width, axis=dim), axis, backward)
        block = jnp.concatenate([low, block, high], axis=dim)
    return block


def window_mask(tile_size, radius):
    window_side = tile_size + 2 * radius
    query_pos = jnp.arange(tile_size * tile_size)
    key_pos = jnp.arange(window_side * window_side)
    delta_row = (key_pos // window_side)[None, :] - radius - (query_pos // tile_size)[:, None]
    delta_col = (key_pos % window_side)[None, :] - radius - (query_pos % tile_size)[:, None]
    inside = (jnp.abs(delta_row) <= radius) & (jnp.abs(delta_col) <= radius)
    itself = (delta_row == 0) & (delta_col == 0)
    return (inside, itself)


def into_tiles(field, tile_size):
    row_count, col_count, channels = field.shape
    shaped = field.reshape(
        row_count // tile_size, tile_size, col_count // tile_size, tile_size, channels
    )
    return shaped.transpose(0, 2, 1, 3, 4).reshape(
        row_count // tile_size, col_count // tile_size, tile_size * tile_size, channels
    )


def from_tiles(tiled, tile_size):
    row_tiles, col_tiles, cells, channels = tiled.shape
    shaped = tiled.reshape(row_tiles, col_tiles, tile_size, tile_size, channels)
    return shaped.transpose(0, 2, 1, 3, 4).reshape(
        row_tiles * tile_size, col_tiles * tile_size, channels
    )


def attend(query_row, windows, grad_row, allowed, heads):
    tile_count, queries, width = query_row.shape
    window_keys = windows.shape[1]
    head_dim = width // heads
    query_heads = query_row.reshape(tile_count, queries, heads, head_dim)
    key_heads = windows[:, :, :width].reshape(tile_count, window_keys, heads, head_dim)
    value_heads = windows[:, :, width:].reshape(tile_count, window_keys, heads, head_dim)
    grad_heads = grad_row.reshape(tile_count, queries, heads, head_dim)
    score_scale = head_dim ** (-0.5)
    scores = (
        jnp.einsum("tqhd,tkhd->thqk", query_heads, key_heads, preferred_element_type=jnp.float32)
        * score_scale
    )
    mask_here = allowed[:, None]
    row_peak = jnp.max(jnp.where(mask_here, scores, -jnp.inf), axis=-1, keepdims=True)
    weights = jnp.where(mask_here, jnp.exp(scores - row_peak), 0.0)
    probabilities = weights / jnp.sum(weights, axis=-1, keepdims=True)
    probs_low = probabilities.astype(jnp.bfloat16)
    attended = jnp.einsum(
        "thqk,tkhd->tqhd", probs_low, value_heads, preferred_element_type=jnp.float32
    ).astype(jnp.bfloat16)
    grad_probs = jnp.einsum(
        "tqhd,tkhd->thqk", grad_heads, value_heads, preferred_element_type=jnp.float32
    )
    centre = jnp.sum(probabilities * grad_probs, axis=-1, keepdims=True)
    grad_scores = (probabilities * (grad_probs - centre) * score_scale).astype(jnp.bfloat16)
    grad_query = jnp.einsum(
        "thqk,tkhd->tqhd", grad_scores, key_heads, preferred_element_type=jnp.float32
    ).astype(jnp.bfloat16)
    grad_keys = jnp.einsum(
        "thqk,tqhd->tkhd", grad_scores, query_heads, preferred_element_type=jnp.float32
    )
    grad_values = jnp.einsum(
        "thqk,tqhd->tkhd", probs_low, grad_heads, preferred_element_type=jnp.float32
    )
    grad_window = jnp.concatenate(
        [
            grad_keys.reshape(tile_count, window_keys, width),
            grad_values.reshape(tile_count, window_keys, width),
        ],
        axis=-1,
    )
    return (
        attended.reshape(tile_count, queries, width),
        grad_query.reshape(tile_count, queries, width),
        grad_window,
    )


def return_lon(rim_terms, offset_by):
    return passed_along(rim_terms.astype(jnp.bfloat16), "lon", offset_by).astype(rim_terms.dtype)


def return_lat(rim_terms, offset_by):
    return shifted(rim_terms.astype(jnp.bfloat16), "lat", offset_by).astype(rim_terms.dtype)


def shards(tokens, cotangent, valid_cells, w_qkv, w_out):
    inputs_here = tokens[0]
    grad_here = cotangent[0]
    height, breadth, width = inputs_here.shape
    radius = RADIUS
    tile_size = TILE
    window_side = tile_size + 2 * radius
    row_tiles = height // tile_size
    col_tiles = breadth // tile_size
    token_count = height * breadth
    flat_inputs = inputs_here.reshape(token_count, width)
    flat_grad = grad_here.reshape(token_count, width)
    panels = lax.all_gather(w_qkv, "dp", axis=0, tiled=True)
    projected = jnp.dot(flat_inputs, panels, preferred_element_type=jnp.float32)
    projected = projected.astype(jnp.bfloat16)
    grad_attn = lax.dot_general(
        flat_grad,
        lax.all_gather(w_out, "dp", axis=0, tiled=True),
        (((1,), (1,)), ((), ())),
        preferred_element_type=jnp.float32,
    ).astype(jnp.bfloat16)
    key_values = projected[:, width:].reshape(height, breadth, 2 * width)
    key_lon = extended(key_values, (("lon", 1),), radius, True)
    key_ext = extended(key_lon, (("lat", 0),), radius, False)
    wrapped = jnp.concatenate(
        [valid_cells[:, -radius:], valid_cells, valid_cells[:, :radius]], axis=1
    )
    framed = jnp.pad(wrapped, ((radius, radius), (0, 0)))
    valid_ext = lax.dynamic_slice(
        framed,
        (lax.axis_index("lat") * height, lax.axis_index("lon") * breadth),
        (height + 2 * radius, breadth + 2 * radius),
    )
    inside, itself = window_mask(tile_size, radius)
    query_tiles = into_tiles(projected[:, :width].reshape(height, breadth, width), tile_size)
    grad_tiles = into_tiles(grad_attn.reshape(height, breadth, width), tile_size)

    def tile_row(grad_ext, slices):
        row_index, query_row, grad_row = slices
        windows = jnp.stack(
            [
                key_ext[:, column * tile_size : column * tile_size + window_side].reshape(
                    window_side * window_side, 2 * width
                )
                for column in range(col_tiles)
            ]
        )
        key_valid = jnp.stack(
            [
                valid_ext[:, column * tile_size : column * tile_size + window_side].reshape(
                    window_side * window_side
                )
                for column in range(col_tiles)
            ]
        )
        allowed = inside[None] & ((key_valid[:, None, :] == 1) | itself[None])
        attended, grad_query, grad_window = attend(query_row, windows, grad_row, allowed, HEADS)
        update = grad_ext
        for column in range(col_tiles):
            update = update.at[:, column * tile_size : column * tile_size + window_side].add(
                grad_window[column].reshape(window_side, window_side, 2 * width)
            )
        return (update, (attended, grad_query))

    grad_start = jnp.zeros((height + 2 * radius, breadth + 2 * radius, 2 * width), jnp.float32)
    grad_ext, outputs = lax.scan(
        tile_row, grad_start, (jnp.arange(row_tiles, dtype=jnp.int32), query_tiles, grad_tiles)
    )
    attended_tiles, grad_query_tiles = outputs
    from_right = return_lon(grad_ext[:, :radius], -1)
    from_left = return_lon(grad_ext[:, breadth + radius :], 1)
    middle = grad_ext[:, radius : breadth + radius]
    middle = middle.at[:, breadth - radius :].add(from_right)
    middle = middle.at[:, :radius].add(from_left)
    from_below = return_lat(middle[:radius], -1)
    from_above = return_lat(middle[height + radius :], 1)
    own_grad = middle[radius : height + radius]
    own_grad = own_grad.at[height - radius :].add(from_below)
    own_grad = own_grad.at[:radius].add(from_above)
    grad_kv = own_grad.astype(jnp.bfloat16).reshape(token_count, 2 * width)
    grad_q_flat = from_tiles(grad_query_tiles, tile_size).reshape(token_count, width)
    grad_proj = jnp.concatenate([grad_q_flat, grad_kv], axis=1)
    d_flat = lax.dot_general(
        grad_proj, panels, (((1,), (1,)), ((), ())), preferred_element_type=jnp.float32
    )
    d_input = d_flat.astype(jnp.bfloat16).reshape(1, height, breadth, width)
    attended_flat = from_tiles(attended_tiles, tile_size).reshape(token_count, width)
    device_count = lax.axis_size("dp") * lax.axis_size("lat") * lax.axis_size("lon")
    factor = 1.0 / device_count
    band_rows = lax.psum_scatter(
        (
            lax.dot_general(
                attended_flat,
                flat_grad,
                (((0,), (0,)), ((), ())),
                preferred_element_type=jnp.float32,
            )
            * factor
        ).astype(jnp.bfloat16),
        ("dp", "lat"),
        scatter_dimension=0,
        tiled=True,
    )
    d_w_out = lax.psum_scatter(band_rows, "lon", scatter_dimension=1, tiled=True).astype(
        jnp.float32
    )
    return (d_input, d_w_out)


def solution(mesh):
    in_specs = (
        P("dp", "lat", "lon", None),
        P("dp", "lat", "lon", None),
        P(),
        P("dp", None),
        P("dp", None),
    )
    out_specs = (P("dp", "lat", "lon", None), P(("dp", "lat"), "lon"))
    return jax.shard_map(shards, mesh=mesh, in_specs=in_specs, out_specs=out_specs, check_vma=False)
```

profile of v0, /device:TPU:0, one launch (start us, length us, event | category | flops | bytes accessed | tf_op | source)
XLA Modules:
  0.0 269.5 jit_solution(11306766659723694488)
XLA Ops:
  7.2 0.7 all-gather.3.cloned.1.call-update
  8.0 0.7 all-gather.5.cloned.1.call-update
  9.3 19.8 %all-gather.3.cloned.1.call-done = bf16[1024,3072]{1,0:T(8,128)(2,1)} async-done(((bf16[512,3072]{1,0:T(8,128)(2,1)}), bf16[1024,3072]{1,0:T(8,128)(2,1)}) %all-gather.3.cloned.1.call-update) | async-done | bytes 6291472 | tf_op jit(solution)/shard_map/all_gather | solution.py:136
  29.1 3.8 %convolution_convert_fusion = bf16[128,3072]{1,0:T(8,128)(2,1)S(1)} fusion(bf16[128,1024]{1,0:T(8,128)(2,1)S(1)} %bitcast.74, bf16[1024,3072]{1,0:T(8,128)(2,1)} %all-gather.3.cloned.1.call-done), kind=kOutput, calls=%fused_computation.15 | convolution fusion | flops 805699584 | bytes 7340032 | tf_op jit(solution)/shard_map/dot_general | solution.py:137
  33.0 1.8 collective-permute-start
  35.1 7.1 %collective-permute-done = bf16[8,6,2048]{2,1,0:T(8,128)(2,1)S(1)} collective-permute-done((bf16[8,6,2048]{2,1,0:T(8,128)(2,1)S(1)}, bf16[8,6,2048]{2,1,0:T(8,128)(2,1)S(1)}, u32[]{:S(2)}, u32[]{:S(2)}) %collective-permute-start) | collective-permute-done | bytes 196640 | tf_op jit(solution)/shard_map/ppermute | solution.py:30
  42.2 5.0 %collective-permute-done.1 = bf16[8,6,2048]{2,1,0:T(8,128)(2,1)S(1)} collective-permute-done((bf16[8,6,2048]{2,1,0:T(8,128)(2,1)S(1)}, bf16[8,6,2048]{2,1,0:T(8,128)(2,1)S(1)}, u32[]{:S(2)}, u32[]{:S(2)}) %collective-permute-start.1) | collective-permute-done | bytes 196640 | tf_op jit(solution)/shard_map/ppermute | solution.py:33
  47.1 0.4 pad_maximum_fusion.3
  47.5 1.4 fusion.61
  48.9 4.5 %collective-permute-start.2 = (bf16[6,28,2048]{2,1,0:T(8,128)(2,1)}, bf16[6,28,2048]{2,1,0:T(8,128)(2,1)}, u32[]{:S(2)}, u32[]{:S(2)}) collective-permute-start(bf16[6,28,2048]{2,1,0:T(8,128)(2,1)} %get-tuple-element.124), channel_id=1, source_target_pairs={{0,2},{2,4},{4,6},{6,8},{8,10},{10,12},{12,14},{1,3},{3,5},{5,7},{... | collective-permute-start | bytes 2064392 | tf_op jit(solution)/shard_map/ppermute | solution.py:30
  53.4 1.3 collective-permute-start.3
  55.0 2.4 convolution_convert_fusion.3
  57.4 0.3 reshape.455
  57.8 0.5 copy.39
  58.7 1.3 copy.38
  60.0 26.1 %collective-permute-done.2 = bf16[6,28,2048]{2,1,0:T(8,128)(2,1)} collective-permute-done((bf16[6,28,2048]{2,1,0:T(8,128)(2,1)}, bf16[6,28,2048]{2,1,0:T(8,128)(2,1)}, u32[]{:S(2)}, u32[]{:S(2)}) %collective-permute-start.2) | collective-permute-done | bytes 688160 | tf_op jit(solution)/shard_map/ppermute | solution.py:30
  86.1 1.8 pad_maximum_fusion.1
  87.9 1.9 fusion.59
  89.8 1.4 reshape.451
  91.2 2.8 %copy.28 = bf16[1,400,2048]{1,2,0:T(8,128)(2,1)S(1)} copy(bf16[1,400,2048]{2,1,0:T(8,128)(2,1)} %reshape.451) | data formatting | bytes 3276800 | tf_op jit(solution)/shard_map/while/body/eval_jaxpr/stack;while/body/eval_jaxpr/reshape | solution.py:163
  94.0 3.7 %reshape.452 = bf16[1,400,2048]{2,1,0:T(8,128)(2,1)} reshape(bf16[20,20,2048]{2,1,0:T(8,128)(2,1)} %get-tuple-element.121) | data formatting | bytes 3276800 | tf_op jit(solution)/shard_map/while/body/eval_jaxpr/stack;while/body/eval_jaxpr/reshape | solution.py:163
  97.6 3.8 %copy.29 = bf16[1,400,2048]{1,2,0:T(8,128)(2,1)} copy(bf16[1,400,2048]{2,1,0:T(8,128)(2,1)} %reshape.452) | data formatting | bytes 3276800 | tf_op jit(solution)/shard_map/while/body/eval_jaxpr/stack;while/body/eval_jaxpr/reshape | solution.py:163
  101.4 2.9 %fusion.16 = (bf16[2,400,1024]{1,2,0:T(8,128)(2,1)}, bf16[2,400,1024]{1,2,0:T(8,128)(2,1)S(1)}) fusion(bf16[1,400,2048]{1,2,0:T(8,128)(2,1)S(1)} %copy.28, bf16[1,400,2048]{1,2,0:T(8,128)(2,1)} %copy.29), kind=kLoop, calls=%fused_computation.21 | loop fusion | flops 6553600 | bytes 6553600 | tf_op jit(solution)/shard_map/while/body/eval_jaxpr/stack | solution.py:163
  104.3 1.3 copy-done.6
  105.6 2.7 %fusion.65 = f32[2,16,64,400]{3,2,1,0:T(8,128)} fusion(bf16[2,64,16,64]{1,3,2,0:T(8,128)(2,1)S(1)} %copy.39, bf16[2,400,16,64]{1,3,2,0:T(8,128)(2,1)S(1)} %bitcast.59), kind=kOutput, calls=%fused_computation.98 | convolution fusion | flops 104857600 | bytes 5177344 | tf_op jit(solution)/shard_map/while/body/eval_jaxpr/tqhd,tkhd->thqk/dot_general | solution.py:88
  108.4 6.4 %fusion.64 = (f32[2,16,64]{2,1,0:T(8,128)S(1)}, f32[2,16,64,400]{3,2,1,0:T(8,128)}) fusion(pred[2,64,400]{2,1,0:T(8,128)(4,1)S(1)} %or_and_fusion, bf16[2,64,16,64]{1,3,2,0:T(8,128)(2,1)S(1)} %copy-done.10, bf16[2,400,16,64]{1,3,2,0:T(8,128)(2,1)} %bitcast.64), kind=kOutput, calls=%fused_computation.97 | convolution fusion | flops 214630800 | bytes 5236736 | tf_op jit(solution)/shard_map/while/body/eval_jaxpr/sub | solution.py:82
  114.8 3.9 %fusion.25 = bf16[2,64,16,64]{1,3,2,0:T(8,128)(2,1)} fusion(bf16[2,400,16,64]{1,3,2,0:T(8,128)(2,1)S(1)} %bitcast.60, f32[2,16,64,400]{3,2,1,0:T(8,128)} %get-tuple-element.135, f32[2,16,64]{2,1,0:T(8,128)S(1)} %get-tuple-element.134), kind=kOutput, calls=%fused_computation.35 | convolution fusion | flops 106627072 | bytes 5185536 | tf_op jit(solution)/shard_map/while/body/eval_jaxpr/thqk,tkhd->tqhd/dot_general | solution.py:85
  118.7 2.7 %fusion.30 = f32[2,16,64,400]{3,2,1,0:T(8,128)} fusion(bf16[2,64,16,64]{1,3,2,0:T(8,128)(2,1)S(1)} %copy.39, f32[2,16,64,400]{3,2,1,0:T(8,128)S(1)} %copy-done.13, f32[2,16,64]{2,1,0:T(8,128)S(1)} %get-tuple-element.134), kind=kOutput, calls=%fused_computation.41 | convolution fusion | flops 106496000 | bytes 6823936 | tf_op jit(solution)/shard_map/while/body/eval_jaxpr/thqk,tqhd->tkhd/dot_general | solution.py:99
  121.5 0.4 copy.46
  122.2 0.7 copy.47
  123.0 18.3 %fusion.11 = f32[2,16,64,400]{3,2,1,0:T(8,128)} fusion(bf16[2,64,16,64]{1,3,2,0:T(8,128)(2,1)S(1)} %copy-done.10, f32[2,16,64,400]{3,2,1,0:T(8,128)} %fusion.65, f32[2,16,64,400]{3,2,1,0:T(8,128)} %get-tuple-element.135, f32[2,16,64]{2,1,0:T(8,128)S(1)} %get-tuple-element.134), kind=kOutput, calls=%fused_computation.19 | convolution fusion | flops 110594448 | bytes 10100736 | tf_op jit(solution)/shard_map/while/body/eval_jaxpr/thqk,tqhd->tkhd/dot_general | solution.py:96
  141.2 3.8 %copy.41 = f32[2,400,1024]{2,1,0:T(8,128)S(1)} copy(f32[2,400,1024]{1,2,0:T(8,128)} %bitcast.61) | data formatting | bytes 6553600 | tf_op jit(solution)/shard_map/while/body/eval_jaxpr/reshape | solution.py:105
  145.1 5.3 %copy.40 = f32[2,400,1024]{2,1,0:T(8,128)} copy(f32[2,400,1024]{1,2,0:T(8,128)} %bitcast.62) | data formatting | bytes 6553600 | tf_op jit(solution)/shard_map/while/body/eval_jaxpr/reshape | solution.py:104
  150.3 5.3 %pad_maximum_fusion = (f32[1,400,2048]{2,1,0:T(8,128)}, f32[1,400,2048]{2,1,0:T(8,128)}) fusion(f32[2,400,1024]{2,1,0:T(8,128)S(1)} %copy.41, f32[2,400,1024]{2,1,0:T(8,128)} %copy.40), kind=kLoop, calls=%fused_computation.17 | loop fusion | flops 1638400 | bytes 13107200 | tf_op jit(solution)/shard_map/while/body/eval_jaxpr/concatenate | solution.py:102
  155.7 4.9 %reshape.460 = f32[20,20,2048]{2,1,0:T(8,128)} reshape(f32[1,400,2048]{2,1,0:T(8,128)} %get-tuple-element.116) | data formatting | bytes 6553600 | tf_op jit(solution)/shard_map/reshape.170
  160.6 2.1 add.112
  162.6 3.0 %scatter-add.22 = f32[20,28,2048]{2,1,0:T(8,128)S(1)} pad(f32[20,20,2048]{2,1,0:T(8,128)} %add.112, f32[]{:T(128)} %constant.259.clone.1), padding=0_0x0_8x0_0 | pad | bytes 7864324 | tf_op jit(solution)/shard_map/while/body/eval_jaxpr/scatter-add | solution.py:183
  165.9 1.2 copy-done.2
  167.1 3.3 %constant_dynamic-update-slice_fusion = (f32[20,28,2048]{2,1,0:T(8,128)S(1)}, f32[20,20,2048]{2,1,0:T(8,128)}) fusion(f32[20,28,2048]{2,1,0:T(8,128)S(1)} %scatter-add.22, f32[20,20,2048]{2,1,0:T(8,128)S(1)} %copy-done.2, f32[20,20,2048]{2,1,0:T(8,128)S(1)} %copy-done.1), kind=kLoop, calls=%fused_computation.84 | loop fusion | flops 819200 | bytes 15073280 | tf_op jit(solution)/shard_map/while/body/eval_jaxpr/scatter-add | solution.py:183
  170.4 2.3 copy-done.3
  173.1 1.5 collective-permute-start.4
  174.6 2.1 multiply_convert_fusion
  176.8 2.6 slice.280
  179.4 0.7 copy-done.5
  180.3 1.1 copy.44
  181.4 0.6 collective-permute-start.5
  181.9 7.6 %collective-permute-done.4 = bf16[20,6,2048]{2,0,1:T(8,128)(2,1)} collective-permute-done((bf16[20,6,2048]{2,0,1:T(8,128)(2,1)S(1)}, bf16[20,6,2048]{2,0,1:T(8,128)(2,1)}, u32[]{:S(2)}, u32[]{:S(2)}) %collective-permute-start.4) | collective-permute-done | bytes 491552 | tf_op jit(solution)/shard_map/ppermute | solution.py:14
  189.5 2.6 slice_add_fusion.2
  192.1 5.5 %scatter-add.26 = f32[20,16,2048]{2,1,0:T(8,128)S(1)} dynamic-update-slice(f32[20,16,2048]{2,1,0:T(8,128)S(1)} %slice.280, f32[20,6,2048]{2,1,0:T(8,128)} %slice_add_fusion.2, s32[]{:T(128)} %constant.245.clone.1, s32[]{:T(128)} %constant.260.clone.1, s32[]{:T(128)} %constant.245.clone.1) | dynamic-update-slice | bytes 1966084 | tf_op jit(solution)/shard_map/scatter-add | solution.py:196
  197.6 2.1 collective-permute-done.5
  199.7 2.5 slice_add_fusion.1
  202.2 5.6 %scatter-add.27 = f32[20,16,2048]{2,1,0:T(8,128)S(1)} dynamic-update-slice(f32[20,16,2048]{2,1,0:T(8,128)S(1)} %scatter-add.26, f32[20,6,2048]{2,1,0:T(8,128)} %slice_add_fusion.1, s32[]{:T(128)} %constant.245.clone.1, s32[]{:T(128)} %constant.245.clone.1, s32[]{:T(128)} %constant.245.clone.1) | dynamic-update-slice | bytes 1966084 | tf_op jit(solution)/shard_map/scatter-add | solution.py:197
  207.9 1.0 fusion.60
  208.9 1.3 collective-permute-start.6
  210.2 18.7 %fusion.26 = bf16[2,64,16,64]{1,3,2,0:T(8,128)(2,1)} fusion(bf16[2,400,16,64]{1,3,2,0:T(8,128)(2,1)} %bitcast.65, f32[2,16,64,400]{3,2,1,0:T(8,128)} %fusion.65, f32[2,16,64,400]{3,2,1,0:T(8,128)} %get-tuple-element.135, f32[2,16,64]{2,1,0:T(8,128)S(1)} %get-tuple-element.134), kind=kOutput, calls=%fused_computation.36 | convolution fusion | flops 110725520 | bytes 8462336 | tf_op jit(solution)/shard_map/while/body/eval_jaxpr/thqk,tkhd->tqhd/dot_general | solution.py:93
  228.9 1.5 copy.36
  230.4 1.1 reshape.457
  231.4 1.0 copy.37
  232.5 5.1 %collective-permute-start.7 = (bf16[6,16,2048]{2,1,0:T(8,128)(2,1)}, bf16[6,16,2048]{2,1,0:T(8,128)(2,1)S(1)}, u32[]{:S(2)}, u32[]{:S(2)}) collective-permute-start(bf16[6,16,2048]{2,1,0:T(8,128)(2,1)} %get-tuple-element.122), channel_id=1, source_target_pairs={{0,2},{2,4},{4,6},{6,8},{8,10},{10,12},{12,14},{1,3},{3,5},{5,7},{... | collective-permute-start | bytes 1179656 | tf_op jit(solution)/shard_map/ppermute | solution.py:20
  237.6 1.1 fusion.33
  238.7 5.5 %collective-permute-done.7 = bf16[6,16,2048]{2,1,0:T(8,128)(2,1)S(1)} collective-permute-done((bf16[6,16,2048]{2,1,0:T(8,128)(2,1)}, bf16[6,16,2048]{2,1,0:T(8,128)(2,1)S(1)}, u32[]{:S(2)}, u32[]{:S(2)}) %collective-permute-start.7) | collective-permute-done | bytes 393248 | tf_op jit(solution)/shard_map/ppermute | solution.py:20
  244.4 5.7 %convolution_convert_fusion.2 = bf16[128,1024]{1,0:T(8,128)(2,1)} fusion(bf16[1024,3072]{1,0:T(8,128)(2,1)} %all-gather.3.cloned.1.call-done, bf16[128,2048]{1,0:T(8,128)(2,1)S(1)} %bitcast.63, bf16[128,1024]{1,0:T(8,128)(2,1)S(1)} %bitcast.66), kind=kOutput, calls=%fused_computation.37 | convolution fusion | flops 807010304 | bytes 7340032 | tf_op jit(solution)/shard_map/dot_general | solution.py:206
  250.1 11.3 %reduce-scatter.5.cloned.1.call-done = bf16[64,512]{1,0:T(8,128)(2,1)} async-done(((bf16[64,1024]{1,0:T(8,128)(2,1)}), bf16[64,512]{1,0:T(8,128)(2,1)}) %reduce-scatter.5.cloned.1.call-update) | async-done | bytes 65552 | tf_op jit(solution)/shard_map/reduce_scatter | solution.py:227
  261.4 1.5 convert_element_type.71
  (61 shorter events, 3.5 us)
Async XLA Ops:
  7.2 47.8 %copy-start = (bf16[1,8,16,1024]{3,2,1,0:T(8,128)(2,1)S(1)}, bf16[1,8,16,1024]{3,2,1,0:T(8,128)(2,1)}, u32[]{:S(2)}) copy-start(bf16[1,8,16,1024]{3,2,1,0:T(8,128)(2,1)} %param.18) | copy-start | bytes 786436
  7.2 1.6 copy-start.12
  7.2 21.9 %copy-start.9 = (bf16[1,8,16,1024]{3,2,1,0:T(8,128)(2,1)S(1)}, bf16[1,8,16,1024]{3,2,1,0:T(8,128)(2,1)}, u32[]{:S(2)}) copy-start(bf16[1,8,16,1024]{3,2,1,0:T(8,128)(2,1)} %param.17) | copy-start | bytes 786436
  7.2 21.9 %all-gather.3.cloned.1.call-start = ((), (), s32[]{:S(2)}) async-start(), calls=%async_computation.2 | async-start | bytes 9437184 | tf_op jit(solution)/shard_map/all_gather | solution.py:136
  7.9 47.0 %all-gather.5.cloned.1.call-start = ((), (), s32[]{:S(2)}) async-start(), calls=%async_computation.3 | async-start | bytes 3145728 | tf_op jit(solution)/shard_map/all_gather | solution.py:141
  8.7 235.7 %reduce-scatter.3.cloned.1.call-start = ((), (), s32[]{:S(2)}) async-start(), calls=%async_computation.4 | async-start | bytes 2228224 | tf_op jit(solution)/shard_map/reduce_scatter | solution.py:213
  33.0 9.2 %collective-permute-start = (bf16[8,6,2048]{2,1,0:T(8,128)(2,1)S(1)}, bf16[8,6,2048]{2,1,0:T(8,128)(2,1)S(1)}, u32[]{:S(2)}, u32[]{:S(2)}) collective-permute-start(bf16[8,6,2048]{2,1,0:T(8,128)(2,1)S(1)} %get-tuple-element.126), channel_id=1, source_target_pairs={{0,1},{1,0},{2,3},{3,2},{4,5},{5,4},{6,7},{7,6},{8,9},{9,8},{10,11... | collective-permute-start | bytes 589832 | tf_op jit(solution)/shard_map/ppermute | solution.py:30
  34.8 12.4 %collective-permute-start.1 = (bf16[8,6,2048]{2,1,0:T(8,128)(2,1)S(1)}, bf16[8,6,2048]{2,1,0:T(8,128)(2,1)S(1)}, u32[]{:S(2)}, u32[]{:S(2)}) collective-permute-start(bf16[8,6,2048]{2,1,0:T(8,128)(2,1)S(1)} %get-tuple-element.127), channel_id=1, source_target_pairs={{1,0},{0,1},{3,2},{2,3},{5,4},{4,5},{7,6},{6,7},{9,8},{8,9},{11,10... | collective-permute-start | bytes 589832 | tf_op jit(solution)/shard_map/ppermute | solution.py:33
  48.9 37.3 %collective-permute-start.2 = (bf16[6,28,2048]{2,1,0:T(8,128)(2,1)}, bf16[6,28,2048]{2,1,0:T(8,128)(2,1)}, u32[]{:S(2)}, u32[]{:S(2)}) collective-permute-start(bf16[6,28,2048]{2,1,0:T(8,128)(2,1)} %get-tuple-element.124), channel_id=1, source_target_pairs={{0,2},{2,4},{4,6},{6,8},{8,10},{10,12},{12,14},{1,3},{3,5},{5,7},{... | collective-permute-start | bytes 2064392 | tf_op jit(solution)/shard_map/ppermute | solution.py:30
  53.4 32.7 %collective-permute-start.3 = (bf16[6,28,2048]{2,1,0:T(8,128)(2,1)}, bf16[6,28,2048]{2,1,0:T(8,128)(2,1)}, u32[]{:S(2)}, u32[]{:S(2)}) collective-permute-start(bf16[6,28,2048]{2,1,0:T(8,128)(2,1)} %get-tuple-element.125), channel_id=1, source_target_pairs={{2,0},{4,2},{6,4},{8,6},{10,8},{12,10},{14,12},{3,1},{5,3},{7,5},{... | collective-permute-start | bytes 2064392 | tf_op jit(solution)/shard_map/ppermute | solution.py:33
  104.3 1.3 copy-start.6
  104.3 4.1 %copy-start.10 = (bf16[2,64,16,64]{1,3,2,0:T(8,128)(2,1)S(1)}, bf16[2,64,16,64]{1,3,2,0:T(8,128)(2,1)}, u32[]{:S(2)}) copy-start(bf16[2,64,16,64]{1,3,2,0:T(8,128)(2,1)} %copy.38) | copy-start | bytes 786436
  108.4 6.4 %copy-start.7 = (bf16[2,400,1024]{1,2,0:T(8,128)(2,1)S(1)}, bf16[2,400,1024]{1,2,0:T(8,128)(2,1)}, u32[]{:S(2)}) copy-start(bf16[2,400,1024]{1,2,0:T(8,128)(2,1)} %copy-done.6) | copy-start | bytes 4915204
  114.8 3.9 %copy-start.13 = (f32[2,16,64,400]{3,2,1,0:T(8,128)S(1)}, f32[2,16,64,400]{3,2,1,0:T(8,128)}, u32[]{:S(2)}) copy-start(f32[2,16,64,400]{3,2,1,0:T(8,128)} %get-tuple-element.135) | copy-start | bytes 9830404
  118.7 2.7 %copy-start.11 = (bf16[2,64,16,64]{1,3,2,0:T(8,128)(2,1)S(1)}, bf16[2,64,16,64]{1,3,2,0:T(8,128)(2,1)}, u32[]{:S(2)}) copy-start(bf16[2,64,16,64]{1,3,2,0:T(8,128)(2,1)} %fusion.25) | copy-start | bytes 786436
  155.6 4.9 %copy-start.4 = (f32[1,400,2048]{2,1,0:T(8,128)S(1)}, f32[1,400,2048]{2,1,0:T(8,128)}, u32[]{:S(2)}) copy-start(f32[1,400,2048]{2,1,0:T(8,128)} %get-tuple-element.117) | copy-start | bytes 9830404
  162.6 3.3 %copy-start.1 = (f32[20,20,2048]{2,1,0:T(8,128)S(1)}, f32[20,20,2048]{2,1,0:T(8,128)}, u32[]{:S(2)}) copy-start(f32[20,20,2048]{2,1,0:T(8,128)} %add.112) | copy-start | bytes 9830404
  162.6 4.5 %copy-start.2 = (f32[20,20,2048]{2,1,0:T(8,128)S(1)}, f32[20,20,2048]{2,1,0:T(8,128)}, u32[]{:S(2)}) copy-start(f32[20,20,2048]{2,1,0:T(8,128)} %reshape.460) | copy-start | bytes 9830404
  167.1 7.5 %copy-start.8 = (bf16[1,8,2,8,1024]{4,3,2,1,0:T(8,128)(2,1)S(1)}, bf16[1,8,2,8,1024]{4,3,2,1,0:T(8,128)(2,1)}, u32[]{:S(2)}) copy-start(bf16[1,8,2,8,1024]{4,3,2,1,0:T(8,128)(2,1)} %copy.47) | copy-start | bytes 786436
  170.4 2.3 copy-start.3
  173.1 16.4 %collective-permute-start.4 = (bf16[20,6,2048]{2,0,1:T(8,128)(2,1)S(1)}, bf16[20,6,2048]{2,0,1:T(8,128)(2,1)}, u32[]{:S(2)}, u32[]{:S(2)}) collective-permute-start(bf16[20,6,2048]{2,0,1:T(8,128)(2,1)S(1)} %copy.42), channel_id=1, source_target_pairs={{0,1},{1,0},{2,3},{3,2},{4,5},{5,4},{6,7},{7,6},{8,9},{9,8},{10,11... | collective-permute-start | bytes 1474568 | tf_op jit(solution)/shard_map/ppermute | solution.py:14
  176.7 84.7 %reduce-scatter.5.cloned.1.call-start = ((), (), s32[]{:S(2)}) async-start(), calls=%async_computation.5 | async-start | bytes 196608 | tf_op jit(solution)/shard_map/reduce_scatter | solution.py:227
  176.8 3.3 %copy-start.5 = (f32[20,20,2048]{2,1,0:T(8,128)S(1)}, f32[20,20,2048]{2,1,0:T(8,128)}, u32[]{:S(2)}) copy-start(f32[20,20,2048]{2,1,0:T(8,128)} %get-tuple-element.115) | copy-start | bytes 9830404
  181.4 18.3 %collective-permute-start.5 = (bf16[20,6,2048]{2,0,1:T(8,128)(2,1)}, bf16[20,6,2048]{2,0,1:T(8,128)(2,1)}, u32[]{:S(2)}, u32[]{:S(2)}) collective-permute-start(bf16[20,6,2048]{2,0,1:T(8,128)(2,1)} %copy.44), channel_id=1, source_target_pairs={{0,1},{1,0},{2,3},{3,2},{4,5},{5,4},{6,7},{7,6},{8,9},{9,8},{10,11... | collective-permute-start | bytes 1474568 | tf_op jit(solution)/shard_map/ppermute | solution.py:14
  208.9 28.7 %collective-permute-start.6 = (bf16[6,16,2048]{2,1,0:T(8,128)(2,1)}, bf16[6,16,2048]{2,1,0:T(8,128)(2,1)}, u32[]{:S(2)}, u32[]{:S(2)}) collective-permute-start(bf16[6,16,2048]{2,1,0:T(8,128)(2,1)} %get-tuple-element.123), channel_id=1, source_target_pairs={{2,0},{4,2},{6,4},{8,6},{10,8},{12,10},{14,12},{3,1},{5,3},{7,5},{... | collective-permute-start | bytes 1179656 | tf_op jit(solution)/shard_map/ppermute | solution.py:20
  232.5 11.6 %collective-permute-start.7 = (bf16[6,16,2048]{2,1,0:T(8,128)(2,1)}, bf16[6,16,2048]{2,1,0:T(8,128)(2,1)S(1)}, u32[]{:S(2)}, u32[]{:S(2)}) collective-permute-start(bf16[6,16,2048]{2,1,0:T(8,128)(2,1)} %get-tuple-element.122), channel_id=1, source_target_pairs={{0,2},{2,4},{4,6},{6,8},{8,10},{10,12},{12,14},{1,3},{3,5},{5,7},{... | collective-permute-start | bytes 1179656 | tf_op jit(solution)/shard_map/ppermute | solution.py:20
Sparse Core Ops, SparseCore 0:
  9.6 19.4 all-gather.2
  30.6 11.7 all-gather.4
  176.8 64.2 reduce-scatter.2
  244.5 16.8 reduce-scatter.4
where the time goes:
time: 271 us; the launch traced here: 269 us
  waiting for transfers between devices  85.9 us (32%)
  matrix products  66.8 us (25%)
  local copies, waits for them, and re-layouts  64.2 us (24%)
  other arithmetic  21.9 us (8%)
  starting transfers between devices  16.5 us (6%)
  between operations  14.2 us (5%)
    ppermute x2, waiting for transfers between devices, extended(): lax.ppermute(lax.slice_in_dim(block, block.shape[dim] - width, None, axis...  33.2 us
    all_gather x1, waiting for transfers between devices, shards(): panels = lax.all_gather(w_qkv, 'dp', axis=0, tiled=True)  19.8 us
    dot_general x1, matrix products, attend(): jnp.einsum('thqk,tkhd->tqhd', grad_scores, key_heads, preferred_element_t...  18.7 us
    dot_general x1, matrix products, attend(): jnp.einsum('thqk,tqhd->tkhd', grad_scores, query_heads, preferred_element...  18.3 us
    reshape x4, local copies, waits for them, and re-layouts, tile_row(): jnp.stack([key_ext[:, column * tile_size:column * tile_size + window_side...  11.6 us
    reduce_scatter x1, waiting for transfers between devices, shards(): lax.psum_scatter(band_rows, 'lon', scatter_dimension=1, tiled=True)  11.3 us
    ppermute x2, waiting for transfers between devices, passed_along(): return lax.ppermute(value, axis, pairs)  9.65 us
    sub x1, matrix products, attend(): weights = jnp.where(mask_here, jnp.exp(scores - row_peak), 0.0)  6.41 us
  transfers between devices with their start and end apart: 12, of which 8 were waited for; matrix products, arithmetic and copies ran while one was open for 24% of the time, Pallas kernels for 0%

commit v1 on v0

v1 whole, which is shorter than its diff:
```python
import functools

import jax
import jax.numpy as jnp
from jax import lax
from jax.experimental import pallas as pl
from jax.sharding import PartitionSpec as P

HEADS = 16
RADIUS = 6

TRANS_B = (((1,), (1,)), ((), ()))


def passed_along(value, axis, steps):
    count = lax.axis_size(axis)
    pairs = [(source, (source + steps) % count) for source in range(count)]
    return lax.ppermute(value, axis, pairs)


def shifted(value, axis, by):
    count = lax.axis_size(axis)
    pairs = [(i, i + by) for i in range(count) if 0 <= i + by < count]
    return lax.ppermute(value, axis, pairs)


def extended(block, sides, width, periodic):
    for axis, dim in sides:
        count = lax.axis_size(axis)
        forward = [(i, i + 1) for i in range(count - 1)]
        if periodic:
            forward.append((count - 1, 0))
        backward = [(target, source) for source, target in forward]
        low = lax.ppermute(
            lax.slice_in_dim(block, block.shape[dim] - width, None, axis=dim), axis, forward
        )
        high = lax.ppermute(lax.slice_in_dim(block, 0, width, axis=dim), axis, backward)
        block = jnp.concatenate([low, block, high], axis=dim)
    return block


def attention_kernel(q_ref, k_ref, v_ref, g_ref, allow_ref, att_ref, gq_ref, gk_ref, gv_ref,
                     *, head_dim, scale):
    q = q_ref[...]
    k = k_ref[...]
    v = v_ref[...]
    g = g_ref[...]
    allowed = allow_ref[...] > 0.0
    lanes = q.shape[1]
    lane = lax.broadcasted_iota(jnp.int32, (1, lanes), 1)
    q32 = q.astype(jnp.float32)
    g32 = g.astype(jnp.float32)
    att = jnp.zeros(q.shape, jnp.float32)
    gq = jnp.zeros(q.shape, jnp.float32)
    gk = jnp.zeros(k.shape, jnp.float32)
    gv = jnp.zeros(v.shape, jnp.float32)
    for j in range(lanes // head_dim):
        sel = (lane >= j * head_dim) & (lane < (j + 1) * head_dim)
        qj = jnp.where(sel, q32, 0.0).astype(jnp.bfloat16)
        gj = jnp.where(sel, g32, 0.0).astype(jnp.bfloat16)
        scores = lax.dot_general(qj, k, TRANS_B, preferred_element_type=jnp.float32) * scale
        peak = jnp.max(jnp.where(allowed, scores, -jnp.inf), axis=1, keepdims=True)
        weights = jnp.where(allowed, jnp.exp(scores - peak), 0.0)
        probs = weights / jnp.sum(weights, axis=1, keepdims=True)
        probs_low = probs.astype(jnp.bfloat16)
        att_j = jnp.dot(probs_low, v, preferred_element_type=jnp.float32)
        grad_probs = lax.dot_general(gj, v, TRANS_B, preferred_element_type=jnp.float32)
        centre = jnp.sum(probs * grad_probs, axis=1, keepdims=True)
        grad_scores = (probs * (grad_probs - centre) * scale).astype(jnp.bfloat16)
        gq_j = jnp.dot(grad_scores, k, preferred_element_type=jnp.float32)
        scores_t = grad_scores.astype(jnp.float32).T.astype(jnp.bfloat16)
        probs_t = probs_low.astype(jnp.float32).T.astype(jnp.bfloat16)
        gk_j = jnp.dot(scores_t, q, preferred_element_type=jnp.float32)
        gv_j = jnp.dot(probs_t, g, preferred_element_type=jnp.float32)
        att = jnp.where(sel, att_j, att)
        gq = jnp.where(sel, gq_j, gq)
        gk = jnp.where(sel, gk_j, gk)
        gv = jnp.where(sel, gv_j, gv)
    att_ref[...] = att.astype(att_ref.dtype)
    gq_ref[...] = gq.astype(gq_ref.dtype)
    gk_ref[...] = gk
    gv_ref[...] = gv


def block_attention(query, key_values, grad_attn, allowed, heads):
    queries, width = query.shape
    keys = key_values.shape[0]
    head_dim = width // heads
    lanes = 128
    pairs = width // lanes
    kernel = functools.partial(attention_kernel, head_dim=head_dim, scale=head_dim ** (-0.5))
    flops = 2 * queries * keys * width * 2 * 6
    cost = pl.CostEstimate(
        flops=flops,
        transcendentals=queries * keys * heads,
        bytes_accessed=2 * (2 * queries * width + 2 * keys * width + 2 * queries * width)
        + 4 * queries * keys + 4 * 2 * keys * width,
    )
    return pl.pallas_call(
        kernel,
        grid=(pairs,),
        in_specs=[
            pl.BlockSpec((queries, lanes), lambda h: (0, h)),
            pl.BlockSpec((keys, lanes), lambda h: (0, h)),
            pl.BlockSpec((keys, lanes), lambda h: (0, h + pairs)),
            pl.BlockSpec((queries, lanes), lambda h: (0, h)),
            pl.BlockSpec((queries, keys), lambda h: (0, 0)),
        ],
        out_specs=[
            pl.BlockSpec((queries, lanes), lambda h: (0, h)),
            pl.BlockSpec((queries, lanes), lambda h: (0, h)),
            pl.BlockSpec((keys, lanes), lambda h: (0, h)),
            pl.BlockSpec((keys, lanes), lambda h: (0, h)),
        ],
        out_shape=[
            jax.ShapeDtypeStruct((queries, width), jnp.bfloat16),
            jax.ShapeDtypeStruct((queries, width), jnp.bfloat16),
            jax.ShapeDtypeStruct((keys, width), jnp.float32),
            jax.ShapeDtypeStruct((keys, width), jnp.float32),
        ],
        cost_estimate=cost,
        name="block_attention",
    )(query, key_values, key_values, grad_attn, allowed)


def fold_rims(grad_ext, height, breadth, radius):
    def return_lon(rim, by):
        return passed_along(rim.astype(jnp.bfloat16), "lon", by).astype(jnp.float32)

    def return_lat(rim, by):
        return shifted(rim.astype(jnp.bfloat16), "lat", by).astype(jnp.float32)

    from_right = return_lon(grad_ext[:, :radius], -1)
    from_left = return_lon(grad_ext[:, breadth + radius :], 1)
    middle = (
        grad_ext[:, radius : breadth + radius]
        + jnp.pad(from_right, ((0, 0), (breadth - radius, 0), (0, 0)))
        + jnp.pad(from_left, ((0, 0), (0, breadth - radius), (0, 0)))
    )
    from_below = return_lat(middle[:radius], -1)
    from_above = return_lat(middle[height + radius :], 1)
    own = (
        middle[radius : height + radius]
        + jnp.pad(from_below, ((height - radius, 0), (0, 0), (0, 0)))
        + jnp.pad(from_above, ((0, height - radius), (0, 0), (0, 0)))
    )
    return own


def partner_rows_product(lhs, weights, axis):
    count = lax.axis_size(axis)
    if count != 2:
        full = lax.all_gather(weights, axis, axis=0, tiled=True)
        return lax.dot_general(lhs, full, TRANS_B, preferred_element_type=jnp.float32).astype(
            jnp.bfloat16
        )
    other = lax.ppermute(weights, axis, [(0, 1), (1, 0)])
    mine_part = lax.dot_general(lhs, weights, TRANS_B, preferred_element_type=jnp.float32)
    other_part = lax.dot_general(lhs, other, TRANS_B, preferred_element_type=jnp.float32)
    mine_part = mine_part.astype(jnp.bfloat16)
    other_part = other_part.astype(jnp.bfloat16)
    first = lax.axis_index(axis) == 0
    return jnp.where(
        first,
        jnp.concatenate([mine_part, other_part], axis=1),
        jnp.concatenate([other_part, mine_part], axis=1),
    )


def shards(tokens, cotangent, valid_cells, w_qkv, w_out):
    inputs_here = tokens[0]
    grad_here = cotangent[0]
    height, breadth, width = inputs_here.shape
    radius = RADIUS
    ext_rows = height + 2 * radius
    ext_cols = breadth + 2 * radius
    pad_cols = -(-ext_cols // 8) * 8
    token_count = height * breadth
    key_count = ext_rows * pad_cols
    flat_inputs = inputs_here.reshape(token_count, width)
    flat_grad = grad_here.reshape(token_count, width)

    tok_lon = extended(inputs_here, (("lon", 1),), radius, True)
    tok_ext = extended(tok_lon, (("lat", 0),), radius, False)
    tok_ext = jnp.pad(tok_ext, ((0, 0), (0, pad_cols - ext_cols), (0, 0)))
    tok_ext = tok_ext.reshape(key_count, width)

    panels = lax.all_gather(w_qkv, "dp", axis=0, tiled=True)
    grad_attn = partner_rows_product(flat_grad, w_out, "dp")

    query = jnp.dot(flat_inputs, panels[:, :width], preferred_element_type=jnp.float32)
    query = query.astype(jnp.bfloat16)
    key_values = jnp.dot(tok_ext, panels[:, width:], preferred_element_type=jnp.float32)
    key_values = key_values.astype(jnp.bfloat16)

    wrapped = jnp.concatenate(
        [valid_cells[:, -radius:], valid_cells, valid_cells[:, :radius]], axis=1
    )
    framed = jnp.pad(wrapped, ((radius, radius), (0, 0)))
    valid_ext = lax.dynamic_slice(
        framed,
        (lax.axis_index("lat") * height, lax.axis_index("lon") * breadth),
        (ext_rows, ext_cols),
    )
    valid_ext = jnp.pad(valid_ext, ((0, 0), (0, pad_cols - ext_cols))).reshape(1, key_count)
    query_pos = jnp.arange(token_count)
    key_pos = jnp.arange(key_count)
    delta_row = (key_pos // pad_cols)[None, :] - radius - (query_pos // breadth)[:, None]
    delta_col = (key_pos % pad_cols)[None, :] - radius - (query_pos % breadth)[:, None]
    inside = (jnp.abs(delta_row) <= radius) & (jnp.abs(delta_col) <= radius)
    itself = (delta_row == 0) & (delta_col == 0)
    allowed = (inside & ((valid_ext == 1) | itself)).astype(jnp.float32)

    attended, grad_query, grad_keys, grad_values = block_attention(
        query, key_values, grad_attn, allowed, HEADS
    )

    device_count = lax.axis_size("dp") * lax.axis_size("lat") * lax.axis_size("lon")
    factor = 1.0 / device_count
    weight_term = (
        lax.dot_general(
            attended, flat_grad, (((0,), (0,)), ((), ())), preferred_element_type=jnp.float32
        )
        * factor
    ).astype(jnp.bfloat16)
    row_blocks = lax.axis_size("dp") * lax.axis_size("lat")
    col_blocks = lax.axis_size("lon")
    rows_each = width // row_blocks
    cols_each = width // col_blocks
    ordered = (
        weight_term.reshape(row_blocks, rows_each, col_blocks, cols_each)
        .transpose(0, 2, 1, 3)
        .reshape(row_blocks * col_blocks * rows_each, cols_each)
    )
    d_w_out = lax.psum_scatter(
        ordered, ("dp", "lat", "lon"), scatter_dimension=0, tiled=True
    ).astype(jnp.float32)

    grad_k_own = fold_rims(
        grad_keys.reshape(ext_rows, pad_cols, width)[:, :ext_cols], height, breadth, radius
    )
    grad_v_own = fold_rims(
        grad_values.reshape(ext_rows, pad_cols, width)[:, :ext_cols], height, breadth, radius
    )
    grad_proj = jnp.concatenate(
        [
            grad_query,
            grad_k_own.astype(jnp.bfloat16).reshape(token_count, width),
            grad_v_own.astype(jnp.bfloat16).reshape(token_count, width),
        ],
        axis=1,
    )
    d_flat = lax.dot_general(grad_proj, panels, TRANS_B, preferred_element_type=jnp.float32)
    d_input = d_flat.astype(jnp.bfloat16).reshape(1, height, breadth, width)
    return (d_input, d_w_out)


def solution(mesh):
    in_specs = (
        P("dp", "lat", "lon", None),
        P("dp", "lat", "lon", None),
        P(),
        P("dp", None),
        P("dp", None),
    )
    out_specs = (P("dp", "lat", "lon", None), P(("dp", "lat"), "lon"))
    return jax.shard_map(shards, mesh=mesh, in_specs=in_specs, out_specs=out_specs, check_vma=False)
```

time: 271 us -> 229 us (0.85)
  local copies, waits for them, and re-layouts: 64.2 us -> 7.45 us
  waiting for transfers between devices: 85.9 us -> 141 us
  matrix products: 66.8 us -> 15.8 us
  Pallas kernels: 0 us -> 18 us
  other arithmetic: 21.9 us -> 6.22 us
  starting transfers between devices: 16.5 us -> 26.4 us
    reduce_scatter x2 -> x1, waiting for transfers between devices: 11.3 us -> 86.2 us  [shards(): lax.psum_scatter(ordered, ('dp', 'lat', 'lon'), scatter_dimension=0, tile...]
    dot_general x9 -> x6, matrix products: 60.4 us -> 15.8 us  [the longest x1 6.31 us: shards(): jnp.dot(tok_ext, panels[:, width:], preferred_element_type=jnp.float32)]
    reshape x12 -> x1, local copies, waits for them, and re-layouts: 24.5 us -> 2.76 us  [shards(): weight_term.reshape(row_blocks, rows_each, col_blocks, cols_each)]
    all_gather x1, waiting for transfers between devices: 19.8 us -> 0.01 us  [shards(): panels = lax.all_gather(w_qkv, 'dp', axis=0, tiled=True)]
    pallas_call x0 -> x1, Pallas kernels: none -> 18 us  [block_attention(): pl.pallas_call(kernel, grid=(pairs,), in_specs=[pl.BlockSpec((queries, la...]
    ppermute x2 -> x4, waiting for transfers between devices: 9.65 us -> 27.4 us  [passed_along(): return lax.ppermute(value, axis, pairs)]
    ppermute x2, waiting for transfers between devices: 33.2 us -> 16.8 us  [extended(): lax.ppermute(lax.slice_in_dim(block, block.shape[dim] - width, None, axis...]
    scatter-add x3 -> x0, local copies, waits for them, and re-layouts: 14 us -> none  [the longest x1 5.57 us: shards(): middle = middle.at[:, :radius].add(from_left)]
  transfers between devices with their start and end apart: 12 -> 15, of which waited for: 8 -> 10; matrix products, arithmetic and copies ran while one was open for 24% -> 5% of each run, Pallas kernels for 0% -> 0%
where the time goes in v1:
time: 229 us
  waiting for transfers between devices  141 us (62%)
  starting transfers between devices  26.4 us (12%)
  Pallas kernels  18 us (8%)
  matrix products  15.8 us (7%)
  between operations  14.4 us (6%)
  local copies, waits for them, and re-layouts  7.45 us (3%)
  other arithmetic  6.22 us (3%)
    reduce_scatter x1, waiting for transfers between devices, shards(): lax.psum_scatter(ordered, ('dp', 'lat', 'lon'), scatter_dimension=0, tile...  86.2 us
    ppermute x4, waiting for transfers between devices, passed_along(): return lax.ppermute(value, axis, pairs)  27.4 us
    pallas_call x1, Pallas kernels, block_attention(): pl.pallas_call(kernel, grid=(pairs,), in_specs=[pl.BlockSpec((queries, la...  18 us
    ppermute x2, waiting for transfers between devices, extended(): lax.ppermute(lax.slice_in_dim(block, block.shape[dim] - width, None, axis...  16.8 us
    ppermute x4, starting transfers between devices, shifted(): return lax.ppermute(value, axis, pairs)  14.1 us
    ppermute x4, waiting for transfers between devices, shifted(): return lax.ppermute(value, axis, pairs)  7.54 us
    ppermute x2, starting transfers between devices, extended(): lax.ppermute(lax.slice_in_dim(block, block.shape[dim] - width, None, axis...  6.7 us
    dot_general x1, matrix products, shards(): jnp.dot(tok_ext, panels[:, width:], preferred_element_type=jnp.float32)  6.31 us
  transfers between devices with their start and end apart: 15, of which 10 were waited for; matrix products, arithmetic and copies ran while one was open for 5% of the time, Pallas kernels for 0%

profile of v1, /device:TPU:0, one launch (start us, length us, event | category | flops | bytes accessed | tf_op | source)
XLA Modules:
  0.0 228.9 jit_solution(9495227766430814004)
XLA Ops:
  7.2 0.0 copy-start
  7.2 0.0 copy-start.3
  7.2 0.0 copy-start.4
  7.2 0.0 all-gather.2.cloned.1.call-start
  7.3 0.7 all-gather.2.cloned.1.call-update
  7.9 0.0 reduce-scatter.2.cloned.1.call-start
  8.0 0.2 copy-done.3
  8.2 3.0 %collective-permute-start = (bf16[8,6,1024]{2,1,0:T(8,128)(2,1)S(1)}, bf16[8,6,1024]{2,1,0:T(8,128)(2,1)S(1)}, u32[]{:S(2)}, u32[]{:S(2)}) collective-permute-start(bf16[8,6,1024]{2,1,0:T(8,128)(2,1)S(1)} %get-tuple-element.24), channel_id=1, source_target_pairs={{0,1},{1,0},{2,3},{3,2},{4,5},{5,4},{6,7},{7,6},{8,9},{9,8},{10,11... | collective-permute-start | bytes 294920 | tf_op jit(solution)/shard_map/ppermute | solution.py:34
  11.2 0.1 collective-permute-start.1
  11.3 0.0 collective-permute-start.4
  11.3 0.1 copy.11
  11.4 0.1 copy.10
  11.5 0.1 copy.12
  11.6 0.1 pad_add_fusion
  11.7 0.1 pad_dynamic-slice_fusion
  11.8 0.1 eq.27
  11.9 3.7 %collective-permute-done = bf16[8,6,1024]{2,1,0:T(8,128)(2,1)S(1)} collective-permute-done((bf16[8,6,1024]{2,1,0:T(8,128)(2,1)S(1)}, bf16[8,6,1024]{2,1,0:T(8,128)(2,1)S(1)}, u32[]{:S(2)}, u32[]{:S(2)}) %collective-permute-start) | collective-permute-done | bytes 98336 | tf_op jit(solution)/shard_map/ppermute | solution.py:34
  15.5 2.0 collective-permute-done.1
  17.5 0.2 pad_maximum_fusion
  17.7 0.1 fusion.55
  17.8 3.7 %collective-permute-start.2 = (bf16[6,28,1024]{2,1,0:T(8,128)(2,1)S(1)}, bf16[6,28,1024]{2,1,0:T(8,128)(2,1)S(1)}, u32[]{:S(2)}, u32[]{:S(2)}) collective-permute-start(bf16[6,28,1024]{2,1,0:T(8,128)(2,1)S(1)} %get-tuple-element.22), channel_id=1, source_target_pairs={{0,2},{2,4},{4,6},{6,8},{8,10},{10,12},{12,14},{1,3},{3,5},{5,7},{... | collective-permute-start | bytes 1032200 | tf_op jit(solution)/shard_map/ppermute | solution.py:34
  21.5 1.3 collective-permute-start.3
  22.8 1.0 fusion.34.allow_ref
  23.8 0.5 convolution_convert_fusion.2
  24.3 13.1 %collective-permute-done.2 = bf16[6,28,1024]{2,1,0:T(8,128)(2,1)S(1)} collective-permute-done((bf16[6,28,1024]{2,1,0:T(8,128)(2,1)S(1)}, bf16[6,28,1024]{2,1,0:T(8,128)(2,1)S(1)}, u32[]{:S(2)}, u32[]{:S(2)}) %collective-permute-start.2) | collective-permute-done | bytes 344096 | tf_op jit(solution)/shard_map/ppermute | solution.py:34
  37.4 0.0 collective-permute-done.3
  37.4 1.3 fusion.13
  38.7 0.0 collective-permute-done.4
  38.7 1.7 convolution_convert_fusion.1
  40.4 0.8 maximum_select_fusion.g_ref
  41.2 2.7 %fusion.18.q_ref = bf16[128,1024]{1,0:T(8,128)(2,1)} fusion(bf16[128,1024]{1,0:T(8,128)(2,1)S(1)} %bitcast.32, bf16[1024,3072]{1,0:T(8,128)(2,1)} %all-gather.2.cloned.1.call-done), kind=kOutput, calls=%fused_computation.20 | convolution fusion | flops 268566528 | bytes 2621440 | tf_op jit(solution)/shard_map/dot_general | solution.py:191
  44.0 6.3 %fusion.2.k_ref.v_ref = bf16[640,2048]{1,0:T(8,128)(2,1)} fusion(bf16[640,1024]{1,0:T(8,128)(2,1)S(1)} %bitcast.33, bf16[1024,3072]{1,0:T(8,128)(2,1)} %all-gather.2.cloned.1.call-done), kind=kOutput, calls=%fused_computation.3 | convolution fusion | flops 2685665280 | bytes 8126464 | tf_op jit(solution)/shard_map/dot_general | solution.py:193
  50.3 18.0 %block_attention.1 = (bf16[128,1024]{1,0:T(8,128)(2,1)}, bf16[128,1024]{1,0:T(8,128)(2,1)}, f32[640,1024]{1,0:T(8,128)}, f32[640,1024]{1,0:T(8,128)}) custom-call(bf16[128,1024]{1,0:T(8,128)(2,1)} %fusion.18.q_ref, bf16[640,2048]{1,0:T(8,128)(2,1)} %fusion.2.k_ref.v_ref, bf16[640,2048]{1,0:T(8,128)(2,1)} %fusion.2.k_ref.v_ref, ...), custom_call_target="tpu_custom_call" | custom-call | flops 2013265920 | bytes 9240576 | tf_op jit(solution)/shard_map/block_attention/pallas_call | solution.py:99
  68.3 1.7 multiply_convert_fusion
  70.0 2.8 %reshape.92 = bf16[16,64,2,512]{3,2,1,0:T(2,128)(2,1)} reshape(bf16[1024,1024]{1,0:T(8,128)(2,1)S(1)} %multiply_convert_fusion) | data formatting | bytes 4194304 | tf_op jit(solution)/shard_map/reshape | solution.py:231
  72.8 3.6 %copy.13 = bf16[16,2,64,512]{3,2,1,0:T(8,128)(2,1)} copy(bf16[16,2,64,512]{3,1,2,0:T(2,128)(2,1)} %bitcast.24) | data formatting | bytes 4194304 | tf_op jit(solution)/shard_map/transpose | solution.py:232
  76.3 0.0 reduce-scatter.2.cloned.1.call-update
  76.4 0.2 convert.32
  76.6 0.1 fusion.51
  76.7 1.5 collective-permute-start.5
  78.2 0.6 collective-permute-start.6
  78.8 0.2 convert.34
  79.0 0.1 fusion.52
  79.2 1.5 collective-permute-start.9
  80.7 0.6 collective-permute-start.10
  81.3 6.8 %collective-permute-done.5 = bf16[20,6,1024]{2,1,0:T(8,128)(2,1)S(1)} collective-permute-done((bf16[20,6,1024]{2,1,0:T(8,128)(2,1)S(1)}, bf16[20,6,1024]{2,1,0:T(8,128)(2,1)S(1)}, u32[]{:S(2)}, u32[]{:S(2)}) %collective-permute-start.5) | collective-permute-done | bytes 245792 | tf_op jit(solution)/shard_map/ppermute | solution.py:18
  88.1 10.9 %collective-permute-done.6 = bf16[20,6,1024]{2,1,0:T(8,128)(2,1)S(1)} collective-permute-done((bf16[20,6,1024]{2,1,0:T(8,128)(2,1)S(1)}, bf16[20,6,1024]{2,1,0:T(8,128)(2,1)S(1)}, u32[]{:S(2)}, u32[]{:S(2)}) %collective-permute-start.6) | collective-permute-done | bytes 245792 | tf_op jit(solution)/shard_map/ppermute | solution.py:18
  99.0 0.4 fusion.47
  99.4 1.3 collective-permute-start.7
  100.7 5.6 %collective-permute-start.8 = (bf16[6,16,1024]{2,1,0:T(8,128)(2,1)S(1)}, bf16[6,16,1024]{2,1,0:T(8,128)(2,1)S(1)}, u32[]{:S(2)}, u32[]{:S(2)}) collective-permute-start(bf16[6,16,1024]{2,1,0:T(8,128)(2,1)S(1)} %get-tuple-element.19), channel_id=1, source_target_pairs={{0,2},{2,4},{4,6},{6,8},{8,10},{10,12},{12,14},{1,3},{3,5},{5,7},{... | collective-permute-start | bytes 589832 | tf_op jit(solution)/shard_map/ppermute | solution.py:24
  106.3 3.6 %collective-permute-done.9 = bf16[20,6,1024]{2,1,0:T(8,128)(2,1)S(1)} collective-permute-done((bf16[20,6,1024]{2,1,0:T(8,128)(2,1)S(1)}, bf16[20,6,1024]{2,1,0:T(8,128)(2,1)S(1)}, u32[]{:S(2)}, u32[]{:S(2)}) %collective-permute-start.9) | collective-permute-done | bytes 245792 | tf_op jit(solution)/shard_map/ppermute | solution.py:18
  109.9 6.1 %collective-permute-done.10 = bf16[20,6,1024]{2,1,0:T(8,128)(2,1)S(1)} collective-permute-done((bf16[20,6,1024]{2,1,0:T(8,128)(2,1)S(1)}, bf16[20,6,1024]{2,1,0:T(8,128)(2,1)S(1)}, u32[]{:S(2)}, u32[]{:S(2)}) %collective-permute-start.10) | collective-permute-done | bytes 245792 | tf_op jit(solution)/shard_map/ppermute | solution.py:18
  116.0 0.4 fusion.49
  116.5 1.4 collective-permute-start.11
  117.9 5.7 %collective-permute-start.12 = (bf16[6,16,1024]{2,1,0:T(8,128)(2,1)S(1)}, bf16[6,16,1024]{2,1,0:T(8,128)(2,1)S(1)}, u32[]{:S(2)}, u32[]{:S(2)}) collective-permute-start(bf16[6,16,1024]{2,1,0:T(8,128)(2,1)S(1)} %get-tuple-element.21), channel_id=1, source_target_pairs={{0,2},{2,4},{4,6},{6,8},{8,10},{10,12},{12,14},{1,3},{3,5},{5,7},{... | collective-permute-start | bytes 589832 | tf_op jit(solution)/shard_map/ppermute | solution.py:24
  123.7 0.0 collective-permute-done.7
  123.7 0.0 collective-permute-done.8
  123.7 0.1 fusion.29
  123.8 2.3 %collective-permute-done.11 = bf16[6,16,1024]{2,1,0:T(8,128)(2,1)S(1)} collective-permute-done((bf16[6,16,1024]{2,1,0:T(8,128)(2,1)S(1)}, bf16[6,16,1024]{2,1,0:T(8,128)(2,1)S(1)}, u32[]{:S(2)}, u32[]{:S(2)}) %collective-permute-start.11) | collective-permute-done | bytes 196640 | tf_op jit(solution)/shard_map/ppermute | solution.py:24
  126.1 5.2 %collective-permute-done.12 = bf16[6,16,1024]{2,1,0:T(8,128)(2,1)S(1)} collective-permute-done((bf16[6,16,1024]{2,1,0:T(8,128)(2,1)S(1)}, bf16[6,16,1024]{2,1,0:T(8,128)(2,1)S(1)}, u32[]{:S(2)}, u32[]{:S(2)}) %collective-permute-start.12) | collective-permute-done | bytes 196640 | tf_op jit(solution)/shard_map/ppermute | solution.py:24
  131.3 0.1 fusion.27
  131.4 2.9 %convolution_convert_fusion = bf16[128,1024]{1,0:T(8,128)(2,1)} fusion(bf16[1024,3072]{1,0:T(8,128)(2,1)S(1)} %bitcast.37, bf16[128,1024]{1,0:T(8,128)(2,1)S(1)} %bitcast.35, bf16[128,1024]{1,0:T(8,128)(2,1)S(1)} %bitcast.34, bf16[128,1024]{1,0:T(8,128)(2,1)S(1)} %copy-done.6), kind=kOutput, calls=%fused_computation.21 | convolution fusion | flops 807796736 | bytes 7340032 | tf_op jit(solution)/shard_map/dot_general | solution.py:253
  134.3 86.2 %reduce-scatter.2.cloned.1.call-done = bf16[64,512]{1,0:T(8,128)(2,1)} async-done(((bf16[2048,512]{1,0:T(8,128)(2,1)}), bf16[64,512]{1,0:T(8,128)(2,1)}) %reduce-scatter.2.cloned.1.call-update) | async-done | bytes 65552 | tf_op jit(solution)/shard_map/reduce_scatter | solution.py:235
  220.5 1.5 convert_element_type.69
  (23 shorter events, 0.1 us)
Async XLA Ops:
  7.2 16.7 %copy-start = (bf16[1,8,16,1024]{3,2,1,0:T(8,128)(2,1)S(1)}, bf16[1,8,16,1024]{3,2,1,0:T(8,128)(2,1)}, u32[]{:S(2)}) copy-start(bf16[1,8,16,1024]{3,2,1,0:T(8,128)(2,1)} %param.6) | copy-start | bytes 786436
  7.2 1.0 copy-start.3
  7.2 4.1 %copy-start.4 = (bf16[512,1024]{1,0:T(8,128)(2,1)S(1)}, bf16[512,1024]{1,0:T(8,128)(2,1)}, u32[]{:S(2)}) copy-start(bf16[512,1024]{1,0:T(8,128)(2,1)} %param.9) | copy-start | bytes 3145732
  7.2 4.1 %copy-start.5 = (s32[64,32]{0,1:T(8,128)S(1)}, s32[64,32]{0,1:T(8,128)}, u32[]{:S(2)}) copy-start(s32[64,32]{0,1:T(8,128)} %param.7) | copy-start | bytes 24580
  7.2 34.0 %all-gather.2.cloned.1.call-start = ((), (), s32[]{:S(2)}) async-start(), calls=%async_computation.1 | async-start | bytes 9437184 | tf_op jit(solution)/shard_map/all_gather | solution.py:188
  7.9 212.6 %reduce-scatter.2.cloned.1.call-start = ((), (), s32[]{:S(2)}) async-start(), calls=%async_computation.2 | async-start | bytes 2162688 | tf_op jit(solution)/shard_map/reduce_scatter | solution.py:235
  8.2 7.3 %collective-permute-start = (bf16[8,6,1024]{2,1,0:T(8,128)(2,1)S(1)}, bf16[8,6,1024]{2,1,0:T(8,128)(2,1)S(1)}, u32[]{:S(2)}, u32[]{:S(2)}) collective-permute-start(bf16[8,6,1024]{2,1,0:T(8,128)(2,1)S(1)} %get-tuple-element.24), channel_id=1, source_target_pairs={{0,1},{1,0},{2,3},{3,2},{4,5},{5,4},{6,7},{7,6},{8,9},{9,8},{10,11... | collective-permute-start | bytes 294920 | tf_op jit(solution)/shard_map/ppermute | solution.py:34
  11.2 6.3 %collective-permute-start.1 = (bf16[8,6,1024]{2,1,0:T(8,128)(2,1)S(1)}, bf16[8,6,1024]{2,1,0:T(8,128)(2,1)S(1)}, u32[]{:S(2)}, u32[]{:S(2)}) collective-permute-start(bf16[8,6,1024]{2,1,0:T(8,128)(2,1)S(1)} %get-tuple-element.25), channel_id=1, source_target_pairs={{1,0},{0,1},{3,2},{2,3},{5,4},{4,5},{7,6},{6,7},{9,8},{8,9},{11,10... | collective-permute-start | bytes 294920 | tf_op jit(solution)/shard_map/ppermute | solution.py:37
  11.3 27.4 %collective-permute-start.4 = (bf16[512,1024]{1,0:T(8,128)(2,1)S(1)}, bf16[512,1024]{1,0:T(8,128)(2,1)}, u32[]{:S(2)}, u32[]{:S(2)}) collective-permute-start(bf16[512,1024]{1,0:T(8,128)(2,1)S(1)} %copy-done.4), channel_id=1, source_target_pairs={{0,16},{16,0},{1,17},{17,1},{2,18},{18,2},{3,19},{19,3},{4,20},{20... | collective-permute-start | bytes 3145736 | tf_op jit(solution)/shard_map/ppermute | solution.py:157
  17.8 19.6 %collective-permute-start.2 = (bf16[6,28,1024]{2,1,0:T(8,128)(2,1)S(1)}, bf16[6,28,1024]{2,1,0:T(8,128)(2,1)S(1)}, u32[]{:S(2)}, u32[]{:S(2)}) collective-permute-start(bf16[6,28,1024]{2,1,0:T(8,128)(2,1)S(1)} %get-tuple-element.22), channel_id=1, source_target_pairs={{0,2},{2,4},{4,6},{6,8},{8,10},{10,12},{12,14},{1,3},{3,5},{5,7},{... | collective-permute-start | bytes 1032200 | tf_op jit(solution)/shard_map/ppermute | solution.py:34
  21.5 15.9 %collective-permute-start.3 = (bf16[6,28,1024]{2,1,0:T(8,128)(2,1)S(1)}, bf16[6,28,1024]{2,1,0:T(8,128)(2,1)}, u32[]{:S(2)}, u32[]{:S(2)}) collective-permute-start(bf16[6,28,1024]{2,1,0:T(8,128)(2,1)S(1)} %get-tuple-element.23), channel_id=1, source_target_pairs={{2,0},{4,2},{6,4},{8,6},{10,8},{12,10},{14,12},{3,1},{5,3},{7,5},{... | collective-permute-start | bytes 1032200 | tf_op jit(solution)/shard_map/ppermute | solution.py:37
  72.8 3.6 %copy-start.2 = (f32[640,1024]{1,0:T(8,128)S(1)}, f32[640,1024]{1,0:T(8,128)}, u32[]{:S(2)}) copy-start(f32[640,1024]{1,0:T(8,128)} %get-tuple-element.7) | copy-start | bytes 7864324
  76.4 2.4 %copy-start.1 = (f32[640,1024]{1,0:T(8,128)S(1)}, f32[640,1024]{1,0:T(8,128)}, u32[]{:S(2)}) copy-start(f32[640,1024]{1,0:T(8,128)} %get-tuple-element.8) | copy-start | bytes 7864324
  76.7 11.3 %collective-permute-start.5 = (bf16[20,6,1024]{2,1,0:T(8,128)(2,1)S(1)}, bf16[20,6,1024]{2,1,0:T(8,128)(2,1)S(1)}, u32[]{:S(2)}, u32[]{:S(2)}) collective-permute-start(bf16[20,6,1024]{2,1,0:T(8,128)(2,1)S(1)} %get-tuple-element.14), channel_id=1, source_target_pairs={{0,1},{1,0},{2,3},{3,2},{4,5},{5,4},{6,7},{7,6},{8,9},{9,8},{10,11... | collective-permute-start | bytes 737288 | tf_op jit(solution)/shard_map/ppermute | solution.py:18
  78.2 20.7 %collective-permute-start.6 = (bf16[20,6,1024]{2,1,0:T(8,128)(2,1)S(1)}, bf16[20,6,1024]{2,1,0:T(8,128)(2,1)S(1)}, u32[]{:S(2)}, u32[]{:S(2)}) collective-permute-start(bf16[20,6,1024]{2,1,0:T(8,128)(2,1)S(1)} %get-tuple-element.15), channel_id=1, source_target_pairs={{0,1},{1,0},{2,3},{3,2},{4,5},{5,4},{6,7},{7,6},{8,9},{9,8},{10,11... | collective-permute-start | bytes 737288 | tf_op jit(solution)/shard_map/ppermute | solution.py:18
  78.8 52.6 %slice-start = ((s8[6291456]{0:T(1024)(128)(4,1)}), s8[4194304]{0:T(1024)(128)(4,1)S(1)}, s32[]{:S(2)}) async-start(s8[6291456]{0:T(1024)(128)(4,1)} %bitcast.36), calls=%async_computation.3 | async-start | bytes 8388608
  79.2 30.7 %collective-permute-start.9 = (bf16[20,6,1024]{2,1,0:T(8,128)(2,1)S(1)}, bf16[20,6,1024]{2,1,0:T(8,128)(2,1)S(1)}, u32[]{:S(2)}, u32[]{:S(2)}) collective-permute-start(bf16[20,6,1024]{2,1,0:T(8,128)(2,1)S(1)} %get-tuple-element.16), channel_id=1, source_target_pairs={{0,1},{1,0},{2,3},{3,2},{4,5},{5,4},{6,7},{7,6},{8,9},{9,8},{10,11... | collective-permute-start | bytes 737288 | tf_op jit(solution)/shard_map/ppermute | solution.py:18
  80.7 50.7 %slice-start.1 = ((s8[6291456]{0:T(1024)(128)(4,1)}), s8[2097152]{0:T(1024)(128)(4,1)S(1)}, s32[]{:S(2)}) async-start(s8[6291456]{0:T(1024)(128)(4,1)} %bitcast.36), calls=%async_computation.4 | async-start | bytes 4194304
  80.7 35.3 %collective-permute-start.10 = (bf16[20,6,1024]{2,1,0:T(8,128)(2,1)S(1)}, bf16[20,6,1024]{2,1,0:T(8,128)(2,1)S(1)}, u32[]{:S(2)}, u32[]{:S(2)}) collective-permute-start(bf16[20,6,1024]{2,1,0:T(8,128)(2,1)S(1)} %get-tuple-element.17), channel_id=1, source_target_pairs={{0,1},{1,0},{2,3},{3,2},{4,5},{5,4},{6,7},{7,6},{8,9},{9,8},{10,11... | collective-permute-start | bytes 737288 | tf_op jit(solution)/shard_map/ppermute | solution.py:18
  99.4 24.3 %collective-permute-start.7 = (bf16[6,16,1024]{2,1,0:T(8,128)(2,1)S(1)}, bf16[6,16,1024]{2,1,0:T(8,128)(2,1)S(1)}, u32[]{:S(2)}, u32[]{:S(2)}) collective-permute-start(bf16[6,16,1024]{2,1,0:T(8,128)(2,1)S(1)} %get-tuple-element.18), channel_id=1, source_target_pairs={{2,0},{4,2},{6,4},{8,6},{10,8},{12,10},{14,12},{3,1},{5,3},{7,5},{... | collective-permute-start | bytes 589832 | tf_op jit(solution)/shard_map/ppermute | solution.py:24
  100.7 23.0 %collective-permute-start.8 = (bf16[6,16,1024]{2,1,0:T(8,128)(2,1)S(1)}, bf16[6,16,1024]{2,1,0:T(8,128)(2,1)S(1)}, u32[]{:S(2)}, u32[]{:S(2)}) collective-permute-start(bf16[6,16,1024]{2,1,0:T(8,128)(2,1)S(1)} %get-tuple-element.19), channel_id=1, source_target_pairs={{0,2},{2,4},{4,6},{6,8},{8,10},{10,12},{12,14},{1,3},{3,5},{5,7},{... | collective-permute-start | bytes 589832 | tf_op jit(solution)/shard_map/ppermute | solution.py:24
  116.4 15.0 %copy-start.6 = (bf16[128,1024]{1,0:T(8,128)(2,1)S(1)}, bf16[128,1024]{1,0:T(8,128)(2,1)}, u32[]{:S(2)}) copy-start(bf16[128,1024]{1,0:T(8,128)(2,1)} %get-tuple-element.6) | copy-start | bytes 786436
  116.5 9.6 %collective-permute-start.11 = (bf16[6,16,1024]{2,1,0:T(8,128)(2,1)S(1)}, bf16[6,16,1024]{2,1,0:T(8,128)(2,1)S(1)}, u32[]{:S(2)}, u32[]{:S(2)}) collective-permute-start(bf16[6,16,1024]{2,1,0:T(8,128)(2,1)S(1)} %get-tuple-element.20), channel_id=1, source_target_pairs={{2,0},{4,2},{6,4},{8,6},{10,8},{12,10},{14,12},{3,1},{5,3},{7,5},{... | collective-permute-start | bytes 589832 | tf_op jit(solution)/shard_map/ppermute | solution.py:24
  117.9 13.4 %collective-permute-start.12 = (bf16[6,16,1024]{2,1,0:T(8,128)(2,1)S(1)}, bf16[6,16,1024]{2,1,0:T(8,128)(2,1)S(1)}, u32[]{:S(2)}, u32[]{:S(2)}) collective-permute-start(bf16[6,16,1024]{2,1,0:T(8,128)(2,1)S(1)} %get-tuple-element.21), channel_id=1, source_target_pairs={{0,2},{2,4},{4,6},{6,8},{8,10},{10,12},{12,14},{1,3},{3,5},{5,7},{... | collective-permute-start | bytes 589832 | tf_op jit(solution)/shard_map/ppermute | solution.py:24
Sparse Core Ops, SparseCore 0:
  9.6 19.4 all-gather.1
  76.5 144.0 reduce-scatter.1

commit v2 on v1

--- a/solution.py
+++ b/solution.py
@@ -123,28 +123,67 @@
     )(query, key_values, key_values, grad_attn, allowed)
 
 
-def fold_rims(grad_ext, height, breadth, radius):
-    def return_lon(rim, by):
-        return passed_along(rim.astype(jnp.bfloat16), "lon", by).astype(jnp.float32)
-
-    def return_lat(rim, by):
-        return shifted(rim.astype(jnp.bfloat16), "lat", by).astype(jnp.float32)
-
-    from_right = return_lon(grad_ext[:, :radius], -1)
-    from_left = return_lon(grad_ext[:, breadth + radius :], 1)
-    middle = (
-        grad_ext[:, radius : breadth + radius]
-        + jnp.pad(from_right, ((0, 0), (breadth - radius, 0), (0, 0)))
-        + jnp.pad(from_left, ((0, 0), (0, breadth - radius), (0, 0)))
-    )
-    from_below = return_lat(middle[:radius], -1)
-    from_above = return_lat(middle[height + radius :], 1)
-    own = (
-        middle[radius : height + radius]
-        + jnp.pad(from_below, ((height - radius, 0), (0, 0), (0, 0)))
-        + jnp.pad(from_above, ((0, height - radius), (0, 0), (0, 0)))
-    )
-    return own
+def grid_pairs(delta_lat, delta_lon):
+    lat_count = lax.axis_size("lat")
+    lon_count = lax.axis_size("lon")
+    pairs = []
+    for la in range(lat_count):
+        if 0 <= la + delta_lat < lat_count:
+            for lo in range(lon_count):
+                target = (la + delta_lat) * lon_count + (lo + delta_lon) % lon_count
+                pairs.append((la * lon_count + lo, target))
+    return pairs
+
+
+def sent_to(value, delta_lat, delta_lon):
+    return lax.ppermute(value, ("lat", "lon"), grid_pairs(delta_lat, delta_lon))
+
+
+def part(count, radius, step, giving):
+    if step == 0:
+        return slice(0, count)
+    if (step < 0) == giving:
+        return slice(count - radius, count)
+    return slice(0, radius)
+
+
+def halo_gather(block, radius):
+    height, breadth = block.shape[0], block.shape[1]
+    rows = []
+    for da in (-1, 0, 1):
+        row = []
+        for db in (-1, 0, 1):
+            if da == 0 and db == 0:
+                row.append(block)
+                continue
+            piece = block[part(height, radius, da, True), part(breadth, radius, db, True)]
+            row.append(sent_to(piece, -da, -db))
+        rows.append(jnp.concatenate(row, axis=1))
+    return jnp.concatenate(rows, axis=0)
+
+
+def halo_return(ext_list, height, breadth, radius):
+    row_slices = {-1: slice(0, radius), 0: slice(radius, radius + height), 1: slice(radius + height, None)}
+    col_slices = {-1: slice(0, radius), 0: slice(radius, radius + breadth), 1: slice(radius + breadth, None)}
+    owns = [ext[row_slices[0], col_slices[0]] for ext in ext_list]
+    widths = [ext.shape[-1] for ext in ext_list]
+    for da in (-1, 0, 1):
+        for db in (-1, 0, 1):
+            if da == 0 and db == 0:
+                continue
+            pieces = [ext[row_slices[da], col_slices[db]] for ext in ext_list]
+            joined = jnp.concatenate(pieces, axis=-1).astype(jnp.bfloat16)
+            got = sent_to(joined, da, db).astype(jnp.float32)
+            rs = part(height, radius, da, True)
+            cs = part(breadth, radius, db, True)
+            pad_rows = (rs.start, height - rs.stop)
+            pad_cols = (cs.start, breadth - cs.stop)
+            offset = 0
+            for index, width in enumerate(widths):
+                piece = got[..., offset : offset + width]
+                offset += width
+                owns[index] = owns[index] + jnp.pad(piece, (pad_rows, pad_cols, (0, 0)))
+    return owns
 
 
 def partner_rows_product(lhs, weights, axis):
@@ -167,6 +206,28 @@
     )
 
 
+def exchange_blocks(blocks, axis):
+    count = lax.axis_size(axis)
+    if count == 2:
+        me = lax.axis_index(axis)
+        mine = lax.dynamic_index_in_dim(blocks, me, 0, keepdims=False)
+        theirs = lax.dynamic_index_in_dim(blocks, 1 - me, 0, keepdims=False)
+        got = lax.ppermute(theirs, axis, [(0, 1), (1, 0)])
+        return jnp.where(me == 0, jnp.stack([mine, got]), jnp.stack([got, mine]))
+    flat = blocks.reshape((-1,) + blocks.shape[2:])
+    out = lax.all_to_all(flat, axis, 0, 0, tiled=True)
+    return out.reshape(blocks.shape)
+
+
+def gather_members(value, axis):
+    count = lax.axis_size(axis)
+    if count == 2:
+        me = lax.axis_index(axis)
+        got = lax.ppermute(value, axis, [(0, 1), (1, 0)])
+        return jnp.where(me == 0, jnp.stack([value, got]), jnp.stack([got, value]))
+    return lax.all_gather(value, axis, axis=0, tiled=False)
+
+
 def shards(tokens, cotangent, valid_cells, w_qkv, w_out):
     inputs_here = tokens[0]
     grad_here = cotangent[0]
@@ -179,11 +240,20 @@
     key_count = ext_rows * pad_cols
     flat_inputs = inputs_here.reshape(token_count, width)
     flat_grad = grad_here.reshape(token_count, width)
-
-    tok_lon = extended(inputs_here, (("lon", 1),), radius, True)
-    tok_ext = extended(tok_lon, (("lat", 0),), radius, False)
+    dp_count = lax.axis_size("dp")
+    lat_count = lax.axis_size("lat")
+    lon_count = lax.axis_size("lon")
+    rows_half = width // dp_count
+    cols_block = width // lon_count
+    rows_block = rows_half // lat_count
+
+    tok_ext = halo_gather(inputs_here, radius)
     tok_ext = jnp.pad(tok_ext, ((0, 0), (0, pad_cols - ext_cols), (0, 0)))
     tok_ext = tok_ext.reshape(key_count, width)
+
+    cot_blocks = flat_grad.reshape(token_count, lon_count, cols_block).transpose(1, 0, 2)
+    cot_lon = exchange_blocks(cot_blocks, "lon")
+    cot_group = gather_members(cot_lon, "dp")
 
     panels = lax.all_gather(w_qkv, "dp", axis=0, tiled=True)
     grad_attn = partner_rows_product(flat_grad, w_out, "dp")
@@ -215,33 +285,27 @@
         query, key_values, grad_attn, allowed, HEADS
     )
 
-    device_count = lax.axis_size("dp") * lax.axis_size("lat") * lax.axis_size("lon")
-    factor = 1.0 / device_count
-    weight_term = (
-        lax.dot_general(
-            attended, flat_grad, (((0,), (0,)), ((), ())), preferred_element_type=jnp.float32
-        )
-        * factor
-    ).astype(jnp.bfloat16)
-    row_blocks = lax.axis_size("dp") * lax.axis_size("lat")
-    col_blocks = lax.axis_size("lon")
-    rows_each = width // row_blocks
-    cols_each = width // col_blocks
-    ordered = (
-        weight_term.reshape(row_blocks, rows_each, col_blocks, cols_each)
-        .transpose(0, 2, 1, 3)
-        .reshape(row_blocks * col_blocks * rows_each, cols_each)
-    )
-    d_w_out = lax.psum_scatter(
-        ordered, ("dp", "lat", "lon"), scatter_dimension=0, tiled=True
-    ).astype(jnp.float32)
-
-    grad_k_own = fold_rims(
-        grad_keys.reshape(ext_rows, pad_cols, width)[:, :ext_cols], height, breadth, radius
-    )
-    grad_v_own = fold_rims(
-        grad_values.reshape(ext_rows, pad_cols, width)[:, :ext_cols], height, breadth, radius
-    )
+    att_blocks = attended.reshape(token_count, dp_count, rows_half).transpose(1, 0, 2)
+    att_dp = exchange_blocks(att_blocks, "dp")
+    att_group = gather_members(att_dp, "lon")
+    att_group = att_group.transpose(1, 0, 2, 3).reshape(-1, rows_half)
+    cot_group = cot_group.reshape(-1, cols_block)
+    device_count = dp_count * lat_count * lon_count
+    partial = lax.dot_general(
+        att_group, cot_group, (((0,), (0,)), ((), ())), preferred_element_type=jnp.float32
+    ) * (1.0 / device_count)
+    lat_index = lax.axis_index("lat")
+    total = lax.dynamic_slice_in_dim(partial, lat_index * rows_block, rows_block, axis=0)
+    for shift in range(1, lat_count):
+        target = (lat_index + shift) % lat_count
+        piece = lax.dynamic_slice_in_dim(partial, target * rows_block, rows_block, axis=0)
+        pairs = [(i, (i + shift) % lat_count) for i in range(lat_count)]
+        total = total + lax.ppermute(piece, "lat", pairs)
+    d_w_out = total
+
+    grad_k_ext = grad_keys.reshape(ext_rows, pad_cols, width)[:, :ext_cols]
+    grad_v_ext = grad_values.reshape(ext_rows, pad_cols, width)[:, :ext_cols]
+    grad_k_own, grad_v_own = halo_return([grad_k_ext, grad_v_ext], height, breadth, radius)
     grad_proj = jnp.concatenate(
         [
             grad_query,

time: 229 us -> 172 us (0.75)
  waiting for transfers between devices: 141 us -> 30.5 us
  starting transfers between devices: 26.4 us -> 66.6 us
  other arithmetic: 6.22 us -> 16.8 us
    reduce_scatter x1 -> x0, waiting for transfers between devices: 86.2 us -> none  [shards(): lax.psum_scatter(ordered, ('dp', 'lat', 'lon'), scatter_dimension=0, tile...]
    ppermute x12 -> x27, starting transfers between devices: 26.3 us -> 66.4 us  [the longest x16 43.7 us: sent_to(): return lax.ppermute(value, ('lat', 'lon'), grid_pairs(delta_lat, delta_lon))]
    ppermute x12 -> x27, waiting for transfers between devices: 53.7 us -> 29.8 us  [the longest x16 14.8 us: sent_to(): return lax.ppermute(value, ('lat', 'lon'), grid_pairs(delta_lat, delta_lon))]
    concatenate x2 -> x9, other arithmetic: 1.47 us -> 8.59 us  [the longest x8 7.03 us: halo_return(): joined = jnp.concatenate(pieces, axis=-1).astype(jnp.bfloat16)]
    slice x6 -> x17, local copies, waits for them, and re-layouts: 0.44 us -> 5.89 us  [the longest x6 4.77 us: halo_return(): pieces = [ext[row_slices[da], col_slices[db]] for ext in ext_list]]
    transpose x1 -> x0, local copies, waits for them, and re-layouts: 3.58 us -> none  [shards(): ordered = weight_term.reshape(row_blocks, rows_each, col_blocks, cols_eac...]
    reshape x1, local copies, waits for them, and re-layouts: 2.76 us -> 0.18 us  [shards(): attended.reshape(token_count, dp_count, rows_half).transpose(1, 0, 2)]
  transfers between devices with their start and end apart: 15 -> 29, of which waited for: 10 -> 8; matrix products, arithmetic and copies ran while one was open for 5% -> 24% of each run, Pallas kernels for 0% -> 11%
where the time goes in v2:
time: 172 us; the launch traced here: 171 us
  starting transfers between devices  66.6 us (39%)
  waiting for transfers between devices  30.5 us (18%)
  Pallas kernels  18 us (10%)
  other arithmetic  16.8 us (10%)
  matrix products  15.8 us (9%)
  between operations  14.7 us (9%)
  local copies, waits for them, and re-layouts  8.52 us (5%)
    ppermute x16, starting transfers between devices, sent_to(): return lax.ppermute(value, ('lat', 'lon'), grid_pairs(delta_lat, delta_lon))  43.7 us
    ppermute x7, starting transfers between devices, shards(): total = total + lax.ppermute(piece, 'lat', pairs)  19.1 us
    pallas_call x1, Pallas kernels, block_attention(): pl.pallas_call(kernel, grid=(pairs,), in_specs=[pl.BlockSpec((queries, la...  18 us
    ppermute x16, waiting for transfers between devices, sent_to(): return lax.ppermute(value, ('lat', 'lon'), grid_pairs(delta_lat, delta_lon))  14.8 us
    ppermute x7, waiting for transfers between devices, shards(): total = total + lax.ppermute(piece, 'lat', pairs)  8.54 us
    concatenate x8, other arithmetic, halo_return(): joined = jnp.concatenate(pieces, axis=-1).astype(jnp.bfloat16)  7.03 us
    ppermute x2, waiting for transfers between devices, gather_members(): got = lax.ppermute(value, axis, [(0, 1), (1, 0)])  6.4 us
    dot_general x1, matrix products, shards(): jnp.dot(tok_ext, panels[:, width:], preferred_element_type=jnp.float32)  6.32 us
  transfers between devices with their start and end apart: 29, of which 8 were waited for; matrix products, arithmetic and copies ran while one was open for 24% of the time, Pallas kernels for 11%

profile of v2, /device:TPU:0, one launch (start us, length us, event | category | flops | bytes accessed | tf_op | source)
XLA Modules:
  0.0 170.8 jit_solution(1483752000880400582)
XLA Ops:
  7.2 0.7 all-gather.2.cloned.1.call-update
  8.3 0.6 constant_dynamic-slice_fusion.8
  8.9 3.0 %collective-permute-start.19 = (bf16[128,512]{1,0:T(8,128)(2,1)S(1)}, bf16[128,512]{1,0:T(8,128)(2,1)S(1)}, u32[]{:S(2)}, u32[]{:S(2)}) collective-permute-start(bf16[128,512]{1,0:T(8,128)(2,1)S(1)} %bitcast.77), channel_id=1, source_target_pairs={{0,1},{1,0},{2,3},{3,2},{4,5},{5,4},{6,7},{7,6},{8,9},{9,8},{10,11... | collective-permute-start | bytes 393224 | tf_op jit(solution)/shard_map/ppermute | solution.py:215
  11.9 0.7 fusion.92
  12.6 3.4 %collective-permute-start = (bf16[6,6,1024]{2,1,0:T(8,128)(2,1)}, bf16[6,6,1024]{2,1,0:T(8,128)(2,1)S(1)}, u32[]{:S(2)}, u32[]{:S(2)}) collective-permute-start(bf16[6,6,1024]{2,1,0:T(8,128)(2,1)} %get-tuple-element.47), channel_id=1, source_target_pairs={{0,3},{1,2},{2,5},{3,4},{4,7},{5,6},{6,9},{7,8},{8,11},{9,10},{10,... | collective-permute-start | bytes 221192 | tf_op jit(solution)/shard_map/ppermute | solution.py:139
  16.0 1.3 collective-permute-start.7
  17.3 1.3 collective-permute-start.5
  19.4 0.5 convolution_convert_fusion.2
  19.9 1.0 fusion.67.allow_ref
  20.9 6.1 %collective-permute-start.2 = (bf16[6,6,1024]{2,1,0:T(8,128)(2,1)S(1)}, bf16[6,6,1024]{2,1,0:T(8,128)(2,1)S(1)}, u32[]{:S(2)}, u32[]{:S(2)}) collective-permute-start(bf16[6,6,1024]{2,1,0:T(8,128)(2,1)S(1)} %get-tuple-element.50), channel_id=1, source_target_pairs={{0,3},{1,2},{2,5},{3,4},{4,7},{5,6},{6,9},{7,8},{8,11},{9,10},{10,... | collective-permute-start | bytes 221192 | tf_op jit(solution)/shard_map/ppermute | solution.py:139
  27.0 5.8 %collective-permute-start.1 = (bf16[6,16,1024]{2,1,0:T(8,128)(2,1)S(1)}, bf16[6,16,1024]{2,1,0:T(8,128)(2,1)S(1)}, u32[]{:S(2)}, u32[]{:S(2)}) collective-permute-start(bf16[6,16,1024]{2,1,0:T(8,128)(2,1)S(1)} %get-tuple-element.51), channel_id=1, source_target_pairs={{0,2},{1,3},{2,4},{3,5},{4,6},{5,7},{6,8},{7,9},{8,10},{9,11},{10,... | collective-permute-start | bytes 589832 | tf_op jit(solution)/shard_map/ppermute | solution.py:139
  32.8 1.3 collective-permute-start.6
  34.1 0.7 maximum_select_fusion.5
  34.8 0.5 collective-permute-start.3
  35.4 1.5 collective-permute-start.4
  36.9 0.7 maximum_select_fusion.6
  37.6 3.6 %collective-permute-done.3 = bf16[8,6,1024]{2,1,0:T(8,128)(2,1)S(1)} collective-permute-done((bf16[8,6,1024]{2,1,0:T(8,128)(2,1)S(1)}, bf16[8,6,1024]{2,1,0:T(8,128)(2,1)S(1)}, u32[]{:S(2)}, u32[]{:S(2)}) %collective-permute-start.3) | collective-permute-done | bytes 98336 | tf_op jit(solution)/shard_map/ppermute | solution.py:139
  41.2 1.8 %collective-permute-done.4 = bf16[8,6,1024]{2,1,0:T(8,128)(2,1)S(1)} collective-permute-done((bf16[8,6,1024]{2,1,0:T(8,128)(2,1)S(1)}, bf16[8,6,1024]{2,1,0:T(8,128)(2,1)S(1)}, u32[]{:S(2)}, u32[]{:S(2)}) %collective-permute-start.4) | collective-permute-done | bytes 98336 | tf_op jit(solution)/shard_map/ppermute | solution.py:139
  43.0 1.6 fusion.20
  44.6 1.7 convolution_convert_fusion.1
  46.3 0.8 maximum_select_fusion.3.g_ref
  47.1 2.7 %fusion.25.q_ref = bf16[128,1024]{1,0:T(8,128)(2,1)} fusion(bf16[128,1024]{1,0:T(8,128)(2,1)S(1)} %bitcast.59, bf16[1024,3072]{1,0:T(8,128)(2,1)} %all-gather.2.cloned.1.call-done), kind=kOutput, calls=%fused_computation.25 | convolution fusion | flops 268566528 | bytes 2621440 | tf_op jit(solution)/shard_map/dot_general | solution.py:261
  49.8 6.3 %fusion.2.k_ref.v_ref = bf16[640,2048]{1,0:T(8,128)(2,1)} fusion(bf16[640,1024]{1,0:T(8,128)(2,1)S(1)} %bitcast.66, bf16[1024,3072]{1,0:T(8,128)(2,1)} %all-gather.2.cloned.1.call-done), kind=kOutput, calls=%fused_computation.2 | convolution fusion | flops 2685665280 | bytes 8126464 | tf_op jit(solution)/shard_map/dot_general | solution.py:263
  56.1 18.0 %block_attention.1 = (bf16[128,1024]{1,0:T(8,128)(2,1)}, bf16[128,1024]{1,0:T(8,128)(2,1)}, f32[640,1024]{1,0:T(8,128)}, f32[640,1024]{1,0:T(8,128)}) custom-call(bf16[128,1024]{1,0:T(8,128)(2,1)} %fusion.25.q_ref, bf16[640,2048]{1,0:T(8,128)(2,1)} %fusion.2.k_ref.v_ref, bf16[640,2048]{1,0:T(8,128)(2,1)} %fusion.2.k_ref.v_ref, ...), custom_call_target="tpu_custom_call" | custom-call | flops 2013265920 | bytes 9240576 | tf_op jit(solution)/shard_map/block_attention/pallas_call | solution.py:99
  74.2 2.1 %convert.36 = bf16[20,32,1024]{2,1,0:T(8,128)(2,1)S(1)} convert(f32[20,32,1024]{2,1,0:T(8,128)} %bitcast.60) | non-fusion elementwise | flops 655360 | bytes 3932160 | tf_op jit(solution)/shard_map/convert.31
  76.2 0.7 fusion.86
  76.9 0.8 fusion.82
  77.7 0.9 fusion.84
  78.8 0.7 fusion.87
  79.6 0.8 fusion.83
  80.4 0.9 fusion.85
  81.4 0.6 constant_dynamic-slice_fusion.10
  82.4 1.0 pad_maximum_fusion.3
  83.5 0.5 collective-permute-start.13
  84.0 0.9 pad_maximum_fusion.2
  84.9 1.6 collective-permute-start.12
  86.6 1.0 pad_maximum_fusion.5
  87.5 1.3 collective-permute-start.11
  88.8 1.1 pad_maximum_fusion
  89.9 1.0 pad_maximum_fusion.4
  90.9 1.0 pad_maximum_fusion.7
  91.9 1.1 pad_maximum_fusion.1
  93.0 5.5 %collective-permute-start.14 = (bf16[6,6,2048]{2,1,0:T(8,128)(2,1)S(1)}, bf16[6,6,2048]{2,1,0:T(8,128)(2,1)S(1)}, u32[]{:S(2)}, u32[]{:S(2)}) collective-permute-start(bf16[6,6,2048]{2,1,0:T(8,128)(2,1)S(1)} %pad_maximum_fusion.6), channel_id=1, source_target_pairs={{0,3},{1,2},{2,5},{3,4},{4,7},{5,6},{6,9},{7,8},{8,11},{9,10},{10,... | collective-permute-start | bytes 442376 | tf_op jit(solution)/shard_map/ppermute | solution.py:139
  98.5 5.3 %collective-permute-done.11 = bf16[6,6,2048]{2,1,0:T(8,128)(2,1)S(1)} collective-permute-done((bf16[6,6,2048]{2,1,0:T(8,128)(2,1)S(1)}, bf16[6,6,2048]{2,1,0:T(8,128)(2,1)S(1)}, u32[]{:S(2)}, u32[]{:S(2)}) %collective-permute-start.11) | collective-permute-done | bytes 147488 | tf_op jit(solution)/shard_map/ppermute | solution.py:139
  103.9 1.4 collective-permute-start.16
  105.4 1.4 collective-permute-start.9
  106.8 2.6 %collective-permute-done.16 = bf16[6,6,2048]{2,1,0:T(8,128)(2,1)S(1)} collective-permute-done((bf16[6,6,2048]{2,1,0:T(8,128)(2,1)S(1)}, bf16[6,6,2048]{2,1,0:T(8,128)(2,1)S(1)}, u32[]{:S(2)}, u32[]{:S(2)}) %collective-permute-start.16) | collective-permute-done | bytes 147488 | tf_op jit(solution)/shard_map/ppermute | solution.py:139
  109.4 9.5 %collective-permute-start.15 = (bf16[6,16,2048]{2,1,0:T(8,128)(2,1)S(1)}, bf16[6,16,2048]{2,1,0:T(8,128)(2,1)S(1)}, u32[]{:S(2)}, u32[]{:S(2)}) collective-permute-start(bf16[6,16,2048]{2,1,0:T(8,128)(2,1)S(1)} %pad_maximum_fusion.1), channel_id=1, source_target_pairs={{0,2},{1,3},{2,4},{3,5},{4,6},{5,7},{6,8},{7,9},{8,10},{9,11},{10,... | collective-permute-start | bytes 1179656 | tf_op jit(solution)/shard_map/ppermute | solution.py:139
  119.0 1.5 collective-permute-done.9
  120.5 1.3 collective-permute-start.10
  121.8 0.6 collective-permute-start.18
  122.5 6.4 %collective-permute-done.18 = bf16[2,128,512]{1,2,0:T(8,128)(2,1)S(1)} collective-permute-done((bf16[2,128,512]{1,2,0:T(8,128)(2,1)S(1)}, bf16[2,128,512]{1,2,0:T(8,128)(2,1)S(1)}, u32[]{:S(2)}, u32[]{:S(2)}) %collective-permute-start.18) | collective-permute-done | bytes 262176 | tf_op jit(solution)/shard_map/ppermute | solution.py:226
  128.9 1.6 fusion.16
  130.7 3.2 %collective-permute-start.21 = (f32[64,512]{1,0:T(8,128)S(1)}, f32[64,512]{1,0:T(8,128)S(1)}, u32[]{:S(2)}, u32[]{:S(2)}) collective-permute-start(f32[64,512]{1,0:T(8,128)S(1)} %get-tuple-element.26), channel_id=1, source_target_pairs={{0,2},{2,4},{4,6},{6,8},{8,10},{10,12},{12,14},{14,0},{1,3},{3,5},... | collective-permute-start | bytes 393224 | tf_op jit(solution)/shard_map/ppermute | solution.py:303
  133.9 4.3 %collective-permute-start.27 = (f32[64,512]{1,0:T(8,128)S(1)}, f32[64,512]{1,0:T(8,128)S(1)}, u32[]{:S(2)}, u32[]{:S(2)}) collective-permute-start(f32[64,512]{1,0:T(8,128)S(1)} %get-tuple-element.27), channel_id=1, source_target_pairs={{0,14},{2,0},{4,2},{6,4},{8,6},{10,8},{12,10},{14,12},{1,15},{3,1}... | collective-permute-start | bytes 393224 | tf_op jit(solution)/shard_map/ppermute | solution.py:303
  138.2 2.1 %collective-permute-start.26 = (f32[64,512]{1,0:T(8,128)S(1)}, f32[64,512]{1,0:T(8,128)S(1)}, u32[]{:S(2)}, u32[]{:S(2)}) collective-permute-start(f32[64,512]{1,0:T(8,128)S(1)} %get-tuple-element.28), channel_id=1, source_target_pairs={{0,12},{2,14},{4,0},{6,2},{8,4},{10,6},{12,8},{14,10},{1,13},{3,15... | collective-permute-start | bytes 393224 | tf_op jit(solution)/shard_map/ppermute | solution.py:303
  140.2 8.8 %collective-permute-start.25 = (f32[64,512]{1,0:T(8,128)S(1)}, f32[64,512]{1,0:T(8,128)S(1)}, u32[]{:S(2)}, u32[]{:S(2)}) collective-permute-start(f32[64,512]{1,0:T(8,128)S(1)} %get-tuple-element.29), channel_id=1, source_target_pairs={{0,10},{2,12},{4,14},{6,0},{8,2},{10,4},{12,6},{14,8},{1,11},{3,13... | collective-permute-start | bytes 393224 | tf_op jit(solution)/shard_map/ppermute | solution.py:303
  149.3 0.3 fusion.40
  149.6 1.5 fusion.48
  151.2 0.6 collective-permute-start.22
  151.8 2.9 %convolution_convert_fusion = bf16[128,1024]{1,0:T(8,128)(2,1)} fusion(bf16[1024,3072]{1,0:T(8,128)(2,1)S(1)} %bitcast.80, bf16[128,1024]{1,0:T(8,128)(2,1)S(1)} %bitcast.75, bf16[128,1024]{1,0:T(8,128)(2,1)S(1)} %bitcast.76, bf16[128,1024]{1,0:T(8,128)(2,1)S(1)} %copy-done.10), kind=kOutput, calls=%fused_computation.26 | convolution fusion | flops 807796736 | bytes 7340032 | tf_op jit(solution)/shard_map/dot_general | solution.py:317
  154.7 6.5 %collective-permute-done.24 = f32[64,512]{1,0:T(8,128)S(1)} collective-permute-done((f32[64,512]{1,0:T(8,128)S(1)}, f32[64,512]{1,0:T(8,128)S(1)}, u32[]{:S(2)}, u32[]{:S(2)}) %collective-permute-start.24) | collective-permute-done | bytes 131104 | tf_op jit(solution)/shard_map/ppermute | solution.py:303
  161.2 2.0 %collective-permute-done.23 = f32[64,512]{1,0:T(8,128)S(1)} collective-permute-done((f32[64,512]{1,0:T(8,128)S(1)}, f32[64,512]{1,0:T(8,128)S(1)}, u32[]{:S(2)}, u32[]{:S(2)}) %collective-permute-start.23) | collective-permute-done | bytes 131104 | tf_op jit(solution)/shard_map/ppermute | solution.py:303
  163.3 0.7 add_add_fusion
  (85 shorter events, 2.7 us)
Async XLA Ops:
  7.2 1.0 copy-start.2
  7.2 4.7 %copy-start = (bf16[1,8,16,1024]{3,2,1,0:T(8,128)(2,1)S(1)}, bf16[1,8,16,1024]{3,2,1,0:T(8,128)(2,1)}, u32[]{:S(2)}) copy-start(bf16[1,8,16,1024]{3,2,1,0:T(8,128)(2,1)} %param.5) | copy-start | bytes 786436
  7.2 39.9 %all-gather.2.cloned.1.call-start = ((), (), s32[]{:S(2)}) async-start(), calls=%async_computation | async-start | bytes 9437184 | tf_op jit(solution)/shard_map/all_gather | solution.py:258
  7.9 10.7 %copy-start.3 = (bf16[512,1024]{1,0:T(8,128)(2,1)S(1)}, bf16[512,1024]{1,0:T(8,128)(2,1)}, u32[]{:S(2)}) copy-start(bf16[512,1024]{1,0:T(8,128)(2,1)} %param.9) | copy-start | bytes 3145732
  7.9 10.8 %copy-start.9 = (s32[64,32]{0,1:T(8,128)S(1)}, s32[64,32]{0,1:T(8,128)}, u32[]{:S(2)}) copy-start(s32[64,32]{0,1:T(8,128)} %param.7) | copy-start | bytes 24580
  8.9 23.9 %collective-permute-start.19 = (bf16[128,512]{1,0:T(8,128)(2,1)S(1)}, bf16[128,512]{1,0:T(8,128)(2,1)S(1)}, u32[]{:S(2)}, u32[]{:S(2)}) collective-permute-start(bf16[128,512]{1,0:T(8,128)(2,1)S(1)} %bitcast.77), channel_id=1, source_target_pairs={{0,1},{1,0},{2,3},{3,2},{4,5},{5,4},{6,7},{7,6},{8,9},{9,8},{10,11... | collective-permute-start | bytes 393224 | tf_op jit(solution)/shard_map/ppermute | solution.py:215
  12.6 8.3 %collective-permute-start = (bf16[6,6,1024]{2,1,0:T(8,128)(2,1)}, bf16[6,6,1024]{2,1,0:T(8,128)(2,1)S(1)}, u32[]{:S(2)}, u32[]{:S(2)}) collective-permute-start(bf16[6,6,1024]{2,1,0:T(8,128)(2,1)} %get-tuple-element.47), channel_id=1, source_target_pairs={{0,3},{1,2},{2,5},{3,4},{4,7},{5,6},{6,9},{7,8},{8,11},{9,10},{10,... | collective-permute-start | bytes 221192 | tf_op jit(solution)/shard_map/ppermute | solution.py:139
  16.0 11.0 %collective-permute-start.7 = (bf16[6,6,1024]{2,1,0:T(8,128)(2,1)}, bf16[6,6,1024]{2,1,0:T(8,128)(2,1)S(1)}, u32[]{:S(2)}, u32[]{:S(2)}) collective-permute-start(bf16[6,6,1024]{2,1,0:T(8,128)(2,1)} %get-tuple-element.48), channel_id=1, source_target_pairs={{2,1},{3,0},{4,3},{5,2},{6,5},{7,4},{8,7},{9,6},{10,9},{11,8},{12,... | collective-permute-start | bytes 221192 | tf_op jit(solution)/shard_map/ppermute | solution.py:139
  17.3 17.5 %collective-permute-start.5 = (bf16[6,6,1024]{2,1,0:T(8,128)(2,1)}, bf16[6,6,1024]{2,1,0:T(8,128)(2,1)S(1)}, u32[]{:S(2)}, u32[]{:S(2)}) collective-permute-start(bf16[6,6,1024]{2,1,0:T(8,128)(2,1)} %get-tuple-element.49), channel_id=1, source_target_pairs={{2,1},{3,0},{4,3},{5,2},{6,5},{7,4},{8,7},{9,6},{10,9},{11,8},{12,... | collective-permute-start | bytes 221192 | tf_op jit(solution)/shard_map/ppermute | solution.py:139
  18.6 25.9 %collective-permute-start.8 = (bf16[512,1024]{1,0:T(8,128)(2,1)S(1)}, bf16[512,1024]{1,0:T(8,128)(2,1)}, u32[]{:S(2)}, u32[]{:S(2)}) collective-permute-start(bf16[512,1024]{1,0:T(8,128)(2,1)S(1)} %copy-done.3), channel_id=1, source_target_pairs={{0,16},{16,0},{1,17},{17,1},{2,18},{18,2},{3,19},{19,3},{4,20},{20... | collective-permute-start | bytes 3145736 | tf_op jit(solution)/shard_map/ppermute | solution.py:196
  20.9 14.4 %collective-permute-start.2 = (bf16[6,6,1024]{2,1,0:T(8,128)(2,1)S(1)}, bf16[6,6,1024]{2,1,0:T(8,128)(2,1)S(1)}, u32[]{:S(2)}, u32[]{:S(2)}) collective-permute-start(bf16[6,6,1024]{2,1,0:T(8,128)(2,1)S(1)} %get-tuple-element.50), channel_id=1, source_target_pairs={{0,3},{1,2},{2,5},{3,4},{4,7},{5,6},{6,9},{7,8},{8,11},{9,10},{10,... | collective-permute-start | bytes 221192 | tf_op jit(solution)/shard_map/ppermute | solution.py:139
  27.0 15.9 %collective-permute-start.1 = (bf16[6,16,1024]{2,1,0:T(8,128)(2,1)S(1)}, bf16[6,16,1024]{2,1,0:T(8,128)(2,1)S(1)}, u32[]{:S(2)}, u32[]{:S(2)}) collective-permute-start(bf16[6,16,1024]{2,1,0:T(8,128)(2,1)S(1)} %get-tuple-element.51), channel_id=1, source_target_pairs={{0,2},{1,3},{2,4},{3,5},{4,6},{5,7},{6,8},{7,9},{8,10},{9,11},{10,... | collective-permute-start | bytes 589832 | tf_op jit(solution)/shard_map/ppermute | solution.py:139
  32.8 10.2 %collective-permute-start.6 = (bf16[6,16,1024]{2,1,0:T(8,128)(2,1)S(1)}, bf16[6,16,1024]{2,1,0:T(8,128)(2,1)S(1)}, u32[]{:S(2)}, u32[]{:S(2)}) collective-permute-start(bf16[6,16,1024]{2,1,0:T(8,128)(2,1)S(1)} %get-tuple-element.52), channel_id=1, source_target_pairs={{2,0},{3,1},{4,2},{5,3},{6,4},{7,5},{8,6},{9,7},{10,8},{11,9},{12,... | collective-permute-start | bytes 589832 | tf_op jit(solution)/shard_map/ppermute | solution.py:139
  34.8 8.1 %copy-start.8 = (bf16[6,6,1024]{2,1,0:T(8,128)(2,1)}, bf16[6,6,1024]{2,1,0:T(8,128)(2,1)S(1)}, u32[]{:S(2)}) copy-start(bf16[6,6,1024]{2,1,0:T(8,128)(2,1)S(1)} %collective-permute-done.5) | copy-start | bytes 221188
  34.8 6.4 %collective-permute-start.3 = (bf16[8,6,1024]{2,1,0:T(8,128)(2,1)S(1)}, bf16[8,6,1024]{2,1,0:T(8,128)(2,1)S(1)}, u32[]{:S(2)}, u32[]{:S(2)}) collective-permute-start(bf16[8,6,1024]{2,1,0:T(8,128)(2,1)S(1)} %get-tuple-element.53), channel_id=1, source_target_pairs={{0,1},{1,0},{2,3},{3,2},{4,5},{5,4},{6,7},{7,6},{8,9},{9,8},{10,11... | collective-permute-start | bytes 294920 | tf_op jit(solution)/shard_map/ppermute | solution.py:139
  35.4 7.6 %collective-permute-start.4 = (bf16[8,6,1024]{2,1,0:T(8,128)(2,1)S(1)}, bf16[8,6,1024]{2,1,0:T(8,128)(2,1)S(1)}, u32[]{:S(2)}, u32[]{:S(2)}) collective-permute-start(bf16[8,6,1024]{2,1,0:T(8,128)(2,1)S(1)} %get-tuple-element.54), channel_id=1, source_target_pairs={{0,1},{1,0},{2,3},{3,2},{4,5},{5,4},{6,7},{7,6},{8,9},{9,8},{10,11... | collective-permute-start | bytes 294920 | tf_op jit(solution)/shard_map/ppermute | solution.py:139
  41.2 81.3 %collective-permute-start.20 = (bf16[2,128,512]{2,1,0:T(8,128)(2,1)}, bf16[2,128,512]{2,1,0:T(8,128)(2,1)}, u32[]{:S(2)}, u32[]{:S(2)}) collective-permute-start(bf16[2,128,512]{2,1,0:T(8,128)(2,1)} %maximum_select_fusion.6), channel_id=1, source_target_pairs={{0,16},{16,0},{1,17},{17,1},{2,18},{18,2},{3,19},{19,3},{4,20},{20... | collective-permute-start | bytes 786440 | tf_op jit(solution)/shard_map/ppermute | solution.py:226
  74.2 4.5 %copy-start.1 = (f32[640,1024]{1,0:T(8,128)S(1)}, f32[640,1024]{1,0:T(8,128)}, u32[]{:S(2)}) copy-start(f32[640,1024]{1,0:T(8,128)} %get-tuple-element.8) | copy-start | bytes 7864324
  78.6 2.6 %copy-start.7 = (bf16[128,1024]{1,0:T(8,128)(2,1)S(1)}, bf16[128,1024]{1,0:T(8,128)(2,1)}, u32[]{:S(2)}) copy-start(bf16[128,1024]{1,0:T(8,128)(2,1)} %get-tuple-element.9) | copy-start | bytes 786436
  82.2 10.8 %copy-start.4 = (bf16[6,6,1024]{2,1,0:T(8,128)(2,1)S(1)}, bf16[6,6,1024]{2,1,0:T(8,128)(2,1)}, u32[]{:S(2)}) copy-start(bf16[6,6,1024]{2,1,0:T(8,128)(2,1)} %get-tuple-element.12) | copy-start | bytes 221188
  82.2 10.8 %copy-start.5 = (bf16[6,6,1024]{2,1,0:T(8,128)(2,1)S(1)}, bf16[6,6,1024]{2,1,0:T(8,128)(2,1)}, u32[]{:S(2)}) copy-start(bf16[6,6,1024]{2,1,0:T(8,128)(2,1)} %get-tuple-element.16) | copy-start | bytes 221188
  82.4 10.6 %collective-permute-start.17 = (bf16[128,512]{0,1:T(8,128)(2,1)S(1)}, bf16[128,512]{0,1:T(8,128)(2,1)S(1)}, u32[]{:S(2)}, u32[]{:S(2)}) collective-permute-start(bf16[128,512]{0,1:T(8,128)(2,1)S(1)} %bitcast.78), channel_id=1, source_target_pairs={{0,16},{16,0},{1,17},{17,1},{2,18},{18,2},{3,19},{19,3},{4,20},{20... | collective-permute-start | bytes 393224 | tf_op jit(solution)/shard_map/ppermute | solution.py:215
  83.5 38.4 %collective-permute-start.13 = (bf16[8,6,2048]{2,1,0:T(8,128)(2,1)S(1)}, bf16[8,6,2048]{2,1,0:T(8,128)(2,1)S(1)}, u32[]{:S(2)}, u32[]{:S(2)}) collective-permute-start(bf16[8,6,2048]{2,1,0:T(8,128)(2,1)S(1)} %pad_maximum_fusion.3), channel_id=1, source_target_pairs={{0,1},{1,0},{2,3},{3,2},{4,5},{5,4},{6,7},{7,6},{8,9},{9,8},{10,11... | collective-permute-start | bytes 589832 | tf_op jit(solution)/shard_map/ppermute | solution.py:139
  84.9 37.5 %collective-permute-start.12 = (bf16[8,6,2048]{2,1,0:T(8,128)(2,1)S(1)}, bf16[8,6,2048]{2,1,0:T(8,128)(2,1)S(1)}, u32[]{:S(2)}, u32[]{:S(2)}) collective-permute-start(bf16[8,6,2048]{2,1,0:T(8,128)(2,1)S(1)} %pad_maximum_fusion.2), channel_id=1, source_target_pairs={{0,1},{1,0},{2,3},{3,2},{4,5},{5,4},{6,7},{7,6},{8,9},{9,8},{10,11... | collective-permute-start | bytes 589832 | tf_op jit(solution)/shard_map/ppermute | solution.py:139
  87.5 16.3 %collective-permute-start.11 = (bf16[6,6,2048]{2,1,0:T(8,128)(2,1)S(1)}, bf16[6,6,2048]{2,1,0:T(8,128)(2,1)S(1)}, u32[]{:S(2)}, u32[]{:S(2)}) collective-permute-start(bf16[6,6,2048]{2,1,0:T(8,128)(2,1)S(1)} %pad_maximum_fusion.5), channel_id=1, source_target_pairs={{2,1},{3,0},{4,3},{5,2},{6,5},{7,4},{8,7},{9,6},{10,9},{11,8},{12,... | collective-permute-start | bytes 442376 | tf_op jit(solution)/shard_map/ppermute | solution.py:139
  93.0 12.4 %collective-permute-start.14 = (bf16[6,6,2048]{2,1,0:T(8,128)(2,1)S(1)}, bf16[6,6,2048]{2,1,0:T(8,128)(2,1)S(1)}, u32[]{:S(2)}, u32[]{:S(2)}) collective-permute-start(bf16[6,6,2048]{2,1,0:T(8,128)(2,1)S(1)} %pad_maximum_fusion.6), channel_id=1, source_target_pairs={{0,3},{1,2},{2,5},{3,4},{4,7},{5,6},{6,9},{7,8},{8,11},{9,10},{10,... | collective-permute-start | bytes 442376 | tf_op jit(solution)/shard_map/ppermute | solution.py:139
  103.9 5.6 %collective-permute-start.16 = (bf16[6,6,2048]{2,1,0:T(8,128)(2,1)S(1)}, bf16[6,6,2048]{2,1,0:T(8,128)(2,1)S(1)}, u32[]{:S(2)}, u32[]{:S(2)}) collective-permute-start(bf16[6,6,2048]{2,1,0:T(8,128)(2,1)S(1)} %pad_maximum_fusion.7), channel_id=1, source_target_pairs={{0,3},{1,2},{2,5},{3,4},{4,7},{5,6},{6,9},{7,8},{8,11},{9,10},{10,... | collective-permute-start | bytes 442376 | tf_op jit(solution)/shard_map/ppermute | solution.py:139
  105.4 23.6 %copy-start.6 = (bf16[1,2,128,512]{3,2,1,0:T(8,128)(2,1)S(1)}, bf16[1,2,128,512]{3,2,1,0:T(8,128)(2,1)}, u32[]{:S(2)}) copy-start(bf16[1,2,128,512]{3,2,1,0:T(8,128)(2,1)} %maximum_select_fusion.5) | copy-start | bytes 786436
  105.4 15.1 %collective-permute-start.9 = (bf16[6,6,2048]{2,1,0:T(8,128)(2,1)S(1)}, bf16[6,6,2048]{2,1,0:T(8,128)(2,1)S(1)}, u32[]{:S(2)}, u32[]{:S(2)}) collective-permute-start(bf16[6,6,2048]{2,1,0:T(8,128)(2,1)S(1)} %pad_maximum_fusion.4), channel_id=1, source_target_pairs={{2,1},{3,0},{4,3},{5,2},{6,5},{7,4},{8,7},{9,6},{10,9},{11,8},{12,... | collective-permute-start | bytes 442376 | tf_op jit(solution)/shard_map/ppermute | solution.py:139
  109.4 30.8 %collective-permute-start.15 = (bf16[6,16,2048]{2,1,0:T(8,128)(2,1)S(1)}, bf16[6,16,2048]{2,1,0:T(8,128)(2,1)S(1)}, u32[]{:S(2)}, u32[]{:S(2)}) collective-permute-start(bf16[6,16,2048]{2,1,0:T(8,128)(2,1)S(1)} %pad_maximum_fusion.1), channel_id=1, source_target_pairs={{0,2},{1,3},{2,4},{3,5},{4,6},{5,7},{6,8},{7,9},{8,10},{9,11},{10,... | collective-permute-start | bytes 1179656 | tf_op jit(solution)/shard_map/ppermute | solution.py:139
  120.5 28.7 %collective-permute-start.10 = (bf16[6,16,2048]{2,1,0:T(8,128)(2,1)S(1)}, bf16[6,16,2048]{2,1,0:T(8,128)(2,1)S(1)}, u32[]{:S(2)}, u32[]{:S(2)}) collective-permute-start(bf16[6,16,2048]{2,1,0:T(8,128)(2,1)S(1)} %pad_maximum_fusion), channel_id=1, source_target_pairs={{2,0},{3,1},{4,2},{5,3},{6,4},{7,5},{8,6},{9,7},{10,8},{11,9},{12,... | collective-permute-start | bytes 1179656 | tf_op jit(solution)/shard_map/ppermute | solution.py:139
  121.8 7.1 %collective-permute-start.18 = (bf16[2,128,512]{1,2,0:T(8,128)(2,1)S(1)}, bf16[2,128,512]{1,2,0:T(8,128)(2,1)S(1)}, u32[]{:S(2)}, u32[]{:S(2)}) collective-permute-start(bf16[2,128,512]{1,2,0:T(8,128)(2,1)S(1)} %maximum_select_fusion.4), channel_id=1, source_target_pairs={{0,1},{1,0},{2,3},{3,2},{4,5},{5,4},{6,7},{7,6},{8,9},{9,8},{10,11... | collective-permute-start | bytes 786440 | tf_op jit(solution)/shard_map/ppermute | solution.py:226
  128.9 22.9 %slice-start = ((s8[6291456]{0:T(1024)(128)(4,1)}), s8[4194304]{0:T(1024)(128)(4,1)S(1)}, s32[]{:S(2)}) async-start(s8[6291456]{0:T(1024)(128)(4,1)} %bitcast.79), calls=%async_computation.1 | async-start | bytes 8388608
  130.7 20.4 %collective-permute-start.21 = (f32[64,512]{1,0:T(8,128)S(1)}, f32[64,512]{1,0:T(8,128)S(1)}, u32[]{:S(2)}, u32[]{:S(2)}) collective-permute-start(f32[64,512]{1,0:T(8,128)S(1)} %get-tuple-element.26), channel_id=1, source_target_pairs={{0,2},{2,4},{4,6},{6,8},{8,10},{10,12},{12,14},{14,0},{1,3},{3,5},... | collective-permute-start | bytes 393224 | tf_op jit(solution)/shard_map/ppermute | solution.py:303
  133.9 17.4 %collective-permute-start.27 = (f32[64,512]{1,0:T(8,128)S(1)}, f32[64,512]{1,0:T(8,128)S(1)}, u32[]{:S(2)}, u32[]{:S(2)}) collective-permute-start(f32[64,512]{1,0:T(8,128)S(1)} %get-tuple-element.27), channel_id=1, source_target_pairs={{0,14},{2,0},{4,2},{6,4},{8,6},{10,8},{12,10},{14,12},{1,15},{3,1}... | collective-permute-start | bytes 393224 | tf_op jit(solution)/shard_map/ppermute | solution.py:303
  138.2 16.5 %collective-permute-start.26 = (f32[64,512]{1,0:T(8,128)S(1)}, f32[64,512]{1,0:T(8,128)S(1)}, u32[]{:S(2)}, u32[]{:S(2)}) collective-permute-start(f32[64,512]{1,0:T(8,128)S(1)} %get-tuple-element.28), channel_id=1, source_target_pairs={{0,12},{2,14},{4,0},{6,2},{8,4},{10,6},{12,8},{14,10},{1,13},{3,15... | collective-permute-start | bytes 393224 | tf_op jit(solution)/shard_map/ppermute | solution.py:303
  140.2 11.6 %slice-start.1 = ((s8[6291456]{0:T(1024)(128)(4,1)}), s8[2097152]{0:T(1024)(128)(4,1)S(1)}, s32[]{:S(2)}) async-start(s8[6291456]{0:T(1024)(128)(4,1)} %bitcast.79), calls=%async_computation.2 | async-start | bytes 4194304
  140.2 14.5 %collective-permute-start.25 = (f32[64,512]{1,0:T(8,128)S(1)}, f32[64,512]{1,0:T(8,128)S(1)}, u32[]{:S(2)}, u32[]{:S(2)}) collective-permute-start(f32[64,512]{1,0:T(8,128)S(1)} %get-tuple-element.29), channel_id=1, source_target_pairs={{0,10},{2,12},{4,14},{6,0},{8,2},{10,4},{12,6},{14,8},{1,11},{3,13... | collective-permute-start | bytes 393224 | tf_op jit(solution)/shard_map/ppermute | solution.py:303
  149.2 12.1 %collective-permute-start.24 = (f32[64,512]{1,0:T(8,128)S(1)}, f32[64,512]{1,0:T(8,128)S(1)}, u32[]{:S(2)}, u32[]{:S(2)}) collective-permute-start(f32[64,512]{1,0:T(8,128)S(1)} %get-tuple-element.30), channel_id=1, source_target_pairs={{0,8},{2,10},{4,12},{6,14},{8,0},{10,2},{12,4},{14,6},{1,9},{3,11}... | collective-permute-start | bytes 393224 | tf_op jit(solution)/shard_map/ppermute | solution.py:303
  149.6 2.2 %copy-start.10 = (bf16[128,1024]{1,0:T(8,128)(2,1)S(1)}, bf16[128,1024]{1,0:T(8,128)(2,1)}, u32[]{:S(2)}) copy-start(bf16[128,1024]{1,0:T(8,128)(2,1)} %get-tuple-element.6) | copy-start | bytes 786436
  151.1 12.1 %collective-permute-start.23 = (f32[64,512]{1,0:T(8,128)S(1)}, f32[64,512]{1,0:T(8,128)S(1)}, u32[]{:S(2)}, u32[]{:S(2)}) collective-permute-start(f32[64,512]{1,0:T(8,128)S(1)} %get-tuple-element.31), channel_id=1, source_target_pairs={{0,6},{2,8},{4,10},{6,12},{8,14},{10,0},{12,2},{14,4},{1,7},{3,9},... | collective-permute-start | bytes 393224 | tf_op jit(solution)/shard_map/ppermute | solution.py:303
  151.2 12.0 %collective-permute-start.22 = (f32[64,512]{1,0:T(8,128)S(1)}, f32[64,512]{1,0:T(8,128)S(1)}, u32[]{:S(2)}, u32[]{:S(2)}) collective-permute-start(f32[64,512]{1,0:T(8,128)S(1)} %get-tuple-element.32), channel_id=1, source_target_pairs={{0,4},{2,6},{4,8},{6,10},{8,12},{10,14},{12,0},{14,2},{1,5},{3,7},... | collective-permute-start | bytes 393224 | tf_op jit(solution)/shard_map/ppermute | solution.py:303
Sparse Core Ops, SparseCore 0:
  9.6 19.4 all-gather.1

commit v3 on v2

--- a/solution.py
+++ b/solution.py
@@ -228,6 +228,59 @@
     return lax.all_gather(value, axis, axis=0, tiled=False)
 
 
+def swap(value, axis):
+    return lax.ppermute(value, axis, [(0, 1), (1, 0)])
+
+
+def columns(value, index, size):
+    return lax.dynamic_slice_in_dim(value, index * size, size, axis=1)
+
+
+def split_rows(joined, shapes):
+    out = []
+    offset = 0
+    for shape in shapes:
+        count = 1
+        for extent in shape[:-1]:
+            count *= extent
+        count = count * shape[-1] // joined.shape[-1]
+        out.append(joined[offset : offset + count].reshape(shape))
+        offset += count
+    return out
+
+
+def join_rows(parts, lanes):
+    return jnp.concatenate([p.reshape(-1, lanes) for p in parts], axis=0)
+
+
+def lat_return(ext_list, height, radius):
+    owns = []
+    tops = join_rows([ext[:radius] for ext in ext_list], ext_list[0].shape[-1])
+    bottoms = join_rows([ext[radius + height :] for ext in ext_list], ext_list[0].shape[-1])
+    shapes = [ext[:radius].shape for ext in ext_list]
+    from_below = split_rows(shifted(tops.astype(jnp.bfloat16), "lat", -1), shapes)
+    from_above = split_rows(shifted(bottoms.astype(jnp.bfloat16), "lat", 1), shapes)
+    for ext, below, above in zip(ext_list, from_below, from_above):
+        middle = (
+            ext[radius : radius + height]
+            + jnp.pad(below.astype(jnp.float32), ((height - radius, 0), (0, 0), (0, 0)))
+            + jnp.pad(above.astype(jnp.float32), ((0, height - radius), (0, 0), (0, 0)))
+        )
+        owns.append(middle)
+    return owns
+
+
+def add_lon_rims(mid_list, from_right, from_left, breadth, radius):
+    owns = []
+    for mid, right, left in zip(mid_list, from_right, from_left):
+        owns.append(
+            mid[:, radius : radius + breadth]
+            + jnp.pad(right.astype(jnp.float32), ((0, 0), (breadth - radius, 0), (0, 0)))
+            + jnp.pad(left.astype(jnp.float32), ((0, 0), (0, breadth - radius), (0, 0)))
+        )
+    return owns
+
+
 def shards(tokens, cotangent, valid_cells, w_qkv, w_out):
     inputs_here = tokens[0]
     grad_here = cotangent[0]
@@ -246,17 +299,56 @@
     rows_half = width // dp_count
     cols_block = width // lon_count
     rows_block = rows_half // lat_count
-
-    tok_ext = halo_gather(inputs_here, radius)
+    dp_index = lax.axis_index("dp")
+    lon_index = lax.axis_index("lon")
+    fast = dp_count == 2 and lon_count == 2
+
+    panels = lax.all_gather(w_qkv, "dp", axis=0, tiled=True)
+
+    if fast:
+        dp_got = swap(jnp.concatenate([w_out, flat_grad], axis=0), "dp")
+        w_out_other = dp_got[: w_out.shape[0]]
+        cot_dp = dp_got[w_out.shape[0] :]
+        cot_send = jnp.concatenate(
+            [columns(flat_grad, 1 - lon_index, cols_block), columns(cot_dp, 1 - lon_index, cols_block)],
+            axis=0,
+        )
+        first = inputs_here[:, :radius]
+        last = inputs_here[:, breadth - radius :]
+        lon_got = swap(join_rows([last, first, cot_send], width), "lon")
+        its_last, its_first, cot_lon = split_rows(
+            lon_got, [last.shape, first.shape, cot_send.shape]
+        )
+        tok_lon = jnp.concatenate([its_last, inputs_here, its_first], axis=1)
+        cot_group = jnp.concatenate(
+            [
+                columns(flat_grad, lon_index, cols_block),
+                columns(cot_dp, lon_index, cols_block),
+                cot_lon,
+            ],
+            axis=0,
+        )
+        mine_part = lax.dot_general(flat_grad, w_out, TRANS_B, preferred_element_type=jnp.float32)
+        other_part = lax.dot_general(
+            flat_grad, w_out_other, TRANS_B, preferred_element_type=jnp.float32
+        )
+        mine_part = mine_part.astype(jnp.bfloat16)
+        other_part = other_part.astype(jnp.bfloat16)
+        grad_attn = jnp.where(
+            dp_index == 0,
+            jnp.concatenate([mine_part, other_part], axis=1),
+            jnp.concatenate([other_part, mine_part], axis=1),
+        )
+    else:
+        tok_lon = extended(inputs_here, (("lon", 1),), radius, True)
+        cot_blocks = flat_grad.reshape(token_count, lon_count, cols_block).transpose(1, 0, 2)
+        cot_lon = exchange_blocks(cot_blocks, "lon")
+        cot_group = gather_members(cot_lon, "dp").reshape(-1, cols_block)
+        grad_attn = partner_rows_product(flat_grad, w_out, "dp")
+
+    tok_ext = extended(tok_lon, (("lat", 0),), radius, False)
     tok_ext = jnp.pad(tok_ext, ((0, 0), (0, pad_cols - ext_cols), (0, 0)))
     tok_ext = tok_ext.reshape(key_count, width)
-
-    cot_blocks = flat_grad.reshape(token_count, lon_count, cols_block).transpose(1, 0, 2)
-    cot_lon = exchange_blocks(cot_blocks, "lon")
-    cot_group = gather_members(cot_lon, "dp")
-
-    panels = lax.all_gather(w_qkv, "dp", axis=0, tiled=True)
-    grad_attn = partner_rows_product(flat_grad, w_out, "dp")
 
     query = jnp.dot(flat_inputs, panels[:, :width], preferred_element_type=jnp.float32)
     query = query.astype(jnp.bfloat16)
@@ -269,7 +361,7 @@
     framed = jnp.pad(wrapped, ((radius, radius), (0, 0)))
     valid_ext = lax.dynamic_slice(
         framed,
-        (lax.axis_index("lat") * height, lax.axis_index("lon") * breadth),
+        (lax.axis_index("lat") * height, lon_index * breadth),
         (ext_rows, ext_cols),
     )
     valid_ext = jnp.pad(valid_ext, ((0, 0), (0, pad_cols - ext_cols))).reshape(1, key_count)
@@ -285,27 +377,39 @@
         query, key_values, grad_attn, allowed, HEADS
     )
 
-    att_blocks = attended.reshape(token_count, dp_count, rows_half).transpose(1, 0, 2)
-    att_dp = exchange_blocks(att_blocks, "dp")
-    att_group = gather_members(att_dp, "lon")
-    att_group = att_group.transpose(1, 0, 2, 3).reshape(-1, rows_half)
-    cot_group = cot_group.reshape(-1, cols_block)
+    grad_k_ext = grad_keys.reshape(ext_rows, pad_cols, width)[:, :ext_cols]
+    grad_v_ext = grad_values.reshape(ext_rows, pad_cols, width)[:, :ext_cols]
+    mids = lat_return([grad_k_ext, grad_v_ext], height, radius)
+    lefts = [mid[:, :radius] for mid in mids]
+    rights = [mid[:, radius + breadth :] for mid in mids]
+
+    if fast:
+        own_att = columns(attended, dp_index, rows_half)
+        att_from_dp = swap(columns(attended, 1 - dp_index, rows_half), "dp")
+        att_dp = jnp.concatenate([own_att, att_from_dp], axis=0)
+        lanes = 2 * width
+        rim_parts = [p.astype(jnp.bfloat16) for p in lefts + rights]
+        got = swap(join_rows(rim_parts + [att_dp], lanes), "lon")
+        pieces = split_rows(got, [p.shape for p in rim_parts] + [att_dp.shape])
+        from_right = pieces[:2]
+        from_left = pieces[2:4]
+        att_group = jnp.concatenate([att_dp, pieces[4]], axis=0)
+    else:
+        from_right = [passed_along(p.astype(jnp.bfloat16), "lon", -1) for p in lefts]
+        from_left = [passed_along(p.astype(jnp.bfloat16), "lon", 1) for p in rights]
+        att_blocks = attended.reshape(token_count, dp_count, rows_half).transpose(1, 0, 2)
+        att_dp = exchange_blocks(att_blocks, "dp")
+        att_group = gather_members(att_dp, "lon")
+        att_group = att_group.transpose(1, 0, 2, 3).reshape(-1, rows_half)
+    grad_k_own, grad_v_own = add_lon_rims(mids, from_right, from_left, breadth, radius)
+
     device_count = dp_count * lat_count * lon_count
     partial = lax.dot_general(
         att_group, cot_group, (((0,), (0,)), ((), ())), preferred_element_type=jnp.float32
     ) * (1.0 / device_count)
-    lat_index = lax.axis_index("lat")
-    total = lax.dynamic_slice_in_dim(partial, lat_index * rows_block, rows_block, axis=0)
-    for shift in range(1, lat_count):
-        target = (lat_index + shift) % lat_count
-        piece = lax.dynamic_slice_in_dim(partial, target * rows_block, rows_block, axis=0)
-        pairs = [(i, (i + shift) % lat_count) for i in range(lat_count)]
-        total = total + lax.ppermute(piece, "lat", pairs)
-    d_w_out = total
-
-    grad_k_ext = grad_keys.reshape(ext_rows, pad_cols, width)[:, :ext_cols]
-    grad_v_ext = grad_values.reshape(ext_rows, pad_cols, width)[:, :ext_cols]
-    grad_k_own, grad_v_own = halo_return([grad_k_ext, grad_v_ext], height, breadth, radius)
+    spread = lax.all_to_all(partial, "lat", 0, 0, tiled=True)
+    d_w_out = spread.reshape(lat_count, rows_block, cols_block).sum(axis=0)
+
     grad_proj = jnp.concatenate(
         [
             grad_query,

time: 172 us -> 190 us (1.10)
  waiting for transfers between devices: 30.5 us -> 72.6 us
  starting transfers between devices: 66.6 us -> 25.6 us
  local copies, waits for them, and re-layouts: 8.52 us -> 25.8 us
  matrix products: 15.8 us -> 18.4 us
  other arithmetic: 16.8 us -> 14.4 us
    ppermute x28 -> x8, starting transfers between devices: 66.5 us -> 16.6 us  [the longest x2 6.52 us: shifted(): return lax.ppermute(value, axis, pairs)]
    ppermute x28 -> x8, waiting for transfers between devices: 29.8 us -> 58 us  [the longest x4 24.6 us: swap(): return lax.ppermute(value, axis, [(0, 1), (1, 0)])]
    all_to_all x0 -> x1, waiting for transfers between devices: none -> 13.9 us  [shards(): spread = lax.all_to_all(partial, 'lat', 0, 0, tiled=True)]
    all_to_all x0 -> x1, starting transfers between devices: none -> 8.95 us  [shards(): spread = lax.all_to_all(partial, 'lat', 0, 0, tiled=True)]
    convert_element_type x0 -> x8, local copies, waits for them, and re-layouts: none -> 6.68 us  [the longest x2 2.86 us: lat_return(): below.astype(jnp.float32)]
    reshape x1 -> x16, local copies, waits for them, and re-layouts: 0.18 us -> 6.37 us  [the longest x12 6.04 us: join_rows(): return jnp.concatenate([p.reshape(-1, lanes) for p in parts], axis=0)]
    concatenate x9 -> x8, other arithmetic: 8.59 us -> 4.52 us  [the longest x3 3.92 us: join_rows(): return jnp.concatenate([p.reshape(-1, lanes) for p in parts], axis=0)]
    another operation x2 -> x4, other arithmetic: 2.28 us -> 6.04 us
  transfers between devices with their start and end apart: 29 -> 10, of which waited for: 8 -> 7; matrix products, arithmetic and copies ran while one was open for 24% -> 14% of each run, Pallas kernels for 11% -> 0%
where the time goes in v3:
time: 190 us; the launch traced here: 189 us
  waiting for transfers between devices  72.6 us (38%)
  local copies, waits for them, and re-layouts  25.8 us (14%)
  starting transfers between devices  25.6 us (13%)
  matrix products  18.4 us (10%)
  Pallas kernels  18 us (9%)
  between operations  14.5 us (8%)
  other arithmetic  14.4 us (8%)
    ppermute x4, waiting for transfers between devices, swap(): return lax.ppermute(value, axis, [(0, 1), (1, 0)])  24.6 us
    ppermute x2, waiting for transfers between devices, shifted(): return lax.ppermute(value, axis, pairs)  21 us
    pallas_call x1, Pallas kernels, block_attention(): pl.pallas_call(kernel, grid=(pairs,), in_specs=[pl.BlockSpec((queries, la...  18 us
    all_to_all x1, waiting for transfers between devices, shards(): spread = lax.all_to_all(partial, 'lat', 0, 0, tiled=True)  13.9 us
    ppermute x1, waiting for transfers between devices, extended(): lax.ppermute(lax.slice_in_dim(block, block.shape[dim] - width, None, axis...  12.4 us
    all_to_all x1, starting transfers between devices, shards(): spread = lax.all_to_all(partial, 'lat', 0, 0, tiled=True)  8.95 us
    ppermute x2, starting transfers between devices, shifted(): return lax.ppermute(value, axis, pairs)  6.52 us
    dot_general x1, matrix products, shards(): jnp.dot(tok_ext, panels[:, width:], preferred_element_type=jnp.float32)  6.3 us
  transfers between devices with their start and end apart: 10, of which 7 were waited for; matrix products, arithmetic and copies ran while one was open for 14% of the time, Pallas kernels for 0%

profile of v3, /device:TPU:0, one launch (start us, length us, event | category | flops | bytes accessed | tf_op | source)
XLA Modules:
  0.0 189.2 jit_solution(10916037629209599016)
XLA Ops:
  7.2 0.7 all-gather.2.cloned.1.call-update
  7.9 0.5 copy-done.1
  8.4 0.1 pad_maximum_fusion
  8.5 0.5 collective-permute-start
  9.1 0.1 copy.11
  9.2 0.1 copy.13
  9.8 0.7 constant_dynamic-slice_fusion.1
  10.4 1.4 collective-permute-done
  11.8 1.0 slice.155
  12.8 0.7 constant_dynamic-slice_fusion
  13.5 0.1 reshape.162
  13.7 2.9 %collective-permute-start.1 = (bf16[224,1024]{1,0:T(8,128)(2,1)S(1)}, bf16[224,1024]{1,0:T(8,128)(2,1)S(1)}, u32[]{:S(2)}, u32[]{:S(2)}) collective-permute-start(bf16[224,1024]{1,0:T(8,128)(2,1)S(1)} %pad_maximum_fusion.4), channel_id=1, source_target_pairs={{0,1},{1,0},{2,3},{3,2},{4,5},{5,4},{6,7},{7,6},{8,9},{9,8},{10,11... | collective-permute-start | bytes 1376264 | tf_op jit(solution)/shard_map/ppermute | solution.py:232
  16.6 1.0 fusion.46.allow_ref
  17.6 0.5 convolution_convert_fusion.2
  18.1 9.3 %collective-permute-done.1 = bf16[224,1024]{1,0:T(8,128)(2,1)S(1)} collective-permute-done((bf16[224,1024]{1,0:T(8,128)(2,1)S(1)}, bf16[224,1024]{1,0:T(8,128)(2,1)S(1)}, u32[]{:S(2)}, u32[]{:S(2)}) %collective-permute-start.1) | collective-permute-done | bytes 458784 | tf_op jit(solution)/shard_map/ppermute | solution.py:232
  27.4 0.7 copy-done.7
  28.3 0.2 pad_maximum_fusion.3
  28.5 3.7 %collective-permute-start.2 = (bf16[6,28,1024]{2,1,0:T(8,128)(2,1)S(1)}, bf16[6,28,1024]{2,1,0:T(8,128)(2,1)S(1)}, u32[]{:S(2)}, u32[]{:S(2)}) collective-permute-start(bf16[6,28,1024]{2,1,0:T(8,128)(2,1)S(1)} %get-tuple-element.30), channel_id=1, source_target_pairs={{0,2},{2,4},{4,6},{6,8},{8,10},{10,12},{12,14},{1,3},{3,5},{5,7},{... | collective-permute-start | bytes 1032200 | tf_op jit(solution)/shard_map/ppermute | solution.py:34
  32.2 1.3 collective-permute-start.3
  33.5 1.7 fusion.19
  35.3 0.8 maximum_select_fusion.g_ref
  36.0 12.4 %collective-permute-done.2 = bf16[6,28,1024]{2,1,0:T(8,128)(2,1)S(1)} collective-permute-done((bf16[6,28,1024]{2,1,0:T(8,128)(2,1)S(1)}, bf16[6,28,1024]{2,1,0:T(8,128)(2,1)S(1)}, u32[]{:S(2)}, u32[]{:S(2)}) %collective-permute-start.2) | collective-permute-done | bytes 344096 | tf_op jit(solution)/shard_map/ppermute | solution.py:34
  48.5 0.3 fusion.13
  48.8 2.7 %fusion.16.q_ref = bf16[128,1024]{1,0:T(8,128)(2,1)} fusion(bf16[128,1024]{1,0:T(8,128)(2,1)S(1)} %bitcast.29, bf16[1024,3072]{1,0:T(8,128)(2,1)} %all-gather.2.cloned.1.call-done), kind=kOutput, calls=%fused_computation.17 | convolution fusion | flops 268566528 | bytes 2621440 | tf_op jit(solution)/shard_map/dot_general | solution.py:353
  51.5 6.3 %fusion.2.k_ref.v_ref = bf16[640,2048]{1,0:T(8,128)(2,1)} fusion(bf16[640,1024]{1,0:T(8,128)(2,1)S(1)} %bitcast.30, bf16[1024,3072]{1,0:T(8,128)(2,1)} %all-gather.2.cloned.1.call-done), kind=kOutput, calls=%fused_computation.2 | convolution fusion | flops 2685665280 | bytes 8126464 | tf_op jit(solution)/shard_map/dot_general | solution.py:355
  57.8 18.0 %block_attention.1 = (bf16[128,1024]{1,0:T(8,128)(2,1)}, bf16[128,1024]{1,0:T(8,128)(2,1)}, f32[640,1024]{1,0:T(8,128)}, f32[640,1024]{1,0:T(8,128)}) custom-call(bf16[128,1024]{1,0:T(8,128)(2,1)} %fusion.16.q_ref, bf16[640,2048]{1,0:T(8,128)(2,1)} %fusion.2.k_ref.v_ref, bf16[640,2048]{1,0:T(8,128)(2,1)} %fusion.2.k_ref.v_ref, ...), custom_call_target="tpu_custom_call" | custom-call | flops 2013265920 | bytes 9240576 | tf_op jit(solution)/shard_map/block_attention/pallas_call | solution.py:99
  75.8 2.1 %convert.48 = bf16[20,32,1024]{2,1,0:T(8,128)(2,1)S(1)} convert(f32[20,32,1024]{2,1,0:T(8,128)} %bitcast.20) | non-fusion elementwise | flops 655360 | bytes 3932160 | tf_op jit(solution)/shard_map/convert.39
  78.0 0.8 reshape.170
  78.8 0.2 convert.49
  79.0 0.8 fusion.65
  79.8 1.8 reshape.171
  81.6 2.0 %pad_maximum_fusion.2 = bf16[336,1024]{1,0:T(8,128)(2,1)} fusion(bf16[168,1024]{1,0:T(8,128)(2,1)} %reshape.171, bf16[168,1024]{1,0:T(8,128)(2,1)} %reshape.170), kind=kLoop, calls=%fused_computation.33 | loop fusion | flops 1376256 | bytes 1376256 | tf_op jit(solution)/shard_map/concatenate | solution.py:253
  83.6 5.2 %collective-permute-start.5 = (bf16[336,1024]{1,0:T(8,128)(2,1)}, bf16[336,1024]{1,0:T(8,128)(2,1)}, u32[]{:S(2)}, u32[]{:S(2)}) collective-permute-start(bf16[336,1024]{1,0:T(8,128)(2,1)} %pad_maximum_fusion.2), channel_id=1, source_target_pairs={{0,2},{2,4},{4,6},{6,8},{8,10},{10,12},{12,14},{1,3},{3,5},{5,7},{... | collective-permute-start | bytes 2064392 | tf_op jit(solution)/shard_map/ppermute | solution.py:24
  88.8 0.8 reshape.167
  89.7 1.9 %pad_maximum_fusion.1 = bf16[336,1024]{1,0:T(8,128)(2,1)} fusion(bf16[168,1024]{1,0:T(8,128)(2,1)S(1)} %reshape.169, bf16[168,1024]{1,0:T(8,128)(2,1)} %reshape.167), kind=kLoop, calls=%fused_computation.32 | loop fusion | flops 1376256 | bytes 1376256 | tf_op jit(solution)/shard_map/concatenate | solution.py:253
  91.6 1.3 collective-permute-start.4
  93.0 1.3 collective-permute-done.6
  94.4 0.9 reshape.176
  95.3 21.0 %collective-permute-done.5 = bf16[336,1024]{1,0:T(8,128)(2,1)} collective-permute-done((bf16[336,1024]{1,0:T(8,128)(2,1)}, bf16[336,1024]{1,0:T(8,128)(2,1)}, u32[]{:S(2)}, u32[]{:S(2)}) %collective-permute-start.5) | collective-permute-done | bytes 688160 | tf_op jit(solution)/shard_map/ppermute | solution.py:24
  116.2 1.9 fusion.67
  118.2 1.0 convert_element_type.88
  119.2 2.0 %fusion.66 = (bf16[168,1024]{1,0:T(8,128)(2,1)}, bf16[168,1024]{1,0:T(8,128)(2,1)}) fusion(bf16[336,1024]{1,0:T(8,128)(2,1)} %collective-permute-done.4), kind=kLoop, calls=%fused_computation.104 | loop fusion | bytes 1376256 | tf_op jit(solution)/shard_map/slice | solution.py:247
  121.2 1.8 convert_element_type.85
  123.0 2.6 %fusion.62 = (bf16[8,28,1024]{2,1,0:T(8,128)(2,1)S(1)}, f32[8,28,1024]{2,1,0:T(8,128)}) fusion(bf16[6,28,1024]{2,1,0:T(8,128)(2,1)S(1)} %convert_element_type.86, bf16[6,28,1024]{2,1,0:T(8,128)(2,1)} %convert_element_type.85, f32[20,32,1024]{2,1,0:T(8,128)} %bitcast.21), kind=kLoop, calls=%fused_computation.101 | loop fusion | flops 1146880 | bytes 2981888 | tf_op jit(solution)/shard_map/convert.27
  125.7 0.7 reshape.174
  126.4 0.7 reshape.172
  127.1 1.0 convert_element_type.87
  128.1 1.2 fusion.60
  129.5 0.9 constant_dynamic-update-slice_fusion.4
  130.5 1.0 constant_dynamic-update-slice_fusion.2
  131.5 1.6 collective-permute-start.7
  133.1 12.5 %collective-permute-done.7 = bf16[160,2048]{1,0:T(8,128)(2,1)S(1)} collective-permute-done((bf16[160,2048]{1,0:T(8,128)(2,1)S(1)}, bf16[160,2048]{1,0:T(8,128)(2,1)S(1)}, u32[]{:S(2)}, u32[]{:S(2)}) %collective-permute-start.7) | collective-permute-done | bytes 655392 | tf_op jit(solution)/shard_map/ppermute | solution.py:232
  145.7 0.2 reshape.180
  145.9 1.5 convolution_multiply_fusion
  147.4 8.9 %all-to-all-start = ((f32[8,64,512]{2,1,0:T(8,128)}), f32[8,64,512]{2,1,0:T(8,128)S(1)}, u32[]{:S(2)}, u32[]{:S(2)}) async-start(f32[8,64,512]{2,1,0:T(8,128)} %bitcast.10), calls=%async_computation | async-start | bytes 2097152 | tf_op jit(solution)/shard_map/all_to_all | solution.py:410
  156.3 1.8 fusion.68
  158.2 1.0 convert_element_type.93
  159.2 0.7 convert_element_type.92
  159.9 1.0 convert_element_type.90
  160.9 1.1 fusion.29
  162.0 0.1 fusion.31
  162.1 5.7 %convolution_convert_fusion = bf16[128,1024]{1,0:T(8,128)(2,1)} fusion(bf16[1024,3072]{1,0:T(8,128)(2,1)} %all-gather.2.cloned.1.call-done, bf16[128,1024]{1,0:T(8,128)(2,1)S(1)} %bitcast.31, bf16[128,1024]{1,0:T(8,128)(2,1)S(1)} %bitcast.32, bf16[128,1024]{1,0:T(8,128)(2,1)S(1)} %copy-done.15), kind=kOutput, calls=%fused_computation.18 | convolution fusion | flops 807796736 | bytes 7340032 | tf_op jit(solution)/shard_map/dot_general | solution.py:421
  167.8 13.9 %all-to-all-done = f32[8,64,512]{2,1,0:T(8,128)S(1)} async-done(((f32[8,64,512]{2,1,0:T(8,128)}), f32[8,64,512]{2,1,0:T(8,128)S(1)}, u32[]{:S(2)}, u32[]{:S(2)}) %all-to-all-start) | async-done | bytes 1048608 | tf_op jit(solution)/shard_map/all_to_all | solution.py:410
  181.7 0.7 reduce_sum.9
  (69 shorter events, 1.6 us)
Async XLA Ops:
  7.2 1.2 copy-start.1
  7.2 1.3 copy-start.4
  7.2 41.6 %all-gather.2.cloned.1.call-start = ((), (), s32[]{:S(2)}) async-start(), calls=%async_computation.1 | async-start | bytes 9437184 | tf_op jit(solution)/shard_map/all_gather | solution.py:306
  7.9 1.1 copy-start.14
  7.9 1.7 copy-start.5
  8.5 3.3 %collective-permute-start = (bf16[640,1024]{1,0:T(8,128)(2,1)S(1)}, bf16[640,1024]{1,0:T(8,128)(2,1)}, u32[]{:S(2)}, u32[]{:S(2)}) collective-permute-start(bf16[640,1024]{1,0:T(8,128)(2,1)S(1)} %pad_maximum_fusion), channel_id=1, source_target_pairs={{0,16},{16,0},{1,17},{17,1},{2,18},{18,2},{3,19},{19,3},{4,20},{20... | collective-permute-start | bytes 3932168 | tf_op jit(solution)/shard_map/ppermute | solution.py:232
  13.7 13.7 %collective-permute-start.1 = (bf16[224,1024]{1,0:T(8,128)(2,1)S(1)}, bf16[224,1024]{1,0:T(8,128)(2,1)S(1)}, u32[]{:S(2)}, u32[]{:S(2)}) collective-permute-start(bf16[224,1024]{1,0:T(8,128)(2,1)S(1)} %pad_maximum_fusion.4), channel_id=1, source_target_pairs={{0,1},{1,0},{2,3},{3,2},{4,5},{5,4},{6,7},{7,6},{8,9},{9,8},{10,11... | collective-permute-start | bytes 1376264 | tf_op jit(solution)/shard_map/ppermute | solution.py:232
  27.4 0.8 copy-start.7
  28.5 19.9 %collective-permute-start.2 = (bf16[6,28,1024]{2,1,0:T(8,128)(2,1)S(1)}, bf16[6,28,1024]{2,1,0:T(8,128)(2,1)S(1)}, u32[]{:S(2)}, u32[]{:S(2)}) collective-permute-start(bf16[6,28,1024]{2,1,0:T(8,128)(2,1)S(1)} %get-tuple-element.30), channel_id=1, source_target_pairs={{0,2},{2,4},{4,6},{6,8},{8,10},{10,12},{12,14},{1,3},{3,5},{5,7},{... | collective-permute-start | bytes 1032200 | tf_op jit(solution)/shard_map/ppermute | solution.py:34
  32.2 16.2 %collective-permute-start.3 = (bf16[6,28,1024]{2,1,0:T(8,128)(2,1)S(1)}, bf16[6,28,1024]{2,1,0:T(8,128)(2,1)S(1)}, u32[]{:S(2)}, u32[]{:S(2)}) collective-permute-start(bf16[6,28,1024]{2,1,0:T(8,128)(2,1)S(1)} %get-tuple-element.31), channel_id=1, source_target_pairs={{2,0},{4,2},{6,4},{8,6},{10,8},{12,10},{14,12},{3,1},{5,3},{7,5},{... | collective-permute-start | bytes 1032200 | tf_op jit(solution)/shard_map/ppermute | solution.py:37
  75.8 2.9 %copy-start = (f32[640,1024]{1,0:T(8,128)S(1)}, f32[640,1024]{1,0:T(8,128)}, u32[]{:S(2)}) copy-start(f32[640,1024]{1,0:T(8,128)} %get-tuple-element.8) | copy-start | bytes 7864324
  83.6 32.7 %collective-permute-start.5 = (bf16[336,1024]{1,0:T(8,128)(2,1)}, bf16[336,1024]{1,0:T(8,128)(2,1)}, u32[]{:S(2)}, u32[]{:S(2)}) collective-permute-start(bf16[336,1024]{1,0:T(8,128)(2,1)} %pad_maximum_fusion.2), channel_id=1, source_target_pairs={{0,2},{2,4},{4,6},{6,8},{8,10},{10,12},{12,14},{1,3},{3,5},{5,7},{... | collective-permute-start | bytes 2064392 | tf_op jit(solution)/shard_map/ppermute | solution.py:24
  89.7 3.2 %copy-start.9 = (bf16[128,1024]{1,0:T(8,128)(2,1)S(1)}, bf16[128,1024]{1,0:T(8,128)(2,1)}, u32[]{:S(2)}) copy-start(bf16[128,1024]{1,0:T(8,128)(2,1)} %get-tuple-element.9) | copy-start | bytes 786436
  91.6 27.6 %collective-permute-start.4 = (bf16[336,1024]{1,0:T(8,128)(2,1)}, bf16[336,1024]{1,0:T(8,128)(2,1)}, u32[]{:S(2)}, u32[]{:S(2)}) collective-permute-start(bf16[336,1024]{1,0:T(8,128)(2,1)} %pad_maximum_fusion.1), channel_id=1, source_target_pairs={{2,0},{4,2},{6,4},{8,6},{10,8},{12,10},{14,12},{3,1},{5,3},{7,5},{... | collective-permute-start | bytes 2064392 | tf_op jit(solution)/shard_map/ppermute | solution.py:24
  92.9 1.4 collective-permute-start.6
  94.4 0.9 copy-start.12
  129.3 2.1 %copy-start.6 = (bf16[64,2048]{1,0:T(8,128)(2,1)S(1)}, bf16[64,2048]{1,0:T(8,128)(2,1)}, u32[]{:S(2)}) copy-start(bf16[64,2048]{1,0:T(8,128)(2,1)} %reshape.176) | copy-start | bytes 786436
  129.3 3.7 %slice-start = ((bf16[224,1024]{1,0:T(8,128)(2,1)}), bf16[128,1024]{1,0:T(8,128)(2,1)S(1)}, s32[]{:S(2)}) async-start(bf16[224,1024]{1,0:T(8,128)(2,1)} %copy-done.7), calls=%async_computation.2 | async-start | bytes 524288 | tf_op jit(solution)/shard_map/slice | solution.py:247
  130.4 15.4 %copy-start.10 = (bf16[128,512]{1,0:T(8,128)(2,1)S(1)}, bf16[128,512]{1,0:T(8,128)(2,1)}, u32[]{:S(2)}) copy-start(bf16[128,512]{1,0:T(8,128)(2,1)} %get-tuple-element.34) | copy-start | bytes 393220
  130.4 15.4 %copy-start.11 = (bf16[128,512]{1,0:T(8,128)(2,1)S(1)}, bf16[128,512]{1,0:T(8,128)(2,1)}, u32[]{:S(2)}) copy-start(bf16[128,512]{1,0:T(8,128)(2,1)} %get-tuple-element.36) | copy-start | bytes 393220
  130.4 15.4 %copy-start.13 = (bf16[128,512]{1,0:T(8,128)(2,1)S(1)}, bf16[128,512]{1,0:T(8,128)(2,1)}, u32[]{:S(2)}) copy-start(bf16[128,512]{1,0:T(8,128)(2,1)} %copy-done.12) | copy-start | bytes 393220
  131.5 14.2 %collective-permute-start.7 = (bf16[160,2048]{1,0:T(8,128)(2,1)S(1)}, bf16[160,2048]{1,0:T(8,128)(2,1)S(1)}, u32[]{:S(2)}, u32[]{:S(2)}) collective-permute-start(bf16[160,2048]{1,0:T(8,128)(2,1)S(1)} %constant_dynamic-update-slice_fusion), channel_id=1, source_target_pairs={{0,1},{1,0},{2,3},{3,2},{4,5},{5,4},{6,7},{7,6},{8,9},{9,8},{10,11... | collective-permute-start | bytes 1966088 | tf_op jit(solution)/shard_map/ppermute | solution.py:232
  145.6 1.7 copy-start.8
  147.4 13.5 %copy-start.3 = (f32[8,28,1024]{2,1,0:T(8,128)S(1)}, f32[8,28,1024]{2,1,0:T(8,128)}, u32[]{:S(2)}) copy-start(f32[8,28,1024]{2,1,0:T(8,128)} %get-tuple-element.11) | copy-start | bytes 2752516
  147.4 34.3 %all-to-all-start = ((f32[8,64,512]{2,1,0:T(8,128)}), f32[8,64,512]{2,1,0:T(8,128)S(1)}, u32[]{:S(2)}, u32[]{:S(2)}) async-start(f32[8,64,512]{2,1,0:T(8,128)} %bitcast.10), calls=%async_computation | async-start | bytes 2097152 | tf_op jit(solution)/shard_map/all_to_all | solution.py:410
  156.3 5.6 %copy-start.2 = (f32[8,28,1024]{2,1,0:T(8,128)S(1)}, f32[8,28,1024]{2,1,0:T(8,128)}, u32[]{:S(2)}) copy-start(f32[8,28,1024]{2,1,0:T(8,128)} %get-tuple-element.13) | copy-start | bytes 2752516
  160.9 1.2 copy-start.15
Sparse Core Ops, SparseCore 0:
  9.6 19.4 all-gather.1

commit v4 on v3

--- a/solution.py
+++ b/solution.py
@@ -147,18 +147,34 @@
     return slice(0, radius)
 
 
+def grouped_send(pieces, lanes):
+    lon_count = lax.axis_size("lon")
+    groups = {}
+    for index, (dl, db, value) in enumerate(pieces):
+        groups.setdefault((dl, db % lon_count), []).append(index)
+    out = [None] * len(pieces)
+    for (dl, db), members in groups.items():
+        values = [pieces[i][2] for i in members]
+        got = sent_to(join_rows(values, lanes), dl, db)
+        for i, piece in zip(members, split_rows(got, [v.shape for v in values])):
+            out[i] = piece
+    return out
+
+
 def halo_gather(block, radius):
-    height, breadth = block.shape[0], block.shape[1]
-    rows = []
+    height, breadth, lanes = block.shape
+    spots = []
+    pieces = []
     for da in (-1, 0, 1):
-        row = []
         for db in (-1, 0, 1):
             if da == 0 and db == 0:
-                row.append(block)
                 continue
             piece = block[part(height, radius, da, True), part(breadth, radius, db, True)]
-            row.append(sent_to(piece, -da, -db))
-        rows.append(jnp.concatenate(row, axis=1))
+            spots.append((da, db))
+            pieces.append((-da, -db, piece))
+    got = dict(zip(spots, grouped_send(pieces, lanes)))
+    got[(0, 0)] = block
+    rows = [jnp.concatenate([got[(da, db)] for db in (-1, 0, 1)], axis=1) for da in (-1, 0, 1)]
     return jnp.concatenate(rows, axis=0)
 
 
@@ -167,22 +183,27 @@
     col_slices = {-1: slice(0, radius), 0: slice(radius, radius + breadth), 1: slice(radius + breadth, None)}
     owns = [ext[row_slices[0], col_slices[0]] for ext in ext_list]
     widths = [ext.shape[-1] for ext in ext_list]
+    spots = []
+    pieces = []
     for da in (-1, 0, 1):
         for db in (-1, 0, 1):
             if da == 0 and db == 0:
                 continue
-            pieces = [ext[row_slices[da], col_slices[db]] for ext in ext_list]
-            joined = jnp.concatenate(pieces, axis=-1).astype(jnp.bfloat16)
-            got = sent_to(joined, da, db).astype(jnp.float32)
-            rs = part(height, radius, da, True)
-            cs = part(breadth, radius, db, True)
-            pad_rows = (rs.start, height - rs.stop)
-            pad_cols = (cs.start, breadth - cs.stop)
-            offset = 0
-            for index, width in enumerate(widths):
-                piece = got[..., offset : offset + width]
-                offset += width
-                owns[index] = owns[index] + jnp.pad(piece, (pad_rows, pad_cols, (0, 0)))
+            joined = jnp.concatenate(
+                [ext[row_slices[da], col_slices[db]] for ext in ext_list], axis=-1
+            ).astype(jnp.bfloat16)
+            spots.append((da, db))
+            pieces.append((da, db, joined))
+    for (da, db), got in zip(spots, grouped_send(pieces, sum(widths))):
+        rs = part(height, radius, da, True)
+        cs = part(breadth, radius, db, True)
+        pad_rows = (rs.start, height - rs.stop)
+        pad_cols = (cs.start, breadth - cs.stop)
+        offset = 0
+        for index, width in enumerate(widths):
+            piece = got[..., offset : offset + width].astype(jnp.float32)
+            offset += width
+            owns[index] = owns[index] + jnp.pad(piece, (pad_rows, pad_cols, (0, 0)))
     return owns
 
 
@@ -303,9 +324,8 @@
     lon_index = lax.axis_index("lon")
     fast = dp_count == 2 and lon_count == 2
 
-    panels = lax.all_gather(w_qkv, "dp", axis=0, tiled=True)
-
     if fast:
+        qkv_other = swap(w_qkv, "dp")
         dp_got = swap(jnp.concatenate([w_out, flat_grad], axis=0), "dp")
         w_out_other = dp_got[: w_out.shape[0]]
         cot_dp = dp_got[w_out.shape[0] :]
@@ -313,13 +333,7 @@
             [columns(flat_grad, 1 - lon_index, cols_block), columns(cot_dp, 1 - lon_index, cols_block)],
             axis=0,
         )
-        first = inputs_here[:, :radius]
-        last = inputs_here[:, breadth - radius :]
-        lon_got = swap(join_rows([last, first, cot_send], width), "lon")
-        its_last, its_first, cot_lon = split_rows(
-            lon_got, [last.shape, first.shape, cot_send.shape]
-        )
-        tok_lon = jnp.concatenate([its_last, inputs_here, its_first], axis=1)
+        cot_lon = swap(cot_send, "lon")
         cot_group = jnp.concatenate(
             [
                 columns(flat_grad, lon_index, cols_block),
@@ -339,21 +353,49 @@
             jnp.concatenate([mine_part, other_part], axis=1),
             jnp.concatenate([other_part, mine_part], axis=1),
         )
+
+        def project(rows, start, stop):
+            own = jnp.dot(
+                columns(rows, dp_index, rows_half), w_qkv[:, start:stop],
+                preferred_element_type=jnp.float32,
+            )
+            other = jnp.dot(
+                columns(rows, 1 - dp_index, rows_half), qkv_other[:, start:stop],
+                preferred_element_type=jnp.float32,
+            )
+            return (own + other).astype(jnp.bfloat16)
+
+        def back_project(grads):
+            own = lax.dot_general(grads, w_qkv, TRANS_B, preferred_element_type=jnp.float32)
+            other = lax.dot_general(grads, qkv_other, TRANS_B, preferred_element_type=jnp.float32)
+            own = own.astype(jnp.bfloat16)
+            other = other.astype(jnp.bfloat16)
+            return jnp.where(
+                dp_index == 0,
+                jnp.concatenate([own, other], axis=1),
+                jnp.concatenate([other, own], axis=1),
+            )
     else:
-        tok_lon = extended(inputs_here, (("lon", 1),), radius, True)
+        panels = lax.all_gather(w_qkv, "dp", axis=0, tiled=True)
         cot_blocks = flat_grad.reshape(token_count, lon_count, cols_block).transpose(1, 0, 2)
         cot_lon = exchange_blocks(cot_blocks, "lon")
         cot_group = gather_members(cot_lon, "dp").reshape(-1, cols_block)
         grad_attn = partner_rows_product(flat_grad, w_out, "dp")
 
-    tok_ext = extended(tok_lon, (("lat", 0),), radius, False)
+        def project(rows, start, stop):
+            out = jnp.dot(rows, panels[:, start:stop], preferred_element_type=jnp.float32)
+            return out.astype(jnp.bfloat16)
+
+        def back_project(grads):
+            out = lax.dot_general(grads, panels, TRANS_B, preferred_element_type=jnp.float32)
+            return out.astype(jnp.bfloat16)
+
+    tok_ext = halo_gather(inputs_here, radius)
     tok_ext = jnp.pad(tok_ext, ((0, 0), (0, pad_cols - ext_cols), (0, 0)))
     tok_ext = tok_ext.reshape(key_count, width)
 
-    query = jnp.dot(flat_inputs, panels[:, :width], preferred_element_type=jnp.float32)
-    query = query.astype(jnp.bfloat16)
-    key_values = jnp.dot(tok_ext, panels[:, width:], preferred_element_type=jnp.float32)
-    key_values = key_values.astype(jnp.bfloat16)
+    query = project(flat_inputs, 0, width)
+    key_values = project(tok_ext, width, 3 * width)
 
     wrapped = jnp.concatenate(
         [valid_cells[:, -radius:], valid_cells, valid_cells[:, :radius]], axis=1
@@ -379,36 +421,25 @@
 
     grad_k_ext = grad_keys.reshape(ext_rows, pad_cols, width)[:, :ext_cols]
     grad_v_ext = grad_values.reshape(ext_rows, pad_cols, width)[:, :ext_cols]
-    mids = lat_return([grad_k_ext, grad_v_ext], height, radius)
-    lefts = [mid[:, :radius] for mid in mids]
-    rights = [mid[:, radius + breadth :] for mid in mids]
+    grad_k_own, grad_v_own = halo_return([grad_k_ext, grad_v_ext], height, breadth, radius)
 
     if fast:
         own_att = columns(attended, dp_index, rows_half)
         att_from_dp = swap(columns(attended, 1 - dp_index, rows_half), "dp")
         att_dp = jnp.concatenate([own_att, att_from_dp], axis=0)
-        lanes = 2 * width
-        rim_parts = [p.astype(jnp.bfloat16) for p in lefts + rights]
-        got = swap(join_rows(rim_parts + [att_dp], lanes), "lon")
-        pieces = split_rows(got, [p.shape for p in rim_parts] + [att_dp.shape])
-        from_right = pieces[:2]
-        from_left = pieces[2:4]
-        att_group = jnp.concatenate([att_dp, pieces[4]], axis=0)
+        att_group = jnp.concatenate([att_dp, swap(att_dp, "lon")], axis=0)
     else:
-        from_right = [passed_along(p.astype(jnp.bfloat16), "lon", -1) for p in lefts]
-        from_left = [passed_along(p.astype(jnp.bfloat16), "lon", 1) for p in rights]
         att_blocks = attended.reshape(token_count, dp_count, rows_half).transpose(1, 0, 2)
         att_dp = exchange_blocks(att_blocks, "dp")
         att_group = gather_members(att_dp, "lon")
         att_group = att_group.transpose(1, 0, 2, 3).reshape(-1, rows_half)
-    grad_k_own, grad_v_own = add_lon_rims(mids, from_right, from_left, breadth, radius)
 
     device_count = dp_count * lat_count * lon_count
     partial = lax.dot_general(
         att_group, cot_group, (((0,), (0,)), ((), ())), preferred_element_type=jnp.float32
     ) * (1.0 / device_count)
-    spread = lax.all_to_all(partial, "lat", 0, 0, tiled=True)
-    d_w_out = spread.reshape(lat_count, rows_block, cols_block).sum(axis=0)
+    spread = lax.all_to_all(partial.astype(jnp.bfloat16), "lat", 0, 0, tiled=True)
+    d_w_out = spread.astype(jnp.float32).reshape(lat_count, rows_block, cols_block).sum(axis=0)
 
     grad_proj = jnp.concatenate(
         [
@@ -418,8 +449,7 @@
         ],
         axis=1,
     )
-    d_flat = lax.dot_general(grad_proj, panels, TRANS_B, preferred_element_type=jnp.float32)
-    d_input = d_flat.astype(jnp.bfloat16).reshape(1, height, breadth, width)
+    d_input = back_project(grad_proj).reshape(1, height, breadth, width)
     return (d_input, d_w_out)
 
 

time: 190 us -> 160 us (0.84)
  waiting for transfers between devices: 72.6 us -> 10.5 us
  local copies, waits for them, and re-layouts: 25.8 us -> 51.1 us
  between operations: 14.5 us -> 1.15 us
  starting transfers between devices: 25.6 us -> 38 us
  other arithmetic: 14.4 us -> 19.8 us
  matrix products: 18.4 us -> 20.3 us
    ppermute x4 -> x10, waiting for transfers between devices: 33.4 us -> 0.03 us  [sent_to(): return lax.ppermute(value, ('lat', 'lon'), grid_pairs(delta_lat, delta_lon))]
    ppermute x4 -> x10, starting transfers between devices: 11.5 us -> 31 us  [sent_to(): return lax.ppermute(value, ('lat', 'lon'), grid_pairs(delta_lat, delta_lon))]
    concatenate x1 -> x12, local copies, waits for them, and re-layouts: 0.02 us -> 17.9 us  [halo_return(): jnp.concatenate([ext[row_slices[da], col_slices[db]] for ext in ext_list]...]
    ppermute x4 -> x5, waiting for transfers between devices: 24.6 us -> 10.5 us  [swap(): return lax.ppermute(value, axis, [(0, 1), (1, 0)])]
    all_to_all x1, waiting for transfers between devices: 13.9 us -> 0.01 us  [shards(): lax.all_to_all(partial.astype(jnp.bfloat16), 'lat', 0, 0, tiled=True)]
    slice x6 -> x17, local copies, waits for them, and re-layouts: 1.07 us -> 13.3 us  [the longest x8 7.09 us: halo_return(): piece = got[..., offset:offset + width].astype(jnp.float32)]
    reshape x4 -> x12, local copies, waits for them, and re-layouts: 0.33 us -> 10.2 us  [split_rows(): out.append(joined[offset:offset + count].reshape(shape))]
    convert_element_type x8 -> x0, local copies, waits for them, and re-layouts: 6.68 us -> none  [the longest x2 2.86 us: lat_return(): below.astype(jnp.float32)]
  transfers between devices with their start and end apart: 10 -> 16, of which waited for: 7 -> 1; matrix products, arithmetic and copies ran while one was open for 14% -> 56% of each run, Pallas kernels for 0% -> 11%
where the time goes in v4:
time: 160 us; the launch traced here: 159 us
  local copies, waits for them, and re-layouts  51.1 us (32%)
  starting transfers between devices  38 us (24%)
  matrix products  20.3 us (13%)
  other arithmetic  19.8 us (12%)
  Pallas kernels  18.1 us (11%)
  waiting for transfers between devices  10.5 us (7%)
    ppermute x10, starting transfers between devices, sent_to(): return lax.ppermute(value, ('lat', 'lon'), grid_pairs(delta_lat, delta_lon))  31 us
    pallas_call x1, Pallas kernels, block_attention(): pl.pallas_call(kernel, grid=(pairs,), in_specs=[pl.BlockSpec((queries, la...  18.1 us
    concatenate x12, local copies, waits for them, and re-layouts, halo_return(): jnp.concatenate([ext[row_slices[da], col_slices[db]] for ext in ext_list]...  17.9 us
    ppermute x5, waiting for transfers between devices, swap(): return lax.ppermute(value, axis, [(0, 1), (1, 0)])  10.5 us
    reshape x12, local copies, waits for them, and re-layouts, split_rows(): out.append(joined[offset:offset + count].reshape(shape))  10.2 us
    slice x8, local copies, waits for them, and re-layouts, halo_return(): piece = got[..., offset:offset + width].astype(jnp.float32)  7.09 us
    dot_general x2, matrix products, project(): jnp.dot(columns(rows, 1 - dp_index, rows_half), qkv_other[:, start:stop],...  6.86 us
    slice x6, local copies, waits for them, and re-layouts, split_rows(): out.append(joined[offset:offset + count].reshape(shape))  5.81 us
  transfers between devices with their start and end apart: 16, of which 1 were waited for; matrix products, arithmetic and copies ran while one was open for 56% of the time, Pallas kernels for 11%

profile of v4, /device:TPU:0, one launch (start us, length us, event | category | flops | bytes accessed | tf_op | source)
XLA Modules:
  0.0 158.9 jit_solution(7888552154465220032)
XLA Ops:
  0.7 1.0 fusion.95
  2.5 2.9 %collective-permute-start.3 = (bf16[96,1024]{1,0:T(8,128)(2,1)}, bf16[96,1024]{1,0:T(8,128)(2,1)}, u32[]{:S(2)}, u32[]{:S(2)}) collective-permute-start(bf16[96,1024]{1,0:T(8,128)(2,1)} %pad_maximum_fusion.8), channel_id=1, source_target_pairs={{0,1},{1,0},{2,3},{3,2},{4,5},{5,4},{6,7},{7,6},{8,9},{9,8},{10,11... | collective-permute-start | bytes 589832 | tf_op jit(solution)/shard_map/ppermute | solution.py:139
  5.5 1.1 fusion.94
  6.7 3.4 %collective-permute-start.1 = (bf16[72,1024]{1,0:T(8,128)(2,1)S(1)}, bf16[72,1024]{1,0:T(8,128)(2,1)S(1)}, u32[]{:S(2)}, u32[]{:S(2)}) collective-permute-start(bf16[72,1024]{1,0:T(8,128)(2,1)S(1)} %pad_maximum_fusion.9), channel_id=1, source_target_pairs={{0,3},{1,2},{2,5},{3,4},{4,7},{5,6},{6,9},{7,8},{8,11},{9,10},{10,... | collective-permute-start | bytes 442376 | tf_op jit(solution)/shard_map/ppermute | solution.py:139
  10.2 1.3 collective-permute-start.4
  11.5 0.8 fusion.93
  12.3 1.3 collective-permute-start.5
  14.3 1.0 fusion.59.allow_ref
  15.3 1.1 convolution_convert_fusion.1
  16.4 2.3 %fusion.25 = f32[128,1024]{1,0:T(8,128)} fusion(bf16[512,3072]{1,0:T(8,128)(2,1)} %param.8, bf16[128,1024]{1,0:T(8,128)(2,1)S(1)} %bitcast.30, s32[]{:T(128)S(6)} %select_n.93), kind=kOutput, calls=%fused_computation.35 | convolution fusion | flops 134217728 | bytes 1703940 | tf_op jit(solution)/shard_map/dot_general | solution.py:358
  19.5 1.2 pad_maximum_fusion
  20.7 6.8 %collective-permute-start.2 = (bf16[96,1024]{1,0:T(8,128)(2,1)}, bf16[96,1024]{1,0:T(8,128)(2,1)}, u32[]{:S(2)}, u32[]{:S(2)}) collective-permute-start(bf16[96,1024]{1,0:T(8,128)(2,1)} %bitcast.2), channel_id=1, source_target_pairs={{0,2},{1,3},{2,4},{3,5},{4,6},{5,7},{6,8},{7,9},{8,10},{9,11},{10,... | collective-permute-start | bytes 589832 | tf_op jit(solution)/shard_map/ppermute | solution.py:139
  29.0 1.7 %reshape.254 = bf16[6,6,1024]{2,1,0:T(8,128)(2,1)} reshape(bf16[36,1024]{1,0:T(8,128)(2,1)} %get-tuple-element.64) | data formatting | bytes 147456 | tf_op jit(solution)/shard_map/reshape | solution.py:268
  31.4 1.6 reshape.264
  32.9 1.6 reshape.267
  34.5 1.6 %fusion.100 = (bf16[48,1024]{1,0:T(8,128)(2,1)}, bf16[48,1024]{1,0:T(8,128)(2,1)}) fusion(bf16[96,1024]{1,0:T(8,128)(2,1)} %collective-permute-done.3), kind=kLoop, calls=%fused_computation.147 | loop fusion | bytes 393216 | tf_op jit(solution)/shard_map/slice | solution.py:268
  36.1 0.9 reshape.260
  37.0 1.6 reshape.261
  38.6 1.8 %fusion.15 = bf16[20,32,1024]{2,1,0:T(8,128)(2,1)S(1)} fusion(bf16[6,6,1024]{2,1,0:T(8,128)(2,1)} %reshape.267, bf16[6,16,1024]{2,1,0:T(8,128)(2,1)} %bitcast.5, bf16[6,6,1024]{2,1,0:T(8,128)(2,1)} %reshape.264, bf16[8,6,1024]{2,1,0:T(8,128)(2,1)} %reshape.261, bf16[6,6,1024]{2,1,0:T(8,128)(2,1)} %reshape.257, bf16[8,16,1024]{2,1,0:T(8,128)(2,1)S(1)} %bitcast.31, ...), kind=kLoop, calls=%fused_computation.18 | loop fusion | flops 18350080 | bytes 2457600 | tf_op jit(solution)/shard_map/concatenate | solution.py:178
  40.5 1.5 fusion.10
  42.0 1.0 slice.341
  45.0 1.7 %fusion.22 = bf16[128,512]{1,0:T(8,128)(2,1)S(1)} fusion(bf16[128,1024]{1,0:T(8,128)(2,1)S(1)} %bitcast.42, bf16[640,1024]{1,0:T(8,128)(2,1)} %collective-permute-done.6), kind=kOutput, calls=%fused_computation.31 | convolution fusion | flops 134283264 | bytes 1441792 | tf_op jit(solution)/shard_map/dot_general | solution.py:346
  46.7 0.8 maximum_select_fusion.g_ref
  47.5 2.2 %fusion.21.q_ref = bf16[128,1024]{1,0:T(8,128)(2,1)} fusion(f32[128,1024]{1,0:T(8,128)S(1)} %copy-done.7, bf16[512,3072]{1,0:T(8,128)(2,1)} %collective-permute-done, bf16[128,1024]{1,0:T(8,128)(2,1)S(1)} %bitcast.32, s32[]{:T(128)S(6)} %select_n.94), kind=kOutput, calls=%fused_computation.26 | convolution fusion | flops 134479872 | bytes 1966084 | tf_op jit(solution)/shard_map/dot_general | solution.py:362
  49.8 4.6 %add_convert_fusion.k_ref.v_ref = bf16[640,2048]{1,0:T(8,128)(2,1)} fusion(f32[640,2048]{1,0:T(8,128)S(1)} %fusion.10, bf16[512,3072]{1,0:T(8,128)(2,1)} %collective-permute-done, bf16[640,1024]{1,0:T(8,128)(2,1)S(1)} %bitcast.34, s32[]{:T(128)S(6)} %select_n.94), kind=kOutput, calls=%fused_computation | convolution fusion | flops 1344798720 | bytes 10616836 | tf_op jit(solution)/shard_map/dot_general | solution.py:362
  54.4 18.1 %block_attention.1 = (bf16[128,1024]{1,0:T(8,128)(2,1)}, bf16[128,1024]{1,0:T(8,128)(2,1)}, f32[640,1024]{1,0:T(8,128)}, f32[640,1024]{1,0:T(8,128)}) custom-call(bf16[128,1024]{1,0:T(8,128)(2,1)} %fusion.21.q_ref, bf16[640,2048]{1,0:T(8,128)(2,1)} %add_convert_fusion.k_ref.v_ref, bf16[640,2048]{1,0:T(8,128)(2,1)} %add_convert_fusion.k_ref.v_ref, ...), custom_call_target="tpu_custom_call" | custom-call | flops 2013265920 | bytes 9240576 | tf_op jit(solution)/shard_map/block_attention/pallas_call | solution.py:99
  72.5 2.1 %convert.85 = bf16[20,32,1024]{2,1,0:T(8,128)(2,1)S(1)} convert(f32[20,32,1024]{2,1,0:T(8,128)} %bitcast.37) | non-fusion elementwise | flops 655360 | bytes 3932160 | tf_op jit(solution)/shard_map/convert.77
  75.3 0.8 fusion.83
  77.1 0.8 fusion.82
  78.8 1.6 %concatenate.176 = bf16[48,1024]{1,0:T(8,128)(2,1)} reshape(bf16[8,6,1024]{2,1,0:T(8,128)(2,1)} %get-tuple-element.24) | data formatting | bytes 196608 | tf_op jit(solution)/shard_map/concatenate | solution.py:192
  80.4 1.6 concatenate.179
  82.0 1.6 concatenate.166
  83.5 1.6 concatenate.186
  85.1 1.6 concatenate.183
  86.6 1.6 concatenate.169
  88.2 1.6 concatenate.175
  90.5 1.5 concatenate.165
  92.0 1.6 concatenate.185
  93.6 1.6 concatenate.182
  95.1 1.6 concatenate.168
  96.7 1.1 maximum_maximum_fusion.1
  97.8 1.3 collective-permute-start.7
  99.1 1.8 %maximum_maximum_fusion.2 = bf16[72,2048]{1,0:T(8,128)(2,1)} fusion(bf16[36,1024]{1,0:T(8,128)(2,1)} %concatenate.186, bf16[36,1024]{1,0:T(8,128)(2,1)} %concatenate.185, bf16[36,1024]{1,0:T(8,128)(2,1)} %concatenate.183, bf16[36,1024]{1,0:T(8,128)(2,1)} %concatenate.182), kind=kLoop, calls=%fused_computation.83 | loop fusion | flops 1179648 | bytes 589824 | tf_op jit(solution)/shard_map/concatenate | solution.py:274
  100.9 6.4 %collective-permute-start.10 = (bf16[72,2048]{1,0:T(8,128)(2,1)}, bf16[72,2048]{1,0:T(8,128)(2,1)}, u32[]{:S(2)}, u32[]{:S(2)}) collective-permute-start(bf16[72,2048]{1,0:T(8,128)(2,1)} %maximum_maximum_fusion.2), channel_id=1, source_target_pairs={{0,3},{1,2},{2,5},{3,4},{4,7},{5,6},{6,9},{7,8},{8,11},{9,10},{10,... | collective-permute-start | bytes 884744 | tf_op jit(solution)/shard_map/ppermute | solution.py:139
  107.3 0.8 pad_maximum_fusion.3
  108.1 4.9 %collective-permute-start.11 = (bf16[96,2048]{1,0:T(8,128)(2,1)}, bf16[96,2048]{1,0:T(8,128)(2,1)}, u32[]{:S(2)}, u32[]{:S(2)}) collective-permute-start(bf16[96,2048]{1,0:T(8,128)(2,1)} %pad_maximum_fusion.3), channel_id=1, source_target_pairs={{0,2},{1,3},{2,4},{3,5},{4,6},{5,7},{6,8},{7,9},{8,10},{9,11},{10,... | collective-permute-start | bytes 1179656 | tf_op jit(solution)/shard_map/ppermute | solution.py:139
  113.0 0.8 pad_maximum_fusion.2
  114.6 1.3 collective-permute-start.8
  115.9 0.9 pad_maximum_fusion.6
  116.9 1.5 collective-permute-start.9
  120.5 1.0 fusion.90
  123.1 10.4 %collective-permute-done.13 = bf16[256,512]{1,0:T(8,128)(2,1)} collective-permute-done((bf16[256,512]{1,0:T(8,128)(2,1)S(1)}, bf16[256,512]{1,0:T(8,128)(2,1)}, u32[]{:S(2)}, u32[]{:S(2)}) %collective-permute-start.13) | collective-permute-done | bytes 262176 | tf_op jit(solution)/shard_map/ppermute | solution.py:253
  133.5 2.4 %fusion.20 = bf16[512,512]{1,0:T(8,128)(2,1)} fusion(bf16[256,512]{1,0:T(8,128)(2,1)} %collective-permute-done.13, bf16[128,512]{1,0:T(8,128)(2,1)} %collective-permute-done.12, bf16[128,512]{1,0:T(8,128)(2,1)S(1)} %copy-done.8, bf16[256,512]{1,0:T(8,128)(2,1)} %collective-permute-done.14, bf16[128,512]{1,0:T(8,128)(2,1)} %get-tuple-element.38, ...), kind=kOutput, calls=%fused_computation.24 | convolution fusion | flops 272105472 | bytes 1572864 | tf_op jit(solution)/shard_map/dot_general | solution.py:438
  136.0 5.6 %all-to-all-start = ((bf16[8,64,512]{2,1,0:T(8,128)(2,1)}), bf16[8,64,512]{2,1,0:T(8,128)(2,1)S(1)}, u32[]{:S(2)}, u32[]{:S(2)}) async-start(bf16[8,64,512]{2,1,0:T(8,128)(2,1)} %bitcast.47), calls=%async_computation | async-start | bytes 1048576 | tf_op jit(solution)/shard_map/all_to_all | solution.py:441
  141.6 1.8 %fusion.87 = (bf16[6,16,1024]{2,1,0:T(8,128)(2,1)}, bf16[6,16,1024]{2,1,0:T(8,128)(2,1)}) fusion(bf16[6,16,2048]{2,1,0:T(8,128)(2,1)} %bitcast.16), kind=kLoop, calls=%fused_computation.134 | loop fusion | bytes 786432 | tf_op jit(solution)/shard_map/slice | solution.py:204
  143.4 1.8 %fusion.86 = (bf16[6,16,1024]{2,1,0:T(8,128)(2,1)}, bf16[6,16,1024]{2,1,0:T(8,128)(2,1)}) fusion(bf16[6,16,2048]{2,1,0:T(8,128)(2,1)} %bitcast.13), kind=kLoop, calls=%fused_computation.133 | loop fusion | bytes 786432 | tf_op jit(solution)/shard_map/slice | solution.py:204
  145.2 1.8 %fusion.88 = (bf16[48,2048]{1,0:T(8,128)(2,1)}, bf16[48,2048]{1,0:T(8,128)(2,1)}) fusion(bf16[96,2048]{1,0:T(8,128)(2,1)} %collective-permute-done.9), kind=kLoop, calls=%fused_computation.135 | loop fusion | bytes 786432 | tf_op jit(solution)/shard_map/slice | solution.py:268
  147.0 1.0 reshape.274
  148.7 1.0 reshape.275
  149.7 1.8 %fusion.36 = bf16[8,16,1024]{2,1,0:T(8,128)(2,1)S(1)} fusion(f32[20,32,1024]{2,1,0:T(8,128)} %bitcast.38, bf16[6,6,1024]{2,1,0:T(8,128)(2,1)} %get-tuple-element.61, bf16[6,16,1024]{2,1,0:T(8,128)(2,1)} %get-tuple-element.29, bf16[6,6,1024]{2,1,0:T(8,128)(2,1)} %get-tuple-element.59, bf16[8,6,1024]{2,1,0:T(8,128)(2,1)S(1)} %get-tuple-element.45, ...), kind=kLoop, calls=%fused_computation.48 | loop fusion | flops 2228224 | bytes 1671168 | tf_op jit(solution)/shard_map/convert_element_type | solution.py:448
  151.6 1.5 fusion.44
  153.1 1.2 convolution_convert_fusion.3
  154.3 3.1 %convolution_convert_fusion.2 = bf16[128,512]{1,0:T(8,128)(2,1)S(1)} fusion(bf16[512,3072]{1,0:T(8,128)(2,1)} %collective-permute-done, bf16[128,1024]{1,0:T(8,128)(2,1)S(1)} %bitcast.49, bf16[128,1024]{1,0:T(8,128)(2,1)S(1)} %bitcast.51, bf16[128,1024]{1,0:T(8,128)(2,1)S(1)} %copy-done.17), kind=kOutput, calls=%fused_computation.29 | convolution fusion | flops 405078016 | bytes 4063232 | tf_op jit(solution)/shard_map/dot_general | solution.py:370
  157.4 0.8 maximum_select_fusion.1
  (101 shorter events, 15.7 us)
Async XLA Ops:
  0.6 10.9 %copy-start = (bf16[1,8,16,1024]{3,2,1,0:T(8,128)(2,1)S(1)}, bf16[1,8,16,1024]{3,2,1,0:T(8,128)(2,1)}, u32[]{:S(2)}) copy-start(bf16[1,8,16,1024]{3,2,1,0:T(8,128)(2,1)} %param.5) | copy-start | bytes 786436
  0.6 13.0 %copy-start.16 = (s32[64,32]{0,1:T(8,128)S(1)}, s32[64,32]{0,1:T(8,128)}, u32[]{:S(2)}) copy-start(s32[64,32]{0,1:T(8,128)} %param.7) | copy-start | bytes 24580
  1.7 13.5 %copy-start.1 = (bf16[512,1024]{1,0:T(8,128)(2,1)S(1)}, bf16[512,1024]{1,0:T(8,128)(2,1)}, u32[]{:S(2)}) copy-start(bf16[512,1024]{1,0:T(8,128)(2,1)} %param.9) | copy-start | bytes 3145732
  1.8 13.5 %copy-start.5 = (bf16[1,8,16,1024]{3,2,1,0:T(8,128)(2,1)S(1)}, bf16[1,8,16,1024]{3,2,1,0:T(8,128)(2,1)}, u32[]{:S(2)}) copy-start(bf16[1,8,16,1024]{3,2,1,0:T(8,128)(2,1)} %param.6) | copy-start | bytes 786436
  2.5 32.0 %collective-permute-start.3 = (bf16[96,1024]{1,0:T(8,128)(2,1)}, bf16[96,1024]{1,0:T(8,128)(2,1)}, u32[]{:S(2)}, u32[]{:S(2)}) collective-permute-start(bf16[96,1024]{1,0:T(8,128)(2,1)} %pad_maximum_fusion.8), channel_id=1, source_target_pairs={{0,1},{1,0},{2,3},{3,2},{4,5},{5,4},{6,7},{7,6},{8,9},{9,8},{10,11... | collective-permute-start | bytes 589832 | tf_op jit(solution)/shard_map/ppermute | solution.py:139
  6.7 14.0 %collective-permute-start.1 = (bf16[72,1024]{1,0:T(8,128)(2,1)S(1)}, bf16[72,1024]{1,0:T(8,128)(2,1)S(1)}, u32[]{:S(2)}, u32[]{:S(2)}) collective-permute-start(bf16[72,1024]{1,0:T(8,128)(2,1)S(1)} %pad_maximum_fusion.9), channel_id=1, source_target_pairs={{0,3},{1,2},{2,5},{3,4},{4,7},{5,6},{6,9},{7,8},{8,11},{9,10},{10,... | collective-permute-start | bytes 442376 | tf_op jit(solution)/shard_map/ppermute | solution.py:139
  10.2 17.9 %collective-permute-start.4 = (bf16[72,1024]{1,0:T(8,128)(2,1)S(1)}, bf16[72,1024]{1,0:T(8,128)(2,1)S(1)}, u32[]{:S(2)}, u32[]{:S(2)}) collective-permute-start(bf16[72,1024]{1,0:T(8,128)(2,1)S(1)} %pad_maximum_fusion.10), channel_id=1, source_target_pairs={{2,1},{3,0},{4,3},{5,2},{6,5},{7,4},{8,7},{9,6},{10,9},{11,8},{12,... | collective-permute-start | bytes 442376 | tf_op jit(solution)/shard_map/ppermute | solution.py:139
  12.3 26.3 %collective-permute-start.5 = (bf16[96,1024]{1,0:T(8,128)(2,1)}, bf16[96,1024]{1,0:T(8,128)(2,1)}, u32[]{:S(2)}, u32[]{:S(2)}) collective-permute-start(bf16[96,1024]{1,0:T(8,128)(2,1)} %bitcast.4), channel_id=1, source_target_pairs={{2,0},{3,1},{4,2},{5,3},{6,4},{7,5},{8,6},{9,7},{10,8},{11,9},{12,... | collective-permute-start | bytes 589832 | tf_op jit(solution)/shard_map/ppermute | solution.py:139
  13.6 34.0 %collective-permute-start = (bf16[512,3072]{1,0:T(8,128)(2,1)}, bf16[512,3072]{1,0:T(8,128)(2,1)}, u32[]{:S(2)}, u32[]{:S(2)}) collective-permute-start(bf16[512,3072]{1,0:T(8,128)(2,1)} %param.8), channel_id=1, source_target_pairs={{0,16},{16,0},{1,17},{17,1},{2,18},{18,2},{3,19},{19,3},{4,20},{20... | collective-permute-start | bytes 9437192 | tf_op jit(solution)/shard_map/ppermute | solution.py:253
  20.7 17.9 %collective-permute-start.2 = (bf16[96,1024]{1,0:T(8,128)(2,1)}, bf16[96,1024]{1,0:T(8,128)(2,1)}, u32[]{:S(2)}, u32[]{:S(2)}) collective-permute-start(bf16[96,1024]{1,0:T(8,128)(2,1)} %bitcast.2), channel_id=1, source_target_pairs={{0,2},{1,3},{2,4},{3,5},{4,6},{5,7},{6,8},{7,9},{8,10},{9,11},{10,... | collective-permute-start | bytes 589832 | tf_op jit(solution)/shard_map/ppermute | solution.py:139
  28.1 13.9 %collective-permute-start.6 = (bf16[640,1024]{1,0:T(8,128)(2,1)}, bf16[640,1024]{1,0:T(8,128)(2,1)}, u32[]{:S(2)}, u32[]{:S(2)}) collective-permute-start(bf16[640,1024]{1,0:T(8,128)(2,1)} %pad_maximum_fusion), channel_id=1, source_target_pairs={{0,16},{16,0},{1,17},{17,1},{2,18},{18,2},{3,19},{19,3},{4,20},{20... | collective-permute-start | bytes 3932168 | tf_op jit(solution)/shard_map/ppermute | solution.py:253
  29.0 11.4 %copy-start.3 = (bf16[512,3072]{1,0:T(8,128)(2,1)S(1)}, bf16[512,3072]{1,0:T(8,128)(2,1)}, u32[]{:S(2)}) copy-start(bf16[512,3072]{1,0:T(8,128)(2,1)} %param.8) | copy-start | bytes 9437188
  40.4 3.3 %copy-start.10 = (bf16[128,512]{1,0:T(8,128)(2,1)S(1)}, bf16[128,512]{1,0:T(8,128)(2,1)}, u32[]{:S(2)}) copy-start(bf16[128,512]{1,0:T(8,128)(2,1)} %get-tuple-element.37) | copy-start | bytes 393220
  40.4 4.6 %copy-start.6 = (bf16[1,8,16,1024]{3,2,1,0:T(8,128)(2,1)S(1)}, bf16[1,8,16,1024]{3,2,1,0:T(8,128)(2,1)}, u32[]{:S(2)}) copy-start(bf16[1,8,16,1024]{3,2,1,0:T(8,128)(2,1)} %param.6) | copy-start | bytes 786436
  42.0 4.7 %copy-start.9 = (bf16[128,512]{1,0:T(8,128)(2,1)S(1)}, bf16[128,512]{1,0:T(8,128)(2,1)}, u32[]{:S(2)}) copy-start(bf16[128,512]{1,0:T(8,128)(2,1)} %convolution_convert_fusion.1) | copy-start | bytes 393220
  42.0 5.5 %copy-start.7 = (f32[128,1024]{1,0:T(8,128)S(1)}, f32[128,1024]{1,0:T(8,128)}, u32[]{:S(2)}) copy-start(f32[128,1024]{1,0:T(8,128)} %fusion.25) | copy-start | bytes 1572868
  44.5 78.6 %collective-permute-start.14 = (bf16[256,512]{1,0:T(8,128)(2,1)}, bf16[256,512]{1,0:T(8,128)(2,1)}, u32[]{:S(2)}, u32[]{:S(2)}) collective-permute-start(bf16[256,512]{1,0:T(8,128)(2,1)} %pad_maximum_fusion.7), channel_id=1, source_target_pairs={{0,1},{1,0},{2,3},{3,2},{4,5},{5,4},{6,7},{7,6},{8,9},{9,8},{10,11... | collective-permute-start | bytes 786440 | tf_op jit(solution)/shard_map/ppermute | solution.py:253
  72.5 3.7 %copy-start.2 = (f32[640,1024]{1,0:T(8,128)S(1)}, f32[640,1024]{1,0:T(8,128)}, u32[]{:S(2)}) copy-start(f32[640,1024]{1,0:T(8,128)} %get-tuple-element.7) | copy-start | bytes 7864324
  76.2 1.9 %copy-start.15 = (bf16[128,1024]{1,0:T(8,128)(2,1)S(1)}, bf16[128,1024]{1,0:T(8,128)(2,1)}, u32[]{:S(2)}) copy-start(bf16[128,1024]{1,0:T(8,128)(2,1)} %get-tuple-element.9) | copy-start | bytes 786436
  78.8 35.8 %collective-permute-start.12 = (bf16[128,512]{1,0:T(8,128)(2,1)}, bf16[128,512]{1,0:T(8,128)(2,1)}, u32[]{:S(2)}, u32[]{:S(2)}) collective-permute-start(bf16[128,512]{1,0:T(8,128)(2,1)} %get-tuple-element.41), channel_id=1, source_target_pairs={{0,16},{16,0},{1,17},{17,1},{2,18},{18,2},{3,19},{19,3},{4,20},{20... | collective-permute-start | bytes 393224 | tf_op jit(solution)/shard_map/ppermute | solution.py:253
  92.0 23.9 %copy-start.8 = (bf16[128,512]{1,0:T(8,128)(2,1)S(1)}, bf16[128,512]{1,0:T(8,128)(2,1)}, u32[]{:S(2)}) copy-start(bf16[128,512]{1,0:T(8,128)(2,1)} %get-tuple-element.40) | copy-start | bytes 393220
  96.7 17.1 %copy-start.11 = (bf16[48,1024]{1,0:T(8,128)(2,1)S(1)}, bf16[48,1024]{1,0:T(8,128)(2,1)}, u32[]{:S(2)}) copy-start(bf16[48,1024]{1,0:T(8,128)(2,1)} %concatenate.176) | copy-start | bytes 294916
  96.7 17.1 %copy-start.12 = (bf16[48,1024]{1,0:T(8,128)(2,1)S(1)}, bf16[48,1024]{1,0:T(8,128)(2,1)}, u32[]{:S(2)}) copy-start(bf16[48,1024]{1,0:T(8,128)(2,1)} %concatenate.179) | copy-start | bytes 294916
  96.7 17.1 %copy-start.13 = (bf16[48,1024]{1,0:T(8,128)(2,1)S(1)}, bf16[48,1024]{1,0:T(8,128)(2,1)}, u32[]{:S(2)}) copy-start(bf16[48,1024]{1,0:T(8,128)(2,1)} %concatenate.175) | copy-start | bytes 294916
  96.7 17.1 %copy-start.14 = (bf16[48,1024]{1,0:T(8,128)(2,1)S(1)}, bf16[48,1024]{1,0:T(8,128)(2,1)}, u32[]{:S(2)}) copy-start(bf16[48,1024]{1,0:T(8,128)(2,1)} %concatenate.178) | copy-start | bytes 294916
  97.8 19.0 %collective-permute-start.7 = (bf16[72,2048]{1,0:T(8,128)(2,1)S(1)}, bf16[72,2048]{1,0:T(8,128)(2,1)S(1)}, u32[]{:S(2)}, u32[]{:S(2)}) collective-permute-start(bf16[72,2048]{1,0:T(8,128)(2,1)S(1)} %maximum_maximum_fusion.1), channel_id=1, source_target_pairs={{2,1},{3,0},{4,3},{5,2},{6,5},{7,4},{8,7},{9,6},{10,9},{11,8},{12,... | collective-permute-start | bytes 884744 | tf_op jit(solution)/shard_map/ppermute | solution.py:139
  100.9 19.0 %collective-permute-start.10 = (bf16[72,2048]{1,0:T(8,128)(2,1)}, bf16[72,2048]{1,0:T(8,128)(2,1)}, u32[]{:S(2)}, u32[]{:S(2)}) collective-permute-start(bf16[72,2048]{1,0:T(8,128)(2,1)} %maximum_maximum_fusion.2), channel_id=1, source_target_pairs={{0,3},{1,2},{2,5},{3,4},{4,7},{5,6},{6,9},{7,8},{8,11},{9,10},{10,... | collective-permute-start | bytes 884744 | tf_op jit(solution)/shard_map/ppermute | solution.py:139
  108.1 33.5 %collective-permute-start.11 = (bf16[96,2048]{1,0:T(8,128)(2,1)}, bf16[96,2048]{1,0:T(8,128)(2,1)}, u32[]{:S(2)}, u32[]{:S(2)}) collective-permute-start(bf16[96,2048]{1,0:T(8,128)(2,1)} %pad_maximum_fusion.3), channel_id=1, source_target_pairs={{0,2},{1,3},{2,4},{3,5},{4,6},{5,7},{6,8},{7,9},{8,10},{9,11},{10,... | collective-permute-start | bytes 1179656 | tf_op jit(solution)/shard_map/ppermute | solution.py:139
  114.6 28.8 %collective-permute-start.8 = (bf16[96,2048]{1,0:T(8,128)(2,1)}, bf16[96,2048]{1,0:T(8,128)(2,1)}, u32[]{:S(2)}, u32[]{:S(2)}) collective-permute-start(bf16[96,2048]{1,0:T(8,128)(2,1)} %pad_maximum_fusion.2), channel_id=1, source_target_pairs={{2,0},{3,1},{4,2},{5,3},{6,4},{7,5},{8,6},{9,7},{10,8},{11,9},{12,... | collective-permute-start | bytes 1179656 | tf_op jit(solution)/shard_map/ppermute | solution.py:139
  116.9 28.4 %collective-permute-start.9 = (bf16[96,2048]{1,0:T(8,128)(2,1)}, bf16[96,2048]{1,0:T(8,128)(2,1)}, u32[]{:S(2)}, u32[]{:S(2)}) collective-permute-start(bf16[96,2048]{1,0:T(8,128)(2,1)} %maximum_maximum_fusion), channel_id=1, source_target_pairs={{0,1},{1,0},{2,3},{3,2},{4,5},{5,4},{6,7},{7,6},{8,9},{9,8},{10,11... | collective-permute-start | bytes 1179656 | tf_op jit(solution)/shard_map/ppermute | solution.py:139
  120.0 13.6 %collective-permute-start.13 = (bf16[256,512]{1,0:T(8,128)(2,1)S(1)}, bf16[256,512]{1,0:T(8,128)(2,1)}, u32[]{:S(2)}, u32[]{:S(2)}) collective-permute-start(bf16[256,512]{1,0:T(8,128)(2,1)S(1)} %pad_maximum_fusion.6), channel_id=1, source_target_pairs={{0,1},{1,0},{2,3},{3,2},{4,5},{5,4},{6,7},{7,6},{8,9},{9,8},{10,11... | collective-permute-start | bytes 786440 | tf_op jit(solution)/shard_map/ppermute | solution.py:253
  136.0 22.2 %all-to-all-start = ((bf16[8,64,512]{2,1,0:T(8,128)(2,1)}), bf16[8,64,512]{2,1,0:T(8,128)(2,1)S(1)}, u32[]{:S(2)}, u32[]{:S(2)}) async-start(bf16[8,64,512]{2,1,0:T(8,128)(2,1)} %bitcast.47), calls=%async_computation | async-start | bytes 1048576 | tf_op jit(solution)/shard_map/all_to_all | solution.py:441
  149.7 3.4 %copy-start.4 = (bf16[512,3072]{1,0:T(8,128)(2,1)S(1)}, bf16[512,3072]{1,0:T(8,128)(2,1)}, u32[]{:S(2)}) copy-start(bf16[512,3072]{1,0:T(8,128)(2,1)} %param.8) | copy-start | bytes 9437188
  149.7 3.4 %copy-start.17 = (bf16[128,1024]{1,0:T(8,128)(2,1)S(1)}, bf16[128,1024]{1,0:T(8,128)(2,1)}, u32[]{:S(2)}) copy-start(bf16[128,1024]{1,0:T(8,128)(2,1)} %get-tuple-element.6) | copy-start | bytes 786436

commit v5 on v4

--- a/solution.py
+++ b/solution.py
@@ -39,14 +39,14 @@
     return block
 
 
-def attention_kernel(q_ref, k_ref, v_ref, g_ref, allow_ref, att_ref, gq_ref, gk_ref, gv_ref,
-                     *, head_dim, scale):
+def attention_kernel(q_ref, kv_ref, g_ref, bias_ref, att_ref, gq_ref, gkv_ref, *, head_dim, scale):
     q = q_ref[...]
-    k = k_ref[...]
-    v = v_ref[...]
     g = g_ref[...]
-    allowed = allow_ref[...] > 0.0
     lanes = q.shape[1]
+    kv = kv_ref[...]
+    k = kv[:, :lanes]
+    v = kv[:, lanes:]
+    bias = bias_ref[...]
     lane = lax.broadcasted_iota(jnp.int32, (1, lanes), 1)
     q32 = q.astype(jnp.float32)
     g32 = g.astype(jnp.float32)
@@ -59,9 +59,10 @@
         qj = jnp.where(sel, q32, 0.0).astype(jnp.bfloat16)
         gj = jnp.where(sel, g32, 0.0).astype(jnp.bfloat16)
         scores = lax.dot_general(qj, k, TRANS_B, preferred_element_type=jnp.float32) * scale
-        peak = jnp.max(jnp.where(allowed, scores, -jnp.inf), axis=1, keepdims=True)
-        weights = jnp.where(allowed, jnp.exp(scores - peak), 0.0)
-        probs = weights / jnp.sum(weights, axis=1, keepdims=True)
+        masked = scores + bias
+        peak = jnp.max(masked, axis=1, keepdims=True)
+        weights = jnp.exp(masked - peak)
+        probs = weights * (1.0 / jnp.sum(weights, axis=1, keepdims=True))
         probs_low = probs.astype(jnp.bfloat16)
         att_j = jnp.dot(probs_low, v, preferred_element_type=jnp.float32)
         grad_probs = lax.dot_general(gj, v, TRANS_B, preferred_element_type=jnp.float32)
@@ -78,11 +79,11 @@
         gv = jnp.where(sel, gv_j, gv)
     att_ref[...] = att.astype(att_ref.dtype)
     gq_ref[...] = gq.astype(gq_ref.dtype)
-    gk_ref[...] = gk
-    gv_ref[...] = gv
-
-
-def block_attention(query, key_values, grad_attn, allowed, heads):
+    gkv_ref[:, :lanes] = gk
+    gkv_ref[:, lanes:] = gv
+
+
+def block_attention(query, key_values, grad_attn, bias, heads):
     queries, width = query.shape
     keys = key_values.shape[0]
     head_dim = width // heads
@@ -101,26 +102,23 @@
         grid=(pairs,),
         in_specs=[
             pl.BlockSpec((queries, lanes), lambda h: (0, h)),
-            pl.BlockSpec((keys, lanes), lambda h: (0, h)),
-            pl.BlockSpec((keys, lanes), lambda h: (0, h + pairs)),
+            pl.BlockSpec((keys, 2 * lanes), lambda h: (0, h)),
             pl.BlockSpec((queries, lanes), lambda h: (0, h)),
             pl.BlockSpec((queries, keys), lambda h: (0, 0)),
         ],
         out_specs=[
             pl.BlockSpec((queries, lanes), lambda h: (0, h)),
             pl.BlockSpec((queries, lanes), lambda h: (0, h)),
-            pl.BlockSpec((keys, lanes), lambda h: (0, h)),
-            pl.BlockSpec((keys, lanes), lambda h: (0, h)),
+            pl.BlockSpec((keys, 2 * lanes), lambda h: (0, h)),
         ],
         out_shape=[
             jax.ShapeDtypeStruct((queries, width), jnp.bfloat16),
             jax.ShapeDtypeStruct((queries, width), jnp.bfloat16),
-            jax.ShapeDtypeStruct((keys, width), jnp.float32),
-            jax.ShapeDtypeStruct((keys, width), jnp.float32),
+            jax.ShapeDtypeStruct((keys, 2 * width), jnp.float32),
         ],
         cost_estimate=cost,
         name="block_attention",
-    )(query, key_values, key_values, grad_attn, allowed)
+    )(query, key_values, grad_attn, bias)
 
 
 def grid_pairs(delta_lat, delta_lon):
@@ -147,7 +145,7 @@
     return slice(0, radius)
 
 
-def grouped_send(pieces, lanes):
+def grouped_send(pieces):
     lon_count = lax.axis_size("lon")
     groups = {}
     for index, (dl, db, value) in enumerate(pieces):
@@ -155,9 +153,11 @@
     out = [None] * len(pieces)
     for (dl, db), members in groups.items():
         values = [pieces[i][2] for i in members]
-        got = sent_to(join_rows(values, lanes), dl, db)
-        for i, piece in zip(members, split_rows(got, [v.shape for v in values])):
-            out[i] = piece
+        got = sent_to(jnp.concatenate(values, axis=1), dl, db)
+        offset = 0
+        for i, value in zip(members, values):
+            out[i] = got[:, offset : offset + value.shape[1]]
+            offset += value.shape[1]
     return out
 
 
@@ -172,7 +172,7 @@
             piece = block[part(height, radius, da, True), part(breadth, radius, db, True)]
             spots.append((da, db))
             pieces.append((-da, -db, piece))
-    got = dict(zip(spots, grouped_send(pieces, lanes)))
+    got = dict(zip(spots, grouped_send(pieces)))
     got[(0, 0)] = block
     rows = [jnp.concatenate([got[(da, db)] for db in (-1, 0, 1)], axis=1) for da in (-1, 0, 1)]
     return jnp.concatenate(rows, axis=0)
@@ -194,7 +194,7 @@
             ).astype(jnp.bfloat16)
             spots.append((da, db))
             pieces.append((da, db, joined))
-    for (da, db), got in zip(spots, grouped_send(pieces, sum(widths))):
+    for (da, db), got in zip(spots, grouped_send(pieces)):
         rs = part(height, radius, da, True)
         cs = part(breadth, radius, db, True)
         pad_rows = (rs.start, height - rs.stop)
@@ -247,6 +247,14 @@
         got = lax.ppermute(value, axis, [(0, 1), (1, 0)])
         return jnp.where(me == 0, jnp.stack([value, got]), jnp.stack([got, value]))
     return lax.all_gather(value, axis, axis=0, tiled=False)
+
+
+def arranged(weights, width):
+    rows = weights.shape[0]
+    lanes = 128
+    pairs = width // lanes
+    kv = weights[:, width:].reshape(rows, 2, pairs, lanes).transpose(0, 2, 1, 3)
+    return weights[:, :width], kv.reshape(rows, 2 * width)
 
 
 def swap(value, axis):
@@ -354,20 +362,25 @@
             jnp.concatenate([other_part, mine_part], axis=1),
         )
 
-        def project(rows, start, stop):
+        own_q, own_kv = arranged(w_qkv, width)
+        other_q, other_kv = arranged(qkv_other, width)
+
+        def project(rows, own_w, other_w):
             own = jnp.dot(
-                columns(rows, dp_index, rows_half), w_qkv[:, start:stop],
-                preferred_element_type=jnp.float32,
+                columns(rows, dp_index, rows_half), own_w, preferred_element_type=jnp.float32
             )
             other = jnp.dot(
-                columns(rows, 1 - dp_index, rows_half), qkv_other[:, start:stop],
-                preferred_element_type=jnp.float32,
+                columns(rows, 1 - dp_index, rows_half), other_w, preferred_element_type=jnp.float32
             )
             return (own + other).astype(jnp.bfloat16)
 
-        def back_project(grads):
-            own = lax.dot_general(grads, w_qkv, TRANS_B, preferred_element_type=jnp.float32)
-            other = lax.dot_general(grads, qkv_other, TRANS_B, preferred_element_type=jnp.float32)
+        def back_project(grad_q, grad_kv):
+            own = lax.dot_general(grad_q, own_q, TRANS_B, preferred_element_type=jnp.float32)
+            own = own + lax.dot_general(grad_kv, own_kv, TRANS_B, preferred_element_type=jnp.float32)
+            other = lax.dot_general(grad_q, other_q, TRANS_B, preferred_element_type=jnp.float32)
+            other = other + lax.dot_general(
+                grad_kv, other_kv, TRANS_B, preferred_element_type=jnp.float32
+            )
             own = own.astype(jnp.bfloat16)
             other = other.astype(jnp.bfloat16)
             return jnp.where(
@@ -375,6 +388,9 @@
                 jnp.concatenate([own, other], axis=1),
                 jnp.concatenate([other, own], axis=1),
             )
+
+        query = project(flat_inputs, own_q, other_q)
+        kv_weights = (own_kv, other_kv)
     else:
         panels = lax.all_gather(w_qkv, "dp", axis=0, tiled=True)
         cot_blocks = flat_grad.reshape(token_count, lon_count, cols_block).transpose(1, 0, 2)
@@ -382,20 +398,25 @@
         cot_group = gather_members(cot_lon, "dp").reshape(-1, cols_block)
         grad_attn = partner_rows_product(flat_grad, w_out, "dp")
 
-        def project(rows, start, stop):
-            out = jnp.dot(rows, panels[:, start:stop], preferred_element_type=jnp.float32)
+        full_q, full_kv = arranged(panels, width)
+
+        def project(rows, weights, unused):
+            out = jnp.dot(rows, weights, preferred_element_type=jnp.float32)
             return out.astype(jnp.bfloat16)
 
-        def back_project(grads):
-            out = lax.dot_general(grads, panels, TRANS_B, preferred_element_type=jnp.float32)
+        def back_project(grad_q, grad_kv):
+            out = lax.dot_general(grad_q, full_q, TRANS_B, preferred_element_type=jnp.float32)
+            out = out + lax.dot_general(grad_kv, full_kv, TRANS_B, preferred_element_type=jnp.float32)
             return out.astype(jnp.bfloat16)
+
+        query = project(flat_inputs, full_q, None)
+        kv_weights = (full_kv, None)
 
     tok_ext = halo_gather(inputs_here, radius)
     tok_ext = jnp.pad(tok_ext, ((0, 0), (0, pad_cols - ext_cols), (0, 0)))
     tok_ext = tok_ext.reshape(key_count, width)
 
-    query = project(flat_inputs, 0, width)
-    key_values = project(tok_ext, width, 3 * width)
+    key_values = project(tok_ext, *kv_weights)
 
     wrapped = jnp.concatenate(
         [valid_cells[:, -radius:], valid_cells, valid_cells[:, :radius]], axis=1
@@ -413,15 +434,13 @@
     delta_col = (key_pos % pad_cols)[None, :] - radius - (query_pos % breadth)[:, None]
     inside = (jnp.abs(delta_row) <= radius) & (jnp.abs(delta_col) <= radius)
     itself = (delta_row == 0) & (delta_col == 0)
-    allowed = (inside & ((valid_ext == 1) | itself)).astype(jnp.float32)
-
-    attended, grad_query, grad_keys, grad_values = block_attention(
-        query, key_values, grad_attn, allowed, HEADS
-    )
-
-    grad_k_ext = grad_keys.reshape(ext_rows, pad_cols, width)[:, :ext_cols]
-    grad_v_ext = grad_values.reshape(ext_rows, pad_cols, width)[:, :ext_cols]
-    grad_k_own, grad_v_own = halo_return([grad_k_ext, grad_v_ext], height, breadth, radius)
+    allowed = inside & ((valid_ext == 1) | itself)
+    bias = jnp.where(allowed, 0.0, -jnp.inf).astype(jnp.float32)
+
+    attended, grad_query, grad_kv = block_attention(query, key_values, grad_attn, bias, HEADS)
+
+    grad_kv_ext = grad_kv.reshape(ext_rows, pad_cols, 2 * width)[:, :ext_cols]
+    (grad_kv_own,) = halo_return([grad_kv_ext], height, breadth, radius)
 
     if fast:
         own_att = columns(attended, dp_index, rows_half)
@@ -441,15 +460,8 @@
     spread = lax.all_to_all(partial.astype(jnp.bfloat16), "lat", 0, 0, tiled=True)
     d_w_out = spread.astype(jnp.float32).reshape(lat_count, rows_block, cols_block).sum(axis=0)
 
-    grad_proj = jnp.concatenate(
-        [
-            grad_query,
-            grad_k_own.astype(jnp.bfloat16).reshape(token_count, width),
-            grad_v_own.astype(jnp.bfloat16).reshape(token_count, width),
-        ],
-        axis=1,
-    )
-    d_input = back_project(grad_proj).reshape(1, height, breadth, width)
+    grad_kv_low = grad_kv_own.astype(jnp.bfloat16).reshape(token_count, 2 * width)
+    d_input = back_project(grad_query, grad_kv_low).reshape(1, height, breadth, width)
     return (d_input, d_w_out)
 
 

time: 160 us -> 153 us (0.956)
  local copies, waits for them, and re-layouts: 51.1 us -> 22.6 us
  waiting for transfers between devices: 10.5 us -> 35.8 us
  starting transfers between devices: 38 us -> 43.4 us
  other arithmetic: 19.8 us -> 14.9 us
  matrix products: 20.3 us -> 17.4 us
    ppermute x10, waiting for transfers between devices: 0.03 us -> 22.8 us  [sent_to(): return lax.ppermute(value, ('lat', 'lon'), grid_pairs(delta_lat, delta_lon))]
    concatenate x12 -> x0, local copies, waits for them, and re-layouts: 17.9 us -> none  [halo_return(): jnp.concatenate([ext[row_slices[da], col_slices[db]] for ext in ext_list]...]
    reshape x18 -> x0, local copies, waits for them, and re-layouts: 10.4 us -> none  [the longest x12 10.2 us: split_rows(): out.append(joined[offset:offset + count].reshape(shape))]
    all_to_all x1, waiting for transfers between devices: 0.01 us -> 6.16 us  [shards(): lax.all_to_all(partial.astype(jnp.bfloat16), 'lat', 0, 0, tiled=True)]
    all_to_all x1, starting transfers between devices: 5.62 us -> 11.2 us  [shards(): lax.all_to_all(partial.astype(jnp.bfloat16), 'lat', 0, 0, tiled=True)]
    unnamed x37 -> x32, local copies, waits for them, and re-layouts: 0.16 us -> 5.25 us
    ppermute x5, waiting for transfers between devices: 10.5 us -> 6.77 us  [swap(): return lax.ppermute(value, axis, [(0, 1), (1, 0)])]
    slice x14 -> x8, local copies, waits for them, and re-layouts: 12.9 us -> 9.94 us  [the longest x6 5.18 us: grouped_send(): out[i] = got[:, offset:offset + value.shape[1]]]
  transfers between devices with their start and end apart: 16 -> 16, of which waited for: 1 -> 4; matrix products, arithmetic and copies ran while one was open for 56% -> 34% of each run, Pallas kernels for 11% -> 11%
where the time goes in v5:
time: 153 us; the launch traced here: 152 us
  starting transfers between devices  43.4 us (28%)
  waiting for transfers between devices  35.8 us (23%)
  local copies, waits for them, and re-layouts  22.6 us (15%)
  matrix products  17.4 us (11%)
  Pallas kernels  17.2 us (11%)
  other arithmetic  14.9 us (10%)
    ppermute x10, starting transfers between devices, sent_to(): return lax.ppermute(value, ('lat', 'lon'), grid_pairs(delta_lat, delta_lon))  30.9 us
    ppermute x10, waiting for transfers between devices, sent_to(): return lax.ppermute(value, ('lat', 'lon'), grid_pairs(delta_lat, delta_lon))  22.8 us
    pallas_call x1, Pallas kernels, block_attention(): pl.pallas_call(kernel, grid=(pairs,), in_specs=[pl.BlockSpec((queries, la...  17.2 us
    all_to_all x1, starting transfers between devices, shards(): lax.all_to_all(partial.astype(jnp.bfloat16), 'lat', 0, 0, tiled=True)  11.2 us
    ppermute x5, waiting for transfers between devices, swap(): return lax.ppermute(value, axis, [(0, 1), (1, 0)])  6.77 us
    all_to_all x1, waiting for transfers between devices, shards(): lax.all_to_all(partial.astype(jnp.bfloat16), 'lat', 0, 0, tiled=True)  6.16 us
    dot_general x2, matrix products, project(): jnp.dot(columns(rows, 1 - dp_index, rows_half), other_w, preferred_elemen...  5.47 us
    unnamed x32, local copies, waits for them, and re-layouts  5.25 us
  transfers between devices with their start and end apart: 16, of which 4 were waited for; matrix products, arithmetic and copies ran while one was open for 34% of the time, Pallas kernels for 11%

profile of v5, /device:TPU:0, one launch (start us, length us, event | category | flops | bytes accessed | tf_op | source)
XLA Modules:
  0.0 152.3 jit_solution(11543902839129575671)
XLA Ops:
  0.6 1.1 fusion.80
  1.8 0.7 pad_maximum_fusion.7
  2.5 6.5 %collective-permute-start.1 = (bf16[6,12,1024]{2,1,0:T(8,128)(2,1)}, bf16[6,12,1024]{2,1,0:T(8,128)(2,1)}, u32[]{:S(2)}, u32[]{:S(2)}) collective-permute-start(bf16[6,12,1024]{2,1,0:T(8,128)(2,1)} %pad_maximum_fusion.7), channel_id=1, source_target_pairs={{0,3},{1,2},{2,5},{3,4},{4,7},{5,6},{6,9},{7,8},{8,11},{9,10},{10,... | collective-permute-start | bytes 442376 | tf_op jit(solution)/shard_map/ppermute | solution.py:137
  9.0 0.7 pad_maximum_fusion.8
  9.7 1.3 collective-permute-start.4
  11.0 1.0 fusion.81
  12.0 0.8 pad_maximum_fusion.4
  12.8 0.5 collective-permute-start.3
  13.4 0.8 slice_bitcast_fusion.1
  14.2 6.3 %collective-permute-start.2 = (bf16[6,16,1024]{2,1,0:T(8,128)(2,1)}, bf16[6,16,1024]{2,1,0:T(8,128)(2,1)}, u32[]{:S(2)}, u32[]{:S(2)}) collective-permute-start(bf16[6,16,1024]{2,1,0:T(8,128)(2,1)} %get-tuple-element.28), channel_id=1, source_target_pairs={{0,2},{1,3},{2,4},{3,5},{4,6},{5,7},{6,8},{7,9},{8,10},{9,11},{10,... | collective-permute-start | bytes 589832 | tf_op jit(solution)/shard_map/ppermute | solution.py:137
  20.5 4.6 %copy.16 = bf16[512,3072]{0,1:T(8,128)(2,1)} copy(bf16[512,3072]{1,0:T(8,128)(2,1)} %param.8) | data formatting | bytes 6291456 | tf_op args[3]
  25.2 0.1 copy.21
  25.3 0.1 copy.23
  25.5 0.1 pad_dynamic-slice_fusion
  25.6 0.1 eq.28
  25.7 1.0 fusion.54.bias_ref
  26.7 0.5 convolution_convert_fusion.1
  27.2 2.3 %fusion.35 = f32[128,1024]{1,0:T(8,128)} fusion(bf16[512,3072]{1,0:T(8,128)(2,1)} %param.8, bf16[128,1024]{1,0:T(8,128)(2,1)S(1)} %bitcast.40, s32[]{:T(128)S(6)} %select_n.97), kind=kOutput, calls=%fused_computation.46 | convolution fusion | flops 134217728 | bytes 1703940 | tf_op jit(solution)/shard_map/dot_general | solution.py:369
  29.5 0.7 constant_dynamic-slice_fusion.3
  30.2 3.0 %slice.187 = bf16[512,2048]{0,1:T(8,128)(2,1)} slice(bf16[512,3072]{0,1:T(8,128)(2,1)} %copy.16), slice={[0:512], [1024:3072]} | slice | bytes 4194304 | tf_op jit(solution)/shard_map/slice | solution.py:256
  33.3 1.8 %copy.18 = bf16[512,8,2,128]{0,3,2,1:T(8,128)(2,1)S(1)} copy(bf16[512,8,2,128]{0,3,1,2:T(8,128)(2,1)} %bitcast.43) | data formatting | bytes 4194304 | tf_op jit(solution)/shard_map/transpose | solution.py:256
  35.0 1.1 pad_maximum_fusion
  36.2 1.3 collective-permute-start.5
  37.5 1.0 fusion.82
  38.5 0.6 collective-permute-start.6
  39.1 1.0 fusion.83
  40.1 1.1 fusion.79
  41.2 4.1 %collective-permute-done.5 = bf16[6,16,1024]{2,1,0:T(8,128)(2,1)S(1)} collective-permute-done((bf16[6,16,1024]{2,1,0:T(8,128)(2,1)S(1)}, bf16[6,16,1024]{2,1,0:T(8,128)(2,1)S(1)}, u32[]{:S(2)}, u32[]{:S(2)}) %collective-permute-start.5) | collective-permute-done | bytes 196640 | tf_op jit(solution)/shard_map/ppermute | solution.py:137
  45.4 1.7 %fusion.12 = bf16[20,32,1024]{2,1,0:T(8,128)(2,1)S(1)} fusion(bf16[6,6,1024]{2,1,0:T(8,128)(2,1)S(1)} %get-tuple-element.41, bf16[6,16,1024]{2,1,0:T(8,128)(2,1)S(1)} %collective-permute-done.5, bf16[6,6,1024]{2,1,0:T(8,128)(2,1)S(1)} %get-tuple-element.40, bf16[8,6,1024]{2,1,0:T(8,128)(2,1)S(1)} %get-tuple-element.31, ...), kind=kLoop, calls=%fused_computation.15 | loop fusion | flops 18350080 | bytes 2457600 | tf_op jit(solution)/shard_map/concatenate | solution.py:178
  47.0 1.6 %fusion.38 = f32[640,2048]{1,0:T(8,128)S(1)} fusion(bf16[512,2048]{0,1:T(8,128)(2,1)S(1)} %bitcast.34, bf16[640,1024]{1,0:T(8,128)(2,1)S(1)} %bitcast.47, s32[]{:T(128)S(6)} %select_n.97), kind=kOutput, calls=%fused_computation.49 | convolution fusion | flops 1342177280 | bytes 7995396 | tf_op jit(solution)/shard_map/dot_general | solution.py:369
  48.7 0.6 collective-permute-start.14
  49.3 0.5 fusion.21
  49.8 0.8 maximum_select_fusion.g_ref
  50.6 1.7 %slice.188 = bf16[512,2048]{0,1:T(8,128)(2,1)S(1)} slice(bf16[512,3072]{0,1:T(8,128)(2,1)} %collective-permute-done), slice={[0:512], [1024:3072]} | slice | bytes 4194304 | tf_op jit(solution)/shard_map/slice | solution.py:256
  52.3 0.1 copy.19
  52.5 3.1 %add_convert_fusion.kv_ref = bf16[640,2048]{1,0:T(8,128)(2,1)} fusion(f32[640,2048]{1,0:T(8,128)S(1)} %fusion.38, bf16[512,2048]{0,1:T(8,128)(2,1)S(1)} %bitcast.36, bf16[640,1024]{1,0:T(8,128)(2,1)S(1)} %bitcast.48, s32[]{:T(128)S(6)} %select_n.98), kind=kOutput, calls=%fused_computation | convolution fusion | flops 1344798720 | bytes 10616836 | tf_op jit(solution)/shard_map/dot_general | solution.py:372
  55.6 2.4 %fusion.18.q_ref = bf16[128,1024]{1,0:T(8,128)(2,1)} fusion(f32[128,1024]{1,0:T(8,128)S(1)} %copy-done.6, bf16[512,3072]{0,1:T(8,128)(2,1)} %collective-permute-done, bf16[128,1024]{1,0:T(8,128)(2,1)S(1)} %bitcast.42, s32[]{:T(128)S(6)} %select_n.98), kind=kOutput, calls=%fused_computation.23 | convolution fusion | flops 134479872 | bytes 1966084 | tf_op jit(solution)/shard_map/dot_general | solution.py:372
  58.0 17.2 %block_attention.1 = (bf16[128,1024]{1,0:T(8,128)(2,1)}, bf16[128,1024]{1,0:T(8,128)(2,1)}, f32[640,2048]{1,0:T(8,128)}) custom-call(bf16[128,1024]{1,0:T(8,128)(2,1)} %fusion.18.q_ref, bf16[640,2048]{1,0:T(8,128)(2,1)} %add_convert_fusion.kv_ref, bf16[128,1024]{1,0:T(8,128)(2,1)} %maximum_select_fusion.g_ref, f32[128,640]{1,0:T(8,128)} %fusion.54.bias_ref), custom_call_target="tpu_custom_call" | custom-call | flops 2013265920 | bytes 9240576 | tf_op jit(solution)/shard_map/block_attention/pallas_call | solution.py:100
  75.1 2.9 %convert.26 = bf16[20,32,2048]{2,1,0:T(8,128)(2,1)S(1)} convert(f32[20,32,2048]{2,1,0:T(8,128)} %bitcast.45) | non-fusion elementwise | flops 1310720 | bytes 7864320 | tf_op jit(solution)/shard_map/convert.23
  78.0 0.1 fusion.74
  78.3 1.2 fusion.73
  79.6 0.1 pad_maximum_fusion.2
  79.8 1.3 collective-permute-start.7
  81.0 1.0 pad_maximum_fusion.1
  82.0 1.5 collective-permute-start.9
  83.5 0.1 pad_maximum_fusion.3
  83.7 5.5 %collective-permute-start.10 = (bf16[6,12,2048]{2,1,0:T(8,128)(2,1)S(1)}, bf16[6,12,2048]{2,1,0:T(8,128)(2,1)S(1)}, u32[]{:S(2)}, u32[]{:S(2)}) collective-permute-start(bf16[6,12,2048]{2,1,0:T(8,128)(2,1)S(1)} %pad_maximum_fusion.3), channel_id=1, source_target_pairs={{0,3},{1,2},{2,5},{3,4},{4,7},{5,6},{6,9},{7,8},{8,11},{9,10},{10,... | collective-permute-start | bytes 884744 | tf_op jit(solution)/shard_map/ppermute | solution.py:137
  89.1 2.4 %fusion.33 = f32[128,512]{1,0:T(8,128)} fusion(bf16[128,1024]{1,0:T(8,128)(2,1)S(1)} %copy-done.13, bf16[512,3072]{1,0:T(8,128)(2,1)} %param.8), kind=kOutput, calls=%fused_computation.44 | convolution fusion | flops 134217728 | bytes 1572864 | tf_op jit(solution)/shard_map/dot_general | solution.py:378
  91.6 5.5 %collective-permute-start.11 = (bf16[6,16,2048]{2,1,0:T(8,128)(2,1)}, bf16[6,16,2048]{2,1,0:T(8,128)(2,1)}, u32[]{:S(2)}, u32[]{:S(2)}) collective-permute-start(bf16[6,16,2048]{2,1,0:T(8,128)(2,1)} %get-tuple-element.9), channel_id=1, source_target_pairs={{0,2},{1,3},{2,4},{3,5},{4,6},{5,7},{6,8},{7,9},{8,10},{9,11},{10,... | collective-permute-start | bytes 1179656 | tf_op jit(solution)/shard_map/ppermute | solution.py:137
  97.1 1.3 collective-permute-start.8
  98.5 18.7 %collective-permute-done.10 = bf16[6,12,2048]{2,1,0:T(8,128)(2,1)S(1)} collective-permute-done((bf16[6,12,2048]{2,1,0:T(8,128)(2,1)S(1)}, bf16[6,12,2048]{2,1,0:T(8,128)(2,1)S(1)}, u32[]{:S(2)}, u32[]{:S(2)}) %collective-permute-start.10) | collective-permute-done | bytes 294944 | tf_op jit(solution)/shard_map/ppermute | solution.py:137
  117.2 0.8 fusion.78
  117.9 6.8 %collective-permute-done.13 = bf16[256,512]{1,0:T(8,128)(2,1)S(1)} collective-permute-done((bf16[256,512]{1,0:T(8,128)(2,1)S(1)}, bf16[256,512]{1,0:T(8,128)(2,1)S(1)}, u32[]{:S(2)}, u32[]{:S(2)}) %collective-permute-start.13) | collective-permute-done | bytes 262176 | tf_op jit(solution)/shard_map/ppermute | solution.py:261
  124.7 2.2 %fusion.17 = bf16[512,512]{1,0:T(8,128)(2,1)} fusion(bf16[256,512]{1,0:T(8,128)(2,1)S(1)} %collective-permute-done.13, bf16[128,512]{1,0:T(8,128)(2,1)S(1)} %collective-permute-done.12, bf16[128,512]{1,0:T(8,128)(2,1)S(1)} %get-tuple-element.26, bf16[256,512]{1,0:T(8,128)(2,1)} %collective-permute-done.14, bf16[128,512]{1,0:T(8,128)(2,1)S(1)} %get-tuple-element.24, ...), kind=kOutput, calls=%fused_computation.21 | convolution fusion | flops 272105472 | bytes 1572864 | tf_op jit(solution)/shard_map/dot_general | solution.py:457
  126.9 11.2 %all-to-all-start = ((bf16[8,64,512]{2,1,0:T(8,128)(2,1)}), bf16[8,64,512]{2,1,0:T(8,128)(2,1)S(1)}, u32[]{:S(2)}, u32[]{:S(2)}) async-start(bf16[8,64,512]{2,1,0:T(8,128)(2,1)} %bitcast.56), calls=%async_computation | async-start | bytes 1048576 | tf_op jit(solution)/shard_map/all_to_all | solution.py:460
  138.1 1.2 fusion.76
  139.4 2.4 %fusion.29 = bf16[8,16,2048]{2,1,0:T(8,128)(2,1)S(1)} fusion(f32[20,32,2048]{2,1,0:T(8,128)} %bitcast.46, bf16[6,6,2048]{2,1,0:T(8,128)(2,1)} %get-tuple-element.21, bf16[6,16,2048]{2,1,0:T(8,128)(2,1)} %collective-permute-done.11, bf16[6,6,2048]{2,1,0:T(8,128)(2,1)S(1)} %get-tuple-element.20, bf16[8,6,2048]{2,1,0:T(8,128)(2,1)S(1)} %get-tuple-element.17, ...), kind=kLoop, calls=%fused_computation.39 | loop fusion | flops 4456448 | bytes 3342336 | tf_op jit(solution)/shard_map/convert_element_type | solution.py:463
  141.8 0.4 fusion.85
  142.2 0.5 copy-done.14
  142.7 1.5 %fusion.20 = bf16[128,512]{1,0:T(8,128)(2,1)S(1)} fusion(f32[128,512]{1,0:T(8,128)S(1)} %fusion.85, bf16[128,1024]{1,0:T(8,128)(2,1)S(1)} %copy-done.14, bf16[512,3072]{0,1:T(8,128)(2,1)} %collective-permute-done), kind=kOutput, calls=%fused_computation.29 | convolution fusion | flops 134348800 | bytes 1703936 | tf_op jit(solution)/shard_map/dot_general | solution.py:380
  144.2 0.5 fusion.19
  144.7 0.8 maximum_select_fusion.1
  145.5 6.2 %all-to-all-done = bf16[8,64,512]{2,1,0:T(8,128)(2,1)S(1)} async-done(((bf16[8,64,512]{2,1,0:T(8,128)(2,1)}), bf16[8,64,512]{2,1,0:T(8,128)(2,1)S(1)}, u32[]{:S(2)}, u32[]{:S(2)}) %all-to-all-start) | async-done | bytes 524320 | tf_op jit(solution)/shard_map/all_to_all | solution.py:460
  151.6 0.7 convert_reduce_fusion
  (57 shorter events, 0.6 us)
Async XLA Ops:
  0.6 12.7 %copy-start.2 = (bf16[1,8,16,1024]{3,2,1,0:T(8,128)(2,1)S(1)}, bf16[1,8,16,1024]{3,2,1,0:T(8,128)(2,1)}, u32[]{:S(2)}) copy-start(bf16[1,8,16,1024]{3,2,1,0:T(8,128)(2,1)} %param.5) | copy-start | bytes 786436
  2.5 33.6 %collective-permute-start.1 = (bf16[6,12,1024]{2,1,0:T(8,128)(2,1)}, bf16[6,12,1024]{2,1,0:T(8,128)(2,1)}, u32[]{:S(2)}, u32[]{:S(2)}) collective-permute-start(bf16[6,12,1024]{2,1,0:T(8,128)(2,1)} %pad_maximum_fusion.7), channel_id=1, source_target_pairs={{0,3},{1,2},{2,5},{3,4},{4,7},{5,6},{6,9},{7,8},{8,11},{9,10},{10,... | collective-permute-start | bytes 442376 | tf_op jit(solution)/shard_map/ppermute | solution.py:137
  9.7 28.8 %collective-permute-start.4 = (bf16[6,12,1024]{2,1,0:T(8,128)(2,1)}, bf16[6,12,1024]{2,1,0:T(8,128)(2,1)}, u32[]{:S(2)}, u32[]{:S(2)}) collective-permute-start(bf16[6,12,1024]{2,1,0:T(8,128)(2,1)} %pad_maximum_fusion.8), channel_id=1, source_target_pairs={{2,1},{3,0},{4,3},{5,2},{6,5},{7,4},{8,7},{9,6},{10,9},{11,8},{12,... | collective-permute-start | bytes 442376 | tf_op jit(solution)/shard_map/ppermute | solution.py:137
  12.8 27.3 %collective-permute-start.3 = (bf16[8,12,1024]{2,1,0:T(8,128)(2,1)}, bf16[8,12,1024]{2,1,0:T(8,128)(2,1)}, u32[]{:S(2)}, u32[]{:S(2)}) collective-permute-start(bf16[8,12,1024]{2,1,0:T(8,128)(2,1)} %pad_maximum_fusion.4), channel_id=1, source_target_pairs={{0,1},{1,0},{2,3},{3,2},{4,5},{5,4},{6,7},{7,6},{8,9},{9,8},{10,11... | collective-permute-start | bytes 589832 | tf_op jit(solution)/shard_map/ppermute | solution.py:137
  14.2 10.9 %copy-start.12 = (s32[64,32]{0,1:T(8,128)S(1)}, s32[64,32]{0,1:T(8,128)}, u32[]{:S(2)}) copy-start(s32[64,32]{0,1:T(8,128)} %param.7) | copy-start | bytes 24580
  14.2 12.5 %copy-start.3 = (bf16[512,1024]{1,0:T(8,128)(2,1)S(1)}, bf16[512,1024]{1,0:T(8,128)(2,1)}, u32[]{:S(2)}) copy-start(bf16[512,1024]{1,0:T(8,128)(2,1)} %param.9) | copy-start | bytes 3145732
  14.2 12.5 %copy-start.4 = (bf16[1,8,16,1024]{3,2,1,0:T(8,128)(2,1)S(1)}, bf16[1,8,16,1024]{3,2,1,0:T(8,128)(2,1)}, u32[]{:S(2)}) copy-start(bf16[1,8,16,1024]{3,2,1,0:T(8,128)(2,1)} %param.6) | copy-start | bytes 786436
  14.2 27.0 %collective-permute-start.2 = (bf16[6,16,1024]{2,1,0:T(8,128)(2,1)}, bf16[6,16,1024]{2,1,0:T(8,128)(2,1)}, u32[]{:S(2)}, u32[]{:S(2)}) collective-permute-start(bf16[6,16,1024]{2,1,0:T(8,128)(2,1)} %get-tuple-element.28), channel_id=1, source_target_pairs={{0,2},{1,3},{2,4},{3,5},{4,6},{5,7},{6,8},{7,9},{8,10},{9,11},{10,... | collective-permute-start | bytes 589832 | tf_op jit(solution)/shard_map/ppermute | solution.py:137
  25.1 25.5 %collective-permute-start = (bf16[512,3072]{0,1:T(8,128)(2,1)}, bf16[512,3072]{0,1:T(8,128)(2,1)}, u32[]{:S(2)}, u32[]{:S(2)}) collective-permute-start(bf16[512,3072]{0,1:T(8,128)(2,1)} %copy.16), channel_id=1, source_target_pairs={{0,16},{16,0},{1,17},{17,1},{2,18},{18,2},{3,19},{19,3},{4,20},{20... | collective-permute-start | bytes 9437192 | tf_op jit(solution)/shard_map/ppermute | solution.py:261
  35.0 1.1 copy-start.10
  36.2 9.2 %collective-permute-start.5 = (bf16[6,16,1024]{2,1,0:T(8,128)(2,1)S(1)}, bf16[6,16,1024]{2,1,0:T(8,128)(2,1)S(1)}, u32[]{:S(2)}, u32[]{:S(2)}) collective-permute-start(bf16[6,16,1024]{2,1,0:T(8,128)(2,1)S(1)} %copy-done.10), channel_id=1, source_target_pairs={{2,0},{3,1},{4,2},{5,3},{6,4},{7,5},{8,6},{9,7},{10,8},{11,9},{12,... | collective-permute-start | bytes 589832 | tf_op jit(solution)/shard_map/ppermute | solution.py:137
  38.5 10.1 %collective-permute-start.6 = (bf16[640,1024]{1,0:T(8,128)(2,1)S(1)}, bf16[640,1024]{1,0:T(8,128)(2,1)S(1)}, u32[]{:S(2)}, u32[]{:S(2)}) collective-permute-start(bf16[640,1024]{1,0:T(8,128)(2,1)S(1)} %pad_maximum_fusion), channel_id=1, source_target_pairs={{0,16},{16,0},{1,17},{17,1},{2,18},{18,2},{3,19},{19,3},{4,20},{20... | collective-permute-start | bytes 3932168 | tf_op jit(solution)/shard_map/ppermute | solution.py:261
  47.0 1.7 %copy-start.7 = (bf16[128,512]{1,0:T(8,128)(2,1)S(1)}, bf16[128,512]{1,0:T(8,128)(2,1)}, u32[]{:S(2)}) copy-start(bf16[128,512]{1,0:T(8,128)(2,1)} %get-tuple-element.23) | copy-start | bytes 393220
  47.0 2.3 %copy-start.5 = (bf16[1,8,16,1024]{3,2,1,0:T(8,128)(2,1)S(1)}, bf16[1,8,16,1024]{3,2,1,0:T(8,128)(2,1)}, u32[]{:S(2)}) copy-start(bf16[1,8,16,1024]{3,2,1,0:T(8,128)(2,1)} %param.6) | copy-start | bytes 786436
  48.7 69.2 %collective-permute-start.14 = (bf16[256,512]{1,0:T(8,128)(2,1)S(1)}, bf16[256,512]{1,0:T(8,128)(2,1)}, u32[]{:S(2)}, u32[]{:S(2)}) collective-permute-start(bf16[256,512]{1,0:T(8,128)(2,1)S(1)} %pad_maximum_fusion.6), channel_id=1, source_target_pairs={{0,1},{1,0},{2,3},{3,2},{4,5},{5,4},{6,7},{7,6},{8,9},{9,8},{10,11... | collective-permute-start | bytes 786440 | tf_op jit(solution)/shard_map/ppermute | solution.py:261
  52.5 3.1 %copy-start = (bf16[512,8,2,128]{0,3,2,1:T(8,128)(2,1)}, bf16[512,8,2,128]{0,3,2,1:T(8,128)(2,1)S(1)}, u32[]{:S(2)}) copy-start(bf16[512,8,2,128]{0,3,2,1:T(8,128)(2,1)S(1)} %copy.19) | copy-start | bytes 6291460
  52.5 3.1 %copy-start.6 = (f32[128,1024]{1,0:T(8,128)S(1)}, f32[128,1024]{1,0:T(8,128)}, u32[]{:S(2)}) copy-start(f32[128,1024]{1,0:T(8,128)} %fusion.35) | copy-start | bytes 1572868
  78.0 1.5 copy-start.9
  78.3 10.8 %copy-start.13 = (bf16[128,1024]{1,0:T(8,128)(2,1)S(1)}, bf16[128,1024]{1,0:T(8,128)(2,1)}, u32[]{:S(2)}) copy-start(bf16[128,1024]{1,0:T(8,128)(2,1)} %get-tuple-element.5) | copy-start | bytes 786436
  79.5 12.0 %collective-permute-start.12 = (bf16[128,512]{1,0:T(8,128)(2,1)S(1)}, bf16[128,512]{1,0:T(8,128)(2,1)S(1)}, u32[]{:S(2)}, u32[]{:S(2)}) collective-permute-start(bf16[128,512]{1,0:T(8,128)(2,1)S(1)} %get-tuple-element.27), channel_id=1, source_target_pairs={{0,16},{16,0},{1,17},{17,1},{2,18},{18,2},{3,19},{19,3},{4,20},{20... | collective-permute-start | bytes 393224 | tf_op jit(solution)/shard_map/ppermute | solution.py:261
  79.8 17.4 %collective-permute-start.7 = (bf16[6,12,2048]{2,1,0:T(8,128)(2,1)S(1)}, bf16[6,12,2048]{2,1,0:T(8,128)(2,1)S(1)}, u32[]{:S(2)}, u32[]{:S(2)}) collective-permute-start(bf16[6,12,2048]{2,1,0:T(8,128)(2,1)S(1)} %pad_maximum_fusion.2), channel_id=1, source_target_pairs={{2,1},{3,0},{4,3},{5,2},{6,5},{7,4},{8,7},{9,6},{10,9},{11,8},{12,... | collective-permute-start | bytes 884744 | tf_op jit(solution)/shard_map/ppermute | solution.py:137
  82.0 56.1 %collective-permute-start.9 = (bf16[8,12,2048]{2,1,0:T(8,128)(2,1)}, bf16[8,12,2048]{2,1,0:T(8,128)(2,1)}, u32[]{:S(2)}, u32[]{:S(2)}) collective-permute-start(bf16[8,12,2048]{2,1,0:T(8,128)(2,1)} %pad_maximum_fusion.1), channel_id=1, source_target_pairs={{0,1},{1,0},{2,3},{3,2},{4,5},{5,4},{6,7},{7,6},{8,9},{9,8},{10,11... | collective-permute-start | bytes 1179656 | tf_op jit(solution)/shard_map/ppermute | solution.py:137
  83.5 41.2 %copy-start.11 = (bf16[128,512]{1,0:T(8,128)(2,1)S(1)}, bf16[128,512]{1,0:T(8,128)(2,1)}, u32[]{:S(2)}) copy-start(bf16[128,512]{1,0:T(8,128)(2,1)} %get-tuple-element.22) | copy-start | bytes 393220
  83.7 33.5 %collective-permute-start.10 = (bf16[6,12,2048]{2,1,0:T(8,128)(2,1)S(1)}, bf16[6,12,2048]{2,1,0:T(8,128)(2,1)S(1)}, u32[]{:S(2)}, u32[]{:S(2)}) collective-permute-start(bf16[6,12,2048]{2,1,0:T(8,128)(2,1)S(1)} %pad_maximum_fusion.3), channel_id=1, source_target_pairs={{0,3},{1,2},{2,5},{3,4},{4,7},{5,6},{6,9},{7,8},{8,11},{9,10},{10,... | collective-permute-start | bytes 884744 | tf_op jit(solution)/shard_map/ppermute | solution.py:137
  91.6 47.8 %collective-permute-start.11 = (bf16[6,16,2048]{2,1,0:T(8,128)(2,1)}, bf16[6,16,2048]{2,1,0:T(8,128)(2,1)}, u32[]{:S(2)}, u32[]{:S(2)}) collective-permute-start(bf16[6,16,2048]{2,1,0:T(8,128)(2,1)} %get-tuple-element.9), channel_id=1, source_target_pairs={{0,2},{1,3},{2,4},{3,5},{4,6},{5,7},{6,8},{7,9},{8,10},{9,11},{10,... | collective-permute-start | bytes 1179656 | tf_op jit(solution)/shard_map/ppermute | solution.py:137
  97.1 42.2 %collective-permute-start.8 = (bf16[6,16,2048]{2,1,0:T(8,128)(2,1)}, bf16[6,16,2048]{2,1,0:T(8,128)(2,1)}, u32[]{:S(2)}, u32[]{:S(2)}) collective-permute-start(bf16[6,16,2048]{2,1,0:T(8,128)(2,1)} %get-tuple-element.8), channel_id=1, source_target_pairs={{2,0},{3,1},{4,2},{5,3},{6,4},{7,5},{8,6},{9,7},{10,8},{11,9},{12,... | collective-permute-start | bytes 1179656 | tf_op jit(solution)/shard_map/ppermute | solution.py:137
  117.2 7.5 %collective-permute-start.13 = (bf16[256,512]{1,0:T(8,128)(2,1)S(1)}, bf16[256,512]{1,0:T(8,128)(2,1)S(1)}, u32[]{:S(2)}, u32[]{:S(2)}) collective-permute-start(bf16[256,512]{1,0:T(8,128)(2,1)S(1)} %pad_maximum_fusion.5), channel_id=1, source_target_pairs={{0,1},{1,0},{2,3},{3,2},{4,5},{5,4},{6,7},{7,6},{8,9},{9,8},{10,11... | collective-permute-start | bytes 786440 | tf_op jit(solution)/shard_map/ppermute | solution.py:261
  126.9 24.7 %all-to-all-start = ((bf16[8,64,512]{2,1,0:T(8,128)(2,1)}), bf16[8,64,512]{2,1,0:T(8,128)(2,1)S(1)}, u32[]{:S(2)}, u32[]{:S(2)}) async-start(bf16[8,64,512]{2,1,0:T(8,128)(2,1)} %bitcast.56), calls=%async_computation | async-start | bytes 1048576 | tf_op jit(solution)/shard_map/all_to_all | solution.py:460
  139.3 2.4 %copy-start.1 = (bf16[512,8,2,128]{0,3,2,1:T(8,128)(2,1)S(1)}, bf16[512,8,2,128]{0,3,2,1:T(8,128)(2,1)}, u32[]{:S(2)}) copy-start(bf16[512,8,2,128]{0,3,2,1:T(8,128)(2,1)} %copy-done) | copy-start | bytes 6291460
  141.7 1.0 copy-start.14
  141.7 2.5 %copy-start.8 = (f32[128,512]{1,0:T(8,128)S(1)}, f32[128,512]{1,0:T(8,128)}, u32[]{:S(2)}) copy-start(f32[128,512]{1,0:T(8,128)} %fusion.33) | copy-start | bytes 786436

commit v6 on v5

--- a/solution.py
+++ b/solution.py
@@ -39,13 +39,12 @@
     return block
 
 
-def attention_kernel(q_ref, kv_ref, g_ref, bias_ref, att_ref, gq_ref, gkv_ref, *, head_dim, scale):
+def attention_kernel(q_ref, k_ref, v_ref, g_ref, bias_ref, att_ref, gq_ref, gkv_ref, *, head_dim, scale):
     q = q_ref[...]
     g = g_ref[...]
     lanes = q.shape[1]
-    kv = kv_ref[...]
-    k = kv[:, :lanes]
-    v = kv[:, lanes:]
+    k = k_ref[...]
+    v = v_ref[...]
     bias = bias_ref[...]
     lane = lax.broadcasted_iota(jnp.int32, (1, lanes), 1)
     q32 = q.astype(jnp.float32)
@@ -83,9 +82,9 @@
     gkv_ref[:, lanes:] = gv
 
 
-def block_attention(query, key_values, grad_attn, bias, heads):
+def block_attention(query, projected, grad_attn, bias, heads):
     queries, width = query.shape
-    keys = key_values.shape[0]
+    keys = projected.shape[0]
     head_dim = width // heads
     lanes = 128
     pairs = width // lanes
@@ -102,7 +101,8 @@
         grid=(pairs,),
         in_specs=[
             pl.BlockSpec((queries, lanes), lambda h: (0, h)),
-            pl.BlockSpec((keys, 2 * lanes), lambda h: (0, h)),
+            pl.BlockSpec((keys, lanes), lambda h: (0, h + pairs)),
+            pl.BlockSpec((keys, lanes), lambda h: (0, h + 2 * pairs)),
             pl.BlockSpec((queries, lanes), lambda h: (0, h)),
             pl.BlockSpec((queries, keys), lambda h: (0, 0)),
         ],
@@ -118,7 +118,7 @@
         ],
         cost_estimate=cost,
         name="block_attention",
-    )(query, key_values, grad_attn, bias)
+    )(query, projected, projected, grad_attn, bias)
 
 
 def grid_pairs(delta_lat, delta_lon):
@@ -249,14 +249,6 @@
     return lax.all_gather(value, axis, axis=0, tiled=False)
 
 
-def arranged(weights, width):
-    rows = weights.shape[0]
-    lanes = 128
-    pairs = width // lanes
-    kv = weights[:, width:].reshape(rows, 2, pairs, lanes).transpose(0, 2, 1, 3)
-    return weights[:, :width], kv.reshape(rows, 2 * width)
-
-
 def swap(value, axis):
     return lax.ppermute(value, axis, [(0, 1), (1, 0)])
 
@@ -362,25 +354,18 @@
             jnp.concatenate([other_part, mine_part], axis=1),
         )
 
-        own_q, own_kv = arranged(w_qkv, width)
-        other_q, other_kv = arranged(qkv_other, width)
-
-        def project(rows, own_w, other_w):
+        def project(rows):
             own = jnp.dot(
-                columns(rows, dp_index, rows_half), own_w, preferred_element_type=jnp.float32
+                columns(rows, dp_index, rows_half), w_qkv, preferred_element_type=jnp.float32
             )
             other = jnp.dot(
-                columns(rows, 1 - dp_index, rows_half), other_w, preferred_element_type=jnp.float32
+                columns(rows, 1 - dp_index, rows_half), qkv_other, preferred_element_type=jnp.float32
             )
             return (own + other).astype(jnp.bfloat16)
 
-        def back_project(grad_q, grad_kv):
-            own = lax.dot_general(grad_q, own_q, TRANS_B, preferred_element_type=jnp.float32)
-            own = own + lax.dot_general(grad_kv, own_kv, TRANS_B, preferred_element_type=jnp.float32)
-            other = lax.dot_general(grad_q, other_q, TRANS_B, preferred_element_type=jnp.float32)
-            other = other + lax.dot_general(
-                grad_kv, other_kv, TRANS_B, preferred_element_type=jnp.float32
-            )
+        def back_project(grad_proj):
+            own = lax.dot_general(grad_proj, w_qkv, TRANS_B, preferred_element_type=jnp.float32)
+            other = lax.dot_general(grad_proj, qkv_other, TRANS_B, preferred_element_type=jnp.float32)
             own = own.astype(jnp.bfloat16)
             other = other.astype(jnp.bfloat16)
             return jnp.where(
@@ -388,9 +373,6 @@
                 jnp.concatenate([own, other], axis=1),
                 jnp.concatenate([other, own], axis=1),
             )
-
-        query = project(flat_inputs, own_q, other_q)
-        kv_weights = (own_kv, other_kv)
     else:
         panels = lax.all_gather(w_qkv, "dp", axis=0, tiled=True)
         cot_blocks = flat_grad.reshape(token_count, lon_count, cols_block).transpose(1, 0, 2)
@@ -398,25 +380,23 @@
         cot_group = gather_members(cot_lon, "dp").reshape(-1, cols_block)
         grad_attn = partner_rows_product(flat_grad, w_out, "dp")
 
-        full_q, full_kv = arranged(panels, width)
-
-        def project(rows, weights, unused):
-            out = jnp.dot(rows, weights, preferred_element_type=jnp.float32)
+
+        def project(rows):
+            out = jnp.dot(rows, panels, preferred_element_type=jnp.float32)
             return out.astype(jnp.bfloat16)
 
-        def back_project(grad_q, grad_kv):
-            out = lax.dot_general(grad_q, full_q, TRANS_B, preferred_element_type=jnp.float32)
-            out = out + lax.dot_general(grad_kv, full_kv, TRANS_B, preferred_element_type=jnp.float32)
+        def back_project(grad_proj):
+            out = lax.dot_general(grad_proj, panels, TRANS_B, preferred_element_type=jnp.float32)
             return out.astype(jnp.bfloat16)
-
-        query = project(flat_inputs, full_q, None)
-        kv_weights = (full_kv, None)
 
     tok_ext = halo_gather(inputs_here, radius)
     tok_ext = jnp.pad(tok_ext, ((0, 0), (0, pad_cols - ext_cols), (0, 0)))
     tok_ext = tok_ext.reshape(key_count, width)
 
-    key_values = project(tok_ext, *kv_weights)
+    projected = project(tok_ext)
+    query = projected.reshape(ext_rows, pad_cols, 3 * width)[
+        radius : radius + height, radius : radius + breadth, :width
+    ].reshape(token_count, width)
 
     wrapped = jnp.concatenate(
         [valid_cells[:, -radius:], valid_cells, valid_cells[:, :radius]], axis=1
@@ -437,7 +417,7 @@
     allowed = inside & ((valid_ext == 1) | itself)
     bias = jnp.where(allowed, 0.0, -jnp.inf).astype(jnp.float32)
 
-    attended, grad_query, grad_kv = block_attention(query, key_values, grad_attn, bias, HEADS)
+    attended, grad_query, grad_kv = block_attention(query, projected, grad_attn, bias, HEADS)
 
     grad_kv_ext = grad_kv.reshape(ext_rows, pad_cols, 2 * width)[:, :ext_cols]
     (grad_kv_own,) = halo_return([grad_kv_ext], height, breadth, radius)
@@ -460,8 +440,15 @@
     spread = lax.all_to_all(partial.astype(jnp.bfloat16), "lat", 0, 0, tiled=True)
     d_w_out = spread.astype(jnp.float32).reshape(lat_count, rows_block, cols_block).sum(axis=0)
 
-    grad_kv_low = grad_kv_own.astype(jnp.bfloat16).reshape(token_count, 2 * width)
-    d_input = back_project(grad_query, grad_kv_low).reshape(1, height, breadth, width)
+    pairs = width // 128
+    grad_kv_low = (
+        grad_kv_own.astype(jnp.bfloat16)
+        .reshape(token_count, pairs, 2, 128)
+        .transpose(0, 2, 1, 3)
+        .reshape(token_count, 2 * width)
+    )
+    grad_proj = jnp.concatenate([grad_query, grad_kv_low], axis=1)
+    d_input = back_project(grad_proj).reshape(1, height, breadth, width)
     return (d_input, d_w_out)
 
 

time: 153 us -> 146 us (0.954)
  waiting for transfers between devices: 35.8 us -> 25.1 us
  other arithmetic: 14.9 us -> 19.1 us
  matrix products: 17.4 us -> 15.2 us
    all_to_all x1, waiting for transfers between devices: 6.16 us -> 0.01 us  [shards(): lax.all_to_all(partial.astype(jnp.bfloat16), 'lat', 0, 0, tiled=True)]
    slice x2 -> x1, local copies, waits for them, and re-layouts: 4.76 us -> 0.78 us  [shards(): projected.reshape(ext_rows, pad_cols, 3 * width)]
    unnamed x32 -> x23, local copies, waits for them, and re-layouts: 5.25 us -> 2.08 us
    ppermute x10, waiting for transfers between devices: 22.8 us -> 19.7 us  [sent_to(): return lax.ppermute(value, ('lat', 'lon'), grid_pairs(delta_lat, delta_lon))]
    slice x6, local copies, waits for them, and re-layouts: 5.18 us -> 8.16 us  [grouped_send(): out[i] = got[:, offset:offset + value.shape[1]]]
    dot_general x8 -> x4, matrix products: 14.2 us -> 11.8 us  [the longest x1 4.19 us: project(): jnp.dot(columns(rows, 1 - dp_index, rows_half), qkv_other, preferred_elem...]
    reshape x0 -> x1, local copies, waits for them, and re-layouts: none -> 2.19 us  [shards(): grad_kv_low = grad_kv_own.astype(jnp.bfloat16).reshape(token_count, pairs...]
    pallas_call x0 -> x1, local copies, waits for them, and re-layouts: none -> 1.79 us  [block_attention(): pl.pallas_call(kernel, grid=(pairs,), in_specs=[pl.BlockSpec((queries, la...]
  transfers between devices with their start and end apart: 16 -> 16, of which waited for: 4 -> 3; matrix products, arithmetic and copies ran while one was open for 34% -> 36% of each run, Pallas kernels for 11% -> 12%
where the time goes in v6:
time: 146 us; the launch traced here: 145 us
  starting transfers between devices  43.5 us (30%)
  waiting for transfers between devices  25.1 us (17%)
  local copies, waits for them, and re-layouts  24.1 us (17%)
  other arithmetic  19.1 us (13%)
  Pallas kernels  17.4 us (12%)
  matrix products  15.2 us (10%)
    ppermute x10, starting transfers between devices, sent_to(): return lax.ppermute(value, ('lat', 'lon'), grid_pairs(delta_lat, delta_lon))  31.2 us
    ppermute x10, waiting for transfers between devices, sent_to(): return lax.ppermute(value, ('lat', 'lon'), grid_pairs(delta_lat, delta_lon))  19.7 us
    pallas_call x1, Pallas kernels, block_attention(): pl.pallas_call(kernel, grid=(pairs,), in_specs=[pl.BlockSpec((queries, la...  17.4 us
    all_to_all x1, starting transfers between devices, shards(): lax.all_to_all(partial.astype(jnp.bfloat16), 'lat', 0, 0, tiled=True)  11.1 us
    slice x6, local copies, waits for them, and re-layouts, grouped_send(): out[i] = got[:, offset:offset + value.shape[1]]  8.16 us
    ppermute x5, waiting for transfers between devices, swap(): return lax.ppermute(value, axis, [(0, 1), (1, 0)])  5.44 us
    concatenate x6, other arithmetic, grouped_send(): got = sent_to(jnp.concatenate(values, axis=1), dl, db)  5.11 us
    dot_general x1, matrix products, project(): jnp.dot(columns(rows, 1 - dp_index, rows_half), qkv_other, preferred_elem...  4.19 us
  transfers between devices with their start and end apart: 16, of which 3 were waited for; matrix products, arithmetic and copies ran while one was open for 36% of the time, Pallas kernels for 12%

profile of v6, /device:TPU:0, one launch (start us, length us, event | category | flops | bytes accessed | tf_op | source)
XLA Modules:
  0.0 145.3 jit_solution(14473442366214632067)
XLA Ops:
  0.7 1.2 fusion.69
  1.9 0.7 pad_maximum_fusion.10
  2.6 6.5 %collective-permute-start = (bf16[6,12,1024]{2,1,0:T(8,128)(2,1)}, bf16[6,12,1024]{2,1,0:T(8,128)(2,1)}, u32[]{:S(2)}, u32[]{:S(2)}) collective-permute-start(bf16[6,12,1024]{2,1,0:T(8,128)(2,1)} %pad_maximum_fusion.10), channel_id=1, source_target_pairs={{0,3},{1,2},{2,5},{3,4},{4,7},{5,6},{6,9},{7,8},{8,11},{9,10},{10,... | collective-permute-start | bytes 442376 | tf_op jit(solution)/shard_map/ppermute | solution.py:137
  9.1 0.7 pad_maximum_fusion.11
  9.9 1.3 collective-permute-start.3
  11.1 1.0 fusion.70
  12.2 0.8 pad_maximum_fusion.7
  12.9 0.5 collective-permute-start.2
  13.5 0.8 slice_bitcast_fusion.1
  14.3 6.2 %collective-permute-start.1 = (bf16[6,16,1024]{2,1,0:T(8,128)(2,1)}, bf16[6,16,1024]{2,1,0:T(8,128)(2,1)}, u32[]{:S(2)}, u32[]{:S(2)}) collective-permute-start(bf16[6,16,1024]{2,1,0:T(8,128)(2,1)} %get-tuple-element.28), channel_id=1, source_target_pairs={{0,2},{1,3},{2,4},{3,5},{4,6},{5,7},{6,8},{7,9},{8,10},{9,11},{10,... | collective-permute-start | bytes 589832 | tf_op jit(solution)/shard_map/ppermute | solution.py:137
  20.6 0.1 copy.16
  20.7 0.1 copy.18
  20.9 0.1 pad_dynamic-slice_fusion
  21.0 0.1 eq.28
  21.1 1.0 fusion.45.bias_ref
  22.1 0.5 convolution_convert_fusion.1
  22.6 0.7 constant_dynamic-slice_fusion.3
  23.3 0.1 pad_maximum_fusion
  23.4 1.6 %collective-permute-start.4 = (bf16[6,16,1024]{2,1,0:T(8,128)(2,1)}, bf16[6,16,1024]{2,1,0:T(8,128)(2,1)S(1)}, u32[]{:S(2)}, u32[]{:S(2)}) collective-permute-start(bf16[6,16,1024]{2,1,0:T(8,128)(2,1)} %get-tuple-element.29), channel_id=1, source_target_pairs={{2,0},{3,1},{4,2},{5,3},{6,4},{7,5},{8,6},{9,7},{10,8},{11,9},{12,... | collective-permute-start | bytes 589832 | tf_op jit(solution)/shard_map/ppermute | solution.py:137
  25.0 1.0 fusion.71
  26.1 0.6 collective-permute-start.6
  26.6 1.0 fusion.72
  27.7 1.1 fusion.68
  28.8 4.4 %collective-permute-done.4 = bf16[6,16,1024]{2,1,0:T(8,128)(2,1)S(1)} collective-permute-done((bf16[6,16,1024]{2,1,0:T(8,128)(2,1)}, bf16[6,16,1024]{2,1,0:T(8,128)(2,1)S(1)}, u32[]{:S(2)}, u32[]{:S(2)}) %collective-permute-start.4) | collective-permute-done | bytes 196640 | tf_op jit(solution)/shard_map/ppermute | solution.py:137
  33.1 1.7 %fusion.12 = bf16[20,32,1024]{2,1,0:T(8,128)(2,1)S(1)} fusion(bf16[6,6,1024]{2,1,0:T(8,128)(2,1)S(1)} %get-tuple-element.41, bf16[6,16,1024]{2,1,0:T(8,128)(2,1)S(1)} %collective-permute-done.4, bf16[6,6,1024]{2,1,0:T(8,128)(2,1)S(1)} %get-tuple-element.40, bf16[8,6,1024]{2,1,0:T(8,128)(2,1)S(1)} %get-tuple-element.31, ...), kind=kLoop, calls=%fused_computation.15 | loop fusion | flops 18350080 | bytes 2457600 | tf_op jit(solution)/shard_map/concatenate | solution.py:178
  34.8 2.2 %fusion.29 = f32[640,3072]{1,0:T(8,128)S(1)} fusion(bf16[512,3072]{1,0:T(8,128)(2,1)S(1)} %copy-done.3, bf16[640,1024]{1,0:T(8,128)(2,1)S(1)} %bitcast.30, s32[]{:T(128)S(6)} %select_n.95), kind=kOutput, calls=%fused_computation.40 | convolution fusion | flops 2013265920 | bytes 11665412 | tf_op jit(solution)/shard_map/dot_general | solution.py:358
  37.1 0.7 constant_dynamic-slice_fusion.2
  37.8 0.7 pad_maximum_fusion.9
  38.5 0.5 collective-permute-start.14
  39.0 0.5 fusion.18
  39.5 0.8 maximum_select_fusion.g_ref
  40.3 4.2 %add_convert_fusion.k_ref.v_ref = bf16[640,3072]{1,0:T(8,128)(2,1)S(1)} fusion(f32[640,3072]{1,0:T(8,128)S(1)} %fusion.29, bf16[512,3072]{1,0:T(8,128)(2,1)} %collective-permute-done.5, bf16[640,1024]{1,0:T(8,128)(2,1)S(1)} %bitcast.31, s32[]{:T(128)S(6)} %select_n.96), kind=kOutput, calls=%fused_computation | convolution fusion | flops 2017198080 | bytes 15597572 | tf_op jit(solution)/shard_map/dot_general | solution.py:361
  44.5 1.9 %copy-done = bf16[640,3072]{1,0:T(8,128)(2,1)} copy-done((bf16[640,3072]{1,0:T(8,128)(2,1)}, bf16[640,3072]{1,0:T(8,128)(2,1)S(1)}, u32[]{:S(2)}) %copy-start) | copy-done | bytes 3932184
  46.5 0.8 slice.174
  47.2 17.4 %block_attention.1 = (bf16[128,1024]{1,0:T(8,128)(2,1)}, bf16[128,1024]{1,0:T(8,128)(2,1)}, f32[640,2048]{1,0:T(8,128)}) custom-call(bf16[128,1024]{1,0:T(8,128)(2,1)} %bitcast.37, bf16[640,3072]{1,0:T(8,128)(2,1)} %copy-done, bf16[640,3072]{1,0:T(8,128)(2,1)} %copy-done, bf16[128,1024]{1,0:T(8,128)(2,1)} %maximum_select_fusion.g_ref, ...), custom_call_target="tpu_custom_call" | custom-call | flops 2013265920 | bytes 9240576 | tf_op jit(solution)/shard_map/block_attention/pallas_call | solution.py:99
  64.6 2.9 %convert.26 = bf16[20,32,2048]{2,1,0:T(8,128)(2,1)S(1)} convert(f32[20,32,2048]{2,1,0:T(8,128)} %bitcast.25) | non-fusion elementwise | flops 1310720 | bytes 7864320 | tf_op jit(solution)/shard_map/convert.23
  67.5 0.1 fusion.63
  67.8 1.3 fusion.62
  69.0 0.7 constant_dynamic-slice_fusion.5
  69.7 0.9 pad_maximum_fusion.5
  70.6 1.3 collective-permute-start.7
  71.9 1.0 pad_maximum_fusion.2
  72.9 1.5 %collective-permute-start.9 = (bf16[8,12,2048]{2,1,0:T(8,128)(2,1)}, bf16[8,12,2048]{2,1,0:T(8,128)(2,1)}, u32[]{:S(2)}, u32[]{:S(2)}) collective-permute-start(bf16[8,12,2048]{2,1,0:T(8,128)(2,1)} %pad_maximum_fusion.2), channel_id=1, source_target_pairs={{0,1},{1,0},{2,3},{3,2},{4,5},{5,4},{6,7},{7,6},{8,9},{9,8},{10,11... | collective-permute-start | bytes 1179656 | tf_op jit(solution)/shard_map/ppermute | solution.py:137
  74.4 0.9 pad_maximum_fusion.6
  75.3 6.2 %collective-permute-start.10 = (bf16[6,12,2048]{2,1,0:T(8,128)(2,1)}, bf16[6,12,2048]{2,1,0:T(8,128)(2,1)}, u32[]{:S(2)}, u32[]{:S(2)}) collective-permute-start(bf16[6,12,2048]{2,1,0:T(8,128)(2,1)} %pad_maximum_fusion.6), channel_id=1, source_target_pairs={{0,3},{1,2},{2,5},{3,4},{4,7},{5,6},{6,9},{7,8},{8,11},{9,10},{10,... | collective-permute-start | bytes 884744 | tf_op jit(solution)/shard_map/ppermute | solution.py:137
  81.5 1.8 %copy.20 = bf16[128,1024]{0,1:T(8,128)(2,1)} copy(bf16[128,1024]{1,0:T(8,128)(2,1)} %get-tuple-element.5) | data formatting | bytes 524288 | tf_op jit(solution)/shard_map/block_attention/pallas_call | solution.py:99
  83.3 4.9 %collective-permute-start.11 = (bf16[6,16,2048]{2,1,0:T(8,128)(2,1)}, bf16[6,16,2048]{2,1,0:T(8,128)(2,1)}, u32[]{:S(2)}, u32[]{:S(2)}) collective-permute-start(bf16[6,16,2048]{2,1,0:T(8,128)(2,1)} %get-tuple-element.9), channel_id=1, source_target_pairs={{0,2},{1,3},{2,4},{3,5},{4,6},{5,7},{6,8},{7,9},{8,10},{9,11},{10,... | collective-permute-start | bytes 1179656 | tf_op jit(solution)/shard_map/ppermute | solution.py:137
  88.2 0.9 pad_maximum_fusion.8
  89.1 1.3 collective-permute-start.8
  90.4 1.9 %fusion.66 = (bf16[6,6,2048]{2,1,0:T(8,128)(2,1)}, bf16[6,6,2048]{2,1,0:T(8,128)(2,1)}) fusion(bf16[6,12,2048]{2,1,0:T(8,128)(2,1)} %collective-permute-done.7), kind=kLoop, calls=%fused_computation.111 | loop fusion | bytes 589824 | tf_op jit(solution)/shard_map/slice | solution.py:159
  92.3 15.3 %collective-permute-done.10 = bf16[6,12,2048]{2,1,0:T(8,128)(2,1)} collective-permute-done((bf16[6,12,2048]{2,1,0:T(8,128)(2,1)}, bf16[6,12,2048]{2,1,0:T(8,128)(2,1)}, u32[]{:S(2)}, u32[]{:S(2)}) %collective-permute-start.10) | collective-permute-done | bytes 294944 | tf_op jit(solution)/shard_map/ppermute | solution.py:137
  107.7 0.2 collective-permute-start.13
  107.8 1.9 %fusion.67 = (bf16[6,6,2048]{2,1,0:T(8,128)(2,1)}, bf16[6,6,2048]{2,1,0:T(8,128)(2,1)}) fusion(bf16[6,12,2048]{2,1,0:T(8,128)(2,1)} %collective-permute-done.10), kind=kLoop, calls=%fused_computation.112 | loop fusion | bytes 589824 | tf_op jit(solution)/shard_map/slice | solution.py:159
  109.8 5.4 %collective-permute-done.13 = bf16[256,512]{1,0:T(8,128)(2,1)S(1)} collective-permute-done((bf16[256,512]{1,0:T(8,128)(2,1)S(1)}, bf16[256,512]{1,0:T(8,128)(2,1)S(1)}, u32[]{:S(2)}, u32[]{:S(2)}) %collective-permute-start.13) | collective-permute-done | bytes 262176 | tf_op jit(solution)/shard_map/ppermute | solution.py:253
  115.2 2.4 %fusion.17 = bf16[512,512]{1,0:T(8,128)(2,1)} fusion(bf16[256,512]{1,0:T(8,128)(2,1)S(1)} %collective-permute-done.13, bf16[128,512]{1,0:T(8,128)(2,1)} %collective-permute-done.12, bf16[128,512]{1,0:T(8,128)(2,1)S(1)} %get-tuple-element.26, bf16[256,512]{1,0:T(8,128)(2,1)} %collective-permute-done.14, bf16[128,512]{1,0:T(8,128)(2,1)} %get-tuple-element.24, ...), kind=kOutput, calls=%fused_computation.21 | convolution fusion | flops 272105472 | bytes 1572864 | tf_op jit(solution)/shard_map/dot_general | solution.py:437
  117.6 11.1 %all-to-all-start = ((bf16[8,64,512]{2,1,0:T(8,128)(2,1)}), bf16[8,64,512]{2,1,0:T(8,128)(2,1)}, u32[]{:S(2)}, u32[]{:S(2)}) async-start(bf16[8,64,512]{2,1,0:T(8,128)(2,1)} %bitcast.38), calls=%async_computation | async-start | bytes 1048576 | tf_op jit(solution)/shard_map/all_to_all | solution.py:440
  128.7 1.2 fusion.65
  129.9 3.2 %fusion.26 = bf16[8,16,2048]{2,1,0:T(8,128)(2,1)} fusion(f32[20,32,2048]{2,1,0:T(8,128)} %bitcast.26, bf16[6,6,2048]{2,1,0:T(8,128)(2,1)} %get-tuple-element.21, bf16[6,16,2048]{2,1,0:T(8,128)(2,1)} %collective-permute-done.11, bf16[6,6,2048]{2,1,0:T(8,128)(2,1)} %get-tuple-element.20, bf16[8,6,2048]{2,1,0:T(8,128)(2,1)S(1)} %get-tuple-element.17, ...), kind=kLoop, calls=%fused_computation.35 | loop fusion | flops 4456448 | bytes 3342336 | tf_op jit(solution)/shard_map/convert_element_type | solution.py:445
  133.1 2.2 %reshape.145 = bf16[128,8,2,128]{3,2,1,0:T(2,128)(2,1)} reshape(bf16[8,16,2048]{2,1,0:T(8,128)(2,1)} %fusion.26) | data formatting | bytes 1048576 | tf_op jit(solution)/shard_map/reshape | solution.py:446
  135.3 2.0 %copy.19 = bf16[128,2,8,128]{0,3,2,1:T(8,128)(2,1)} copy(bf16[128,2,8,128]{3,1,2,0:T(2,128)(2,1)} %bitcast.36) | data formatting | bytes 1048576 | tf_op jit(solution)/shard_map/transpose | solution.py:447
  137.3 2.3 %convolution_convert_fusion.3 = bf16[128,512]{1,0:T(8,128)(2,1)S(1)} fusion(bf16[512,3072]{1,0:T(8,128)(2,1)S(1)} %copy-done.3, bf16[128,2048]{0,1:T(8,128)(2,1)} %bitcast.39, bf16[128,1024]{0,1:T(8,128)(2,1)} %copy.20), kind=kOutput, calls=%fused_computation.25 | convolution fusion | flops 404291584 | bytes 4063232 | tf_op jit(solution)/shard_map/dot_general | solution.py:367
  139.7 3.1 %convolution_convert_fusion.2 = bf16[128,512]{1,0:T(8,128)(2,1)S(1)} fusion(bf16[512,3072]{1,0:T(8,128)(2,1)} %collective-permute-done.5, bf16[128,2048]{0,1:T(8,128)(2,1)S(1)} %bitcast.40, bf16[128,1024]{0,1:T(8,128)(2,1)S(1)} %copy-done.8), kind=kOutput, calls=%fused_computation.24 | convolution fusion | flops 404291584 | bytes 4063232 | tf_op jit(solution)/shard_map/dot_general | solution.py:368
  142.8 0.8 maximum_select_fusion.1
  143.6 1.8 %convert_reduce_fusion = f32[64,512]{1,0:T(8,128)} fusion(bf16[8,64,512]{2,1,0:T(8,128)(2,1)} %all-to-all-done), kind=kLoop, calls=%fused_computation.37 | loop fusion | flops 491520 | bytes 655360 | tf_op jit(solution)/shard_map/reduce_sum | solution.py:441
  (44 shorter events, 0.4 us)
Async XLA Ops:
  0.6 12.9 %copy-start.1 = (bf16[1,8,16,1024]{3,2,1,0:T(8,128)(2,1)S(1)}, bf16[1,8,16,1024]{3,2,1,0:T(8,128)(2,1)}, u32[]{:S(2)}) copy-start(bf16[1,8,16,1024]{3,2,1,0:T(8,128)(2,1)} %param.5) | copy-start | bytes 786436
  0.6 19.8 %copy-start.10 = (s32[64,32]{0,1:T(8,128)S(1)}, s32[64,32]{0,1:T(8,128)}, u32[]{:S(2)}) copy-start(s32[64,32]{0,1:T(8,128)} %param.7) | copy-start | bytes 24580
  0.7 21.5 %copy-start.4 = (bf16[1,8,16,1024]{3,2,1,0:T(8,128)(2,1)S(1)}, bf16[1,8,16,1024]{3,2,1,0:T(8,128)(2,1)}, u32[]{:S(2)}) copy-start(bf16[1,8,16,1024]{3,2,1,0:T(8,128)(2,1)} %param.6) | copy-start | bytes 786436
  0.7 21.4 %copy-start.2 = (bf16[512,1024]{1,0:T(8,128)(2,1)S(1)}, bf16[512,1024]{1,0:T(8,128)(2,1)}, u32[]{:S(2)}) copy-start(bf16[512,1024]{1,0:T(8,128)(2,1)} %param.9) | copy-start | bytes 3145732
  2.6 20.8 %collective-permute-start = (bf16[6,12,1024]{2,1,0:T(8,128)(2,1)}, bf16[6,12,1024]{2,1,0:T(8,128)(2,1)}, u32[]{:S(2)}, u32[]{:S(2)}) collective-permute-start(bf16[6,12,1024]{2,1,0:T(8,128)(2,1)} %pad_maximum_fusion.10), channel_id=1, source_target_pairs={{0,3},{1,2},{2,5},{3,4},{4,7},{5,6},{6,9},{7,8},{8,11},{9,10},{10,... | collective-permute-start | bytes 442376 | tf_op jit(solution)/shard_map/ppermute | solution.py:137
  9.9 16.2 %collective-permute-start.3 = (bf16[6,12,1024]{2,1,0:T(8,128)(2,1)}, bf16[6,12,1024]{2,1,0:T(8,128)(2,1)}, u32[]{:S(2)}, u32[]{:S(2)}) collective-permute-start(bf16[6,12,1024]{2,1,0:T(8,128)(2,1)} %pad_maximum_fusion.11), channel_id=1, source_target_pairs={{2,1},{3,0},{4,3},{5,2},{6,5},{7,4},{8,7},{9,6},{10,9},{11,8},{12,... | collective-permute-start | bytes 442376 | tf_op jit(solution)/shard_map/ppermute | solution.py:137
  12.9 14.7 %collective-permute-start.2 = (bf16[8,12,1024]{2,1,0:T(8,128)(2,1)}, bf16[8,12,1024]{2,1,0:T(8,128)(2,1)}, u32[]{:S(2)}, u32[]{:S(2)}) collective-permute-start(bf16[8,12,1024]{2,1,0:T(8,128)(2,1)} %pad_maximum_fusion.7), channel_id=1, source_target_pairs={{0,1},{1,0},{2,3},{3,2},{4,5},{5,4},{6,7},{7,6},{8,9},{9,8},{10,11... | collective-permute-start | bytes 589832 | tf_op jit(solution)/shard_map/ppermute | solution.py:137
  14.3 14.5 %collective-permute-start.1 = (bf16[6,16,1024]{2,1,0:T(8,128)(2,1)}, bf16[6,16,1024]{2,1,0:T(8,128)(2,1)}, u32[]{:S(2)}, u32[]{:S(2)}) collective-permute-start(bf16[6,16,1024]{2,1,0:T(8,128)(2,1)} %get-tuple-element.28), channel_id=1, source_target_pairs={{0,2},{1,3},{2,4},{3,5},{4,6},{5,7},{6,8},{7,9},{8,10},{9,11},{10,... | collective-permute-start | bytes 589832 | tf_op jit(solution)/shard_map/ppermute | solution.py:137
  20.5 19.8 %collective-permute-start.5 = (bf16[512,3072]{1,0:T(8,128)(2,1)}, bf16[512,3072]{1,0:T(8,128)(2,1)}, u32[]{:S(2)}, u32[]{:S(2)}) collective-permute-start(bf16[512,3072]{1,0:T(8,128)(2,1)} %param.8), channel_id=1, source_target_pairs={{0,16},{16,0},{1,17},{17,1},{2,18},{18,2},{3,19},{19,3},{4,20},{20... | collective-permute-start | bytes 9437192 | tf_op jit(solution)/shard_map/ppermute | solution.py:253
  23.4 11.4 %copy-start.3 = (bf16[512,3072]{1,0:T(8,128)(2,1)S(1)}, bf16[512,3072]{1,0:T(8,128)(2,1)}, u32[]{:S(2)}) copy-start(bf16[512,3072]{1,0:T(8,128)(2,1)} %param.8) | copy-start | bytes 9437188
  23.4 9.7 %collective-permute-start.4 = (bf16[6,16,1024]{2,1,0:T(8,128)(2,1)}, bf16[6,16,1024]{2,1,0:T(8,128)(2,1)S(1)}, u32[]{:S(2)}, u32[]{:S(2)}) collective-permute-start(bf16[6,16,1024]{2,1,0:T(8,128)(2,1)} %get-tuple-element.29), channel_id=1, source_target_pairs={{2,0},{3,1},{4,2},{5,3},{6,4},{7,5},{8,6},{9,7},{10,8},{11,9},{12,... | collective-permute-start | bytes 589832 | tf_op jit(solution)/shard_map/ppermute | solution.py:137
  26.1 11.0 %collective-permute-start.6 = (bf16[640,1024]{1,0:T(8,128)(2,1)S(1)}, bf16[640,1024]{1,0:T(8,128)(2,1)S(1)}, u32[]{:S(2)}, u32[]{:S(2)}) collective-permute-start(bf16[640,1024]{1,0:T(8,128)(2,1)S(1)} %pad_maximum_fusion), channel_id=1, source_target_pairs={{0,16},{16,0},{1,17},{17,1},{2,18},{18,2},{3,19},{19,3},{4,20},{20... | collective-permute-start | bytes 3932168 | tf_op jit(solution)/shard_map/ppermute | solution.py:253
  34.8 3.0 %copy-start.7 = (bf16[128,512]{1,0:T(8,128)(2,1)S(1)}, bf16[128,512]{1,0:T(8,128)(2,1)}, u32[]{:S(2)}) copy-start(bf16[128,512]{1,0:T(8,128)(2,1)} %get-tuple-element.23) | copy-start | bytes 393220
  34.8 4.2 %copy-start.5 = (bf16[1,8,16,1024]{3,2,1,0:T(8,128)(2,1)S(1)}, bf16[1,8,16,1024]{3,2,1,0:T(8,128)(2,1)}, u32[]{:S(2)}) copy-start(bf16[1,8,16,1024]{3,2,1,0:T(8,128)(2,1)} %param.6) | copy-start | bytes 786436
  38.5 71.3 %collective-permute-start.14 = (bf16[256,512]{1,0:T(8,128)(2,1)}, bf16[256,512]{1,0:T(8,128)(2,1)}, u32[]{:S(2)}, u32[]{:S(2)}) collective-permute-start(bf16[256,512]{1,0:T(8,128)(2,1)} %pad_maximum_fusion.9), channel_id=1, source_target_pairs={{0,1},{1,0},{2,3},{3,2},{4,5},{5,4},{6,7},{7,6},{8,9},{9,8},{10,11... | collective-permute-start | bytes 786440 | tf_op jit(solution)/shard_map/ppermute | solution.py:253
  44.5 2.0 %copy-start = (bf16[640,3072]{1,0:T(8,128)(2,1)}, bf16[640,3072]{1,0:T(8,128)(2,1)S(1)}, u32[]{:S(2)}) copy-start(bf16[640,3072]{1,0:T(8,128)(2,1)S(1)} %add_convert_fusion.k_ref.v_ref) | copy-start | bytes 11796484
  67.5 1.5 %copy-start.9 = (bf16[128,1024]{1,0:T(8,128)(2,1)S(1)}, bf16[128,1024]{1,0:T(8,128)(2,1)}, u32[]{:S(2)}) copy-start(bf16[128,1024]{1,0:T(8,128)(2,1)} %get-tuple-element.7) | copy-start | bytes 786436
  69.7 13.6 %collective-permute-start.12 = (bf16[128,512]{1,0:T(8,128)(2,1)}, bf16[128,512]{1,0:T(8,128)(2,1)}, u32[]{:S(2)}, u32[]{:S(2)}) collective-permute-start(bf16[128,512]{1,0:T(8,128)(2,1)} %get-tuple-element.27), channel_id=1, source_target_pairs={{0,16},{16,0},{1,17},{17,1},{2,18},{18,2},{3,19},{19,3},{4,20},{20... | collective-permute-start | bytes 393224 | tf_op jit(solution)/shard_map/ppermute | solution.py:253
  70.6 18.5 %collective-permute-start.7 = (bf16[6,12,2048]{2,1,0:T(8,128)(2,1)}, bf16[6,12,2048]{2,1,0:T(8,128)(2,1)}, u32[]{:S(2)}, u32[]{:S(2)}) collective-permute-start(bf16[6,12,2048]{2,1,0:T(8,128)(2,1)} %pad_maximum_fusion.5), channel_id=1, source_target_pairs={{2,1},{3,0},{4,3},{5,2},{6,5},{7,4},{8,7},{9,6},{10,9},{11,8},{12,... | collective-permute-start | bytes 884744 | tf_op jit(solution)/shard_map/ppermute | solution.py:137
  72.9 55.7 %collective-permute-start.9 = (bf16[8,12,2048]{2,1,0:T(8,128)(2,1)}, bf16[8,12,2048]{2,1,0:T(8,128)(2,1)}, u32[]{:S(2)}, u32[]{:S(2)}) collective-permute-start(bf16[8,12,2048]{2,1,0:T(8,128)(2,1)} %pad_maximum_fusion.2), channel_id=1, source_target_pairs={{0,1},{1,0},{2,3},{3,2},{4,5},{5,4},{6,7},{7,6},{8,9},{9,8},{10,11... | collective-permute-start | bytes 1179656 | tf_op jit(solution)/shard_map/ppermute | solution.py:137
  75.3 32.3 %collective-permute-start.10 = (bf16[6,12,2048]{2,1,0:T(8,128)(2,1)}, bf16[6,12,2048]{2,1,0:T(8,128)(2,1)}, u32[]{:S(2)}, u32[]{:S(2)}) collective-permute-start(bf16[6,12,2048]{2,1,0:T(8,128)(2,1)} %pad_maximum_fusion.6), channel_id=1, source_target_pairs={{0,3},{1,2},{2,5},{3,4},{4,7},{5,6},{6,9},{7,8},{8,11},{9,10},{10,... | collective-permute-start | bytes 884744 | tf_op jit(solution)/shard_map/ppermute | solution.py:137
  83.3 46.6 %collective-permute-start.11 = (bf16[6,16,2048]{2,1,0:T(8,128)(2,1)}, bf16[6,16,2048]{2,1,0:T(8,128)(2,1)}, u32[]{:S(2)}, u32[]{:S(2)}) collective-permute-start(bf16[6,16,2048]{2,1,0:T(8,128)(2,1)} %get-tuple-element.9), channel_id=1, source_target_pairs={{0,2},{1,3},{2,4},{3,5},{4,6},{5,7},{6,8},{7,9},{8,10},{9,11},{10,... | collective-permute-start | bytes 1179656 | tf_op jit(solution)/shard_map/ppermute | solution.py:137
  89.1 40.7 %collective-permute-start.8 = (bf16[6,16,2048]{2,1,0:T(8,128)(2,1)}, bf16[6,16,2048]{2,1,0:T(8,128)(2,1)}, u32[]{:S(2)}, u32[]{:S(2)}) collective-permute-start(bf16[6,16,2048]{2,1,0:T(8,128)(2,1)} %get-tuple-element.8), channel_id=1, source_target_pairs={{2,0},{3,1},{4,2},{5,3},{6,4},{7,5},{8,6},{9,7},{10,8},{11,9},{12,... | collective-permute-start | bytes 1179656 | tf_op jit(solution)/shard_map/ppermute | solution.py:137
  107.7 7.5 %collective-permute-start.13 = (bf16[256,512]{1,0:T(8,128)(2,1)S(1)}, bf16[256,512]{1,0:T(8,128)(2,1)S(1)}, u32[]{:S(2)}, u32[]{:S(2)}) collective-permute-start(bf16[256,512]{1,0:T(8,128)(2,1)S(1)} %pad_maximum_fusion.8), channel_id=1, source_target_pairs={{0,1},{1,0},{2,3},{3,2},{4,5},{5,4},{6,7},{7,6},{8,9},{9,8},{10,11... | collective-permute-start | bytes 786440 | tf_op jit(solution)/shard_map/ppermute | solution.py:253
  117.6 26.0 %all-to-all-start = ((bf16[8,64,512]{2,1,0:T(8,128)(2,1)}), bf16[8,64,512]{2,1,0:T(8,128)(2,1)}, u32[]{:S(2)}, u32[]{:S(2)}) async-start(bf16[8,64,512]{2,1,0:T(8,128)(2,1)} %bitcast.38), calls=%async_computation | async-start | bytes 1048576 | tf_op jit(solution)/shard_map/all_to_all | solution.py:440
  135.3 4.4 %copy-start.8 = (bf16[128,1024]{0,1:T(8,128)(2,1)S(1)}, bf16[128,1024]{0,1:T(8,128)(2,1)}, u32[]{:S(2)}) copy-start(bf16[128,1024]{0,1:T(8,128)(2,1)} %copy.20) | copy-start | bytes 786436
  137.3 2.4 %copy-start.6 = (bf16[128,2,8,128]{0,3,2,1:T(8,128)(2,1)S(1)}, bf16[128,2,8,128]{0,3,2,1:T(8,128)(2,1)}, u32[]{:S(2)}) copy-start(bf16[128,2,8,128]{0,3,2,1:T(8,128)(2,1)} %copy.19) | copy-start | bytes 1572868

commit v7 on v6

--- a/solution.py
+++ b/solution.py
@@ -325,7 +325,7 @@
     fast = dp_count == 2 and lon_count == 2
 
     if fast:
-        qkv_other = swap(w_qkv, "dp")
+        panels = lax.all_gather(w_qkv, "dp", axis=0, tiled=True)
         dp_got = swap(jnp.concatenate([w_out, flat_grad], axis=0), "dp")
         w_out_other = dp_got[: w_out.shape[0]]
         cot_dp = dp_got[w_out.shape[0] :]
@@ -355,24 +355,12 @@
         )
 
         def project(rows):
-            own = jnp.dot(
-                columns(rows, dp_index, rows_half), w_qkv, preferred_element_type=jnp.float32
-            )
-            other = jnp.dot(
-                columns(rows, 1 - dp_index, rows_half), qkv_other, preferred_element_type=jnp.float32
-            )
-            return (own + other).astype(jnp.bfloat16)
+            out = jnp.dot(rows, panels, preferred_element_type=jnp.float32)
+            return out.astype(jnp.bfloat16)
 
         def back_project(grad_proj):
-            own = lax.dot_general(grad_proj, w_qkv, TRANS_B, preferred_element_type=jnp.float32)
-            other = lax.dot_general(grad_proj, qkv_other, TRANS_B, preferred_element_type=jnp.float32)
-            own = own.astype(jnp.bfloat16)
-            other = other.astype(jnp.bfloat16)
-            return jnp.where(
-                dp_index == 0,
-                jnp.concatenate([own, other], axis=1),
-                jnp.concatenate([other, own], axis=1),
-            )
+            out = lax.dot_general(grad_proj, panels, TRANS_B, preferred_element_type=jnp.float32)
+            return out.astype(jnp.bfloat16)
     else:
         panels = lax.all_gather(w_qkv, "dp", axis=0, tiled=True)
         cot_blocks = flat_grad.reshape(token_count, lon_count, cols_block).transpose(1, 0, 2)
@@ -437,8 +425,7 @@
     partial = lax.dot_general(
         att_group, cot_group, (((0,), (0,)), ((), ())), preferred_element_type=jnp.float32
     ) * (1.0 / device_count)
-    spread = lax.all_to_all(partial.astype(jnp.bfloat16), "lat", 0, 0, tiled=True)
-    d_w_out = spread.astype(jnp.float32).reshape(lat_count, rows_block, cols_block).sum(axis=0)
+    d_w_out = lax.psum_scatter(partial, "lat", scatter_dimension=0, tiled=True)
 
     pairs = width // 128
     grad_kv_low = (

time: 146 us -> 182 us (1.25)
  waiting for transfers between devices: 25.1 us -> 78.7 us
  starting transfers between devices: 43.5 us -> 28.5 us
  between operations: 1 us -> 14.4 us
  local copies, waits for them, and re-layouts: 24.1 us -> 11.2 us
  other arithmetic: 19.1 us -> 13 us
  matrix products: 15.2 us -> 17.6 us
    reduce_scatter x0 -> x1, waiting for transfers between devices: none -> 39.6 us  [shards(): d_w_out = lax.psum_scatter(partial, 'lat', scatter_dimension=0, tiled=True)]
    ppermute x5 -> x4, waiting for transfers between devices: 5.44 us -> 16.6 us  [swap(): return lax.ppermute(value, axis, [(0, 1), (1, 0)])]
    all_to_all x1 -> x0, starting transfers between devices: 11.1 us -> none  [shards(): lax.all_to_all(partial.astype(jnp.bfloat16), 'lat', 0, 0, tiled=True)]
    slice x6, local copies, waits for them, and re-layouts: 8.16 us -> 3.45 us  [grouped_send(): out[i] = got[:, offset:offset + value.shape[1]]]
    ppermute x10, starting transfers between devices: 31.2 us -> 26.6 us  [sent_to(): return lax.ppermute(value, ('lat', 'lon'), grid_pairs(delta_lat, delta_lon))]
    slice x3, local copies, waits for them, and re-layouts: 3.03 us -> 0.89 us  [halo_gather(): block[part(height, radius, da, True), part(breadth, radius, db, True)]]
    ppermute x10, waiting for transfers between devices: 19.7 us -> 21.8 us  [sent_to(): return lax.ppermute(value, ('lat', 'lon'), grid_pairs(delta_lat, delta_lon))]
    dynamic_slice x3, local copies, waits for them, and re-layouts: 2.09 us -> 0.07 us  [columns(): return lax.dynamic_slice_in_dim(value, index * size, size, axis=1)]
  transfers between devices with their start and end apart: 16 -> 16, of which waited for: 3 -> 5; matrix products, arithmetic and copies ran while one was open for 36% -> 22% of each run, Pallas kernels for 12% -> 10%
where the time goes in v7:
time: 182 us; the launch traced here: 181 us
  waiting for transfers between devices  78.7 us (43%)
  starting transfers between devices  28.5 us (16%)
  matrix products  17.6 us (10%)
  Pallas kernels  17.4 us (10%)
  between operations  14.4 us (8%)
  other arithmetic  13 us (7%)
  local copies, waits for them, and re-layouts  11.2 us (6%)
    reduce_scatter x1, waiting for transfers between devices, shards(): d_w_out = lax.psum_scatter(partial, 'lat', scatter_dimension=0, tiled=True)  39.6 us
    ppermute x10, starting transfers between devices, sent_to(): return lax.ppermute(value, ('lat', 'lon'), grid_pairs(delta_lat, delta_lon))  26.6 us
    ppermute x10, waiting for transfers between devices, sent_to(): return lax.ppermute(value, ('lat', 'lon'), grid_pairs(delta_lat, delta_lon))  21.8 us
    pallas_call x1, Pallas kernels, block_attention(): pl.pallas_call(kernel, grid=(pairs,), in_specs=[pl.BlockSpec((queries, la...  17.4 us
    ppermute x4, waiting for transfers between devices, swap(): return lax.ppermute(value, axis, [(0, 1), (1, 0)])  16.6 us
    dot_general x1, matrix products, project(): out = jnp.dot(rows, panels, preferred_element_type=jnp.float32)  7.21 us
    dot_general x1, matrix products, back_project(): lax.dot_general(grad_proj, panels, TRANS_B, preferred_element_type=jnp.fl...  5.81 us
  transfers between devices with their start and end apart: 16, of which 5 were waited for; matrix products, arithmetic and copies ran while one was open for 22% of the time, Pallas kernels for 10%

profile of v7, /device:TPU:0, one launch (start us, length us, event | category | flops | bytes accessed | tf_op | source)
XLA Modules:
  0.0 180.9 jit_solution(6464122190735029944)
XLA Ops:
  7.2 0.0 all-gather.2.cloned.1.call-start
  7.2 0.7 all-gather.2.cloned.1.call-update
  7.9 0.0 reduce-scatter.2.cloned.1.call-start
  8.0 0.1 copy-done.1
  8.2 0.1 pad_maximum_fusion.4
  8.3 0.0 copy-start.7
  8.3 3.0 %collective-permute-start.2 = (bf16[8,12,1024]{2,1,0:T(8,128)(2,1)S(1)}, bf16[8,12,1024]{2,1,0:T(8,128)(2,1)S(1)}, u32[]{:S(2)}, u32[]{:S(2)}) collective-permute-start(bf16[8,12,1024]{2,1,0:T(8,128)(2,1)S(1)} %pad_maximum_fusion.4), channel_id=1, source_target_pairs={{0,1},{1,0},{2,3},{3,2},{4,5},{5,4},{6,7},{7,6},{8,9},{9,8},{10,11... | collective-permute-start | bytes 589832 | tf_op jit(solution)/shard_map/ppermute | solution.py:137
  11.3 0.8 pad_maximum_fusion.8
  12.1 1.3 collective-permute-start.3
  13.4 0.8 pad_maximum_fusion.7
  14.1 6.1 %collective-permute-start = (bf16[6,12,1024]{2,1,0:T(8,128)(2,1)}, bf16[6,12,1024]{2,1,0:T(8,128)(2,1)}, u32[]{:S(2)}, u32[]{:S(2)}) collective-permute-start(bf16[6,12,1024]{2,1,0:T(8,128)(2,1)} %pad_maximum_fusion.7), channel_id=1, source_target_pairs={{0,3},{1,2},{2,5},{3,4},{4,7},{5,6},{6,9},{7,8},{8,11},{9,10},{10,... | collective-permute-start | bytes 442376 | tf_op jit(solution)/shard_map/ppermute | solution.py:137
  20.3 0.8 slice_bitcast_fusion.1
  21.1 4.3 %collective-permute-start.1 = (bf16[6,16,1024]{2,1,0:T(8,128)(2,1)}, bf16[6,16,1024]{2,1,0:T(8,128)(2,1)}, u32[]{:S(2)}, u32[]{:S(2)}) collective-permute-start(bf16[6,16,1024]{2,1,0:T(8,128)(2,1)} %get-tuple-element.28), channel_id=1, source_target_pairs={{0,2},{1,3},{2,4},{3,5},{4,6},{5,7},{6,8},{7,9},{8,10},{9,11},{10,... | collective-permute-start | bytes 589832 | tf_op jit(solution)/shard_map/ppermute | solution.py:137
  25.4 0.1 pad_maximum_fusion
  25.5 0.1 collective-permute-start.5
  25.6 0.1 copy.17
  25.7 0.1 copy.16
  25.8 0.1 copy.18
  25.9 0.1 pad_add_fusion
  26.0 0.1 pad_dynamic-slice_fusion
  26.1 0.1 eq.27
  26.2 0.5 convolution_convert_fusion.3
  26.7 1.0 fusion.44.bias_ref
  27.7 1.3 collective-permute-start.4
  29.0 1.0 fusion.68
  30.1 1.0 fusion.67
  31.2 5.9 %collective-permute-done.4 = bf16[6,16,1024]{2,1,0:T(8,128)(2,1)S(1)} collective-permute-done((bf16[6,16,1024]{2,1,0:T(8,128)(2,1)}, bf16[6,16,1024]{2,1,0:T(8,128)(2,1)S(1)}, u32[]{:S(2)}, u32[]{:S(2)}) %collective-permute-start.4) | collective-permute-done | bytes 196640 | tf_op jit(solution)/shard_map/ppermute | solution.py:137
  37.1 2.5 %fusion.12 = bf16[20,32,1024]{2,1,0:T(8,128)(2,1)} fusion(bf16[6,6,1024]{2,1,0:T(8,128)(2,1)S(1)} %get-tuple-element.41, bf16[6,16,1024]{2,1,0:T(8,128)(2,1)S(1)} %collective-permute-done.4, bf16[6,6,1024]{2,1,0:T(8,128)(2,1)S(1)} %get-tuple-element.40, bf16[8,6,1024]{2,1,0:T(8,128)(2,1)S(1)} %get-tuple-element.31, ...), kind=kLoop, calls=%fused_computation.15 | loop fusion | flops 18350080 | bytes 2457600 | tf_op jit(solution)/shard_map/concatenate | solution.py:178
  39.7 1.1 slice.191
  40.8 0.6 collective-permute-start.13
  41.4 1.7 fusion.17
  43.1 0.8 maximum_select_fusion.g_ref
  43.9 7.2 %convolution_convert_fusion.k_ref.v_ref = bf16[640,3072]{1,0:T(8,128)(2,1)S(1)} fusion(bf16[640,1024]{1,0:T(8,128)(2,1)S(1)} %bitcast.33, bf16[1024,3072]{1,0:T(8,128)(2,1)} %all-gather.2.cloned.1.call-done), kind=kOutput, calls=%fused_computation | convolution fusion | flops 4028497920 | bytes 11534336 | tf_op jit(solution)/shard_map/dot_general | solution.py:358
  51.1 1.9 %copy-done = bf16[640,3072]{1,0:T(8,128)(2,1)} copy-done((bf16[640,3072]{1,0:T(8,128)(2,1)}, bf16[640,3072]{1,0:T(8,128)(2,1)S(1)}, u32[]{:S(2)}) %copy-start) | copy-done | bytes 3932184
  53.0 0.8 slice.174
  53.8 17.4 %block_attention.1 = (bf16[128,1024]{1,0:T(8,128)(2,1)}, bf16[128,1024]{1,0:T(8,128)(2,1)}, f32[640,2048]{1,0:T(8,128)}) custom-call(bf16[128,1024]{1,0:T(8,128)(2,1)} %bitcast.34, bf16[640,3072]{1,0:T(8,128)(2,1)} %copy-done, bf16[640,3072]{1,0:T(8,128)(2,1)} %copy-done, bf16[128,1024]{1,0:T(8,128)(2,1)} %maximum_select_fusion.g_ref, ...), custom_call_target="tpu_custom_call" | custom-call | flops 2013265920 | bytes 9240576 | tf_op jit(solution)/shard_map/block_attention/pallas_call | solution.py:99
  71.1 2.9 %convert.26 = bf16[20,32,2048]{2,1,0:T(8,128)(2,1)S(1)} convert(f32[20,32,2048]{2,1,0:T(8,128)} %bitcast.22) | non-fusion elementwise | flops 1310720 | bytes 7864320 | tf_op jit(solution)/shard_map/convert.23
  74.0 0.1 fusion.60
  74.1 0.1 fusion.59
  74.3 1.2 fusion.58
  75.4 0.2 copy.20
  75.7 0.1 collective-permute-start.11
  75.7 0.2 pad_maximum_fusion.1
  75.9 1.6 collective-permute-start.8
  77.5 1.1 collective-permute-start.12
  78.7 0.9 pad_maximum_fusion.3
  79.5 5.1 %collective-permute-start.9 = (bf16[6,12,2048]{2,1,0:T(8,128)(2,1)}, bf16[6,12,2048]{2,1,0:T(8,128)(2,1)}, u32[]{:S(2)}, u32[]{:S(2)}) collective-permute-start(bf16[6,12,2048]{2,1,0:T(8,128)(2,1)} %pad_maximum_fusion.3), channel_id=1, source_target_pairs={{0,3},{1,2},{2,5},{3,4},{4,7},{5,6},{6,9},{7,8},{8,11},{9,10},{10,... | collective-permute-start | bytes 884744 | tf_op jit(solution)/shard_map/ppermute | solution.py:137
  84.7 0.9 pad_maximum_fusion.2
  85.6 1.3 collective-permute-start.6
  86.9 1.3 collective-permute-start.7
  88.2 16.6 %collective-permute-done.12 = bf16[256,512]{1,0:T(8,128)(2,1)S(1)} collective-permute-done((bf16[256,512]{1,0:T(8,128)(2,1)S(1)}, bf16[256,512]{1,0:T(8,128)(2,1)S(1)}, u32[]{:S(2)}, u32[]{:S(2)}) %collective-permute-start.12) | collective-permute-done | bytes 262176 | tf_op jit(solution)/shard_map/ppermute | solution.py:253
  104.8 1.3 collective-permute-start.10
  106.1 2.4 %convolution_multiply_fusion = f32[512,512]{1,0:T(8,128)} fusion(bf16[256,512]{1,0:T(8,128)(2,1)S(1)} %collective-permute-done.12, bf16[128,512]{1,0:T(8,128)(2,1)S(1)} %collective-permute-done.11, bf16[128,512]{1,0:T(8,128)(2,1)S(1)} %get-tuple-element.26, bf16[256,512]{1,0:T(8,128)(2,1)} %collective-permute-done.13, ...), kind=kOutput, calls=%fused_computation.11 | convolution fusion | flops 271843328 | bytes 2097152 | tf_op jit(solution)/shard_map/dot_general | solution.py:425
  108.5 0.0 reduce-scatter.2.cloned.1.call-update
  108.5 7.0 %collective-permute-done.9 = bf16[6,12,2048]{2,1,0:T(8,128)(2,1)} collective-permute-done((bf16[6,12,2048]{2,1,0:T(8,128)(2,1)}, bf16[6,12,2048]{2,1,0:T(8,128)(2,1)}, u32[]{:S(2)}, u32[]{:S(2)}) %collective-permute-start.9) | collective-permute-done | bytes 294944 | tf_op jit(solution)/shard_map/ppermute | solution.py:137
  115.5 1.2 fusion.63
  116.7 0.1 fusion.62
  116.8 0.1 fusion.61
  116.9 8.9 %collective-permute-done.10 = bf16[6,16,2048]{2,1,0:T(8,128)(2,1)S(1)} collective-permute-done((bf16[6,16,2048]{2,1,0:T(8,128)(2,1)}, bf16[6,16,2048]{2,1,0:T(8,128)(2,1)S(1)}, u32[]{:S(2)}, u32[]{:S(2)}) %collective-permute-start.10) | collective-permute-done | bytes 393248 | tf_op jit(solution)/shard_map/ppermute | solution.py:137
  125.7 2.0 %fusion.25 = bf16[8,16,2048]{2,1,0:T(8,128)(2,1)S(1)} fusion(f32[20,32,2048]{2,1,0:T(8,128)} %bitcast.23, bf16[6,6,2048]{2,1,0:T(8,128)(2,1)S(1)} %get-tuple-element.21, bf16[6,16,2048]{2,1,0:T(8,128)(2,1)S(1)} %collective-permute-done.10, bf16[6,6,2048]{2,1,0:T(8,128)(2,1)S(1)} %get-tuple-element.20, bf16[8,6,2048]{2,1,0:T(8,128)(2,1)S(1)} %get-tuple-element.17, ...), kind=kLoop, calls=%fused_computation.33 | loop fusion | flops 4456448 | bytes 3342336 | tf_op jit(solution)/shard_map/convert_element_type | solution.py:432
  127.7 0.4 reshape.89
  128.1 0.5 copy.19
  128.6 5.8 %convolution_convert_fusion.1 = bf16[128,1024]{1,0:T(8,128)(2,1)} fusion(bf16[1024,3072]{1,0:T(8,128)(2,1)} %all-gather.2.cloned.1.call-done, bf16[128,2048]{0,1:T(8,128)(2,1)S(1)} %bitcast.31, bf16[128,1024]{0,1:T(8,128)(2,1)S(1)} %copy.20), kind=kOutput, calls=%fused_computation.21 | convolution fusion | flops 807010304 | bytes 7340032 | tf_op jit(solution)/shard_map/dot_general | solution.py:362
  134.5 39.6 %reduce-scatter.2.cloned.1.call-done = f32[64,512]{1,0:T(8,128)} async-done(((f32[512,512]{1,0:T(8,128)}), f32[64,512]{1,0:T(8,128)}) %reduce-scatter.2.cloned.1.call-update) | async-done | bytes 131088 | tf_op jit(solution)/shard_map/reduce_scatter | solution.py:428
  (36 shorter events, 0.3 us)
Async XLA Ops:
  7.2 1.0 copy-start.1
  7.2 18.2 %copy-start.2 = (bf16[512,1024]{1,0:T(8,128)(2,1)S(1)}, bf16[512,1024]{1,0:T(8,128)(2,1)}, u32[]{:S(2)}) copy-start(bf16[512,1024]{1,0:T(8,128)(2,1)} %param.9) | copy-start | bytes 3145732
  7.2 18.2 %copy-start.3 = (bf16[1,8,16,1024]{3,2,1,0:T(8,128)(2,1)S(1)}, bf16[1,8,16,1024]{3,2,1,0:T(8,128)(2,1)}, u32[]{:S(2)}) copy-start(bf16[1,8,16,1024]{3,2,1,0:T(8,128)(2,1)} %param.6) | copy-start | bytes 786436
  7.2 36.7 %all-gather.2.cloned.1.call-start = ((), (), s32[]{:S(2)}) async-start(), calls=%async_computation.1 | async-start | bytes 9437184 | tf_op jit(solution)/shard_map/all_gather | solution.py:328
  7.9 166.1 %reduce-scatter.2.cloned.1.call-start = ((), (), s32[]{:S(2)}) async-start(), calls=%async_computation.2 | async-start | bytes 1179648 | tf_op jit(solution)/shard_map/reduce_scatter | solution.py:428
  8.3 17.3 %copy-start.7 = (s32[64,32]{0,1:T(8,128)S(1)}, s32[64,32]{0,1:T(8,128)}, u32[]{:S(2)}) copy-start(s32[64,32]{0,1:T(8,128)} %param.7) | copy-start | bytes 24580
  8.3 22.9 %collective-permute-start.2 = (bf16[8,12,1024]{2,1,0:T(8,128)(2,1)S(1)}, bf16[8,12,1024]{2,1,0:T(8,128)(2,1)S(1)}, u32[]{:S(2)}, u32[]{:S(2)}) collective-permute-start(bf16[8,12,1024]{2,1,0:T(8,128)(2,1)S(1)} %pad_maximum_fusion.4), channel_id=1, source_target_pairs={{0,1},{1,0},{2,3},{3,2},{4,5},{5,4},{6,7},{7,6},{8,9},{9,8},{10,11... | collective-permute-start | bytes 589832 | tf_op jit(solution)/shard_map/ppermute | solution.py:137
  12.1 15.6 %collective-permute-start.3 = (bf16[6,12,1024]{2,1,0:T(8,128)(2,1)}, bf16[6,12,1024]{2,1,0:T(8,128)(2,1)}, u32[]{:S(2)}, u32[]{:S(2)}) collective-permute-start(bf16[6,12,1024]{2,1,0:T(8,128)(2,1)} %pad_maximum_fusion.8), channel_id=1, source_target_pairs={{2,1},{3,0},{4,3},{5,2},{6,5},{7,4},{8,7},{9,6},{10,9},{11,8},{12,... | collective-permute-start | bytes 442376 | tf_op jit(solution)/shard_map/ppermute | solution.py:137
  14.1 15.9 %collective-permute-start = (bf16[6,12,1024]{2,1,0:T(8,128)(2,1)}, bf16[6,12,1024]{2,1,0:T(8,128)(2,1)}, u32[]{:S(2)}, u32[]{:S(2)}) collective-permute-start(bf16[6,12,1024]{2,1,0:T(8,128)(2,1)} %pad_maximum_fusion.7), channel_id=1, source_target_pairs={{0,3},{1,2},{2,5},{3,4},{4,7},{5,6},{6,9},{7,8},{8,11},{9,10},{10,... | collective-permute-start | bytes 442376 | tf_op jit(solution)/shard_map/ppermute | solution.py:137
  21.1 10.1 %collective-permute-start.1 = (bf16[6,16,1024]{2,1,0:T(8,128)(2,1)}, bf16[6,16,1024]{2,1,0:T(8,128)(2,1)}, u32[]{:S(2)}, u32[]{:S(2)}) collective-permute-start(bf16[6,16,1024]{2,1,0:T(8,128)(2,1)} %get-tuple-element.28), channel_id=1, source_target_pairs={{0,2},{1,3},{2,4},{3,5},{4,6},{5,7},{6,8},{7,9},{8,10},{9,11},{10,... | collective-permute-start | bytes 589832 | tf_op jit(solution)/shard_map/ppermute | solution.py:137
  25.5 14.2 %collective-permute-start.5 = (bf16[640,1024]{1,0:T(8,128)(2,1)S(1)}, bf16[640,1024]{1,0:T(8,128)(2,1)}, u32[]{:S(2)}, u32[]{:S(2)}) collective-permute-start(bf16[640,1024]{1,0:T(8,128)(2,1)S(1)} %pad_maximum_fusion), channel_id=1, source_target_pairs={{0,16},{16,0},{1,17},{17,1},{2,18},{18,2},{3,19},{19,3},{4,20},{20... | collective-permute-start | bytes 3932168 | tf_op jit(solution)/shard_map/ppermute | solution.py:253
  27.7 9.4 %collective-permute-start.4 = (bf16[6,16,1024]{2,1,0:T(8,128)(2,1)}, bf16[6,16,1024]{2,1,0:T(8,128)(2,1)S(1)}, u32[]{:S(2)}, u32[]{:S(2)}) collective-permute-start(bf16[6,16,1024]{2,1,0:T(8,128)(2,1)} %get-tuple-element.29), channel_id=1, source_target_pairs={{2,0},{3,1},{4,2},{5,3},{6,4},{7,5},{8,6},{9,7},{10,8},{11,9},{12,... | collective-permute-start | bytes 589832 | tf_op jit(solution)/shard_map/ppermute | solution.py:137
  39.7 4.2 %copy-start.4 = (bf16[20,32,1024]{2,1,0:T(8,128)(2,1)S(1)}, bf16[20,32,1024]{2,1,0:T(8,128)(2,1)}, u32[]{:S(2)}) copy-start(bf16[20,32,1024]{2,1,0:T(8,128)(2,1)} %fusion.12) | copy-start | bytes 3932164
  40.8 46.0 %collective-permute-start.13 = (bf16[256,512]{1,0:T(8,128)(2,1)S(1)}, bf16[256,512]{1,0:T(8,128)(2,1)}, u32[]{:S(2)}, u32[]{:S(2)}) collective-permute-start(bf16[256,512]{1,0:T(8,128)(2,1)S(1)} %pad_maximum_fusion.6), channel_id=1, source_target_pairs={{0,1},{1,0},{2,3},{3,2},{4,5},{5,4},{6,7},{7,6},{8,9},{9,8},{10,11... | collective-permute-start | bytes 786440 | tf_op jit(solution)/shard_map/ppermute | solution.py:253
  51.1 1.9 %copy-start = (bf16[640,3072]{1,0:T(8,128)(2,1)}, bf16[640,3072]{1,0:T(8,128)(2,1)S(1)}, u32[]{:S(2)}) copy-start(bf16[640,3072]{1,0:T(8,128)(2,1)S(1)} %convolution_convert_fusion.k_ref.v_ref) | copy-start | bytes 11796484
  74.0 1.4 copy-start.6
  74.0 1.6 copy-start.5
  75.7 1.8 %collective-permute-start.11 = (bf16[128,512]{1,0:T(8,128)(2,1)S(1)}, bf16[128,512]{1,0:T(8,128)(2,1)S(1)}, u32[]{:S(2)}, u32[]{:S(2)}) collective-permute-start(bf16[128,512]{1,0:T(8,128)(2,1)S(1)} %get-tuple-element.27), channel_id=1, source_target_pairs={{0,16},{16,0},{1,17},{17,1},{2,18},{18,2},{3,19},{19,3},{4,20},{20... | collective-permute-start | bytes 393224 | tf_op jit(solution)/shard_map/ppermute | solution.py:253
  75.9 40.8 %collective-permute-start.8 = (bf16[8,12,2048]{2,1,0:T(8,128)(2,1)S(1)}, bf16[8,12,2048]{2,1,0:T(8,128)(2,1)S(1)}, u32[]{:S(2)}, u32[]{:S(2)}) collective-permute-start(bf16[8,12,2048]{2,1,0:T(8,128)(2,1)S(1)} %pad_maximum_fusion.1), channel_id=1, source_target_pairs={{0,1},{1,0},{2,3},{3,2},{4,5},{5,4},{6,7},{7,6},{8,9},{9,8},{10,11... | collective-permute-start | bytes 1179656 | tf_op jit(solution)/shard_map/ppermute | solution.py:137
  77.5 27.2 %collective-permute-start.12 = (bf16[256,512]{1,0:T(8,128)(2,1)S(1)}, bf16[256,512]{1,0:T(8,128)(2,1)S(1)}, u32[]{:S(2)}, u32[]{:S(2)}) collective-permute-start(bf16[256,512]{1,0:T(8,128)(2,1)S(1)} %pad_maximum_fusion.5), channel_id=1, source_target_pairs={{0,1},{1,0},{2,3},{3,2},{4,5},{5,4},{6,7},{7,6},{8,9},{9,8},{10,11... | collective-permute-start | bytes 786440 | tf_op jit(solution)/shard_map/ppermute | solution.py:253
  79.5 36.0 %collective-permute-start.9 = (bf16[6,12,2048]{2,1,0:T(8,128)(2,1)}, bf16[6,12,2048]{2,1,0:T(8,128)(2,1)}, u32[]{:S(2)}, u32[]{:S(2)}) collective-permute-start(bf16[6,12,2048]{2,1,0:T(8,128)(2,1)} %pad_maximum_fusion.3), channel_id=1, source_target_pairs={{0,3},{1,2},{2,5},{3,4},{4,7},{5,6},{6,9},{7,8},{8,11},{9,10},{10,... | collective-permute-start | bytes 884744 | tf_op jit(solution)/shard_map/ppermute | solution.py:137
  85.6 31.1 %collective-permute-start.6 = (bf16[6,12,2048]{2,1,0:T(8,128)(2,1)}, bf16[6,12,2048]{2,1,0:T(8,128)(2,1)S(1)}, u32[]{:S(2)}, u32[]{:S(2)}) collective-permute-start(bf16[6,12,2048]{2,1,0:T(8,128)(2,1)} %pad_maximum_fusion.2), channel_id=1, source_target_pairs={{2,1},{3,0},{4,3},{5,2},{6,5},{7,4},{8,7},{9,6},{10,9},{11,8},{12,... | collective-permute-start | bytes 884744 | tf_op jit(solution)/shard_map/ppermute | solution.py:137
  86.9 30.0 %collective-permute-start.7 = (bf16[6,16,2048]{2,1,0:T(8,128)(2,1)}, bf16[6,16,2048]{2,1,0:T(8,128)(2,1)S(1)}, u32[]{:S(2)}, u32[]{:S(2)}) collective-permute-start(bf16[6,16,2048]{2,1,0:T(8,128)(2,1)} %get-tuple-element.8), channel_id=1, source_target_pairs={{2,0},{3,1},{4,2},{5,3},{6,4},{7,5},{8,6},{9,7},{10,8},{11,9},{12,... | collective-permute-start | bytes 1179656 | tf_op jit(solution)/shard_map/ppermute | solution.py:137
  104.8 21.0 %collective-permute-start.10 = (bf16[6,16,2048]{2,1,0:T(8,128)(2,1)}, bf16[6,16,2048]{2,1,0:T(8,128)(2,1)S(1)}, u32[]{:S(2)}, u32[]{:S(2)}) collective-permute-start(bf16[6,16,2048]{2,1,0:T(8,128)(2,1)} %get-tuple-element.9), channel_id=1, source_target_pairs={{0,2},{1,3},{2,4},{3,5},{4,6},{5,7},{6,8},{7,9},{8,10},{9,11},{10,... | collective-permute-start | bytes 1179656 | tf_op jit(solution)/shard_map/ppermute | solution.py:137
Sparse Core Ops, SparseCore 0:
  9.6 21.3 all-gather.1
  108.7 65.3 reduce-scatter.1

commit v8 on v6

--- a/solution.py
+++ b/solution.py
@@ -42,44 +42,46 @@
 def attention_kernel(q_ref, k_ref, v_ref, g_ref, bias_ref, att_ref, gq_ref, gkv_ref, *, head_dim, scale):
     q = q_ref[...]
     g = g_ref[...]
-    lanes = q.shape[1]
     k = k_ref[...]
     v = v_ref[...]
     bias = bias_ref[...]
+    lanes = q.shape[1]
     lane = lax.broadcasted_iota(jnp.int32, (1, lanes), 1)
-    q32 = q.astype(jnp.float32)
-    g32 = g.astype(jnp.float32)
-    att = jnp.zeros(q.shape, jnp.float32)
-    gq = jnp.zeros(q.shape, jnp.float32)
-    gk = jnp.zeros(k.shape, jnp.float32)
-    gv = jnp.zeros(v.shape, jnp.float32)
-    for j in range(lanes // head_dim):
-        sel = (lane >= j * head_dim) & (lane < (j + 1) * head_dim)
-        qj = jnp.where(sel, q32, 0.0).astype(jnp.bfloat16)
-        gj = jnp.where(sel, g32, 0.0).astype(jnp.bfloat16)
-        scores = lax.dot_general(qj, k, TRANS_B, preferred_element_type=jnp.float32) * scale
-        masked = scores + bias
+    zero = jnp.zeros((), q.dtype)
+    sels = [(lane >= j * head_dim) & (lane < (j + 1) * head_dim) for j in range(lanes // head_dim)]
+    q_scaled = (q.astype(jnp.float32) * scale).astype(q.dtype)
+    g_scaled = (g.astype(jnp.float32) * scale).astype(g.dtype)
+    probs_list = []
+    grads_list = []
+    for sel in sels:
+        qj = jnp.where(sel, q_scaled, zero)
+        gj = jnp.where(sel, g_scaled, zero)
+        masked = lax.dot_general(qj, k, TRANS_B, preferred_element_type=jnp.float32) + bias
         peak = jnp.max(masked, axis=1, keepdims=True)
         weights = jnp.exp(masked - peak)
         probs = weights * (1.0 / jnp.sum(weights, axis=1, keepdims=True))
-        probs_low = probs.astype(jnp.bfloat16)
-        att_j = jnp.dot(probs_low, v, preferred_element_type=jnp.float32)
         grad_probs = lax.dot_general(gj, v, TRANS_B, preferred_element_type=jnp.float32)
         centre = jnp.sum(probs * grad_probs, axis=1, keepdims=True)
-        grad_scores = (probs * (grad_probs - centre) * scale).astype(jnp.bfloat16)
-        gq_j = jnp.dot(grad_scores, k, preferred_element_type=jnp.float32)
-        scores_t = grad_scores.astype(jnp.float32).T.astype(jnp.bfloat16)
-        probs_t = probs_low.astype(jnp.float32).T.astype(jnp.bfloat16)
-        gk_j = jnp.dot(scores_t, q, preferred_element_type=jnp.float32)
-        gv_j = jnp.dot(probs_t, g, preferred_element_type=jnp.float32)
-        att = jnp.where(sel, att_j, att)
-        gq = jnp.where(sel, gq_j, gq)
-        gk = jnp.where(sel, gk_j, gk)
-        gv = jnp.where(sel, gv_j, gv)
+        grads_list.append((probs * (grad_probs - centre)).astype(jnp.bfloat16))
+        probs_list.append(probs.astype(jnp.bfloat16))
+    k_sel = jnp.concatenate([jnp.where(sel, k, zero) for sel in sels], axis=0)
+    v_sel = jnp.concatenate([jnp.where(sel, v, zero) for sel in sels], axis=0)
+    q_sel = jnp.concatenate([jnp.where(sel, q, zero) for sel in sels], axis=0)
+    g_sel = jnp.concatenate([jnp.where(sel, g, zero) for sel in sels], axis=0)
+    probs_cat = jnp.concatenate(probs_list, axis=1)
+    grads_cat = jnp.concatenate(grads_list, axis=1)
+    att = jnp.dot(probs_cat, v_sel, preferred_element_type=jnp.float32)
+    gq = jnp.dot(grads_cat, k_sel, preferred_element_type=jnp.float32)
+    grads_t = jnp.concatenate(
+        [x.astype(jnp.float32).T.astype(jnp.bfloat16) for x in grads_list], axis=1
+    )
+    probs_t = jnp.concatenate(
+        [x.astype(jnp.float32).T.astype(jnp.bfloat16) for x in probs_list], axis=1
+    )
     att_ref[...] = att.astype(att_ref.dtype)
     gq_ref[...] = gq.astype(gq_ref.dtype)
-    gkv_ref[:, :lanes] = gk
-    gkv_ref[:, lanes:] = gv
+    gkv_ref[:, :lanes] = jnp.dot(grads_t, q_sel, preferred_element_type=jnp.float32)
+    gkv_ref[:, lanes:] = jnp.dot(probs_t, g_sel, preferred_element_type=jnp.float32)
 
 
 def block_attention(query, projected, grad_attn, bias, heads):

time: 146 us -> 141 us (0.966)
  Pallas kernels: 17.4 us -> 11.5 us
    pallas_call x1, Pallas kernels: 17.4 us -> 11.5 us  [block_attention(): pl.pallas_call(kernel, grid=(pairs,), in_specs=[pl.BlockSpec((queries, la...]
  transfers between devices with their start and end apart: 16 -> 16, of which waited for: 3 -> 3; matrix products, arithmetic and copies ran while one was open for 36% -> 38% of each run, Pallas kernels for 12% -> 8%
where the time goes in v8:
time: 141 us; the launch traced here: 139 us
  starting transfers between devices  43.6 us (31%)
  waiting for transfers between devices  25.1 us (18%)
  local copies, waits for them, and re-layouts  24.1 us (17%)
  other arithmetic  19.1 us (14%)
  matrix products  15.2 us (11%)
  Pallas kernels  11.5 us (8%)
    ppermute x10, starting transfers between devices, sent_to(): return lax.ppermute(value, ('lat', 'lon'), grid_pairs(delta_lat, delta_lon))  31.2 us
    ppermute x10, waiting for transfers between devices, sent_to(): return lax.ppermute(value, ('lat', 'lon'), grid_pairs(delta_lat, delta_lon))  19.7 us
    pallas_call x1, Pallas kernels, block_attention(): pl.pallas_call(kernel, grid=(pairs,), in_specs=[pl.BlockSpec((queries, la...  11.5 us
    all_to_all x1, starting transfers between devices, shards(): lax.all_to_all(partial.astype(jnp.bfloat16), 'lat', 0, 0, tiled=True)  11.1 us
    slice x6, local copies, waits for them, and re-layouts, grouped_send(): out[i] = got[:, offset:offset + value.shape[1]]  8.16 us
    ppermute x5, waiting for transfers between devices, swap(): return lax.ppermute(value, axis, [(0, 1), (1, 0)])  5.42 us
    concatenate x6, other arithmetic, grouped_send(): got = sent_to(jnp.concatenate(values, axis=1), dl, db)  5.11 us
    dot_general x1, matrix products, project(): jnp.dot(columns(rows, 1 - dp_index, rows_half), qkv_other, preferred_elem...  4.19 us
  transfers between devices with their start and end apart: 16, of which 3 were waited for; matrix products, arithmetic and copies ran while one was open for 38% of the time, Pallas kernels for 8%

profile of v8, /device:TPU:0, one launch (start us, length us, event | category | flops | bytes accessed | tf_op | source)
XLA Modules:
  0.0 139.5 jit_solution(12374433992072044730)
XLA Ops:
  0.7 1.2 fusion.69
  1.9 0.7 pad_maximum_fusion.10
  2.6 6.5 %collective-permute-start = (bf16[6,12,1024]{2,1,0:T(8,128)(2,1)}, bf16[6,12,1024]{2,1,0:T(8,128)(2,1)}, u32[]{:S(2)}, u32[]{:S(2)}) collective-permute-start(bf16[6,12,1024]{2,1,0:T(8,128)(2,1)} %pad_maximum_fusion.10), channel_id=1, source_target_pairs={{0,3},{1,2},{2,5},{3,4},{4,7},{5,6},{6,9},{7,8},{8,11},{9,10},{10,... | collective-permute-start | bytes 442376 | tf_op jit(solution)/shard_map/ppermute | solution.py:139
  9.1 0.7 pad_maximum_fusion.11
  9.9 1.3 collective-permute-start.3
  11.1 1.0 fusion.70
  12.2 0.8 pad_maximum_fusion.7
  12.9 0.5 collective-permute-start.2
  13.5 0.8 slice_bitcast_fusion.1
  14.3 6.2 %collective-permute-start.1 = (bf16[6,16,1024]{2,1,0:T(8,128)(2,1)}, bf16[6,16,1024]{2,1,0:T(8,128)(2,1)}, u32[]{:S(2)}, u32[]{:S(2)}) collective-permute-start(bf16[6,16,1024]{2,1,0:T(8,128)(2,1)} %get-tuple-element.28), channel_id=1, source_target_pairs={{0,2},{1,3},{2,4},{3,5},{4,6},{5,7},{6,8},{7,9},{8,10},{9,11},{10,... | collective-permute-start | bytes 589832 | tf_op jit(solution)/shard_map/ppermute | solution.py:139
  20.6 0.1 copy.16
  20.7 0.1 copy.18
  20.9 0.1 pad_dynamic-slice_fusion
  21.0 0.1 eq.28
  21.1 1.0 fusion.45.bias_ref
  22.1 0.5 convolution_convert_fusion.1
  22.6 0.7 constant_dynamic-slice_fusion.3
  23.3 0.1 pad_maximum_fusion
  23.4 1.6 %collective-permute-start.4 = (bf16[6,16,1024]{2,1,0:T(8,128)(2,1)}, bf16[6,16,1024]{2,1,0:T(8,128)(2,1)S(1)}, u32[]{:S(2)}, u32[]{:S(2)}) collective-permute-start(bf16[6,16,1024]{2,1,0:T(8,128)(2,1)} %get-tuple-element.29), channel_id=1, source_target_pairs={{2,0},{3,1},{4,2},{5,3},{6,4},{7,5},{8,6},{9,7},{10,8},{11,9},{12,... | collective-permute-start | bytes 589832 | tf_op jit(solution)/shard_map/ppermute | solution.py:139
  25.0 1.0 fusion.71
  26.1 0.6 collective-permute-start.6
  26.6 1.0 fusion.72
  27.7 1.1 fusion.68
  28.8 4.4 %collective-permute-done.4 = bf16[6,16,1024]{2,1,0:T(8,128)(2,1)S(1)} collective-permute-done((bf16[6,16,1024]{2,1,0:T(8,128)(2,1)}, bf16[6,16,1024]{2,1,0:T(8,128)(2,1)S(1)}, u32[]{:S(2)}, u32[]{:S(2)}) %collective-permute-start.4) | collective-permute-done | bytes 196640 | tf_op jit(solution)/shard_map/ppermute | solution.py:139
  33.1 1.7 %fusion.12 = bf16[20,32,1024]{2,1,0:T(8,128)(2,1)S(1)} fusion(bf16[6,6,1024]{2,1,0:T(8,128)(2,1)S(1)} %get-tuple-element.41, bf16[6,16,1024]{2,1,0:T(8,128)(2,1)S(1)} %collective-permute-done.4, bf16[6,6,1024]{2,1,0:T(8,128)(2,1)S(1)} %get-tuple-element.40, bf16[8,6,1024]{2,1,0:T(8,128)(2,1)S(1)} %get-tuple-element.31, ...), kind=kLoop, calls=%fused_computation.15 | loop fusion | flops 18350080 | bytes 2457600 | tf_op jit(solution)/shard_map/concatenate | solution.py:180
  34.8 2.2 %fusion.29 = f32[640,3072]{1,0:T(8,128)S(1)} fusion(bf16[512,3072]{1,0:T(8,128)(2,1)S(1)} %copy-done.3, bf16[640,1024]{1,0:T(8,128)(2,1)S(1)} %bitcast.30, s32[]{:T(128)S(6)} %select_n.95), kind=kOutput, calls=%fused_computation.40 | convolution fusion | flops 2013265920 | bytes 11665412 | tf_op jit(solution)/shard_map/dot_general | solution.py:360
  37.1 0.7 constant_dynamic-slice_fusion.2
  37.8 0.7 pad_maximum_fusion.9
  38.5 0.5 collective-permute-start.14
  39.0 0.5 fusion.18
  39.5 0.8 maximum_select_fusion.g_ref
  40.3 4.2 %add_convert_fusion.k_ref.v_ref = bf16[640,3072]{1,0:T(8,128)(2,1)S(1)} fusion(f32[640,3072]{1,0:T(8,128)S(1)} %fusion.29, bf16[512,3072]{1,0:T(8,128)(2,1)} %collective-permute-done.5, bf16[640,1024]{1,0:T(8,128)(2,1)S(1)} %bitcast.31, s32[]{:T(128)S(6)} %select_n.96), kind=kOutput, calls=%fused_computation | convolution fusion | flops 2017198080 | bytes 15597572 | tf_op jit(solution)/shard_map/dot_general | solution.py:363
  44.5 1.9 %copy-done = bf16[640,3072]{1,0:T(8,128)(2,1)} copy-done((bf16[640,3072]{1,0:T(8,128)(2,1)}, bf16[640,3072]{1,0:T(8,128)(2,1)S(1)}, u32[]{:S(2)}) %copy-start) | copy-done | bytes 3932184
  46.5 0.8 slice.174
  47.2 11.5 %block_attention.1 = (bf16[128,1024]{1,0:T(8,128)(2,1)}, bf16[128,1024]{1,0:T(8,128)(2,1)}, f32[640,2048]{1,0:T(8,128)}) custom-call(bf16[128,1024]{1,0:T(8,128)(2,1)} %bitcast.37, bf16[640,3072]{1,0:T(8,128)(2,1)} %copy-done, bf16[640,3072]{1,0:T(8,128)(2,1)} %copy-done, bf16[128,1024]{1,0:T(8,128)(2,1)} %maximum_select_fusion.g_ref, ...), custom_call_target="tpu_custom_call" | custom-call | flops 2013265920 | bytes 9240576 | tf_op jit(solution)/shard_map/block_attention/pallas_call | solution.py:101
  58.7 2.9 %convert.26 = bf16[20,32,2048]{2,1,0:T(8,128)(2,1)S(1)} convert(f32[20,32,2048]{2,1,0:T(8,128)} %bitcast.25) | non-fusion elementwise | flops 1310720 | bytes 7864320 | tf_op jit(solution)/shard_map/convert.23
  61.6 0.1 fusion.63
  61.9 1.3 fusion.62
  63.1 0.7 constant_dynamic-slice_fusion.5
  63.8 0.9 pad_maximum_fusion.5
  64.7 1.3 collective-permute-start.7
  66.0 1.0 pad_maximum_fusion.2
  67.0 1.5 %collective-permute-start.9 = (bf16[8,12,2048]{2,1,0:T(8,128)(2,1)}, bf16[8,12,2048]{2,1,0:T(8,128)(2,1)}, u32[]{:S(2)}, u32[]{:S(2)}) collective-permute-start(bf16[8,12,2048]{2,1,0:T(8,128)(2,1)} %pad_maximum_fusion.2), channel_id=1, source_target_pairs={{0,1},{1,0},{2,3},{3,2},{4,5},{5,4},{6,7},{7,6},{8,9},{9,8},{10,11... | collective-permute-start | bytes 1179656 | tf_op jit(solution)/shard_map/ppermute | solution.py:139
  68.5 0.9 pad_maximum_fusion.6
  69.4 6.2 %collective-permute-start.10 = (bf16[6,12,2048]{2,1,0:T(8,128)(2,1)}, bf16[6,12,2048]{2,1,0:T(8,128)(2,1)}, u32[]{:S(2)}, u32[]{:S(2)}) collective-permute-start(bf16[6,12,2048]{2,1,0:T(8,128)(2,1)} %pad_maximum_fusion.6), channel_id=1, source_target_pairs={{0,3},{1,2},{2,5},{3,4},{4,7},{5,6},{6,9},{7,8},{8,11},{9,10},{10,... | collective-permute-start | bytes 884744 | tf_op jit(solution)/shard_map/ppermute | solution.py:139
  75.6 1.8 %copy.20 = bf16[128,1024]{0,1:T(8,128)(2,1)} copy(bf16[128,1024]{1,0:T(8,128)(2,1)} %get-tuple-element.5) | data formatting | bytes 524288 | tf_op jit(solution)/shard_map/block_attention/pallas_call | solution.py:101
  77.4 4.9 %collective-permute-start.11 = (bf16[6,16,2048]{2,1,0:T(8,128)(2,1)}, bf16[6,16,2048]{2,1,0:T(8,128)(2,1)}, u32[]{:S(2)}, u32[]{:S(2)}) collective-permute-start(bf16[6,16,2048]{2,1,0:T(8,128)(2,1)} %get-tuple-element.9), channel_id=1, source_target_pairs={{0,2},{1,3},{2,4},{3,5},{4,6},{5,7},{6,8},{7,9},{8,10},{9,11},{10,... | collective-permute-start | bytes 1179656 | tf_op jit(solution)/shard_map/ppermute | solution.py:139
  82.3 0.9 pad_maximum_fusion.8
  83.3 1.3 collective-permute-start.8
  84.6 1.9 %fusion.66 = (bf16[6,6,2048]{2,1,0:T(8,128)(2,1)}, bf16[6,6,2048]{2,1,0:T(8,128)(2,1)}) fusion(bf16[6,12,2048]{2,1,0:T(8,128)(2,1)} %collective-permute-done.7), kind=kLoop, calls=%fused_computation.111 | loop fusion | bytes 589824 | tf_op jit(solution)/shard_map/slice | solution.py:161
  86.4 15.3 %collective-permute-done.10 = bf16[6,12,2048]{2,1,0:T(8,128)(2,1)} collective-permute-done((bf16[6,12,2048]{2,1,0:T(8,128)(2,1)}, bf16[6,12,2048]{2,1,0:T(8,128)(2,1)}, u32[]{:S(2)}, u32[]{:S(2)}) %collective-permute-start.10) | collective-permute-done | bytes 294944 | tf_op jit(solution)/shard_map/ppermute | solution.py:139
  101.8 0.2 collective-permute-start.13
  102.0 1.9 %fusion.67 = (bf16[6,6,2048]{2,1,0:T(8,128)(2,1)}, bf16[6,6,2048]{2,1,0:T(8,128)(2,1)}) fusion(bf16[6,12,2048]{2,1,0:T(8,128)(2,1)} %collective-permute-done.10), kind=kLoop, calls=%fused_computation.112 | loop fusion | bytes 589824 | tf_op jit(solution)/shard_map/slice | solution.py:161
  103.9 5.4 %collective-permute-done.13 = bf16[256,512]{1,0:T(8,128)(2,1)S(1)} collective-permute-done((bf16[256,512]{1,0:T(8,128)(2,1)S(1)}, bf16[256,512]{1,0:T(8,128)(2,1)S(1)}, u32[]{:S(2)}, u32[]{:S(2)}) %collective-permute-start.13) | collective-permute-done | bytes 262176 | tf_op jit(solution)/shard_map/ppermute | solution.py:255
  109.3 2.4 %fusion.17 = bf16[512,512]{1,0:T(8,128)(2,1)} fusion(bf16[256,512]{1,0:T(8,128)(2,1)S(1)} %collective-permute-done.13, bf16[128,512]{1,0:T(8,128)(2,1)} %collective-permute-done.12, bf16[128,512]{1,0:T(8,128)(2,1)S(1)} %get-tuple-element.26, bf16[256,512]{1,0:T(8,128)(2,1)} %collective-permute-done.14, bf16[128,512]{1,0:T(8,128)(2,1)} %get-tuple-element.24, ...), kind=kOutput, calls=%fused_computation.21 | convolution fusion | flops 272105472 | bytes 1572864 | tf_op jit(solution)/shard_map/dot_general | solution.py:439
  111.7 11.1 %all-to-all-start = ((bf16[8,64,512]{2,1,0:T(8,128)(2,1)}), bf16[8,64,512]{2,1,0:T(8,128)(2,1)}, u32[]{:S(2)}, u32[]{:S(2)}) async-start(bf16[8,64,512]{2,1,0:T(8,128)(2,1)} %bitcast.38), calls=%async_computation | async-start | bytes 1048576 | tf_op jit(solution)/shard_map/all_to_all | solution.py:442
  122.8 1.2 fusion.65
  124.1 3.2 %fusion.26 = bf16[8,16,2048]{2,1,0:T(8,128)(2,1)} fusion(f32[20,32,2048]{2,1,0:T(8,128)} %bitcast.26, bf16[6,6,2048]{2,1,0:T(8,128)(2,1)} %get-tuple-element.21, bf16[6,16,2048]{2,1,0:T(8,128)(2,1)} %collective-permute-done.11, bf16[6,6,2048]{2,1,0:T(8,128)(2,1)} %get-tuple-element.20, bf16[8,6,2048]{2,1,0:T(8,128)(2,1)S(1)} %get-tuple-element.17, ...), kind=kLoop, calls=%fused_computation.35 | loop fusion | flops 4456448 | bytes 3342336 | tf_op jit(solution)/shard_map/convert_element_type | solution.py:447
  127.2 2.2 %reshape.145 = bf16[128,8,2,128]{3,2,1,0:T(2,128)(2,1)} reshape(bf16[8,16,2048]{2,1,0:T(8,128)(2,1)} %fusion.26) | data formatting | bytes 1048576 | tf_op jit(solution)/shard_map/reshape | solution.py:448
  129.4 2.0 %copy.19 = bf16[128,2,8,128]{0,3,2,1:T(8,128)(2,1)} copy(bf16[128,2,8,128]{3,1,2,0:T(2,128)(2,1)} %bitcast.36) | data formatting | bytes 1048576 | tf_op jit(solution)/shard_map/transpose | solution.py:449
  131.5 2.3 %convolution_convert_fusion.3 = bf16[128,512]{1,0:T(8,128)(2,1)S(1)} fusion(bf16[512,3072]{1,0:T(8,128)(2,1)S(1)} %copy-done.3, bf16[128,2048]{0,1:T(8,128)(2,1)} %bitcast.39, bf16[128,1024]{0,1:T(8,128)(2,1)} %copy.20), kind=kOutput, calls=%fused_computation.25 | convolution fusion | flops 404291584 | bytes 4063232 | tf_op jit(solution)/shard_map/dot_general | solution.py:369
  133.8 3.1 %convolution_convert_fusion.2 = bf16[128,512]{1,0:T(8,128)(2,1)S(1)} fusion(bf16[512,3072]{1,0:T(8,128)(2,1)} %collective-permute-done.5, bf16[128,2048]{0,1:T(8,128)(2,1)S(1)} %bitcast.40, bf16[128,1024]{0,1:T(8,128)(2,1)S(1)} %copy-done.8), kind=kOutput, calls=%fused_computation.24 | convolution fusion | flops 404291584 | bytes 4063232 | tf_op jit(solution)/shard_map/dot_general | solution.py:370
  136.9 0.8 maximum_select_fusion.1
  137.7 1.8 %convert_reduce_fusion = f32[64,512]{1,0:T(8,128)} fusion(bf16[8,64,512]{2,1,0:T(8,128)(2,1)} %all-to-all-done), kind=kLoop, calls=%fused_computation.37 | loop fusion | flops 491520 | bytes 655360 | tf_op jit(solution)/shard_map/reduce_sum | solution.py:443
  (44 shorter events, 0.4 us)
Async XLA Ops:
  0.6 12.9 %copy-start.1 = (bf16[1,8,16,1024]{3,2,1,0:T(8,128)(2,1)S(1)}, bf16[1,8,16,1024]{3,2,1,0:T(8,128)(2,1)}, u32[]{:S(2)}) copy-start(bf16[1,8,16,1024]{3,2,1,0:T(8,128)(2,1)} %param.5) | copy-start | bytes 786436
  0.6 19.8 %copy-start.10 = (s32[64,32]{0,1:T(8,128)S(1)}, s32[64,32]{0,1:T(8,128)}, u32[]{:S(2)}) copy-start(s32[64,32]{0,1:T(8,128)} %param.7) | copy-start | bytes 24580
  0.7 21.5 %copy-start.4 = (bf16[1,8,16,1024]{3,2,1,0:T(8,128)(2,1)S(1)}, bf16[1,8,16,1024]{3,2,1,0:T(8,128)(2,1)}, u32[]{:S(2)}) copy-start(bf16[1,8,16,1024]{3,2,1,0:T(8,128)(2,1)} %param.6) | copy-start | bytes 786436
  0.7 21.4 %copy-start.2 = (bf16[512,1024]{1,0:T(8,128)(2,1)S(1)}, bf16[512,1024]{1,0:T(8,128)(2,1)}, u32[]{:S(2)}) copy-start(bf16[512,1024]{1,0:T(8,128)(2,1)} %param.9) | copy-start | bytes 3145732
  2.6 20.8 %collective-permute-start = (bf16[6,12,1024]{2,1,0:T(8,128)(2,1)}, bf16[6,12,1024]{2,1,0:T(8,128)(2,1)}, u32[]{:S(2)}, u32[]{:S(2)}) collective-permute-start(bf16[6,12,1024]{2,1,0:T(8,128)(2,1)} %pad_maximum_fusion.10), channel_id=1, source_target_pairs={{0,3},{1,2},{2,5},{3,4},{4,7},{5,6},{6,9},{7,8},{8,11},{9,10},{10,... | collective-permute-start | bytes 442376 | tf_op jit(solution)/shard_map/ppermute | solution.py:139
  9.9 16.2 %collective-permute-start.3 = (bf16[6,12,1024]{2,1,0:T(8,128)(2,1)}, bf16[6,12,1024]{2,1,0:T(8,128)(2,1)}, u32[]{:S(2)}, u32[]{:S(2)}) collective-permute-start(bf16[6,12,1024]{2,1,0:T(8,128)(2,1)} %pad_maximum_fusion.11), channel_id=1, source_target_pairs={{2,1},{3,0},{4,3},{5,2},{6,5},{7,4},{8,7},{9,6},{10,9},{11,8},{12,... | collective-permute-start | bytes 442376 | tf_op jit(solution)/shard_map/ppermute | solution.py:139
  12.9 14.7 %collective-permute-start.2 = (bf16[8,12,1024]{2,1,0:T(8,128)(2,1)}, bf16[8,12,1024]{2,1,0:T(8,128)(2,1)}, u32[]{:S(2)}, u32[]{:S(2)}) collective-permute-start(bf16[8,12,1024]{2,1,0:T(8,128)(2,1)} %pad_maximum_fusion.7), channel_id=1, source_target_pairs={{0,1},{1,0},{2,3},{3,2},{4,5},{5,4},{6,7},{7,6},{8,9},{9,8},{10,11... | collective-permute-start | bytes 589832 | tf_op jit(solution)/shard_map/ppermute | solution.py:139
  14.3 14.5 %collective-permute-start.1 = (bf16[6,16,1024]{2,1,0:T(8,128)(2,1)}, bf16[6,16,1024]{2,1,0:T(8,128)(2,1)}, u32[]{:S(2)}, u32[]{:S(2)}) collective-permute-start(bf16[6,16,1024]{2,1,0:T(8,128)(2,1)} %get-tuple-element.28), channel_id=1, source_target_pairs={{0,2},{1,3},{2,4},{3,5},{4,6},{5,7},{6,8},{7,9},{8,10},{9,11},{10,... | collective-permute-start | bytes 589832 | tf_op jit(solution)/shard_map/ppermute | solution.py:139
  20.5 19.8 %collective-permute-start.5 = (bf16[512,3072]{1,0:T(8,128)(2,1)}, bf16[512,3072]{1,0:T(8,128)(2,1)}, u32[]{:S(2)}, u32[]{:S(2)}) collective-permute-start(bf16[512,3072]{1,0:T(8,128)(2,1)} %param.8), channel_id=1, source_target_pairs={{0,16},{16,0},{1,17},{17,1},{2,18},{18,2},{3,19},{19,3},{4,20},{20... | collective-permute-start | bytes 9437192 | tf_op jit(solution)/shard_map/ppermute | solution.py:255
  23.4 11.4 %copy-start.3 = (bf16[512,3072]{1,0:T(8,128)(2,1)S(1)}, bf16[512,3072]{1,0:T(8,128)(2,1)}, u32[]{:S(2)}) copy-start(bf16[512,3072]{1,0:T(8,128)(2,1)} %param.8) | copy-start | bytes 9437188
  23.4 9.7 %collective-permute-start.4 = (bf16[6,16,1024]{2,1,0:T(8,128)(2,1)}, bf16[6,16,1024]{2,1,0:T(8,128)(2,1)S(1)}, u32[]{:S(2)}, u32[]{:S(2)}) collective-permute-start(bf16[6,16,1024]{2,1,0:T(8,128)(2,1)} %get-tuple-element.29), channel_id=1, source_target_pairs={{2,0},{3,1},{4,2},{5,3},{6,4},{7,5},{8,6},{9,7},{10,8},{11,9},{12,... | collective-permute-start | bytes 589832 | tf_op jit(solution)/shard_map/ppermute | solution.py:139
  26.1 11.0 %collective-permute-start.6 = (bf16[640,1024]{1,0:T(8,128)(2,1)S(1)}, bf16[640,1024]{1,0:T(8,128)(2,1)S(1)}, u32[]{:S(2)}, u32[]{:S(2)}) collective-permute-start(bf16[640,1024]{1,0:T(8,128)(2,1)S(1)} %pad_maximum_fusion), channel_id=1, source_target_pairs={{0,16},{16,0},{1,17},{17,1},{2,18},{18,2},{3,19},{19,3},{4,20},{20... | collective-permute-start | bytes 3932168 | tf_op jit(solution)/shard_map/ppermute | solution.py:255
  34.8 3.0 %copy-start.7 = (bf16[128,512]{1,0:T(8,128)(2,1)S(1)}, bf16[128,512]{1,0:T(8,128)(2,1)}, u32[]{:S(2)}) copy-start(bf16[128,512]{1,0:T(8,128)(2,1)} %get-tuple-element.23) | copy-start | bytes 393220
  34.8 4.2 %copy-start.5 = (bf16[1,8,16,1024]{3,2,1,0:T(8,128)(2,1)S(1)}, bf16[1,8,16,1024]{3,2,1,0:T(8,128)(2,1)}, u32[]{:S(2)}) copy-start(bf16[1,8,16,1024]{3,2,1,0:T(8,128)(2,1)} %param.6) | copy-start | bytes 786436
  38.5 65.4 %collective-permute-start.14 = (bf16[256,512]{1,0:T(8,128)(2,1)}, bf16[256,512]{1,0:T(8,128)(2,1)}, u32[]{:S(2)}, u32[]{:S(2)}) collective-permute-start(bf16[256,512]{1,0:T(8,128)(2,1)} %pad_maximum_fusion.9), channel_id=1, source_target_pairs={{0,1},{1,0},{2,3},{3,2},{4,5},{5,4},{6,7},{7,6},{8,9},{9,8},{10,11... | collective-permute-start | bytes 786440 | tf_op jit(solution)/shard_map/ppermute | solution.py:255
  44.5 2.0 %copy-start = (bf16[640,3072]{1,0:T(8,128)(2,1)}, bf16[640,3072]{1,0:T(8,128)(2,1)S(1)}, u32[]{:S(2)}) copy-start(bf16[640,3072]{1,0:T(8,128)(2,1)S(1)} %add_convert_fusion.k_ref.v_ref) | copy-start | bytes 11796484
  61.6 1.5 %copy-start.9 = (bf16[128,1024]{1,0:T(8,128)(2,1)S(1)}, bf16[128,1024]{1,0:T(8,128)(2,1)}, u32[]{:S(2)}) copy-start(bf16[128,1024]{1,0:T(8,128)(2,1)} %get-tuple-element.7) | copy-start | bytes 786436
  63.8 13.6 %collective-permute-start.12 = (bf16[128,512]{1,0:T(8,128)(2,1)}, bf16[128,512]{1,0:T(8,128)(2,1)}, u32[]{:S(2)}, u32[]{:S(2)}) collective-permute-start(bf16[128,512]{1,0:T(8,128)(2,1)} %get-tuple-element.27), channel_id=1, source_target_pairs={{0,16},{16,0},{1,17},{17,1},{2,18},{18,2},{3,19},{19,3},{4,20},{20... | collective-permute-start | bytes 393224 | tf_op jit(solution)/shard_map/ppermute | solution.py:255
  64.7 18.5 %collective-permute-start.7 = (bf16[6,12,2048]{2,1,0:T(8,128)(2,1)}, bf16[6,12,2048]{2,1,0:T(8,128)(2,1)}, u32[]{:S(2)}, u32[]{:S(2)}) collective-permute-start(bf16[6,12,2048]{2,1,0:T(8,128)(2,1)} %pad_maximum_fusion.5), channel_id=1, source_target_pairs={{2,1},{3,0},{4,3},{5,2},{6,5},{7,4},{8,7},{9,6},{10,9},{11,8},{12,... | collective-permute-start | bytes 884744 | tf_op jit(solution)/shard_map/ppermute | solution.py:139
  67.0 55.8 %collective-permute-start.9 = (bf16[8,12,2048]{2,1,0:T(8,128)(2,1)}, bf16[8,12,2048]{2,1,0:T(8,128)(2,1)}, u32[]{:S(2)}, u32[]{:S(2)}) collective-permute-start(bf16[8,12,2048]{2,1,0:T(8,128)(2,1)} %pad_maximum_fusion.2), channel_id=1, source_target_pairs={{0,1},{1,0},{2,3},{3,2},{4,5},{5,4},{6,7},{7,6},{8,9},{9,8},{10,11... | collective-permute-start | bytes 1179656 | tf_op jit(solution)/shard_map/ppermute | solution.py:139
  69.4 32.3 %collective-permute-start.10 = (bf16[6,12,2048]{2,1,0:T(8,128)(2,1)}, bf16[6,12,2048]{2,1,0:T(8,128)(2,1)}, u32[]{:S(2)}, u32[]{:S(2)}) collective-permute-start(bf16[6,12,2048]{2,1,0:T(8,128)(2,1)} %pad_maximum_fusion.6), channel_id=1, source_target_pairs={{0,3},{1,2},{2,5},{3,4},{4,7},{5,6},{6,9},{7,8},{8,11},{9,10},{10,... | collective-permute-start | bytes 884744 | tf_op jit(solution)/shard_map/ppermute | solution.py:139
  77.4 46.6 %collective-permute-start.11 = (bf16[6,16,2048]{2,1,0:T(8,128)(2,1)}, bf16[6,16,2048]{2,1,0:T(8,128)(2,1)}, u32[]{:S(2)}, u32[]{:S(2)}) collective-permute-start(bf16[6,16,2048]{2,1,0:T(8,128)(2,1)} %get-tuple-element.9), channel_id=1, source_target_pairs={{0,2},{1,3},{2,4},{3,5},{4,6},{5,7},{6,8},{7,9},{8,10},{9,11},{10,... | collective-permute-start | bytes 1179656 | tf_op jit(solution)/shard_map/ppermute | solution.py:139
  83.3 40.8 %collective-permute-start.8 = (bf16[6,16,2048]{2,1,0:T(8,128)(2,1)}, bf16[6,16,2048]{2,1,0:T(8,128)(2,1)}, u32[]{:S(2)}, u32[]{:S(2)}) collective-permute-start(bf16[6,16,2048]{2,1,0:T(8,128)(2,1)} %get-tuple-element.8), channel_id=1, source_target_pairs={{2,0},{3,1},{4,2},{5,3},{6,4},{7,5},{8,6},{9,7},{10,8},{11,9},{12,... | collective-permute-start | bytes 1179656 | tf_op jit(solution)/shard_map/ppermute | solution.py:139
  101.8 7.5 %collective-permute-start.13 = (bf16[256,512]{1,0:T(8,128)(2,1)S(1)}, bf16[256,512]{1,0:T(8,128)(2,1)S(1)}, u32[]{:S(2)}, u32[]{:S(2)}) collective-permute-start(bf16[256,512]{1,0:T(8,128)(2,1)S(1)} %pad_maximum_fusion.8), channel_id=1, source_target_pairs={{0,1},{1,0},{2,3},{3,2},{4,5},{5,4},{6,7},{7,6},{8,9},{9,8},{10,11... | collective-permute-start | bytes 786440 | tf_op jit(solution)/shard_map/ppermute | solution.py:255
  111.7 26.0 %all-to-all-start = ((bf16[8,64,512]{2,1,0:T(8,128)(2,1)}), bf16[8,64,512]{2,1,0:T(8,128)(2,1)}, u32[]{:S(2)}, u32[]{:S(2)}) async-start(bf16[8,64,512]{2,1,0:T(8,128)(2,1)} %bitcast.38), calls=%async_computation | async-start | bytes 1048576 | tf_op jit(solution)/shard_map/all_to_all | solution.py:442
  129.4 4.4 %copy-start.8 = (bf16[128,1024]{0,1:T(8,128)(2,1)S(1)}, bf16[128,1024]{0,1:T(8,128)(2,1)}, u32[]{:S(2)}) copy-start(bf16[128,1024]{0,1:T(8,128)(2,1)} %copy.20) | copy-start | bytes 786436
  131.5 2.4 %copy-start.6 = (bf16[128,2,8,128]{0,3,2,1:T(8,128)(2,1)S(1)}, bf16[128,2,8,128]{0,3,2,1:T(8,128)(2,1)}, u32[]{:S(2)}) copy-start(bf16[128,2,8,128]{0,3,2,1:T(8,128)(2,1)} %copy.19) | copy-start | bytes 1572868

commit v9 on v8

--- a/solution.py
+++ b/solution.py
@@ -39,7 +39,8 @@
     return block
 
 
-def attention_kernel(q_ref, k_ref, v_ref, g_ref, bias_ref, att_ref, gq_ref, gkv_ref, *, head_dim, scale):
+def attention_kernel(q_ref, k_ref, v_ref, g_ref, bias_ref, att_ref, gq_ref, gkv_ref, gkv_low_ref,
+                     *, head_dim, scale):
     q = q_ref[...]
     g = g_ref[...]
     k = k_ref[...]
@@ -80,8 +81,12 @@
     )
     att_ref[...] = att.astype(att_ref.dtype)
     gq_ref[...] = gq.astype(gq_ref.dtype)
-    gkv_ref[:, :lanes] = jnp.dot(grads_t, q_sel, preferred_element_type=jnp.float32)
-    gkv_ref[:, lanes:] = jnp.dot(probs_t, g_sel, preferred_element_type=jnp.float32)
+    grad_k = jnp.dot(grads_t, q_sel, preferred_element_type=jnp.float32)
+    grad_v = jnp.dot(probs_t, g_sel, preferred_element_type=jnp.float32)
+    gkv_ref[0] = grad_k
+    gkv_ref[1] = grad_v
+    gkv_low_ref[0] = grad_k.astype(gkv_low_ref.dtype)
+    gkv_low_ref[1] = grad_v.astype(gkv_low_ref.dtype)
 
 
 def block_attention(query, projected, grad_attn, bias, heads):
@@ -111,12 +116,14 @@
         out_specs=[
             pl.BlockSpec((queries, lanes), lambda h: (0, h)),
             pl.BlockSpec((queries, lanes), lambda h: (0, h)),
-            pl.BlockSpec((keys, 2 * lanes), lambda h: (0, h)),
+            pl.BlockSpec((2, keys, lanes), lambda h: (0, 0, h)),
+            pl.BlockSpec((2, keys, lanes), lambda h: (0, 0, h)),
         ],
         out_shape=[
             jax.ShapeDtypeStruct((queries, width), jnp.bfloat16),
             jax.ShapeDtypeStruct((queries, width), jnp.bfloat16),
-            jax.ShapeDtypeStruct((keys, 2 * width), jnp.float32),
+            jax.ShapeDtypeStruct((2, keys, width), jnp.float32),
+            jax.ShapeDtypeStruct((2, keys, width), jnp.bfloat16),
         ],
         cost_estimate=cost,
         name="block_attention",
@@ -147,7 +154,7 @@
     return slice(0, radius)
 
 
-def grouped_send(pieces):
+def grouped_send(pieces, axis):
     lon_count = lax.axis_size("lon")
     groups = {}
     for index, (dl, db, value) in enumerate(pieces):
@@ -155,11 +162,11 @@
     out = [None] * len(pieces)
     for (dl, db), members in groups.items():
         values = [pieces[i][2] for i in members]
-        got = sent_to(jnp.concatenate(values, axis=1), dl, db)
+        got = sent_to(jnp.concatenate(values, axis=axis), dl, db)
         offset = 0
         for i, value in zip(members, values):
-            out[i] = got[:, offset : offset + value.shape[1]]
-            offset += value.shape[1]
+            out[i] = lax.slice_in_dim(got, offset, offset + value.shape[axis], axis=axis)
+            offset += value.shape[axis]
     return out
 
 
@@ -174,39 +181,31 @@
             piece = block[part(height, radius, da, True), part(breadth, radius, db, True)]
             spots.append((da, db))
             pieces.append((-da, -db, piece))
-    got = dict(zip(spots, grouped_send(pieces)))
+    got = dict(zip(spots, grouped_send(pieces, 1)))
     got[(0, 0)] = block
     rows = [jnp.concatenate([got[(da, db)] for db in (-1, 0, 1)], axis=1) for da in (-1, 0, 1)]
     return jnp.concatenate(rows, axis=0)
 
 
-def halo_return(ext_list, height, breadth, radius):
+def halo_return(ext, ext_low, height, breadth, radius):
     row_slices = {-1: slice(0, radius), 0: slice(radius, radius + height), 1: slice(radius + height, None)}
     col_slices = {-1: slice(0, radius), 0: slice(radius, radius + breadth), 1: slice(radius + breadth, None)}
-    owns = [ext[row_slices[0], col_slices[0]] for ext in ext_list]
-    widths = [ext.shape[-1] for ext in ext_list]
+    own = ext[:, row_slices[0], col_slices[0]]
     spots = []
     pieces = []
     for da in (-1, 0, 1):
         for db in (-1, 0, 1):
             if da == 0 and db == 0:
                 continue
-            joined = jnp.concatenate(
-                [ext[row_slices[da], col_slices[db]] for ext in ext_list], axis=-1
-            ).astype(jnp.bfloat16)
             spots.append((da, db))
-            pieces.append((da, db, joined))
-    for (da, db), got in zip(spots, grouped_send(pieces)):
+            pieces.append((da, db, ext_low[:, row_slices[da], col_slices[db]]))
+    for (da, db), got in zip(spots, grouped_send(pieces, 2)):
         rs = part(height, radius, da, True)
         cs = part(breadth, radius, db, True)
         pad_rows = (rs.start, height - rs.stop)
         pad_cols = (cs.start, breadth - cs.stop)
-        offset = 0
-        for index, width in enumerate(widths):
-            piece = got[..., offset : offset + width].astype(jnp.float32)
-            offset += width
-            owns[index] = owns[index] + jnp.pad(piece, (pad_rows, pad_cols, (0, 0)))
-    return owns
+        own = own + jnp.pad(got.astype(jnp.float32), ((0, 0), pad_rows, pad_cols, (0, 0)))
+    return own
 
 
 def partner_rows_product(lhs, weights, axis):
@@ -419,10 +418,13 @@
     allowed = inside & ((valid_ext == 1) | itself)
     bias = jnp.where(allowed, 0.0, -jnp.inf).astype(jnp.float32)
 
-    attended, grad_query, grad_kv = block_attention(query, projected, grad_attn, bias, HEADS)
-
-    grad_kv_ext = grad_kv.reshape(ext_rows, pad_cols, 2 * width)[:, :ext_cols]
-    (grad_kv_own,) = halo_return([grad_kv_ext], height, breadth, radius)
+    attended, grad_query, grad_kv, grad_kv_low = block_attention(
+        query, projected, grad_attn, bias, HEADS
+    )
+
+    grad_kv_ext = grad_kv.reshape(2, ext_rows, pad_cols, width)[:, :, :ext_cols]
+    grad_kv_low_ext = grad_kv_low.reshape(2, ext_rows, pad_cols, width)[:, :, :ext_cols]
+    grad_kv_own = halo_return(grad_kv_ext, grad_kv_low_ext, height, breadth, radius)
 
     if fast:
         own_att = columns(attended, dp_index, rows_half)
@@ -442,14 +444,8 @@
     spread = lax.all_to_all(partial.astype(jnp.bfloat16), "lat", 0, 0, tiled=True)
     d_w_out = spread.astype(jnp.float32).reshape(lat_count, rows_block, cols_block).sum(axis=0)
 
-    pairs = width // 128
-    grad_kv_low = (
-        grad_kv_own.astype(jnp.bfloat16)
-        .reshape(token_count, pairs, 2, 128)
-        .transpose(0, 2, 1, 3)
-        .reshape(token_count, 2 * width)
-    )
-    grad_proj = jnp.concatenate([grad_query, grad_kv_low], axis=1)
+    grad_kv_own = grad_kv_own.astype(jnp.bfloat16).reshape(2, token_count, width)
+    grad_proj = jnp.concatenate([grad_query, grad_kv_own[0], grad_kv_own[1]], axis=1)
     d_input = back_project(grad_proj).reshape(1, height, breadth, width)
     return (d_input, d_w_out)
 

time: 141 us -> 130 us (0.922)
  waiting for transfers between devices: 25.1 us -> 34.4 us
  starting transfers between devices: 43.6 us -> 35.7 us
  other arithmetic: 19.1 us -> 13.1 us
  local copies, waits for them, and re-layouts: 24.1 us -> 19.1 us
    ppermute x10, waiting for transfers between devices: 19.7 us -> 29.7 us  [sent_to(): return lax.ppermute(value, ('lat', 'lon'), grid_pairs(delta_lat, delta_lon))]
    all_to_all x1, starting transfers between devices: 11.1 us -> 4.74 us  [shards(): lax.all_to_all(partial.astype(jnp.bfloat16), 'lat', 0, 0, tiled=True)]
    ppermute x5, waiting for transfers between devices: 5.42 us -> 0.01 us  [swap(): return lax.ppermute(value, axis, [(0, 1), (1, 0)])]
    all_to_all x1, waiting for transfers between devices: 0.01 us -> 4.62 us  [shards(): lax.all_to_all(partial.astype(jnp.bfloat16), 'lat', 0, 0, tiled=True)]
    another operation x1 -> x0, other arithmetic: 2.87 us -> none
    reshape x1 -> x0, local copies, waits for them, and re-layouts: 2.19 us -> none  [shards(): grad_kv_low = grad_kv_own.astype(jnp.bfloat16).reshape(token_count, pairs...]
    transpose x1 -> x0, local copies, waits for them, and re-layouts: 2.05 us -> none  [shards(): grad_kv_low = grad_kv_own.astype(jnp.bfloat16).reshape(token_count, pairs...]
    ppermute x10, starting transfers between devices: 31.2 us -> 29.3 us  [sent_to(): return lax.ppermute(value, ('lat', 'lon'), grid_pairs(delta_lat, delta_lon))]
  transfers between devices with their start and end apart: 16 -> 16, of which waited for: 3 -> 3; matrix products, arithmetic and copies ran while one was open for 38% -> 31% of each run, Pallas kernels for 8% -> 9%
where the time goes in v9:
time: 130 us; the launch traced here: 129 us
  starting transfers between devices  35.7 us (27%)
  waiting for transfers between devices  34.4 us (26%)
  local copies, waits for them, and re-layouts  19.1 us (15%)
  matrix products  13.8 us (11%)
  other arithmetic  13.1 us (10%)
  Pallas kernels  11.9 us (9%)
    ppermute x10, waiting for transfers between devices, sent_to(): return lax.ppermute(value, ('lat', 'lon'), grid_pairs(delta_lat, delta_lon))  29.7 us
    ppermute x10, starting transfers between devices, sent_to(): return lax.ppermute(value, ('lat', 'lon'), grid_pairs(delta_lat, delta_lon))  29.3 us
    pallas_call x1, Pallas kernels, block_attention(): pl.pallas_call(kernel, grid=(pairs,), in_specs=[pl.BlockSpec((queries, la...  11.9 us
    slice x6, local copies, waits for them, and re-layouts, grouped_send(): lax.slice_in_dim(got, offset, offset + value.shape[axis], axis=axis)  6.07 us
    slice x3, local copies, waits for them, and re-layouts, halo_return(): pieces.append((da, db, ext_low[:, row_slices[da], col_slices[db]]))  5.32 us
    all_to_all x1, starting transfers between devices, shards(): lax.all_to_all(partial.astype(jnp.bfloat16), 'lat', 0, 0, tiled=True)  4.74 us
    all_to_all x1, waiting for transfers between devices, shards(): lax.all_to_all(partial.astype(jnp.bfloat16), 'lat', 0, 0, tiled=True)  4.62 us
    dot_general x1, matrix products, project(): jnp.dot(columns(rows, 1 - dp_index, rows_half), qkv_other, preferred_elem...  4.19 us
  transfers between devices with their start and end apart: 16, of which 3 were waited for; matrix products, arithmetic and copies ran while one was open for 31% of the time, Pallas kernels for 9%

profile of v9, /device:TPU:0, one launch (start us, length us, event | category | flops | bytes accessed | tf_op | source)
XLA Modules:
  0.0 129.1 jit_solution(6249922423243748196)
XLA Ops:
  0.6 0.0 copy-start.1
  0.7 1.1 fusion.71
  1.8 0.8 pad_maximum_fusion.7
  2.6 2.9 %collective-permute-start.2 = (bf16[8,12,1024]{2,1,0:T(8,128)(2,1)}, bf16[8,12,1024]{2,1,0:T(8,128)(2,1)}, u32[]{:S(2)}, u32[]{:S(2)}) collective-permute-start(bf16[8,12,1024]{2,1,0:T(8,128)(2,1)} %pad_maximum_fusion.7), channel_id=1, source_target_pairs={{0,1},{1,0},{2,3},{3,2},{4,5},{5,4},{6,7},{7,6},{8,9},{9,8},{10,11... | collective-permute-start | bytes 589832 | tf_op jit(solution)/shard_map/ppermute | solution.py:146
  5.5 1.1 fusion.70
  6.6 0.7 pad_maximum_fusion.11
  7.4 1.3 collective-permute-start.3
  8.7 0.7 pad_maximum_fusion.10
  9.4 6.1 %collective-permute-start = (bf16[6,12,1024]{2,1,0:T(8,128)(2,1)}, bf16[6,12,1024]{2,1,0:T(8,128)(2,1)}, u32[]{:S(2)}, u32[]{:S(2)}) collective-permute-start(bf16[6,12,1024]{2,1,0:T(8,128)(2,1)} %pad_maximum_fusion.10), channel_id=1, source_target_pairs={{0,3},{1,2},{2,5},{3,4},{4,7},{5,6},{6,9},{7,8},{8,11},{9,10},{10,... | collective-permute-start | bytes 442376 | tf_op jit(solution)/shard_map/ppermute | solution.py:146
  15.5 0.8 slice_bitcast_fusion.1
  16.3 4.3 %collective-permute-start.1 = (bf16[6,16,1024]{2,1,0:T(8,128)(2,1)}, bf16[6,16,1024]{2,1,0:T(8,128)(2,1)}, u32[]{:S(2)}, u32[]{:S(2)}) collective-permute-start(bf16[6,16,1024]{2,1,0:T(8,128)(2,1)} %get-tuple-element.32), channel_id=1, source_target_pairs={{0,2},{1,3},{2,4},{3,5},{4,6},{5,7},{6,8},{7,9},{8,10},{9,11},{10,... | collective-permute-start | bytes 589832 | tf_op jit(solution)/shard_map/ppermute | solution.py:146
  20.7 0.1 copy.12
  20.8 0.1 copy.11
  20.9 0.1 copy.13
  21.0 0.1 pad_add_fusion
  21.1 0.1 pad_dynamic-slice_fusion
  21.2 0.1 eq.28
  21.3 1.0 fusion.45.bias_ref
  22.3 0.5 convolution_convert_fusion.1
  22.8 0.7 constant_dynamic-slice_fusion.3
  23.5 0.1 pad_maximum_fusion
  23.6 0.0 copy-start.3
  23.6 1.6 %collective-permute-start.4 = (bf16[6,16,1024]{2,1,0:T(8,128)(2,1)}, bf16[6,16,1024]{2,1,0:T(8,128)(2,1)S(1)}, u32[]{:S(2)}, u32[]{:S(2)}) collective-permute-start(bf16[6,16,1024]{2,1,0:T(8,128)(2,1)} %get-tuple-element.33), channel_id=1, source_target_pairs={{2,0},{3,1},{4,2},{5,3},{6,4},{7,5},{8,6},{9,7},{10,8},{11,9},{12,... | collective-permute-start | bytes 589832 | tf_op jit(solution)/shard_map/ppermute | solution.py:146
  25.2 1.0 fusion.73
  26.3 0.6 collective-permute-start.6
  26.8 1.0 fusion.72
  27.9 1.1 fusion.69
  29.0 4.4 %collective-permute-done.4 = bf16[6,16,1024]{2,1,0:T(8,128)(2,1)S(1)} collective-permute-done((bf16[6,16,1024]{2,1,0:T(8,128)(2,1)}, bf16[6,16,1024]{2,1,0:T(8,128)(2,1)S(1)}, u32[]{:S(2)}, u32[]{:S(2)}) %collective-permute-start.4) | collective-permute-done | bytes 196640 | tf_op jit(solution)/shard_map/ppermute | solution.py:146
  33.3 1.7 %fusion.12 = bf16[20,32,1024]{2,1,0:T(8,128)(2,1)S(1)} fusion(bf16[6,6,1024]{2,1,0:T(8,128)(2,1)S(1)} %get-tuple-element.45, bf16[6,16,1024]{2,1,0:T(8,128)(2,1)S(1)} %collective-permute-done.4, bf16[6,6,1024]{2,1,0:T(8,128)(2,1)S(1)} %get-tuple-element.44, bf16[8,6,1024]{2,1,0:T(8,128)(2,1)S(1)} %get-tuple-element.35, ...), kind=kLoop, calls=%fused_computation.15 | loop fusion | flops 18350080 | bytes 2457600 | tf_op jit(solution)/shard_map/concatenate | solution.py:187
  35.0 2.2 %fusion.29 = f32[640,3072]{1,0:T(8,128)S(1)} fusion(bf16[512,3072]{1,0:T(8,128)(2,1)S(1)} %copy-done.3, bf16[640,1024]{1,0:T(8,128)(2,1)S(1)} %bitcast.29, s32[]{:T(128)S(6)} %select_n.95), kind=kOutput, calls=%fused_computation.40 | convolution fusion | flops 2013265920 | bytes 11665412 | tf_op jit(solution)/shard_map/dot_general | solution.py:359
  37.3 0.7 constant_dynamic-slice_fusion.2
  38.0 0.7 pad_maximum_fusion.9
  38.7 0.5 collective-permute-start.14
  39.2 0.5 fusion.18
  39.7 0.8 maximum_select_fusion.g_ref
  40.5 4.2 %add_convert_fusion.k_ref.v_ref = bf16[640,3072]{1,0:T(8,128)(2,1)S(1)} fusion(f32[640,3072]{1,0:T(8,128)S(1)} %fusion.29, bf16[512,3072]{1,0:T(8,128)(2,1)} %collective-permute-done.5, bf16[640,1024]{1,0:T(8,128)(2,1)S(1)} %bitcast.30, s32[]{:T(128)S(6)} %select_n.96), kind=kOutput, calls=%fused_computation | convolution fusion | flops 2017198080 | bytes 15597572 | tf_op jit(solution)/shard_map/dot_general | solution.py:362
  44.7 1.9 %copy-done = bf16[640,3072]{1,0:T(8,128)(2,1)} copy-done((bf16[640,3072]{1,0:T(8,128)(2,1)}, bf16[640,3072]{1,0:T(8,128)(2,1)S(1)}, u32[]{:S(2)}) %copy-start) | copy-done | bytes 3932184
  46.7 0.8 slice.177
  47.4 11.9 %block_attention.1 = (bf16[128,1024]{1,0:T(8,128)(2,1)}, bf16[128,1024]{1,0:T(8,128)(2,1)}, f32[2,640,1024]{2,1,0:T(8,128)}, bf16[2,640,1024]{2,1,0:T(8,128)(2,1)}) custom-call(bf16[128,1024]{1,0:T(8,128)(2,1)} %bitcast.38, bf16[640,3072]{1,0:T(8,128)(2,1)} %copy-done, bf16[640,3072]{1,0:T(8,128)(2,1)} %copy-done, ...), custom_call_target="tpu_custom_call" | custom-call | flops 2013265920 | bytes 9240576 | tf_op jit(solution)/shard_map/block_attention/pallas_call | solution.py:106
  59.4 1.3 fusion.64
  60.6 1.5 %fusion.63 = (bf16[2,6,6,1024]{3,2,1,0:T(8,128)(2,1)S(1)}, bf16[2,6,6,1024]{3,2,1,0:T(8,128)(2,1)S(1)}, bf16[2,6,6,1024]{3,2,1,0:T(8,128)(2,1)S(1)}, bf16[2,6,6,1024]{3,2,1,0:T(8,128)(2,1)S(1)}) fusion(bf16[2,20,32,1024]{3,2,1,0:T(8,128)(2,1)} %bitcast.36), kind=kLoop, calls=%fused_computation.108 | loop fusion | bytes 1179648 | tf_op jit(solution)/shard_map/slice | solution.py:201
  62.2 0.1 collective-permute-start.12
  62.2 1.0 pad_maximum_fusion.2
  63.2 1.5 %collective-permute-start.9 = (bf16[2,8,12,1024]{3,2,1,0:T(8,128)(2,1)}, bf16[2,8,12,1024]{3,2,1,0:T(8,128)(2,1)}, u32[]{:S(2)}, u32[]{:S(2)}) collective-permute-start(bf16[2,8,12,1024]{3,2,1,0:T(8,128)(2,1)} %pad_maximum_fusion.2), channel_id=1, source_target_pairs={{0,1},{1,0},{2,3},{3,2},{4,5},{5,4},{6,7},{7,6},{8,9},{9,8},{10,11... | collective-permute-start | bytes 1179656 | tf_op jit(solution)/shard_map/ppermute | solution.py:146
  64.7 0.1 pad_maximum_fusion.4
  64.9 2.8 %collective-permute-start.10 = (bf16[2,6,12,1024]{3,2,1,0:T(8,128)(2,1)S(1)}, bf16[2,6,12,1024]{3,2,1,0:T(8,128)(2,1)S(1)}, u32[]{:S(2)}, u32[]{:S(2)}) collective-permute-start(bf16[2,6,12,1024]{3,2,1,0:T(8,128)(2,1)S(1)} %pad_maximum_fusion.4), channel_id=1, source_target_pairs={{0,3},{1,2},{2,5},{3,4},{4,7},{5,6},{6,9},{7,8},{8,11},{9,10},{10,... | collective-permute-start | bytes 884744 | tf_op jit(solution)/shard_map/ppermute | solution.py:146
  67.7 0.1 pad_maximum_fusion.3
  67.8 1.3 %collective-permute-start.7 = (bf16[2,6,12,1024]{3,2,1,0:T(8,128)(2,1)S(1)}, bf16[2,6,12,1024]{3,2,1,0:T(8,128)(2,1)S(1)}, u32[]{:S(2)}, u32[]{:S(2)}) collective-permute-start(bf16[2,6,12,1024]{3,2,1,0:T(8,128)(2,1)S(1)} %pad_maximum_fusion.3), channel_id=1, source_target_pairs={{2,1},{3,0},{4,3},{5,2},{6,5},{7,4},{8,7},{9,6},{10,9},{11,8},{12,... | collective-permute-start | bytes 884744 | tf_op jit(solution)/shard_map/ppermute | solution.py:146
  69.1 2.6 %fusion.62 = (bf16[2,6,16,1024]{3,2,1,0:T(8,128)(2,1)}, bf16[2,6,16,1024]{3,2,1,0:T(8,128)(2,1)}) fusion(bf16[2,20,32,1024]{3,2,1,0:T(8,128)(2,1)} %bitcast.37), kind=kLoop, calls=%fused_computation.107 | loop fusion | bytes 1572864 | tf_op jit(solution)/shard_map/slice | solution.py:201
  71.7 1.3 collective-permute-start.8
  73.0 25.4 %collective-permute-done.10 = bf16[2,6,12,1024]{3,2,1,0:T(8,128)(2,1)S(1)} collective-permute-done((bf16[2,6,12,1024]{3,2,1,0:T(8,128)(2,1)S(1)}, bf16[2,6,12,1024]{3,2,1,0:T(8,128)(2,1)S(1)}, u32[]{:S(2)}, u32[]{:S(2)}) %collective-permute-start.10) | collective-permute-done | bytes 294944 | tf_op jit(solution)/shard_map/ppermute | solution.py:146
  98.4 0.6 collective-permute-start.13
  99.0 0.8 fusion.68
  99.8 6.1 %collective-permute-start.11 = (bf16[2,6,16,1024]{3,2,1,0:T(8,128)(2,1)}, bf16[2,6,16,1024]{3,2,1,0:T(8,128)(2,1)}, u32[]{:S(2)}, u32[]{:S(2)}) collective-permute-start(bf16[2,6,16,1024]{3,2,1,0:T(8,128)(2,1)} %get-tuple-element.11), channel_id=1, source_target_pairs={{0,2},{1,3},{2,4},{3,5},{4,6},{5,7},{6,8},{7,9},{8,10},{9,11},{10,... | collective-permute-start | bytes 1179656 | tf_op jit(solution)/shard_map/ppermute | solution.py:146
  106.0 0.9 fusion.67
  106.9 2.2 %fusion.17 = bf16[512,512]{1,0:T(8,128)(2,1)} fusion(bf16[256,512]{1,0:T(8,128)(2,1)S(1)} %collective-permute-done.13, bf16[128,512]{1,0:T(8,128)(2,1)S(1)} %collective-permute-done.12, bf16[128,512]{1,0:T(8,128)(2,1)S(1)} %get-tuple-element.30, bf16[256,512]{1,0:T(8,128)(2,1)} %collective-permute-done.14, bf16[128,512]{1,0:T(8,128)(2,1)S(1)} %copy-done.9, ...), kind=kOutput, calls=%fused_computation.21 | convolution fusion | flops 272105472 | bytes 1572864 | tf_op jit(solution)/shard_map/dot_general | solution.py:441
  109.1 4.7 %all-to-all-start = ((bf16[8,64,512]{2,1,0:T(8,128)(2,1)}), bf16[8,64,512]{2,1,0:T(8,128)(2,1)}, u32[]{:S(2)}, u32[]{:S(2)}) async-start(bf16[8,64,512]{2,1,0:T(8,128)(2,1)} %bitcast.39), calls=%async_computation | async-start | bytes 1048576 | tf_op jit(solution)/shard_map/all_to_all | solution.py:444
  113.8 1.2 fusion.66
  115.1 2.5 %fusion.26 = bf16[2,8,16,1024]{3,2,1,0:T(8,128)(2,1)S(1)} fusion(f32[2,20,32,1024]{3,2,1,0:T(8,128)} %bitcast.44, bf16[2,6,6,1024]{3,2,1,0:T(8,128)(2,1)} %get-tuple-element.25, bf16[2,6,16,1024]{3,2,1,0:T(8,128)(2,1)} %collective-permute-done.11, bf16[2,6,6,1024]{3,2,1,0:T(8,128)(2,1)} %get-tuple-element.24, ...), kind=kLoop, calls=%fused_computation.35 | loop fusion | flops 4456448 | bytes 3342336 | tf_op jit(solution)/shard_map/convert_element_type | solution.py:447
  117.7 1.2 convolution_convert_fusion.3
  118.8 3.1 %convolution_convert_fusion.2 = bf16[128,512]{1,0:T(8,128)(2,1)S(1)} fusion(bf16[512,3072]{1,0:T(8,128)(2,1)} %collective-permute-done.5, bf16[128,1024]{1,0:T(8,128)(2,1)S(1)} %bitcast.43, bf16[128,1024]{1,0:T(8,128)(2,1)S(1)} %bitcast.41, bf16[128,1024]{1,0:T(8,128)(2,1)S(1)} %copy-done.11), kind=kOutput, calls=%fused_computation.24 | convolution fusion | flops 405078016 | bytes 4063232 | tf_op jit(solution)/shard_map/dot_general | solution.py:369
  121.9 0.8 maximum_select_fusion.1
  122.7 4.6 %all-to-all-done = bf16[8,64,512]{2,1,0:T(8,128)(2,1)} async-done(((bf16[8,64,512]{2,1,0:T(8,128)(2,1)}), bf16[8,64,512]{2,1,0:T(8,128)(2,1)}, u32[]{:S(2)}, u32[]{:S(2)}) %all-to-all-start) | async-done | bytes 524320 | tf_op jit(solution)/shard_map/all_to_all | solution.py:444
  127.3 1.8 %convert_reduce_fusion = f32[64,512]{1,0:T(8,128)} fusion(bf16[8,64,512]{2,1,0:T(8,128)(2,1)} %all-to-all-done), kind=kLoop, calls=%fused_computation.37 | loop fusion | flops 491520 | bytes 655360 | tf_op jit(solution)/shard_map/reduce_sum | solution.py:445
  (43 shorter events, 0.2 us)
Async XLA Ops:
  0.6 14.9 %copy-start.1 = (bf16[1,8,16,1024]{3,2,1,0:T(8,128)(2,1)S(1)}, bf16[1,8,16,1024]{3,2,1,0:T(8,128)(2,1)}, u32[]{:S(2)}) copy-start(bf16[1,8,16,1024]{3,2,1,0:T(8,128)(2,1)} %param.5) | copy-start | bytes 786436
  0.6 20.1 %copy-start.10 = (s32[64,32]{0,1:T(8,128)S(1)}, s32[64,32]{0,1:T(8,128)}, u32[]{:S(2)}) copy-start(s32[64,32]{0,1:T(8,128)} %param.7) | copy-start | bytes 24580
  0.7 21.6 %copy-start.2 = (bf16[512,1024]{1,0:T(8,128)(2,1)S(1)}, bf16[512,1024]{1,0:T(8,128)(2,1)}, u32[]{:S(2)}) copy-start(bf16[512,1024]{1,0:T(8,128)(2,1)} %param.9) | copy-start | bytes 3145732
  0.7 21.6 %copy-start.4 = (bf16[1,8,16,1024]{3,2,1,0:T(8,128)(2,1)S(1)}, bf16[1,8,16,1024]{3,2,1,0:T(8,128)(2,1)}, u32[]{:S(2)}) copy-start(bf16[1,8,16,1024]{3,2,1,0:T(8,128)(2,1)} %param.6) | copy-start | bytes 786436
  2.6 25.3 %collective-permute-start.2 = (bf16[8,12,1024]{2,1,0:T(8,128)(2,1)}, bf16[8,12,1024]{2,1,0:T(8,128)(2,1)}, u32[]{:S(2)}, u32[]{:S(2)}) collective-permute-start(bf16[8,12,1024]{2,1,0:T(8,128)(2,1)} %pad_maximum_fusion.7), channel_id=1, source_target_pairs={{0,1},{1,0},{2,3},{3,2},{4,5},{5,4},{6,7},{7,6},{8,9},{9,8},{10,11... | collective-permute-start | bytes 589832 | tf_op jit(solution)/shard_map/ppermute | solution.py:146
  7.4 16.3 %collective-permute-start.3 = (bf16[6,12,1024]{2,1,0:T(8,128)(2,1)}, bf16[6,12,1024]{2,1,0:T(8,128)(2,1)}, u32[]{:S(2)}, u32[]{:S(2)}) collective-permute-start(bf16[6,12,1024]{2,1,0:T(8,128)(2,1)} %pad_maximum_fusion.11), channel_id=1, source_target_pairs={{2,1},{3,0},{4,3},{5,2},{6,5},{7,4},{8,7},{9,6},{10,9},{11,8},{12,... | collective-permute-start | bytes 442376 | tf_op jit(solution)/shard_map/ppermute | solution.py:146
  9.4 16.8 %collective-permute-start = (bf16[6,12,1024]{2,1,0:T(8,128)(2,1)}, bf16[6,12,1024]{2,1,0:T(8,128)(2,1)}, u32[]{:S(2)}, u32[]{:S(2)}) collective-permute-start(bf16[6,12,1024]{2,1,0:T(8,128)(2,1)} %pad_maximum_fusion.10), channel_id=1, source_target_pairs={{0,3},{1,2},{2,5},{3,4},{4,7},{5,6},{6,9},{7,8},{8,11},{9,10},{10,... | collective-permute-start | bytes 442376 | tf_op jit(solution)/shard_map/ppermute | solution.py:146
  16.3 12.6 %collective-permute-start.1 = (bf16[6,16,1024]{2,1,0:T(8,128)(2,1)}, bf16[6,16,1024]{2,1,0:T(8,128)(2,1)}, u32[]{:S(2)}, u32[]{:S(2)}) collective-permute-start(bf16[6,16,1024]{2,1,0:T(8,128)(2,1)} %get-tuple-element.32), channel_id=1, source_target_pairs={{0,2},{1,3},{2,4},{3,5},{4,6},{5,7},{6,8},{7,9},{8,10},{9,11},{10,... | collective-permute-start | bytes 589832 | tf_op jit(solution)/shard_map/ppermute | solution.py:146
  20.7 19.8 %collective-permute-start.5 = (bf16[512,3072]{1,0:T(8,128)(2,1)}, bf16[512,3072]{1,0:T(8,128)(2,1)}, u32[]{:S(2)}, u32[]{:S(2)}) collective-permute-start(bf16[512,3072]{1,0:T(8,128)(2,1)} %param.8), channel_id=1, source_target_pairs={{0,16},{16,0},{1,17},{17,1},{2,18},{18,2},{3,19},{19,3},{4,20},{20... | collective-permute-start | bytes 9437192 | tf_op jit(solution)/shard_map/ppermute | solution.py:254
  23.6 11.4 %copy-start.3 = (bf16[512,3072]{1,0:T(8,128)(2,1)S(1)}, bf16[512,3072]{1,0:T(8,128)(2,1)}, u32[]{:S(2)}) copy-start(bf16[512,3072]{1,0:T(8,128)(2,1)} %param.8) | copy-start | bytes 9437188
  23.6 9.7 %collective-permute-start.4 = (bf16[6,16,1024]{2,1,0:T(8,128)(2,1)}, bf16[6,16,1024]{2,1,0:T(8,128)(2,1)S(1)}, u32[]{:S(2)}, u32[]{:S(2)}) collective-permute-start(bf16[6,16,1024]{2,1,0:T(8,128)(2,1)} %get-tuple-element.33), channel_id=1, source_target_pairs={{2,0},{3,1},{4,2},{5,3},{6,4},{7,5},{8,6},{9,7},{10,8},{11,9},{12,... | collective-permute-start | bytes 589832 | tf_op jit(solution)/shard_map/ppermute | solution.py:146
  26.3 11.0 %collective-permute-start.6 = (bf16[640,1024]{1,0:T(8,128)(2,1)S(1)}, bf16[640,1024]{1,0:T(8,128)(2,1)S(1)}, u32[]{:S(2)}, u32[]{:S(2)}) collective-permute-start(bf16[640,1024]{1,0:T(8,128)(2,1)S(1)} %pad_maximum_fusion), channel_id=1, source_target_pairs={{0,16},{16,0},{1,17},{17,1},{2,18},{18,2},{3,19},{19,3},{4,20},{20... | collective-permute-start | bytes 3932168 | tf_op jit(solution)/shard_map/ppermute | solution.py:254
  35.0 3.0 %copy-start.6 = (bf16[128,512]{1,0:T(8,128)(2,1)S(1)}, bf16[128,512]{1,0:T(8,128)(2,1)}, u32[]{:S(2)}) copy-start(bf16[128,512]{1,0:T(8,128)(2,1)} %get-tuple-element.27) | copy-start | bytes 393220
  35.0 4.2 %copy-start.5 = (bf16[1,8,16,1024]{3,2,1,0:T(8,128)(2,1)S(1)}, bf16[1,8,16,1024]{3,2,1,0:T(8,128)(2,1)}, u32[]{:S(2)}) copy-start(bf16[1,8,16,1024]{3,2,1,0:T(8,128)(2,1)} %param.6) | copy-start | bytes 786436
  38.7 68.1 %collective-permute-start.14 = (bf16[256,512]{1,0:T(8,128)(2,1)}, bf16[256,512]{1,0:T(8,128)(2,1)}, u32[]{:S(2)}, u32[]{:S(2)}) collective-permute-start(bf16[256,512]{1,0:T(8,128)(2,1)} %pad_maximum_fusion.9), channel_id=1, source_target_pairs={{0,1},{1,0},{2,3},{3,2},{4,5},{5,4},{6,7},{7,6},{8,9},{9,8},{10,11... | collective-permute-start | bytes 786440 | tf_op jit(solution)/shard_map/ppermute | solution.py:254
  44.7 1.9 %copy-start = (bf16[640,3072]{1,0:T(8,128)(2,1)}, bf16[640,3072]{1,0:T(8,128)(2,1)S(1)}, u32[]{:S(2)}) copy-start(bf16[640,3072]{1,0:T(8,128)(2,1)S(1)} %add_convert_fusion.k_ref.v_ref) | copy-start | bytes 11796484
  59.4 2.7 %copy-start.7 = (bf16[128,1024]{1,0:T(8,128)(2,1)S(1)}, bf16[128,1024]{1,0:T(8,128)(2,1)}, u32[]{:S(2)}) copy-start(bf16[128,1024]{1,0:T(8,128)(2,1)} %get-tuple-element.9) | copy-start | bytes 786436
  62.2 9.6 %collective-permute-start.12 = (bf16[128,512]{1,0:T(8,128)(2,1)S(1)}, bf16[128,512]{1,0:T(8,128)(2,1)S(1)}, u32[]{:S(2)}, u32[]{:S(2)}) collective-permute-start(bf16[128,512]{1,0:T(8,128)(2,1)S(1)} %get-tuple-element.31), channel_id=1, source_target_pairs={{0,16},{16,0},{1,17},{17,1},{2,18},{18,2},{3,19},{19,3},{4,20},{20... | collective-permute-start | bytes 393224 | tf_op jit(solution)/shard_map/ppermute | solution.py:254
  63.2 50.6 %collective-permute-start.9 = (bf16[2,8,12,1024]{3,2,1,0:T(8,128)(2,1)}, bf16[2,8,12,1024]{3,2,1,0:T(8,128)(2,1)}, u32[]{:S(2)}, u32[]{:S(2)}) collective-permute-start(bf16[2,8,12,1024]{3,2,1,0:T(8,128)(2,1)} %pad_maximum_fusion.2), channel_id=1, source_target_pairs={{0,1},{1,0},{2,3},{3,2},{4,5},{5,4},{6,7},{7,6},{8,9},{9,8},{10,11... | collective-permute-start | bytes 1179656 | tf_op jit(solution)/shard_map/ppermute | solution.py:146
  64.7 42.1 %copy-start.8 = (bf16[128,512]{1,0:T(8,128)(2,1)S(1)}, bf16[128,512]{1,0:T(8,128)(2,1)}, u32[]{:S(2)}) copy-start(bf16[128,512]{1,0:T(8,128)(2,1)} %get-tuple-element.26) | copy-start | bytes 393220
  64.7 42.1 %copy-start.9 = (bf16[128,512]{1,0:T(8,128)(2,1)S(1)}, bf16[128,512]{1,0:T(8,128)(2,1)}, u32[]{:S(2)}) copy-start(bf16[128,512]{1,0:T(8,128)(2,1)} %get-tuple-element.28) | copy-start | bytes 393220
  64.9 33.5 %collective-permute-start.10 = (bf16[2,6,12,1024]{3,2,1,0:T(8,128)(2,1)S(1)}, bf16[2,6,12,1024]{3,2,1,0:T(8,128)(2,1)S(1)}, u32[]{:S(2)}, u32[]{:S(2)}) collective-permute-start(bf16[2,6,12,1024]{3,2,1,0:T(8,128)(2,1)S(1)} %pad_maximum_fusion.4), channel_id=1, source_target_pairs={{0,3},{1,2},{2,5},{3,4},{4,7},{5,6},{6,9},{7,8},{8,11},{9,10},{10,... | collective-permute-start | bytes 884744 | tf_op jit(solution)/shard_map/ppermute | solution.py:146
  67.8 32.0 %collective-permute-start.7 = (bf16[2,6,12,1024]{3,2,1,0:T(8,128)(2,1)S(1)}, bf16[2,6,12,1024]{3,2,1,0:T(8,128)(2,1)S(1)}, u32[]{:S(2)}, u32[]{:S(2)}) collective-permute-start(bf16[2,6,12,1024]{3,2,1,0:T(8,128)(2,1)S(1)} %pad_maximum_fusion.3), channel_id=1, source_target_pairs={{2,1},{3,0},{4,3},{5,2},{6,5},{7,4},{8,7},{9,6},{10,9},{11,8},{12,... | collective-permute-start | bytes 884744 | tf_op jit(solution)/shard_map/ppermute | solution.py:146
  71.7 43.3 %collective-permute-start.8 = (bf16[2,6,16,1024]{3,2,1,0:T(8,128)(2,1)}, bf16[2,6,16,1024]{3,2,1,0:T(8,128)(2,1)}, u32[]{:S(2)}, u32[]{:S(2)}) collective-permute-start(bf16[2,6,16,1024]{3,2,1,0:T(8,128)(2,1)} %get-tuple-element.10), channel_id=1, source_target_pairs={{2,0},{3,1},{4,2},{5,3},{6,4},{7,5},{8,6},{9,7},{10,8},{11,9},{12,... | collective-permute-start | bytes 1179656 | tf_op jit(solution)/shard_map/ppermute | solution.py:146
  98.4 8.4 %collective-permute-start.13 = (bf16[256,512]{1,0:T(8,128)(2,1)S(1)}, bf16[256,512]{1,0:T(8,128)(2,1)S(1)}, u32[]{:S(2)}, u32[]{:S(2)}) collective-permute-start(bf16[256,512]{1,0:T(8,128)(2,1)S(1)} %pad_maximum_fusion.8), channel_id=1, source_target_pairs={{0,1},{1,0},{2,3},{3,2},{4,5},{5,4},{6,7},{7,6},{8,9},{9,8},{10,11... | collective-permute-start | bytes 786440 | tf_op jit(solution)/shard_map/ppermute | solution.py:254
  99.8 15.3 %collective-permute-start.11 = (bf16[2,6,16,1024]{3,2,1,0:T(8,128)(2,1)}, bf16[2,6,16,1024]{3,2,1,0:T(8,128)(2,1)}, u32[]{:S(2)}, u32[]{:S(2)}) collective-permute-start(bf16[2,6,16,1024]{3,2,1,0:T(8,128)(2,1)} %get-tuple-element.11), channel_id=1, source_target_pairs={{0,2},{1,3},{2,4},{3,5},{4,6},{5,7},{6,8},{7,9},{8,10},{9,11},{10,... | collective-permute-start | bytes 1179656 | tf_op jit(solution)/shard_map/ppermute | solution.py:146
  109.1 18.3 %all-to-all-start = ((bf16[8,64,512]{2,1,0:T(8,128)(2,1)}), bf16[8,64,512]{2,1,0:T(8,128)(2,1)}, u32[]{:S(2)}, u32[]{:S(2)}) async-start(bf16[8,64,512]{2,1,0:T(8,128)(2,1)} %bitcast.39), calls=%async_computation | async-start | bytes 1048576 | tf_op jit(solution)/shard_map/all_to_all | solution.py:444
  115.0 2.6 %copy-start.11 = (bf16[128,1024]{1,0:T(8,128)(2,1)S(1)}, bf16[128,1024]{1,0:T(8,128)(2,1)}, u32[]{:S(2)}) copy-start(bf16[128,1024]{1,0:T(8,128)(2,1)} %get-tuple-element.6) | copy-start | bytes 786436

commit v10 on v9

--- a/solution.py
+++ b/solution.py
@@ -188,24 +188,39 @@
 
 
 def halo_return(ext, ext_low, height, breadth, radius):
-    row_slices = {-1: slice(0, radius), 0: slice(radius, radius + height), 1: slice(radius + height, None)}
-    col_slices = {-1: slice(0, radius), 0: slice(radius, radius + breadth), 1: slice(radius + breadth, None)}
-    own = ext[:, row_slices[0], col_slices[0]]
-    spots = []
-    pieces = []
-    for da in (-1, 0, 1):
-        for db in (-1, 0, 1):
-            if da == 0 and db == 0:
-                continue
-            spots.append((da, db))
-            pieces.append((da, db, ext_low[:, row_slices[da], col_slices[db]]))
-    for (da, db), got in zip(spots, grouped_send(pieces, 2)):
-        rs = part(height, radius, da, True)
-        cs = part(breadth, radius, db, True)
-        pad_rows = (rs.start, height - rs.stop)
-        pad_cols = (cs.start, breadth - cs.stop)
-        own = own + jnp.pad(got.astype(jnp.float32), ((0, 0), pad_rows, pad_cols, (0, 0)))
-    return own
+    lon_count = lax.axis_size("lon")
+    lefts = ext_low[:, :, :radius]
+    rights = ext_low[:, :, radius + breadth :]
+    if lon_count == 2:
+        got = swap(jnp.concatenate([lefts, rights], axis=2), "lon")
+        from_right = got[:, :, :radius]
+        from_left = got[:, :, radius:]
+    else:
+        from_right = passed_along(lefts, "lon", -1)
+        from_left = passed_along(rights, "lon", 1)
+    middle = (
+        ext[:, :, radius : radius + breadth]
+        + jnp.pad(from_right.astype(jnp.float32), ((0, 0), (0, 0), (breadth - radius, 0), (0, 0)))
+        + jnp.pad(from_left.astype(jnp.float32), ((0, 0), (0, 0), (0, breadth - radius), (0, 0)))
+    )
+    from_below = shifted(middle[:, :radius].astype(jnp.bfloat16), "lat", -1)
+    from_above = shifted(middle[:, radius + height :].astype(jnp.bfloat16), "lat", 1)
+    return (
+        middle[:, radius : radius + height]
+        + jnp.pad(from_below.astype(jnp.float32), ((0, 0), (height - radius, 0), (0, 0), (0, 0)))
+        + jnp.pad(from_above.astype(jnp.float32), ((0, 0), (0, height - radius), (0, 0), (0, 0)))
+    )
+
+
+def halo_tokens(block, radius):
+    breadth = block.shape[1]
+    rows_ext = extended(block, (("lat", 0),), radius, False)
+    if lax.axis_size("lon") != 2:
+        return extended(rows_ext, (("lon", 1),), radius, True)
+    got = swap(
+        jnp.concatenate([rows_ext[:, breadth - radius :], rows_ext[:, :radius]], axis=1), "lon"
+    )
+    return jnp.concatenate([got[:, :radius], rows_ext, got[:, radius:]], axis=1)
 
 
 def partner_rows_product(lhs, weights, axis):
@@ -390,7 +405,7 @@
             out = lax.dot_general(grad_proj, panels, TRANS_B, preferred_element_type=jnp.float32)
             return out.astype(jnp.bfloat16)
 
-    tok_ext = halo_gather(inputs_here, radius)
+    tok_ext = halo_tokens(inputs_here, radius)
     tok_ext = jnp.pad(tok_ext, ((0, 0), (0, pad_cols - ext_cols), (0, 0)))
     tok_ext = tok_ext.reshape(key_count, width)
 

time: 130 us -> 138 us (1.062)
  waiting for transfers between devices: 34.4 us -> 57.9 us
  starting transfers between devices: 35.7 us -> 27.6 us
  local copies, waits for them, and re-layouts: 19.1 us -> 12.5 us
  other arithmetic: 13.1 us -> 11.2 us
    ppermute x5 -> x7, waiting for transfers between devices: 0.01 us -> 39.9 us  [swap(): return lax.ppermute(value, axis, [(0, 1), (1, 0)])]
    ppermute x10 -> x4, starting transfers between devices: 29.3 us -> 12.8 us  [the longest x2 6.59 us: shifted(): return lax.ppermute(value, axis, pairs)]
    ppermute x10 -> x4, waiting for transfers between devices: 29.7 us -> 14.8 us  [the longest x2 10.6 us: shifted(): return lax.ppermute(value, axis, pairs)]
    slice x12 -> x6, local copies, waits for them, and re-layouts: 14.4 us -> 5.5 us  [the longest x1 1.92 us: extended(): lax.slice_in_dim(block, block.shape[dim] - width, None, axis=dim)]
    all_to_all x1, starting transfers between devices: 4.74 us -> 9.65 us  [shards(): lax.all_to_all(partial.astype(jnp.bfloat16), 'lat', 0, 0, tiled=True)]
    ppermute x5 -> x7, starting transfers between devices: 1.74 us -> 5.18 us  [swap(): return lax.ppermute(value, axis, [(0, 1), (1, 0)])]
    concatenate x7 -> x4, other arithmetic: 5.2 us -> 2.18 us  [the longest x1 1.27 us: halo_return(): got = swap(jnp.concatenate([lefts, rights], axis=2), 'lon')]
    another operation x0 -> x1, other arithmetic: none -> 2.86 us
  transfers between devices with their start and end apart: 16 -> 12, of which waited for: 3 -> 9; matrix products, arithmetic and copies ran while one was open for 31% -> 13% of each run, Pallas kernels for 9% -> 0%
where the time goes in v10:
time: 138 us; the launch traced here: 137 us
  waiting for transfers between devices  57.9 us (42%)
  starting transfers between devices  27.6 us (20%)
  matrix products  15.1 us (11%)
  local copies, waits for them, and re-layouts  12.5 us (9%)
  Pallas kernels  12 us (9%)
  other arithmetic  11.2 us (8%)
    ppermute x7, waiting for transfers between devices, swap(): return lax.ppermute(value, axis, [(0, 1), (1, 0)])  39.9 us
    pallas_call x1, Pallas kernels, block_attention(): pl.pallas_call(kernel, grid=(pairs,), in_specs=[pl.BlockSpec((queries, la...  12 us
    ppermute x2, waiting for transfers between devices, shifted(): return lax.ppermute(value, axis, pairs)  10.6 us
    all_to_all x1, starting transfers between devices, shards(): lax.all_to_all(partial.astype(jnp.bfloat16), 'lat', 0, 0, tiled=True)  9.65 us
    ppermute x2, starting transfers between devices, shifted(): return lax.ppermute(value, axis, pairs)  6.59 us
    ppermute x7, starting transfers between devices, swap(): return lax.ppermute(value, axis, [(0, 1), (1, 0)])  5.18 us
    ppermute x1, starting transfers between devices, extended(): lax.ppermute(lax.slice_in_dim(block, block.shape[dim] - width, None, axis...  4.87 us
    dot_general x1, matrix products, project(): jnp.dot(columns(rows, 1 - dp_index, rows_half), qkv_other, preferred_elem...  4.19 us
  transfers between devices with their start and end apart: 12, of which 9 were waited for; matrix products, arithmetic and copies ran while one was open for 13% of the time, Pallas kernels for 0%

profile of v10, /device:TPU:0, one launch (start us, length us, event | category | flops | bytes accessed | tf_op | source)
XLA Modules:
  0.0 137.3 jit_solution(18379508851773465931)
XLA Ops:
  0.6 0.0 copy-start.1
  0.7 0.0 copy-start.5
  0.7 1.9 %slice_bitcast_fusion.1 = (bf16[6,16,1024]{2,1,0:T(8,128)(2,1)}, bf16[6,16,1024]{2,1,0:T(8,128)(2,1)}) fusion(bf16[1,8,16,1024]{3,2,1,0:T(8,128)(2,1)} %param.5), kind=kLoop, calls=%fused_computation.59 | loop fusion | bytes 786432 | tf_op jit(solution)/shard_map/slice | solution.py:35
  2.6 4.9 %collective-permute-start = (bf16[6,16,1024]{2,1,0:T(8,128)(2,1)}, bf16[6,16,1024]{2,1,0:T(8,128)(2,1)S(1)}, u32[]{:S(2)}, u32[]{:S(2)}) collective-permute-start(bf16[6,16,1024]{2,1,0:T(8,128)(2,1)} %get-tuple-element.30), channel_id=1, source_target_pairs={{0,2},{2,4},{4,6},{6,8},{8,10},{10,12},{12,14},{1,3},{3,5},{5,7},{... | collective-permute-start | bytes 589832 | tf_op jit(solution)/shard_map/ppermute | solution.py:34
  7.5 1.3 collective-permute-start.1
  8.8 1.4 %pad_maximum_fusion = bf16[640,1024]{1,0:T(8,128)(2,1)S(1)} fusion(bf16[128,1024]{1,0:T(8,128)(2,1)} %bitcast.30, bf16[512,1024]{1,0:T(8,128)(2,1)} %param.9), kind=kLoop, calls=%fused_computation.14 | loop fusion | flops 2621440 | bytes 2621440 | tf_op jit(solution)/shard_map/concatenate | solution.py:345
  10.2 0.1 collective-permute-start.4
  10.3 0.5 collective-permute-start.3
  10.8 0.1 copy.32
  10.8 0.1 copy.31
  10.9 0.1 copy.33
  11.0 0.1 pad_add_fusion
  11.1 0.1 pad_dynamic-slice_fusion
  11.2 0.5 convolution_convert_fusion.1
  11.7 0.2 collective-permute-done
  12.0 4.0 %collective-permute-done.1 = bf16[6,16,1024]{2,1,0:T(8,128)(2,1)S(1)} collective-permute-done((bf16[6,16,1024]{2,1,0:T(8,128)(2,1)}, bf16[6,16,1024]{2,1,0:T(8,128)(2,1)S(1)}, u32[]{:S(2)}, u32[]{:S(2)}) %collective-permute-start.1) | collective-permute-done | bytes 196640 | tf_op jit(solution)/shard_map/ppermute | solution.py:37
  15.9 0.1 pad_maximum_fusion.3
  16.0 0.1 fusion.54
  16.1 0.2 pad_maximum_fusion.4
  16.4 1.2 copy.27
  17.5 1.5 %collective-permute-start.2 = (bf16[20,12,1024]{2,0,1:T(8,128)(2,1)}, bf16[20,12,1024]{2,0,1:T(8,128)(2,1)S(1)}, u32[]{:S(2)}, u32[]{:S(2)}) collective-permute-start(bf16[20,12,1024]{2,0,1:T(8,128)(2,1)} %copy.27), channel_id=1, source_target_pairs={{0,1},{1,0},{2,3},{3,2},{4,5},{5,4},{6,7},{7,6},{8,9},{9,8},{10,11... | collective-permute-start | bytes 1474568 | tf_op jit(solution)/shard_map/ppermute | solution.py:269
  19.1 0.1 eq.28
  19.1 1.0 fusion.32.bias_ref
  20.2 11.5 %collective-permute-done.2 = bf16[20,12,1024]{2,0,1:T(8,128)(2,1)S(1)} collective-permute-done((bf16[20,12,1024]{2,0,1:T(8,128)(2,1)}, bf16[20,12,1024]{2,0,1:T(8,128)(2,1)S(1)}, u32[]{:S(2)}, u32[]{:S(2)}) %collective-permute-start.2) | collective-permute-done | bytes 491552 | tf_op jit(solution)/shard_map/ppermute | solution.py:269
  31.7 0.1 copy.39
  31.8 0.1 copy.40
  32.0 0.6 fusion.7
  32.6 2.2 %fusion.16 = f32[640,3072]{1,0:T(8,128)S(1)} fusion(bf16[512,3072]{1,0:T(8,128)(2,1)S(1)} %copy-done.3, bf16[640,1024]{1,0:T(8,128)(2,1)S(1)} %bitcast.28, s32[]{:T(128)S(6)} %select_n.95), kind=kOutput, calls=%fused_computation.31 | convolution fusion | flops 2013265920 | bytes 11665412 | tf_op jit(solution)/shard_map/dot_general | solution.py:374
  34.8 0.0 collective-permute-done.4
  34.8 1.7 %fusion.11 = bf16[128,512]{1,0:T(8,128)(2,1)S(1)} fusion(bf16[128,1024]{1,0:T(8,128)(2,1)S(1)} %bitcast.32, bf16[640,1024]{1,0:T(8,128)(2,1)} %collective-permute-done.4), kind=kOutput, calls=%fused_computation.20 | convolution fusion | flops 134283264 | bytes 1441792 | tf_op jit(solution)/shard_map/dot_general | solution.py:362
  36.5 0.8 maximum_select_fusion.g_ref
  37.3 4.2 %add_convert_fusion.k_ref.v_ref = bf16[640,3072]{1,0:T(8,128)(2,1)S(1)} fusion(f32[640,3072]{1,0:T(8,128)S(1)} %fusion.16, bf16[512,3072]{1,0:T(8,128)(2,1)} %collective-permute-done.3, bf16[640,1024]{1,0:T(8,128)(2,1)S(1)} %bitcast.29, s32[]{:T(128)S(6)} %select_n.96), kind=kOutput, calls=%fused_computation | convolution fusion | flops 2017198080 | bytes 15597572 | tf_op jit(solution)/shard_map/dot_general | solution.py:377
  41.5 1.9 %copy-done = bf16[640,3072]{1,0:T(8,128)(2,1)} copy-done((bf16[640,3072]{1,0:T(8,128)(2,1)}, bf16[640,3072]{1,0:T(8,128)(2,1)S(1)}, u32[]{:S(2)}) %copy-start) | copy-done | bytes 3932184
  43.5 0.8 slice.105
  44.2 12.0 %block_attention.1 = (bf16[128,1024]{1,0:T(8,128)(2,1)}, bf16[128,1024]{1,0:T(8,128)(2,1)}, f32[2,640,1024]{2,1,0:T(8,128)}, bf16[2,640,1024]{2,1,0:T(8,128)(2,1)}) custom-call(bf16[128,1024]{1,0:T(8,128)(2,1)} %bitcast.35, bf16[640,3072]{1,0:T(8,128)(2,1)} %copy-done, bf16[640,3072]{1,0:T(8,128)(2,1)} %copy-done, ...), custom_call_target="tpu_custom_call" | custom-call | flops 2013265920 | bytes 9240576 | tf_op jit(solution)/shard_map/block_attention/pallas_call | solution.py:106
  56.2 1.8 %fusion.51 = (bf16[2,20,6,1024]{3,2,1,0:T(8,128)(2,1)S(1)}, bf16[2,20,6,1024]{3,2,1,0:T(8,128)(2,1)S(1)}) fusion(bf16[2,20,32,1024]{3,2,1,0:T(8,128)(2,1)} %bitcast.36), kind=kLoop, calls=%fused_computation.93 | loop fusion | bytes 1966080 | tf_op jit(solution)/shard_map/slice | solution.py:192
  58.0 0.5 copy.41
  58.5 0.5 copy.42
  59.0 1.3 pad_maximum_fusion.1
  60.3 1.6 %collective-permute-start.5 = (bf16[2,20,12,1024]{3,0,2,1:T(2,128)(2,1)S(1)}, bf16[2,20,12,1024]{3,0,2,1:T(2,128)(2,1)S(1)}, u32[]{:S(2)}, u32[]{:S(2)}) collective-permute-start(bf16[2,20,12,1024]{3,0,2,1:T(2,128)(2,1)S(1)} %pad_maximum_fusion.1), channel_id=1, source_target_pairs={{0,1},{1,0},{2,3},{3,2},{4,5},{5,4},{6,7},{7,6},{8,9},{9,8},{10,11... | collective-permute-start | bytes 2949128 | tf_op jit(solution)/shard_map/ppermute | solution.py:269
  61.9 1.0 slice.117
  62.9 0.1 collective-permute-start.8
  63.1 0.6 collective-permute-start.10
  63.7 0.7 collective-permute-done.8
  64.4 0.9 collective-permute-start.9
  65.2 24.9 %collective-permute-done.10 = bf16[256,512]{1,0:T(8,128)(2,1)S(1)} collective-permute-done((bf16[256,512]{1,0:T(8,128)(2,1)S(1)}, bf16[256,512]{1,0:T(8,128)(2,1)S(1)}, u32[]{:S(2)}, u32[]{:S(2)}) %collective-permute-start.10) | collective-permute-done | bytes 262176 | tf_op jit(solution)/shard_map/ppermute | solution.py:269
  90.2 2.8 %collective-permute-done.9 = bf16[256,512]{1,0:T(8,128)(2,1)S(1)} collective-permute-done((bf16[256,512]{1,0:T(8,128)(2,1)S(1)}, bf16[256,512]{1,0:T(8,128)(2,1)S(1)}, u32[]{:S(2)}, u32[]{:S(2)}) %collective-permute-start.9) | collective-permute-done | bytes 262176 | tf_op jit(solution)/shard_map/ppermute | solution.py:269
  93.0 1.3 fusion.10
  94.3 9.6 %all-to-all-start = ((bf16[8,64,512]{2,1,0:T(8,128)(2,1)}), bf16[8,64,512]{2,1,0:T(8,128)(2,1)S(1)}, u32[]{:S(2)}, u32[]{:S(2)}) async-start(bf16[8,64,512]{2,1,0:T(8,128)(2,1)} %bitcast.14), calls=%async_computation | async-start | bytes 1048576 | tf_op jit(solution)/shard_map/all_to_all | solution.py:459
  103.9 0.7 fusion.53
  104.6 0.1 copy.43
  104.7 0.1 copy.44
  104.9 2.9 %fusion.49 = (bf16[2,20,16,1024]{3,2,1,0:T(8,128)(2,1)S(1)}, f32[2,20,16,1024]{3,2,1,0:T(8,128)S(1)}) fusion(bf16[2,20,6,1024]{3,2,1,0:T(8,128)(2,1)S(1)} %copy.44, bf16[2,20,6,1024]{3,2,1,0:T(8,128)(2,1)S(1)} %copy.43, f32[2,20,32,1024]{3,2,1,0:T(8,128)} %bitcast.34), kind=kLoop, calls=%fused_computation.92 | loop fusion | flops 3276800 | bytes 7536640 | tf_op jit(solution)/shard_map/convert.9
  107.8 1.0 fusion.52
  108.7 1.3 collective-permute-start.6
  110.0 5.3 %collective-permute-start.7 = (bf16[2,6,16,1024]{3,2,1,0:T(8,128)(2,1)}, bf16[2,6,16,1024]{3,2,1,0:T(8,128)(2,1)}, u32[]{:S(2)}, u32[]{:S(2)}) collective-permute-start(bf16[2,6,16,1024]{3,2,1,0:T(8,128)(2,1)} %get-tuple-element.15), channel_id=1, source_target_pairs={{0,2},{2,4},{4,6},{6,8},{8,10},{10,12},{12,14},{1,3},{3,5},{5,7},{... | collective-permute-start | bytes 1179656 | tf_op jit(solution)/shard_map/ppermute | solution.py:24
  115.3 3.2 %all-to-all-done = bf16[8,64,512]{2,1,0:T(8,128)(2,1)S(1)} async-done(((bf16[8,64,512]{2,1,0:T(8,128)(2,1)}), bf16[8,64,512]{2,1,0:T(8,128)(2,1)S(1)}, u32[]{:S(2)}, u32[]{:S(2)}) %all-to-all-start) | async-done | bytes 524320 | tf_op jit(solution)/shard_map/all_to_all | solution.py:459
  118.5 0.7 convert_reduce_fusion
  119.2 2.1 %collective-permute-done.6 = bf16[2,6,16,1024]{3,2,1,0:T(8,128)(2,1)} collective-permute-done((bf16[2,6,16,1024]{3,2,1,0:T(8,128)(2,1)}, bf16[2,6,16,1024]{3,2,1,0:T(8,128)(2,1)}, u32[]{:S(2)}, u32[]{:S(2)}) %collective-permute-start.6) | collective-permute-done | bytes 393248 | tf_op jit(solution)/shard_map/ppermute | solution.py:24
  121.3 8.5 %collective-permute-done.7 = bf16[2,6,16,1024]{3,2,1,0:T(8,128)(2,1)} collective-permute-done((bf16[2,6,16,1024]{3,2,1,0:T(8,128)(2,1)}, bf16[2,6,16,1024]{3,2,1,0:T(8,128)(2,1)}, u32[]{:S(2)}, u32[]{:S(2)}) %collective-permute-start.7) | collective-permute-done | bytes 393248 | tf_op jit(solution)/shard_map/ppermute | solution.py:24
  129.8 1.3 fusion.13
  131.2 2.2 %convolution_convert_fusion.3 = bf16[128,512]{1,0:T(8,128)(2,1)S(1)} fusion(bf16[512,3072]{1,0:T(8,128)(2,1)S(1)} %copy-done.4, bf16[128,1024]{1,0:T(8,128)(2,1)S(1)} %bitcast.39, bf16[128,1024]{1,0:T(8,128)(2,1)S(1)} %bitcast.37, bf16[128,1024]{1,0:T(8,128)(2,1)} %get-tuple-element.6), kind=kOutput, calls=%fused_computation.19 | convolution fusion | flops 405078016 | bytes 4063232 | tf_op jit(solution)/shard_map/dot_general | solution.py:383
  133.4 3.1 %convolution_convert_fusion.2 = bf16[128,512]{1,0:T(8,128)(2,1)S(1)} fusion(bf16[512,3072]{1,0:T(8,128)(2,1)} %collective-permute-done.3, bf16[128,1024]{1,0:T(8,128)(2,1)S(1)} %bitcast.40, bf16[128,1024]{1,0:T(8,128)(2,1)S(1)} %bitcast.38, bf16[128,1024]{1,0:T(8,128)(2,1)S(1)} %copy-done.8), kind=kOutput, calls=%fused_computation.18 | convolution fusion | flops 405078016 | bytes 4063232 | tf_op jit(solution)/shard_map/dot_general | solution.py:384
  136.5 0.8 maximum_select_fusion.1
  (28 shorter events, 0.2 us)
Async XLA Ops:
  0.6 15.3 %copy-start.2 = (bf16[1,8,16,1024]{3,2,1,0:T(8,128)(2,1)S(1)}, bf16[1,8,16,1024]{3,2,1,0:T(8,128)(2,1)}, u32[]{:S(2)}) copy-start(bf16[1,8,16,1024]{3,2,1,0:T(8,128)(2,1)} %param.5) | copy-start | bytes 786436
  0.6 10.6 %copy-start.1 = (bf16[512,1024]{1,0:T(8,128)(2,1)S(1)}, bf16[512,1024]{1,0:T(8,128)(2,1)}, u32[]{:S(2)}) copy-start(bf16[512,1024]{1,0:T(8,128)(2,1)} %param.9) | copy-start | bytes 3145732
  0.7 10.6 %copy-start.5 = (bf16[1,8,16,1024]{3,2,1,0:T(8,128)(2,1)S(1)}, bf16[1,8,16,1024]{3,2,1,0:T(8,128)(2,1)}, u32[]{:S(2)}) copy-start(bf16[1,8,16,1024]{3,2,1,0:T(8,128)(2,1)} %param.6) | copy-start | bytes 786436
  0.7 10.1 %copy-start.7 = (s32[64,32]{0,1:T(8,128)S(1)}, s32[64,32]{0,1:T(8,128)}, u32[]{:S(2)}) copy-start(s32[64,32]{0,1:T(8,128)} %param.7) | copy-start | bytes 24580
  2.6 9.4 %collective-permute-start = (bf16[6,16,1024]{2,1,0:T(8,128)(2,1)}, bf16[6,16,1024]{2,1,0:T(8,128)(2,1)S(1)}, u32[]{:S(2)}, u32[]{:S(2)}) collective-permute-start(bf16[6,16,1024]{2,1,0:T(8,128)(2,1)} %get-tuple-element.30), channel_id=1, source_target_pairs={{0,2},{2,4},{4,6},{6,8},{8,10},{10,12},{12,14},{1,3},{3,5},{5,7},{... | collective-permute-start | bytes 589832 | tf_op jit(solution)/shard_map/ppermute | solution.py:34
  7.5 8.5 %collective-permute-start.1 = (bf16[6,16,1024]{2,1,0:T(8,128)(2,1)}, bf16[6,16,1024]{2,1,0:T(8,128)(2,1)S(1)}, u32[]{:S(2)}, u32[]{:S(2)}) collective-permute-start(bf16[6,16,1024]{2,1,0:T(8,128)(2,1)} %get-tuple-element.31), channel_id=1, source_target_pairs={{2,0},{4,2},{6,4},{8,6},{10,8},{12,10},{14,12},{3,1},{5,3},{7,5},{... | collective-permute-start | bytes 589832 | tf_op jit(solution)/shard_map/ppermute | solution.py:37
  10.2 24.6 %collective-permute-start.4 = (bf16[640,1024]{1,0:T(8,128)(2,1)S(1)}, bf16[640,1024]{1,0:T(8,128)(2,1)}, u32[]{:S(2)}, u32[]{:S(2)}) collective-permute-start(bf16[640,1024]{1,0:T(8,128)(2,1)S(1)} %pad_maximum_fusion), channel_id=1, source_target_pairs={{0,16},{16,0},{1,17},{17,1},{2,18},{18,2},{3,19},{19,3},{4,20},{20... | collective-permute-start | bytes 3932168 | tf_op jit(solution)/shard_map/ppermute | solution.py:269
  10.3 27.1 %collective-permute-start.3 = (bf16[512,3072]{1,0:T(8,128)(2,1)}, bf16[512,3072]{1,0:T(8,128)(2,1)}, u32[]{:S(2)}, u32[]{:S(2)}) collective-permute-start(bf16[512,3072]{1,0:T(8,128)(2,1)} %param.8), channel_id=1, source_target_pairs={{0,16},{16,0},{1,17},{17,1},{2,18},{18,2},{3,19},{19,3},{4,20},{20... | collective-permute-start | bytes 9437192 | tf_op jit(solution)/shard_map/ppermute | solution.py:269
  17.5 14.1 %collective-permute-start.2 = (bf16[20,12,1024]{2,0,1:T(8,128)(2,1)}, bf16[20,12,1024]{2,0,1:T(8,128)(2,1)S(1)}, u32[]{:S(2)}, u32[]{:S(2)}) collective-permute-start(bf16[20,12,1024]{2,0,1:T(8,128)(2,1)} %copy.27), channel_id=1, source_target_pairs={{0,1},{1,0},{2,3},{3,2},{4,5},{5,4},{6,7},{7,6},{8,9},{9,8},{10,11... | collective-permute-start | bytes 1474568 | tf_op jit(solution)/shard_map/ppermute | solution.py:269
  19.1 13.4 %copy-start.3 = (bf16[512,3072]{1,0:T(8,128)(2,1)S(1)}, bf16[512,3072]{1,0:T(8,128)(2,1)}, u32[]{:S(2)}) copy-start(bf16[512,3072]{1,0:T(8,128)(2,1)} %param.8) | copy-start | bytes 9437188
  41.5 1.9 %copy-start = (bf16[640,3072]{1,0:T(8,128)(2,1)}, bf16[640,3072]{1,0:T(8,128)(2,1)S(1)}, u32[]{:S(2)}) copy-start(bf16[640,3072]{1,0:T(8,128)(2,1)S(1)} %add_convert_fusion.k_ref.v_ref) | copy-start | bytes 11796484
  58.0 4.9 %copy-start.6 = (bf16[128,1024]{1,0:T(8,128)(2,1)S(1)}, bf16[128,1024]{1,0:T(8,128)(2,1)}, u32[]{:S(2)}) copy-start(bf16[128,1024]{1,0:T(8,128)(2,1)} %get-tuple-element.9) | copy-start | bytes 786436
  60.3 43.6 %collective-permute-start.5 = (bf16[2,20,12,1024]{3,0,2,1:T(2,128)(2,1)S(1)}, bf16[2,20,12,1024]{3,0,2,1:T(2,128)(2,1)S(1)}, u32[]{:S(2)}, u32[]{:S(2)}) collective-permute-start(bf16[2,20,12,1024]{3,0,2,1:T(2,128)(2,1)S(1)} %pad_maximum_fusion.1), channel_id=1, source_target_pairs={{0,1},{1,0},{2,3},{3,2},{4,5},{5,4},{6,7},{7,6},{8,9},{9,8},{10,11... | collective-permute-start | bytes 2949128 | tf_op jit(solution)/shard_map/ppermute | solution.py:269
  62.9 1.4 %collective-permute-start.8 = (bf16[128,512]{1,0:T(8,128)(2,1)S(1)}, bf16[128,512]{1,0:T(8,128)(2,1)S(1)}, u32[]{:S(2)}, u32[]{:S(2)}) collective-permute-start(bf16[128,512]{1,0:T(8,128)(2,1)S(1)} %get-tuple-element.29), channel_id=1, source_target_pairs={{0,16},{16,0},{1,17},{17,1},{2,18},{18,2},{3,19},{19,3},{4,20},{20... | collective-permute-start | bytes 393224 | tf_op jit(solution)/shard_map/ppermute | solution.py:269
  63.1 27.1 %collective-permute-start.10 = (bf16[256,512]{1,0:T(8,128)(2,1)S(1)}, bf16[256,512]{1,0:T(8,128)(2,1)S(1)}, u32[]{:S(2)}, u32[]{:S(2)}) collective-permute-start(bf16[256,512]{1,0:T(8,128)(2,1)S(1)} %pad_maximum_fusion.8), channel_id=1, source_target_pairs={{0,1},{1,0},{2,3},{3,2},{4,5},{5,4},{6,7},{7,6},{8,9},{9,8},{10,11... | collective-permute-start | bytes 786440 | tf_op jit(solution)/shard_map/ppermute | solution.py:269
  64.4 28.6 %collective-permute-start.9 = (bf16[256,512]{1,0:T(8,128)(2,1)S(1)}, bf16[256,512]{1,0:T(8,128)(2,1)S(1)}, u32[]{:S(2)}, u32[]{:S(2)}) collective-permute-start(bf16[256,512]{1,0:T(8,128)(2,1)S(1)} %pad_maximum_fusion.7), channel_id=1, source_target_pairs={{0,1},{1,0},{2,3},{3,2},{4,5},{5,4},{6,7},{7,6},{8,9},{9,8},{10,11... | collective-permute-start | bytes 786440 | tf_op jit(solution)/shard_map/ppermute | solution.py:269
  94.3 24.3 %all-to-all-start = ((bf16[8,64,512]{2,1,0:T(8,128)(2,1)}), bf16[8,64,512]{2,1,0:T(8,128)(2,1)S(1)}, u32[]{:S(2)}, u32[]{:S(2)}) async-start(bf16[8,64,512]{2,1,0:T(8,128)(2,1)} %bitcast.14), calls=%async_computation | async-start | bytes 1048576 | tf_op jit(solution)/shard_map/all_to_all | solution.py:459
  108.7 12.6 %collective-permute-start.6 = (bf16[2,6,16,1024]{3,2,1,0:T(8,128)(2,1)}, bf16[2,6,16,1024]{3,2,1,0:T(8,128)(2,1)}, u32[]{:S(2)}, u32[]{:S(2)}) collective-permute-start(bf16[2,6,16,1024]{3,2,1,0:T(8,128)(2,1)} %get-tuple-element.14), channel_id=1, source_target_pairs={{2,0},{4,2},{6,4},{8,6},{10,8},{12,10},{14,12},{3,1},{5,3},{7,5},{... | collective-permute-start | bytes 1179656 | tf_op jit(solution)/shard_map/ppermute | solution.py:24
  110.0 19.8 %collective-permute-start.7 = (bf16[2,6,16,1024]{3,2,1,0:T(8,128)(2,1)}, bf16[2,6,16,1024]{3,2,1,0:T(8,128)(2,1)}, u32[]{:S(2)}, u32[]{:S(2)}) collective-permute-start(bf16[2,6,16,1024]{3,2,1,0:T(8,128)(2,1)} %get-tuple-element.15), channel_id=1, source_target_pairs={{0,2},{2,4},{4,6},{6,8},{8,10},{10,12},{12,14},{1,3},{3,5},{5,7},{... | collective-permute-start | bytes 1179656 | tf_op jit(solution)/shard_map/ppermute | solution.py:24
  118.5 12.7 %copy-start.4 = (bf16[512,3072]{1,0:T(8,128)(2,1)S(1)}, bf16[512,3072]{1,0:T(8,128)(2,1)}, u32[]{:S(2)}) copy-start(bf16[512,3072]{1,0:T(8,128)(2,1)} %param.8) | copy-start | bytes 9437188
  131.2 2.2 %copy-start.8 = (bf16[128,1024]{1,0:T(8,128)(2,1)S(1)}, bf16[128,1024]{1,0:T(8,128)(2,1)}, u32[]{:S(2)}) copy-start(bf16[128,1024]{1,0:T(8,128)(2,1)} %get-tuple-element.6) | copy-start | bytes 786436

commit v11 on v9

--- a/solution.py
+++ b/solution.py
@@ -187,7 +187,7 @@
     return jnp.concatenate(rows, axis=0)
 
 
-def halo_return(ext, ext_low, height, breadth, radius):
+def halo_return(ext, ext_low, height, breadth, radius, extra=None):
     row_slices = {-1: slice(0, radius), 0: slice(radius, radius + height), 1: slice(radius + height, None)}
     col_slices = {-1: slice(0, radius), 0: slice(radius, radius + breadth), 1: slice(radius + breadth, None)}
     own = ext[:, row_slices[0], col_slices[0]]
@@ -199,13 +199,21 @@
                 continue
             spots.append((da, db))
             pieces.append((da, db, ext_low[:, row_slices[da], col_slices[db]]))
-    for (da, db), got in zip(spots, grouped_send(pieces, 2)):
+    if extra is not None:
+        spots.append(None)
+        pieces.append((0, 1, extra))
+    received = grouped_send(pieces, 2)
+    extra_got = received[-1] if extra is not None else None
+    for spot, got in zip(spots, received):
+        if spot is None:
+            continue
+        da, db = spot
         rs = part(height, radius, da, True)
         cs = part(breadth, radius, db, True)
         pad_rows = (rs.start, height - rs.stop)
         pad_cols = (cs.start, breadth - cs.stop)
         own = own + jnp.pad(got.astype(jnp.float32), ((0, 0), pad_rows, pad_cols, (0, 0)))
-    return own
+    return own, extra_got
 
 
 def partner_rows_product(lhs, weights, axis):
@@ -424,18 +432,29 @@
 
     grad_kv_ext = grad_kv.reshape(2, ext_rows, pad_cols, width)[:, :, :ext_cols]
     grad_kv_low_ext = grad_kv_low.reshape(2, ext_rows, pad_cols, width)[:, :, :ext_cols]
-    grad_kv_own = halo_return(grad_kv_ext, grad_kv_low_ext, height, breadth, radius)
-
-    if fast:
+
+    att_fits = (2 * token_count * rows_half) % (2 * height * width) == 0
+    if fast and att_fits:
         own_att = columns(attended, dp_index, rows_half)
         att_from_dp = swap(columns(attended, 1 - dp_index, rows_half), "dp")
         att_dp = jnp.concatenate([own_att, att_from_dp], axis=0)
-        att_group = jnp.concatenate([att_dp, swap(att_dp, "lon")], axis=0)
+        carried = att_dp.reshape(2, height, -1, width)
+        grad_kv_own, att_lon = halo_return(
+            grad_kv_ext, grad_kv_low_ext, height, breadth, radius, carried
+        )
+        att_group = jnp.concatenate([att_dp, att_lon.reshape(att_dp.shape)], axis=0)
     else:
-        att_blocks = attended.reshape(token_count, dp_count, rows_half).transpose(1, 0, 2)
-        att_dp = exchange_blocks(att_blocks, "dp")
-        att_group = gather_members(att_dp, "lon")
-        att_group = att_group.transpose(1, 0, 2, 3).reshape(-1, rows_half)
+        grad_kv_own, _ = halo_return(grad_kv_ext, grad_kv_low_ext, height, breadth, radius)
+        if fast:
+            own_att = columns(attended, dp_index, rows_half)
+            att_from_dp = swap(columns(attended, 1 - dp_index, rows_half), "dp")
+            att_dp = jnp.concatenate([own_att, att_from_dp], axis=0)
+            att_group = jnp.concatenate([att_dp, swap(att_dp, "lon")], axis=0)
+        else:
+            att_blocks = attended.reshape(token_count, dp_count, rows_half).transpose(1, 0, 2)
+            att_dp = exchange_blocks(att_blocks, "dp")
+            att_group = gather_members(att_dp, "lon")
+            att_group = att_group.transpose(1, 0, 2, 3).reshape(-1, rows_half)
 
     device_count = dp_count * lat_count * lon_count
     partial = lax.dot_general(

time: 130 us -> 123 us (0.946)
  waiting for transfers between devices: 34.4 us -> 29.7 us
  other arithmetic: 13.1 us -> 8.53 us
  starting transfers between devices: 35.7 us -> 37.9 us
    ppermute x10, waiting for transfers between devices: 29.7 us -> 23.1 us  [sent_to(): return lax.ppermute(value, ('lat', 'lon'), grid_pairs(delta_lat, delta_lon))]
    slice x6 -> x8, local copies, waits for them, and re-layouts: 6.07 us -> 2.42 us  [grouped_send(): lax.slice_in_dim(got, offset, offset + value.shape[axis], axis=axis)]
    unnamed x25 -> x31, local copies, waits for them, and re-layouts: 2.07 us -> 4.56 us
    concatenate x6, other arithmetic: 3.54 us -> 1.2 us  [grouped_send(): got = sent_to(jnp.concatenate(values, axis=axis), dl, db)]
    all_to_all x1, waiting for transfers between devices: 4.62 us -> 6.54 us  [shards(): lax.all_to_all(partial.astype(jnp.bfloat16), 'lat', 0, 0, tiled=True)]
    slice x0 -> x2, local copies, waits for them, and re-layouts: none -> 1.69 us  [the longest x1 1.53 us: halo_return(): own = ext[:, row_slices[0], col_slices[0]]]
    all_to_all x1, starting transfers between devices: 4.74 us -> 6.33 us  [shards(): lax.all_to_all(partial.astype(jnp.bfloat16), 'lat', 0, 0, tiled=True)]
  transfers between devices with their start and end apart: 16 -> 15, of which waited for: 3 -> 5; matrix products, arithmetic and copies ran while one was open for 31% -> 30% of each run, Pallas kernels for 9% -> 10%
where the time goes in v11:
time: 123 us; the launch traced here: 122 us
  starting transfers between devices  37.9 us (31%)
  waiting for transfers between devices  29.7 us (24%)
  local copies, waits for them, and re-layouts  19 us (15%)
  matrix products  14.1 us (11%)
  Pallas kernels  12 us (10%)
  other arithmetic  8.53 us (7%)
    ppermute x10, starting transfers between devices, sent_to(): return lax.ppermute(value, ('lat', 'lon'), grid_pairs(delta_lat, delta_lon))  30.3 us
    ppermute x10, waiting for transfers between devices, sent_to(): return lax.ppermute(value, ('lat', 'lon'), grid_pairs(delta_lat, delta_lon))  23.1 us
    pallas_call x1, Pallas kernels, block_attention(): pl.pallas_call(kernel, grid=(pairs,), in_specs=[pl.BlockSpec((queries, la...  12 us
    all_to_all x1, waiting for transfers between devices, shards(): lax.all_to_all(partial.astype(jnp.bfloat16), 'lat', 0, 0, tiled=True)  6.54 us
    all_to_all x1, starting transfers between devices, shards(): lax.all_to_all(partial.astype(jnp.bfloat16), 'lat', 0, 0, tiled=True)  6.33 us
    unnamed x31, local copies, waits for them, and re-layouts  4.56 us
    slice x3, local copies, waits for them, and re-layouts, halo_return(): pieces.append((da, db, ext_low[:, row_slices[da], col_slices[db]]))  4.34 us
    dot_general x1, matrix products, project(): jnp.dot(columns(rows, 1 - dp_index, rows_half), qkv_other, preferred_elem...  4.19 us
  transfers between devices with their start and end apart: 15, of which 5 were waited for; matrix products, arithmetic and copies ran while one was open for 30% of the time, Pallas kernels for 10%

profile of v11, /device:TPU:0, one launch (start us, length us, event | category | flops | bytes accessed | tf_op | source)
XLA Modules:
  0.0 122.3 jit_solution(7713791130106859325)
XLA Ops:
  0.7 1.1 fusion.71
  1.8 0.1 pad_maximum_fusion.7
  1.9 3.0 %collective-permute-start.2 = (bf16[8,12,1024]{2,1,0:T(8,128)(2,1)S(1)}, bf16[8,12,1024]{2,1,0:T(8,128)(2,1)S(1)}, u32[]{:S(2)}, u32[]{:S(2)}) collective-permute-start(bf16[8,12,1024]{2,1,0:T(8,128)(2,1)S(1)} %pad_maximum_fusion.7), channel_id=1, source_target_pairs={{0,1},{1,0},{2,3},{3,2},{4,5},{5,4},{6,7},{7,6},{8,9},{9,8},{10,11... | collective-permute-start | bytes 589832 | tf_op jit(solution)/shard_map/ppermute | solution.py:146
  4.9 1.1 fusion.70
  6.1 1.3 %collective-permute-start.3 = (bf16[6,12,1024]{2,1,0:T(8,128)(2,1)S(1)}, bf16[6,12,1024]{2,1,0:T(8,128)(2,1)S(1)}, u32[]{:S(2)}, u32[]{:S(2)}) collective-permute-start(bf16[6,12,1024]{2,1,0:T(8,128)(2,1)S(1)} %pad_maximum_fusion.11), channel_id=1, source_target_pairs={{2,1},{3,0},{4,3},{5,2},{6,5},{7,4},{8,7},{9,6},{10,9},{11,8},{12,... | collective-permute-start | bytes 442376 | tf_op jit(solution)/shard_map/ppermute | solution.py:146
  7.4 5.5 %collective-permute-start = (bf16[6,12,1024]{2,1,0:T(8,128)(2,1)S(1)}, bf16[6,12,1024]{2,1,0:T(8,128)(2,1)S(1)}, u32[]{:S(2)}, u32[]{:S(2)}) collective-permute-start(bf16[6,12,1024]{2,1,0:T(8,128)(2,1)S(1)} %pad_maximum_fusion.10), channel_id=1, source_target_pairs={{0,3},{1,2},{2,5},{3,4},{4,7},{5,6},{6,9},{7,8},{8,11},{9,10},{10,... | collective-permute-start | bytes 442376 | tf_op jit(solution)/shard_map/ppermute | solution.py:146
  12.9 0.7 slice_bitcast_fusion.1
  13.6 4.3 %collective-permute-start.1 = (bf16[6,16,1024]{2,1,0:T(8,128)(2,1)}, bf16[6,16,1024]{2,1,0:T(8,128)(2,1)S(1)}, u32[]{:S(2)}, u32[]{:S(2)}) collective-permute-start(bf16[6,16,1024]{2,1,0:T(8,128)(2,1)} %get-tuple-element.32), channel_id=1, source_target_pairs={{0,2},{1,3},{2,4},{3,5},{4,6},{5,7},{6,8},{7,9},{8,10},{9,11},{10,... | collective-permute-start | bytes 589832 | tf_op jit(solution)/shard_map/ppermute | solution.py:146
  18.2 0.1 copy.40
  18.3 0.1 copy.42
  18.6 0.1 eq.28
  18.6 1.0 fusion.45.bias_ref
  19.7 0.5 convolution_convert_fusion.1
  20.2 0.7 constant_dynamic-slice_fusion.3
  20.9 0.1 pad_maximum_fusion
  21.0 1.6 %collective-permute-start.4 = (bf16[6,16,1024]{2,1,0:T(8,128)(2,1)S(1)}, bf16[6,16,1024]{2,1,0:T(8,128)(2,1)S(1)}, u32[]{:S(2)}, u32[]{:S(2)}) collective-permute-start(bf16[6,16,1024]{2,1,0:T(8,128)(2,1)S(1)} %get-tuple-element.33), channel_id=1, source_target_pairs={{2,0},{3,1},{4,2},{5,3},{6,4},{7,5},{8,6},{9,7},{10,8},{11,9},{12,... | collective-permute-start | bytes 589832 | tf_op jit(solution)/shard_map/ppermute | solution.py:146
  22.6 0.5 collective-permute-start.6
  23.2 0.5 collective-permute-done.1
  23.7 6.7 %collective-permute-done.4 = bf16[6,16,1024]{2,1,0:T(8,128)(2,1)S(1)} collective-permute-done((bf16[6,16,1024]{2,1,0:T(8,128)(2,1)S(1)}, bf16[6,16,1024]{2,1,0:T(8,128)(2,1)S(1)}, u32[]{:S(2)}, u32[]{:S(2)}) %collective-permute-start.4) | collective-permute-done | bytes 196640 | tf_op jit(solution)/shard_map/ppermute | solution.py:146
  30.4 0.7 fusion.12
  31.2 2.2 %fusion.29 = f32[640,3072]{1,0:T(8,128)S(1)} fusion(bf16[512,3072]{1,0:T(8,128)(2,1)S(1)} %copy-done.3, bf16[640,1024]{1,0:T(8,128)(2,1)S(1)} %bitcast.31, s32[]{:T(128)S(6)} %select_n.95), kind=kOutput, calls=%fused_computation.41 | convolution fusion | flops 2013265920 | bytes 11665412 | tf_op jit(solution)/shard_map/dot_general | solution.py:367
  33.4 0.7 constant_dynamic-slice_fusion.2
  34.1 0.7 pad_maximum_fusion.9
  34.9 0.5 collective-permute-start.13
  35.4 0.5 fusion.18
  35.9 0.8 maximum_select_fusion.g_ref
  36.7 4.2 %add_convert_fusion.k_ref.v_ref = bf16[640,3072]{1,0:T(8,128)(2,1)S(1)} fusion(f32[640,3072]{1,0:T(8,128)S(1)} %fusion.29, bf16[512,3072]{1,0:T(8,128)(2,1)} %collective-permute-done.5, bf16[640,1024]{1,0:T(8,128)(2,1)S(1)} %bitcast.32, s32[]{:T(128)S(6)} %select_n.96), kind=kOutput, calls=%fused_computation | convolution fusion | flops 2017198080 | bytes 15597572 | tf_op jit(solution)/shard_map/dot_general | solution.py:370
  40.9 1.9 %copy-done = bf16[640,3072]{1,0:T(8,128)(2,1)} copy-done((bf16[640,3072]{1,0:T(8,128)(2,1)}, bf16[640,3072]{1,0:T(8,128)(2,1)S(1)}, u32[]{:S(2)}) %copy-start) | copy-done | bytes 3932184
  42.8 0.8 slice.181
  43.6 12.0 %block_attention.1 = (bf16[128,1024]{1,0:T(8,128)(2,1)}, bf16[128,1024]{1,0:T(8,128)(2,1)}, f32[2,640,1024]{2,1,0:T(8,128)}, bf16[2,640,1024]{2,1,0:T(8,128)(2,1)}) custom-call(bf16[128,1024]{1,0:T(8,128)(2,1)} %bitcast.40, bf16[640,3072]{1,0:T(8,128)(2,1)} %copy-done, bf16[640,3072]{1,0:T(8,128)(2,1)} %copy-done, ...), custom_call_target="tpu_custom_call" | custom-call | flops 2013265920 | bytes 9240576 | tf_op jit(solution)/shard_map/block_attention/pallas_call | solution.py:106
  55.6 1.3 %fusion.64 = (bf16[2,8,6,1024]{3,2,1,0:T(8,128)(2,1)S(1)}, bf16[2,8,6,1024]{3,2,1,0:T(8,128)(2,1)S(1)}) fusion(bf16[2,20,32,1024]{3,2,1,0:T(8,128)(2,1)} %bitcast.37), kind=kLoop, calls=%fused_computation.109 | loop fusion | bytes 786432 | tf_op jit(solution)/shard_map/slice | solution.py:201
  56.8 1.5 %fusion.63 = (bf16[2,6,6,1024]{3,2,1,0:T(8,128)(2,1)S(1)}, bf16[2,6,6,1024]{3,2,1,0:T(8,128)(2,1)S(1)}, bf16[2,6,6,1024]{3,2,1,0:T(8,128)(2,1)S(1)}, bf16[2,6,6,1024]{3,2,1,0:T(8,128)(2,1)S(1)}) fusion(bf16[2,20,32,1024]{3,2,1,0:T(8,128)(2,1)} %bitcast.38), kind=kLoop, calls=%fused_computation.108 | loop fusion | bytes 1179648 | tf_op jit(solution)/shard_map/slice | solution.py:201
  58.4 0.1 copy.58
  58.7 0.1 copy.61
  58.8 0.1 copy.62
  59.2 1.3 %collective-permute-start.7 = (bf16[2,6,12,1024]{3,1,2,0:T(8,128)(2,1)S(1)}, bf16[2,6,12,1024]{3,1,2,0:T(8,128)(2,1)}, u32[]{:S(2)}, u32[]{:S(2)}) collective-permute-start(bf16[2,6,12,1024]{3,1,2,0:T(8,128)(2,1)S(1)} %pad_maximum_fusion.3), channel_id=1, source_target_pairs={{2,1},{3,0},{4,3},{5,2},{6,5},{7,4},{8,7},{9,6},{10,9},{11,8},{12,... | collective-permute-start | bytes 884744 | tf_op jit(solution)/shard_map/ppermute | solution.py:146
  60.5 0.8 pad_maximum_fusion.4
  61.3 6.2 %collective-permute-start.11 = (bf16[2,6,12,1024]{3,1,2,0:T(8,128)(2,1)}, bf16[2,6,12,1024]{3,1,2,0:T(8,128)(2,1)}, u32[]{:S(2)}, u32[]{:S(2)}) collective-permute-start(bf16[2,6,12,1024]{3,1,2,0:T(8,128)(2,1)} %pad_maximum_fusion.4), channel_id=1, source_target_pairs={{0,3},{1,2},{2,5},{3,4},{4,7},{5,6},{6,9},{7,8},{8,11},{9,10},{10,... | collective-permute-start | bytes 884744 | tf_op jit(solution)/shard_map/ppermute | solution.py:146
  67.5 0.7 copy-done.8
  68.2 0.1 reshape.154
  68.3 0.2 copy.49
  68.5 1.6 %collective-permute-start.10 = (bf16[2,8,20,1024]{3,1,2,0:T(8,128)(2,1)S(1)}, bf16[2,8,20,1024]{3,1,2,0:T(8,128)(2,1)S(1)}, u32[]{:S(2)}, u32[]{:S(2)}) collective-permute-start(bf16[2,8,20,1024]{3,1,2,0:T(8,128)(2,1)S(1)} %pad_maximum_fusion.2), channel_id=1, source_target_pairs={{0,1},{1,0},{2,3},{3,2},{4,5},{5,4},{6,7},{7,6},{8,9},{9,8},{10,11... | collective-permute-start | bytes 1966088 | tf_op jit(solution)/shard_map/ppermute | solution.py:146
  70.1 1.6 %fusion.62 = (bf16[2,6,16,1024]{3,2,1,0:T(8,128)(2,1)S(1)}, bf16[2,6,16,1024]{3,2,1,0:T(8,128)(2,1)S(1)}) fusion(bf16[2,20,32,1024]{3,2,1,0:T(8,128)(2,1)} %bitcast.39), kind=kLoop, calls=%fused_computation.107 | loop fusion | bytes 1572864 | tf_op jit(solution)/shard_map/slice | solution.py:201
  71.7 1.5 %slice.183 = f32[2,8,16,1024]{3,2,1,0:T(8,128)S(1)} slice(f32[2,20,32,1024]{3,2,1,0:T(8,128)} %bitcast.46), slice={[0:2], [6:14], [6:22], [0:1024]} | slice | bytes 2097152 | tf_op jit(solution)/shard_map/slice | solution.py:193
  73.2 0.2 copy.60
  73.4 1.0 copy.65
  74.5 4.4 %collective-permute-start.12 = (bf16[2,6,16,1024]{3,1,2,0:T(8,128)(2,1)}, bf16[2,6,16,1024]{3,1,2,0:T(8,128)(2,1)}, u32[]{:S(2)}, u32[]{:S(2)}) collective-permute-start(bf16[2,6,16,1024]{3,1,2,0:T(8,128)(2,1)} %copy.65), channel_id=1, source_target_pairs={{0,2},{1,3},{2,4},{3,5},{4,6},{5,7},{6,8},{7,9},{8,10},{9,11},{10,... | collective-permute-start | bytes 1179656 | tf_op jit(solution)/shard_map/ppermute | solution.py:146
  78.9 1.3 %collective-permute-start.8 = (bf16[2,6,16,1024]{3,1,2,0:T(8,128)(2,1)S(1)}, bf16[2,6,16,1024]{3,1,2,0:T(8,128)(2,1)}, u32[]{:S(2)}, u32[]{:S(2)}) collective-permute-start(bf16[2,6,16,1024]{3,1,2,0:T(8,128)(2,1)S(1)} %copy.60), channel_id=1, source_target_pairs={{2,0},{3,1},{4,2},{5,3},{6,4},{7,5},{8,6},{9,7},{10,8},{11,9},{12,... | collective-permute-start | bytes 1179656 | tf_op jit(solution)/shard_map/ppermute | solution.py:146
  80.1 1.1 fusion.67
  81.2 0.9 collective-permute-done.11
  82.1 1.0 fusion.68
  83.1 15.1 %collective-permute-done.10 = bf16[2,8,20,1024]{3,1,2,0:T(8,128)(2,1)S(1)} collective-permute-done((bf16[2,8,20,1024]{3,1,2,0:T(8,128)(2,1)S(1)}, bf16[2,8,20,1024]{3,1,2,0:T(8,128)(2,1)S(1)}, u32[]{:S(2)}, u32[]{:S(2)}) %collective-permute-start.10) | collective-permute-done | bytes 655392 | tf_op jit(solution)/shard_map/ppermute | solution.py:146
  98.2 0.2 copy.55
  98.4 0.1 reshape.155
  98.5 2.4 %fusion.17 = bf16[512,512]{1,0:T(8,128)(2,1)} fusion(bf16[256,512]{1,0:T(8,128)(2,1)S(1)} %reshape.155, bf16[128,512]{1,0:T(8,128)(2,1)} %copy-done.8, bf16[128,512]{1,0:T(8,128)(2,1)} %copy-done.6, bf16[256,512]{1,0:T(8,128)(2,1)} %collective-permute-done.13, bf16[128,512]{1,0:T(8,128)(2,1)} %get-tuple-element.28, bf16[128,512]{1,0:T(8,128)(2,1)} %get-tuple-element.26), kind=kOutput, calls=%fused_computation.21 | convolution fusion | flops 272105472 | bytes 1572864 | tf_op jit(solution)/shard_map/dot_general | solution.py:460
  100.9 6.3 %all-to-all-start = ((bf16[8,64,512]{2,1,0:T(8,128)(2,1)}), bf16[8,64,512]{2,1,0:T(8,128)(2,1)S(1)}, u32[]{:S(2)}, u32[]{:S(2)}) async-start(bf16[8,64,512]{2,1,0:T(8,128)(2,1)} %bitcast.41), calls=%async_computation | async-start | bytes 1048576 | tf_op jit(solution)/shard_map/all_to_all | solution.py:463
  107.3 2.3 %fusion.27 = bf16[2,8,16,1024]{3,1,2,0:T(8,128)(2,1)S(1)} fusion(f32[2,8,16,1024]{3,2,1,0:T(8,128)S(1)} %slice.183, bf16[2,6,6,1024]{3,1,2,0:T(8,128)(2,1)S(1)} %get-tuple-element.25, bf16[2,6,16,1024]{3,1,2,0:T(8,128)(2,1)} %collective-permute-done.12, bf16[2,6,6,1024]{3,1,2,0:T(8,128)(2,1)S(1)} %get-tuple-element.24, ...), kind=kLoop, calls=%fused_computation.36 | loop fusion | flops 4456448 | bytes 3342336 | tf_op jit(solution)/shard_map/convert_element_type | solution.py:466
  109.7 0.2 copy.53
  109.9 0.2 copy.54
  110.0 1.2 convolution_convert_fusion.3
  111.2 3.1 %convolution_convert_fusion.2 = bf16[128,512]{1,0:T(8,128)(2,1)S(1)} fusion(bf16[512,3072]{1,0:T(8,128)(2,1)} %collective-permute-done.5, bf16[128,1024]{1,0:T(8,128)(2,1)S(1)} %bitcast.45, bf16[128,1024]{1,0:T(8,128)(2,1)S(1)} %bitcast.43, bf16[128,1024]{1,0:T(8,128)(2,1)S(1)} %copy-done.10), kind=kOutput, calls=%fused_computation.24 | convolution fusion | flops 405078016 | bytes 4063232 | tf_op jit(solution)/shard_map/dot_general | solution.py:377
  114.3 0.8 maximum_select_fusion.1
  115.1 6.5 %all-to-all-done = bf16[8,64,512]{2,1,0:T(8,128)(2,1)S(1)} async-done(((bf16[8,64,512]{2,1,0:T(8,128)(2,1)}), bf16[8,64,512]{2,1,0:T(8,128)(2,1)S(1)}, u32[]{:S(2)}, u32[]{:S(2)}) %all-to-all-start) | async-done | bytes 524320 | tf_op jit(solution)/shard_map/all_to_all | solution.py:463
  121.6 0.7 convert_reduce_fusion
  (55 shorter events, 1.3 us)
Async XLA Ops:
  0.6 12.3 %copy-start.1 = (bf16[1,8,16,1024]{3,2,1,0:T(8,128)(2,1)S(1)}, bf16[1,8,16,1024]{3,2,1,0:T(8,128)(2,1)}, u32[]{:S(2)}) copy-start(bf16[1,8,16,1024]{3,2,1,0:T(8,128)(2,1)} %param.5) | copy-start | bytes 786436
  0.6 17.4 %copy-start.9 = (s32[64,32]{0,1:T(8,128)S(1)}, s32[64,32]{0,1:T(8,128)}, u32[]{:S(2)}) copy-start(s32[64,32]{0,1:T(8,128)} %param.7) | copy-start | bytes 24580
  0.7 19.0 %copy-start.2 = (bf16[512,1024]{1,0:T(8,128)(2,1)S(1)}, bf16[512,1024]{1,0:T(8,128)(2,1)}, u32[]{:S(2)}) copy-start(bf16[512,1024]{1,0:T(8,128)(2,1)} %param.9) | copy-start | bytes 3145732
  0.7 19.0 %copy-start.5 = (bf16[1,8,16,1024]{3,2,1,0:T(8,128)(2,1)S(1)}, bf16[1,8,16,1024]{3,2,1,0:T(8,128)(2,1)}, u32[]{:S(2)}) copy-start(bf16[1,8,16,1024]{3,2,1,0:T(8,128)(2,1)} %param.6) | copy-start | bytes 786436
  1.9 21.3 %collective-permute-start.2 = (bf16[8,12,1024]{2,1,0:T(8,128)(2,1)S(1)}, bf16[8,12,1024]{2,1,0:T(8,128)(2,1)S(1)}, u32[]{:S(2)}, u32[]{:S(2)}) collective-permute-start(bf16[8,12,1024]{2,1,0:T(8,128)(2,1)S(1)} %pad_maximum_fusion.7), channel_id=1, source_target_pairs={{0,1},{1,0},{2,3},{3,2},{4,5},{5,4},{6,7},{7,6},{8,9},{9,8},{10,11... | collective-permute-start | bytes 589832 | tf_op jit(solution)/shard_map/ppermute | solution.py:146
  6.1 14.9 %collective-permute-start.3 = (bf16[6,12,1024]{2,1,0:T(8,128)(2,1)S(1)}, bf16[6,12,1024]{2,1,0:T(8,128)(2,1)S(1)}, u32[]{:S(2)}, u32[]{:S(2)}) collective-permute-start(bf16[6,12,1024]{2,1,0:T(8,128)(2,1)S(1)} %pad_maximum_fusion.11), channel_id=1, source_target_pairs={{2,1},{3,0},{4,3},{5,2},{6,5},{7,4},{8,7},{9,6},{10,9},{11,8},{12,... | collective-permute-start | bytes 442376 | tf_op jit(solution)/shard_map/ppermute | solution.py:146
  7.4 15.1 %collective-permute-start = (bf16[6,12,1024]{2,1,0:T(8,128)(2,1)S(1)}, bf16[6,12,1024]{2,1,0:T(8,128)(2,1)S(1)}, u32[]{:S(2)}, u32[]{:S(2)}) collective-permute-start(bf16[6,12,1024]{2,1,0:T(8,128)(2,1)S(1)} %pad_maximum_fusion.10), channel_id=1, source_target_pairs={{0,3},{1,2},{2,5},{3,4},{4,7},{5,6},{6,9},{7,8},{8,11},{9,10},{10,... | collective-permute-start | bytes 442376 | tf_op jit(solution)/shard_map/ppermute | solution.py:146
  13.6 10.1 %collective-permute-start.1 = (bf16[6,16,1024]{2,1,0:T(8,128)(2,1)}, bf16[6,16,1024]{2,1,0:T(8,128)(2,1)S(1)}, u32[]{:S(2)}, u32[]{:S(2)}) collective-permute-start(bf16[6,16,1024]{2,1,0:T(8,128)(2,1)} %get-tuple-element.32), channel_id=1, source_target_pairs={{0,2},{1,3},{2,4},{3,5},{4,6},{5,7},{6,8},{7,9},{8,10},{9,11},{10,... | collective-permute-start | bytes 589832 | tf_op jit(solution)/shard_map/ppermute | solution.py:146
  18.0 18.7 %collective-permute-start.5 = (bf16[512,3072]{1,0:T(8,128)(2,1)}, bf16[512,3072]{1,0:T(8,128)(2,1)}, u32[]{:S(2)}, u32[]{:S(2)}) collective-permute-start(bf16[512,3072]{1,0:T(8,128)(2,1)} %param.8), channel_id=1, source_target_pairs={{0,16},{16,0},{1,17},{17,1},{2,18},{18,2},{3,19},{19,3},{4,20},{20... | collective-permute-start | bytes 9437192 | tf_op jit(solution)/shard_map/ppermute | solution.py:262
  20.9 10.2 %copy-start.3 = (bf16[512,3072]{1,0:T(8,128)(2,1)S(1)}, bf16[512,3072]{1,0:T(8,128)(2,1)}, u32[]{:S(2)}) copy-start(bf16[512,3072]{1,0:T(8,128)(2,1)} %param.8) | copy-start | bytes 9437188
  21.0 9.4 %collective-permute-start.4 = (bf16[6,16,1024]{2,1,0:T(8,128)(2,1)S(1)}, bf16[6,16,1024]{2,1,0:T(8,128)(2,1)S(1)}, u32[]{:S(2)}, u32[]{:S(2)}) collective-permute-start(bf16[6,16,1024]{2,1,0:T(8,128)(2,1)S(1)} %get-tuple-element.33), channel_id=1, source_target_pairs={{2,0},{3,1},{4,2},{5,3},{6,4},{7,5},{8,6},{9,7},{10,8},{11,9},{12,... | collective-permute-start | bytes 589832 | tf_op jit(solution)/shard_map/ppermute | solution.py:146
  22.6 10.8 %collective-permute-start.6 = (bf16[640,1024]{1,0:T(8,128)(2,1)S(1)}, bf16[640,1024]{1,0:T(8,128)(2,1)S(1)}, u32[]{:S(2)}, u32[]{:S(2)}) collective-permute-start(bf16[640,1024]{1,0:T(8,128)(2,1)S(1)} %pad_maximum_fusion), channel_id=1, source_target_pairs={{0,16},{16,0},{1,17},{17,1},{2,18},{18,2},{3,19},{19,3},{4,20},{20... | collective-permute-start | bytes 3932168 | tf_op jit(solution)/shard_map/ppermute | solution.py:262
  34.9 63.6 %collective-permute-start.13 = (bf16[256,512]{1,0:T(8,128)(2,1)}, bf16[256,512]{1,0:T(8,128)(2,1)}, u32[]{:S(2)}, u32[]{:S(2)}) collective-permute-start(bf16[256,512]{1,0:T(8,128)(2,1)} %pad_maximum_fusion.9), channel_id=1, source_target_pairs={{0,1},{1,0},{2,3},{3,2},{4,5},{5,4},{6,7},{7,6},{8,9},{9,8},{10,11... | collective-permute-start | bytes 786440 | tf_op jit(solution)/shard_map/ppermute | solution.py:262
  40.9 2.0 %copy-start = (bf16[640,3072]{1,0:T(8,128)(2,1)}, bf16[640,3072]{1,0:T(8,128)(2,1)S(1)}, u32[]{:S(2)}) copy-start(bf16[640,3072]{1,0:T(8,128)(2,1)S(1)} %add_convert_fusion.k_ref.v_ref) | copy-start | bytes 11796484
  55.6 2.7 %copy-start.7 = (bf16[128,1024]{1,0:T(8,128)(2,1)S(1)}, bf16[128,1024]{1,0:T(8,128)(2,1)}, u32[]{:S(2)}) copy-start(bf16[128,1024]{1,0:T(8,128)(2,1)} %get-tuple-element.9) | copy-start | bytes 786436
  58.4 9.1 %copy-start.6 = (bf16[128,512]{1,0:T(8,128)(2,1)}, bf16[128,512]{1,0:T(8,128)(2,1)S(1)}, u32[]{:S(2)}) copy-start(bf16[128,512]{1,0:T(8,128)(2,1)S(1)} %get-tuple-element.30) | copy-start | bytes 393220
  58.4 9.1 %collective-permute-start.9 = (bf16[128,512]{1,0:T(8,128)(2,1)S(1)}, bf16[128,512]{1,0:T(8,128)(2,1)S(1)}, u32[]{:S(2)}, u32[]{:S(2)}) collective-permute-start(bf16[128,512]{1,0:T(8,128)(2,1)S(1)} %get-tuple-element.31), channel_id=1, source_target_pairs={{0,16},{16,0},{1,17},{17,1},{2,18},{18,2},{3,19},{19,3},{4,20},{20... | collective-permute-start | bytes 393224 | tf_op jit(solution)/shard_map/ppermute | solution.py:262
  59.2 19.7 %collective-permute-start.7 = (bf16[2,6,12,1024]{3,1,2,0:T(8,128)(2,1)S(1)}, bf16[2,6,12,1024]{3,1,2,0:T(8,128)(2,1)}, u32[]{:S(2)}, u32[]{:S(2)}) collective-permute-start(bf16[2,6,12,1024]{3,1,2,0:T(8,128)(2,1)S(1)} %pad_maximum_fusion.3), channel_id=1, source_target_pairs={{2,1},{3,0},{4,3},{5,2},{6,5},{7,4},{8,7},{9,6},{10,9},{11,8},{12,... | collective-permute-start | bytes 884744 | tf_op jit(solution)/shard_map/ppermute | solution.py:146
  61.3 20.8 %collective-permute-start.11 = (bf16[2,6,12,1024]{3,1,2,0:T(8,128)(2,1)}, bf16[2,6,12,1024]{3,1,2,0:T(8,128)(2,1)}, u32[]{:S(2)}, u32[]{:S(2)}) collective-permute-start(bf16[2,6,12,1024]{3,1,2,0:T(8,128)(2,1)} %pad_maximum_fusion.4), channel_id=1, source_target_pairs={{0,3},{1,2},{2,5},{3,4},{4,7},{5,6},{6,9},{7,8},{8,11},{9,10},{10,... | collective-permute-start | bytes 884744 | tf_op jit(solution)/shard_map/ppermute | solution.py:146
  67.5 0.7 copy-start.8
  68.5 29.7 %collective-permute-start.10 = (bf16[2,8,20,1024]{3,1,2,0:T(8,128)(2,1)S(1)}, bf16[2,8,20,1024]{3,1,2,0:T(8,128)(2,1)S(1)}, u32[]{:S(2)}, u32[]{:S(2)}) collective-permute-start(bf16[2,8,20,1024]{3,1,2,0:T(8,128)(2,1)S(1)} %pad_maximum_fusion.2), channel_id=1, source_target_pairs={{0,1},{1,0},{2,3},{3,2},{4,5},{5,4},{6,7},{7,6},{8,9},{9,8},{10,11... | collective-permute-start | bytes 1966088 | tf_op jit(solution)/shard_map/ppermute | solution.py:146
  74.5 32.8 %collective-permute-start.12 = (bf16[2,6,16,1024]{3,1,2,0:T(8,128)(2,1)}, bf16[2,6,16,1024]{3,1,2,0:T(8,128)(2,1)}, u32[]{:S(2)}, u32[]{:S(2)}) collective-permute-start(bf16[2,6,16,1024]{3,1,2,0:T(8,128)(2,1)} %copy.65), channel_id=1, source_target_pairs={{0,2},{1,3},{2,4},{3,5},{4,6},{5,7},{6,8},{7,9},{8,10},{9,11},{10,... | collective-permute-start | bytes 1179656 | tf_op jit(solution)/shard_map/ppermute | solution.py:146
  78.9 28.4 %collective-permute-start.8 = (bf16[2,6,16,1024]{3,1,2,0:T(8,128)(2,1)S(1)}, bf16[2,6,16,1024]{3,1,2,0:T(8,128)(2,1)}, u32[]{:S(2)}, u32[]{:S(2)}) collective-permute-start(bf16[2,6,16,1024]{3,1,2,0:T(8,128)(2,1)S(1)} %copy.60), channel_id=1, source_target_pairs={{2,0},{3,1},{4,2},{5,3},{6,4},{7,5},{8,6},{9,7},{10,8},{11,9},{12,... | collective-permute-start | bytes 1179656 | tf_op jit(solution)/shard_map/ppermute | solution.py:146
  100.9 20.7 %all-to-all-start = ((bf16[8,64,512]{2,1,0:T(8,128)(2,1)}), bf16[8,64,512]{2,1,0:T(8,128)(2,1)S(1)}, u32[]{:S(2)}, u32[]{:S(2)}) async-start(bf16[8,64,512]{2,1,0:T(8,128)(2,1)} %bitcast.41), calls=%async_computation | async-start | bytes 1048576 | tf_op jit(solution)/shard_map/all_to_all | solution.py:463
  107.3 2.7 %copy-start.4 = (bf16[512,3072]{1,0:T(8,128)(2,1)S(1)}, bf16[512,3072]{1,0:T(8,128)(2,1)}, u32[]{:S(2)}) copy-start(bf16[512,3072]{1,0:T(8,128)(2,1)} %param.8) | copy-start | bytes 9437188
  107.3 2.7 %copy-start.10 = (bf16[128,1024]{1,0:T(8,128)(2,1)S(1)}, bf16[128,1024]{1,0:T(8,128)(2,1)}, u32[]{:S(2)}) copy-start(bf16[128,1024]{1,0:T(8,128)(2,1)} %get-tuple-element.6) | copy-start | bytes 786436

commit v12 on v9

--- a/solution.py
+++ b/solution.py
@@ -89,6 +89,58 @@
     gkv_low_ref[1] = grad_v.astype(gkv_low_ref.dtype)
 
 
+def forward_kernel(q_ref, k_ref, v_ref, bias_ref, att_ref, *, head_dim, scale):
+    q = q_ref[...]
+    k = k_ref[...]
+    v = v_ref[...]
+    bias = bias_ref[...]
+    lanes = q.shape[1]
+    lane = lax.broadcasted_iota(jnp.int32, (1, lanes), 1)
+    zero = jnp.zeros((), q.dtype)
+    sels = [(lane >= j * head_dim) & (lane < (j + 1) * head_dim) for j in range(lanes // head_dim)]
+    q_scaled = (q.astype(jnp.float32) * scale).astype(q.dtype)
+    probs_list = []
+    for sel in sels:
+        qj = jnp.where(sel, q_scaled, zero)
+        masked = lax.dot_general(qj, k, TRANS_B, preferred_element_type=jnp.float32) + bias
+        peak = jnp.max(masked, axis=1, keepdims=True)
+        weights = jnp.exp(masked - peak)
+        probs = weights * (1.0 / jnp.sum(weights, axis=1, keepdims=True))
+        probs_list.append(probs.astype(jnp.bfloat16))
+    v_sel = jnp.concatenate([jnp.where(sel, v, zero) for sel in sels], axis=0)
+    probs_cat = jnp.concatenate(probs_list, axis=1)
+    att = jnp.dot(probs_cat, v_sel, preferred_element_type=jnp.float32)
+    att_ref[...] = att.astype(att_ref.dtype)
+
+
+def block_forward(query, projected, bias, heads):
+    queries, width = query.shape
+    keys = projected.shape[0]
+    head_dim = width // heads
+    lanes = 128
+    pairs = width // lanes
+    kernel = functools.partial(forward_kernel, head_dim=head_dim, scale=head_dim ** (-0.5))
+    cost = pl.CostEstimate(
+        flops=2 * queries * keys * width * 2 * 2,
+        transcendentals=queries * keys * heads,
+        bytes_accessed=2 * (2 * queries * width + 2 * keys * width) + 4 * queries * keys,
+    )
+    return pl.pallas_call(
+        kernel,
+        grid=(pairs,),
+        in_specs=[
+            pl.BlockSpec((queries, lanes), lambda h: (0, h)),
+            pl.BlockSpec((keys, lanes), lambda h: (0, h + pairs)),
+            pl.BlockSpec((keys, lanes), lambda h: (0, h + 2 * pairs)),
+            pl.BlockSpec((queries, keys), lambda h: (0, 0)),
+        ],
+        out_specs=pl.BlockSpec((queries, lanes), lambda h: (0, h)),
+        out_shape=jax.ShapeDtypeStruct((queries, width), jnp.bfloat16),
+        cost_estimate=cost,
+        name="block_forward",
+    )(query, projected, projected, bias)
+
+
 def block_attention(query, projected, grad_attn, bias, heads):
     queries, width = query.shape
     keys = projected.shape[0]
@@ -187,7 +239,7 @@
     return jnp.concatenate(rows, axis=0)
 
 
-def halo_return(ext, ext_low, height, breadth, radius):
+def halo_return(ext, ext_low, height, breadth, radius, extra=None):
     row_slices = {-1: slice(0, radius), 0: slice(radius, radius + height), 1: slice(radius + height, None)}
     col_slices = {-1: slice(0, radius), 0: slice(radius, radius + breadth), 1: slice(radius + breadth, None)}
     own = ext[:, row_slices[0], col_slices[0]]
@@ -199,13 +251,21 @@
                 continue
             spots.append((da, db))
             pieces.append((da, db, ext_low[:, row_slices[da], col_slices[db]]))
-    for (da, db), got in zip(spots, grouped_send(pieces, 2)):
+    if extra is not None:
+        spots.append(None)
+        pieces.append((0, 1, extra))
+    received = grouped_send(pieces, 2)
+    extra_got = received[-1] if extra is not None else None
+    for spot, got in zip(spots, received):
+        if spot is None:
+            continue
+        da, db = spot
         rs = part(height, radius, da, True)
         cs = part(breadth, radius, db, True)
         pad_rows = (rs.start, height - rs.stop)
         pad_cols = (cs.start, breadth - cs.stop)
         own = own + jnp.pad(got.astype(jnp.float32), ((0, 0), pad_rows, pad_cols, (0, 0)))
-    return own
+    return own, extra_got
 
 
 def partner_rows_product(lhs, weights, axis):
@@ -418,14 +478,7 @@
     allowed = inside & ((valid_ext == 1) | itself)
     bias = jnp.where(allowed, 0.0, -jnp.inf).astype(jnp.float32)
 
-    attended, grad_query, grad_kv, grad_kv_low = block_attention(
-        query, projected, grad_attn, bias, HEADS
-    )
-
-    grad_kv_ext = grad_kv.reshape(2, ext_rows, pad_cols, width)[:, :, :ext_cols]
-    grad_kv_low_ext = grad_kv_low.reshape(2, ext_rows, pad_cols, width)[:, :, :ext_cols]
-    grad_kv_own = halo_return(grad_kv_ext, grad_kv_low_ext, height, breadth, radius)
-
+    attended = block_forward(query, projected, bias, HEADS)
     if fast:
         own_att = columns(attended, dp_index, rows_half)
         att_from_dp = swap(columns(attended, 1 - dp_index, rows_half), "dp")
@@ -442,6 +495,15 @@
         att_group, cot_group, (((0,), (0,)), ((), ())), preferred_element_type=jnp.float32
     ) * (1.0 / device_count)
     spread = lax.all_to_all(partial.astype(jnp.bfloat16), "lat", 0, 0, tiled=True)
+    spread, query_after = lax.optimization_barrier((spread, query))
+
+    _, grad_query, grad_kv, grad_kv_low = block_attention(
+        query_after, projected, grad_attn, bias, HEADS
+    )
+    grad_kv_ext = grad_kv.reshape(2, ext_rows, pad_cols, width)[:, :, :ext_cols]
+    grad_kv_low_ext = grad_kv_low.reshape(2, ext_rows, pad_cols, width)[:, :, :ext_cols]
+    grad_kv_own, _ = halo_return(grad_kv_ext, grad_kv_low_ext, height, breadth, radius)
+
     d_w_out = spread.astype(jnp.float32).reshape(lat_count, rows_block, cols_block).sum(axis=0)
 
     grad_kv_own = grad_kv_own.astype(jnp.bfloat16).reshape(2, token_count, width)

time: 130 us -> 148 us (1.14)
  waiting for transfers between devices: 34.4 us -> 53.2 us
  Pallas kernels: 11.9 us -> 20.5 us
  local copies, waits for them, and re-layouts: 19.1 us -> 13.6 us
  other arithmetic: 13.1 us -> 7.98 us
    ppermute x5, waiting for transfers between devices: 0.01 us -> 12.8 us  [swap(): return lax.ppermute(value, axis, [(0, 1), (1, 0)])]
    pallas_call x0 -> x1, Pallas kernels: none -> 8.55 us  [block_forward(): pl.pallas_call(kernel, grid=(pairs,), in_specs=[pl.BlockSpec((queries, la...]
    all_to_all x1, waiting for transfers between devices: 4.62 us -> 12.6 us  [shards(): lax.all_to_all(partial.astype(jnp.bfloat16), 'lat', 0, 0, tiled=True)]
    slice x6, local copies, waits for them, and re-layouts: 6.07 us -> 1.37 us  [grouped_send(): lax.slice_in_dim(got, offset, offset + value.shape[axis], axis=axis)]
    concatenate x6, other arithmetic: 3.54 us -> 0.67 us  [grouped_send(): got = sent_to(jnp.concatenate(values, axis=axis), dl, db)]
    ppermute x10, waiting for transfers between devices: 29.7 us -> 27.8 us  [sent_to(): return lax.ppermute(value, ('lat', 'lon'), grid_pairs(delta_lat, delta_lon))]
  transfers between devices with their start and end apart: 16 -> 16, of which waited for: 3 -> 7; matrix products, arithmetic and copies ran while one was open for 31% -> 10% of each run, Pallas kernels for 9% -> 0%
where the time goes in v12:
time: 148 us; the launch traced here: 147 us
  waiting for transfers between devices  53.2 us (36%)
  starting transfers between devices  36.9 us (25%)
  Pallas kernels  20.5 us (14%)
  local copies, waits for them, and re-layouts  13.6 us (9%)
  matrix products  13.4 us (9%)
  other arithmetic  7.98 us (5%)
    ppermute x10, starting transfers between devices, sent_to(): return lax.ppermute(value, ('lat', 'lon'), grid_pairs(delta_lat, delta_lon))  29.1 us
    ppermute x10, waiting for transfers between devices, sent_to(): return lax.ppermute(value, ('lat', 'lon'), grid_pairs(delta_lat, delta_lon))  27.8 us
    ppermute x5, waiting for transfers between devices, swap(): return lax.ppermute(value, axis, [(0, 1), (1, 0)])  12.8 us
    all_to_all x1, waiting for transfers between devices, shards(): lax.all_to_all(partial.astype(jnp.bfloat16), 'lat', 0, 0, tiled=True)  12.6 us
    pallas_call x1, Pallas kernels, block_attention(): pl.pallas_call(kernel, grid=(pairs,), in_specs=[pl.BlockSpec((queries, la...  12 us
    pallas_call x1, Pallas kernels, block_forward(): pl.pallas_call(kernel, grid=(pairs,), in_specs=[pl.BlockSpec((queries, la...  8.55 us
    all_to_all x1, starting transfers between devices, shards(): lax.all_to_all(partial.astype(jnp.bfloat16), 'lat', 0, 0, tiled=True)  5.94 us
    dot_general x1, matrix products, project(): jnp.dot(columns(rows, 1 - dp_index, rows_half), qkv_other, preferred_elem...  4.66 us
  transfers between devices with their start and end apart: 16, of which 7 were waited for; matrix products, arithmetic and copies ran while one was open for 10% of the time, Pallas kernels for 0%

profile of v12, /device:TPU:0, one launch (start us, length us, event | category | flops | bytes accessed | tf_op | source)
XLA Modules:
  0.0 146.7 jit_solution(17385093989954102407)
XLA Ops:
  0.7 1.2 fusion.70
  1.9 0.1 pad_maximum_fusion.10
  2.0 5.8 %collective-permute-start = (bf16[6,12,1024]{2,1,0:T(8,128)(2,1)S(1)}, bf16[6,12,1024]{2,1,0:T(8,128)(2,1)S(1)}, u32[]{:S(2)}, u32[]{:S(2)}) collective-permute-start(bf16[6,12,1024]{2,1,0:T(8,128)(2,1)S(1)} %pad_maximum_fusion.10), channel_id=1, source_target_pairs={{0,3},{1,2},{2,5},{3,4},{4,7},{5,6},{6,9},{7,8},{8,11},{9,10},{10,... | collective-permute-start | bytes 442376 | tf_op jit(solution)/shard_map/ppermute | solution.py:198
  7.8 0.1 pad_maximum_fusion.11
  7.9 1.3 collective-permute-start.3
  9.2 1.0 fusion.71
  10.2 0.1 pad_maximum_fusion.7
  10.3 0.6 collective-permute-start.2
  10.9 0.8 slice_bitcast_fusion.1
  11.7 6.1 %collective-permute-start.1 = (bf16[6,16,1024]{2,1,0:T(8,128)(2,1)}, bf16[6,16,1024]{2,1,0:T(8,128)(2,1)}, u32[]{:S(2)}, u32[]{:S(2)}) collective-permute-start(bf16[6,16,1024]{2,1,0:T(8,128)(2,1)} %get-tuple-element.34), channel_id=1, source_target_pairs={{0,2},{1,3},{2,4},{3,5},{4,6},{5,7},{6,8},{7,9},{8,10},{9,11},{10,... | collective-permute-start | bytes 589832 | tf_op jit(solution)/shard_map/ppermute | solution.py:198
  17.8 0.1 copy.11
  17.9 0.1 copy.10
  18.0 0.1 copy.12
  18.1 0.1 pad_add_fusion
  18.2 0.1 pad_dynamic-slice_fusion
  18.3 0.1 eq.28
  18.4 1.0 fusion.45.bias_ref
  19.4 0.7 constant_dynamic-slice_fusion.3
  20.1 0.1 pad_maximum_fusion
  20.2 1.6 %collective-permute-start.4 = (bf16[6,16,1024]{2,1,0:T(8,128)(2,1)}, bf16[6,16,1024]{2,1,0:T(8,128)(2,1)S(1)}, u32[]{:S(2)}, u32[]{:S(2)}) collective-permute-start(bf16[6,16,1024]{2,1,0:T(8,128)(2,1)} %get-tuple-element.35), channel_id=1, source_target_pairs={{2,0},{3,1},{4,2},{5,3},{6,4},{7,5},{8,6},{9,7},{10,8},{11,9},{12,... | collective-permute-start | bytes 589832 | tf_op jit(solution)/shard_map/ppermute | solution.py:198
  21.8 0.3 collective-permute-start.8
  22.1 1.0 fusion.73
  23.2 6.4 %collective-permute-done.4 = bf16[6,16,1024]{2,1,0:T(8,128)(2,1)S(1)} collective-permute-done((bf16[6,16,1024]{2,1,0:T(8,128)(2,1)}, bf16[6,16,1024]{2,1,0:T(8,128)(2,1)S(1)}, u32[]{:S(2)}, u32[]{:S(2)}) %collective-permute-start.4) | collective-permute-done | bytes 196640 | tf_op jit(solution)/shard_map/ppermute | solution.py:198
  29.6 1.7 %fusion.12 = bf16[20,32,1024]{2,1,0:T(8,128)(2,1)S(1)} fusion(bf16[6,6,1024]{2,1,0:T(8,128)(2,1)S(1)} %get-tuple-element.47, bf16[6,16,1024]{2,1,0:T(8,128)(2,1)S(1)} %collective-permute-done.4, bf16[6,6,1024]{2,1,0:T(8,128)(2,1)S(1)} %get-tuple-element.46, bf16[8,6,1024]{2,1,0:T(8,128)(2,1)S(1)} %get-tuple-element.37, ...), kind=kLoop, calls=%fused_computation.15 | loop fusion | flops 18350080 | bytes 2457600 | tf_op jit(solution)/shard_map/concatenate | solution.py:239
  31.3 2.2 %fusion.29 = f32[640,3072]{1,0:T(8,128)S(1)} fusion(bf16[512,3072]{1,0:T(8,128)(2,1)S(1)} %copy-done.3, bf16[640,1024]{1,0:T(8,128)(2,1)S(1)} %bitcast.32, s32[]{:T(128)S(6)} %select_n.95), kind=kOutput, calls=%fused_computation.40 | convolution fusion | flops 2013265920 | bytes 11665412 | tf_op jit(solution)/shard_map/dot_general | solution.py:419
  33.6 4.7 %add_convert_fusion.k_ref.v_ref = bf16[640,3072]{1,0:T(8,128)(2,1)S(1)} fusion(f32[640,3072]{1,0:T(8,128)S(1)} %fusion.29, bf16[512,3072]{1,0:T(8,128)(2,1)} %collective-permute-done.5, bf16[640,1024]{1,0:T(8,128)(2,1)S(1)} %bitcast.33, s32[]{:T(128)S(6)} %select_n.96), kind=kOutput, calls=%fused_computation | convolution fusion | flops 2017198080 | bytes 15597572 | tf_op jit(solution)/shard_map/dot_general | solution.py:422
  38.2 1.9 %copy-done = bf16[640,3072]{1,0:T(8,128)(2,1)} copy-done((bf16[640,3072]{1,0:T(8,128)(2,1)}, bf16[640,3072]{1,0:T(8,128)(2,1)S(1)}, u32[]{:S(2)}) %copy-start) | copy-done | bytes 3932184
  40.2 0.8 slice.177
  41.0 8.6 %block_forward.1 = bf16[128,1024]{1,0:T(8,128)(2,1)} custom-call(bf16[128,1024]{1,0:T(8,128)(2,1)} %bitcast.34, bf16[640,3072]{1,0:T(8,128)(2,1)} %copy-done, bf16[640,3072]{1,0:T(8,128)(2,1)} %copy-done, f32[128,640]{1,0:T(8,128)} %fusion.45.bias_ref), custom_call_target="tpu_custom_call" | custom-call | flops 671088640 | bytes 3473408 | tf_op jit(solution)/shard_map/block_forward/pallas_call | solution.py:128
  49.5 1.0 constant_dynamic-slice_fusion.5
  50.5 0.1 collective-permute-start.6
  50.6 0.6 collective-permute-start.9
  51.3 0.6 collective-permute-done.6
  51.9 0.9 collective-permute-start.7
  52.8 7.0 %collective-permute-done.9 = bf16[256,512]{1,0:T(8,128)(2,1)S(1)} collective-permute-done((bf16[256,512]{1,0:T(8,128)(2,1)S(1)}, bf16[256,512]{1,0:T(8,128)(2,1)S(1)}, u32[]{:S(2)}, u32[]{:S(2)}) %collective-permute-start.9) | collective-permute-done | bytes 262176 | tf_op jit(solution)/shard_map/ppermute | solution.py:314
  59.8 5.2 %collective-permute-done.7 = bf16[256,512]{1,0:T(8,128)(2,1)S(1)} collective-permute-done((bf16[256,512]{1,0:T(8,128)(2,1)S(1)}, bf16[256,512]{1,0:T(8,128)(2,1)S(1)}, u32[]{:S(2)}, u32[]{:S(2)}) %collective-permute-start.7) | collective-permute-done | bytes 262176 | tf_op jit(solution)/shard_map/ppermute | solution.py:314
  65.0 1.3 fusion.17
  66.3 5.9 %all-to-all-start = ((bf16[8,64,512]{2,1,0:T(8,128)(2,1)}), bf16[8,64,512]{2,1,0:T(8,128)(2,1)S(1)}, u32[]{:S(2)}, u32[]{:S(2)}) async-start(bf16[8,64,512]{2,1,0:T(8,128)(2,1)} %bitcast.43), calls=%async_computation | async-start | bytes 1048576 | tf_op jit(solution)/shard_map/all_to_all | solution.py:497
  72.2 0.5 convolution_convert_fusion.1
  72.7 0.5 fusion.18
  73.2 0.8 maximum_select_fusion.g_ref
  74.0 12.6 %all-to-all-done = bf16[8,64,512]{2,1,0:T(8,128)(2,1)S(1)} async-done(((bf16[8,64,512]{2,1,0:T(8,128)(2,1)}), bf16[8,64,512]{2,1,0:T(8,128)(2,1)S(1)}, u32[]{:S(2)}, u32[]{:S(2)}) %all-to-all-start) | async-done | bytes 524320 | tf_op jit(solution)/shard_map/all_to_all | solution.py:497
  86.6 12.0 %block_attention.1 = (bf16[128,1024]{1,0:T(8,128)(2,1)}, bf16[128,1024]{1,0:T(8,128)(2,1)}, f32[2,640,1024]{2,1,0:T(8,128)}, bf16[2,640,1024]{2,1,0:T(8,128)(2,1)}) custom-call(bf16[128,1024]{1,0:T(8,128)(2,1)} %bitcast.35, bf16[640,3072]{1,0:T(8,128)(2,1)} %copy-done, bf16[640,3072]{1,0:T(8,128)(2,1)} %copy-done, ...), custom_call_target="tpu_custom_call" | custom-call | flops 2013265920 | bytes 9240576 | tf_op jit(solution)/shard_map/block_attention/pallas_call | solution.py:158
  98.5 1.5 fusion.63
  100.0 1.2 fusion.64
  101.2 0.1 pad_maximum_fusion.3
  101.4 1.3 collective-permute-start.10
  102.7 0.2 pad_maximum_fusion.2
  102.9 0.6 collective-permute-start.12
  103.5 0.1 pad_maximum_fusion.4
  103.6 5.5 %collective-permute-start.13 = (bf16[2,6,12,1024]{3,2,1,0:T(8,128)(2,1)S(1)}, bf16[2,6,12,1024]{3,2,1,0:T(8,128)(2,1)S(1)}, u32[]{:S(2)}, u32[]{:S(2)}) collective-permute-start(bf16[2,6,12,1024]{3,2,1,0:T(8,128)(2,1)S(1)} %pad_maximum_fusion.4), channel_id=1, source_target_pairs={{0,3},{1,2},{2,5},{3,4},{4,7},{5,6},{6,9},{7,8},{8,11},{9,10},{10,... | collective-permute-start | bytes 884744 | tf_op jit(solution)/shard_map/ppermute | solution.py:198
  109.1 1.6 %fusion.62 = (bf16[2,6,16,1024]{3,2,1,0:T(8,128)(2,1)S(1)}, bf16[2,6,16,1024]{3,2,1,0:T(8,128)(2,1)S(1)}) fusion(bf16[2,20,32,1024]{3,2,1,0:T(8,128)(2,1)} %bitcast.42), kind=kLoop, calls=%fused_computation.107 | loop fusion | bytes 1572864 | tf_op jit(solution)/shard_map/slice | solution.py:253
  110.7 1.3 collective-permute-start.11
  112.0 5.1 %collective-permute-start.14 = (bf16[2,6,16,1024]{3,2,1,0:T(8,128)(2,1)S(1)}, bf16[2,6,16,1024]{3,2,1,0:T(8,128)(2,1)S(1)}, u32[]{:S(2)}, u32[]{:S(2)}) collective-permute-start(bf16[2,6,16,1024]{3,2,1,0:T(8,128)(2,1)S(1)} %get-tuple-element.13), channel_id=1, source_target_pairs={{0,2},{1,3},{2,4},{3,5},{4,6},{5,7},{6,8},{7,9},{8,10},{9,11},{10,... | collective-permute-start | bytes 1179656 | tf_op jit(solution)/shard_map/ppermute | solution.py:198
  117.1 0.7 convert_reduce_fusion
  117.8 0.1 fusion.67
  117.9 13.2 %collective-permute-done.13 = bf16[2,6,12,1024]{3,2,1,0:T(8,128)(2,1)S(1)} collective-permute-done((bf16[2,6,12,1024]{3,2,1,0:T(8,128)(2,1)S(1)}, bf16[2,6,12,1024]{3,2,1,0:T(8,128)(2,1)S(1)}, u32[]{:S(2)}, u32[]{:S(2)}) %collective-permute-start.13) | collective-permute-done | bytes 294944 | tf_op jit(solution)/shard_map/ppermute | solution.py:198
  131.1 0.1 fusion.68
  131.2 0.1 fusion.66
  131.3 8.2 %collective-permute-done.14 = bf16[2,6,16,1024]{3,2,1,0:T(8,128)(2,1)S(1)} collective-permute-done((bf16[2,6,16,1024]{3,2,1,0:T(8,128)(2,1)S(1)}, bf16[2,6,16,1024]{3,2,1,0:T(8,128)(2,1)S(1)}, u32[]{:S(2)}, u32[]{:S(2)}) %collective-permute-start.14) | collective-permute-done | bytes 393248 | tf_op jit(solution)/shard_map/ppermute | solution.py:198
  139.5 2.1 %fusion.26 = bf16[2,8,16,1024]{3,2,1,0:T(8,128)(2,1)S(1)} fusion(f32[2,20,32,1024]{3,2,1,0:T(8,128)} %bitcast.48, bf16[2,6,6,1024]{3,2,1,0:T(8,128)(2,1)S(1)} %get-tuple-element.27, bf16[2,6,16,1024]{3,2,1,0:T(8,128)(2,1)S(1)} %collective-permute-done.14, bf16[2,6,6,1024]{3,2,1,0:T(8,128)(2,1)S(1)} %get-tuple-element.26, ...), kind=kLoop, calls=%fused_computation.35 | loop fusion | flops 4456448 | bytes 3342336 | tf_op jit(solution)/shard_map/convert_element_type | solution.py:509
  141.7 1.2 convolution_convert_fusion.3
  142.9 3.1 %convolution_convert_fusion.2 = bf16[128,512]{1,0:T(8,128)(2,1)S(1)} fusion(bf16[512,3072]{1,0:T(8,128)(2,1)} %collective-permute-done.5, bf16[128,1024]{1,0:T(8,128)(2,1)S(1)} %bitcast.47, bf16[128,1024]{1,0:T(8,128)(2,1)S(1)} %bitcast.45, bf16[128,1024]{1,0:T(8,128)(2,1)S(1)} %copy-done.10), kind=kOutput, calls=%fused_computation.24 | convolution fusion | flops 405078016 | bytes 4063232 | tf_op jit(solution)/shard_map/dot_general | solution.py:429
  145.9 0.8 maximum_select_fusion.1
  (43 shorter events, 0.3 us)
Async XLA Ops:
  0.6 10.2 %copy-start.1 = (bf16[1,8,16,1024]{3,2,1,0:T(8,128)(2,1)S(1)}, bf16[1,8,16,1024]{3,2,1,0:T(8,128)(2,1)}, u32[]{:S(2)}) copy-start(bf16[1,8,16,1024]{3,2,1,0:T(8,128)(2,1)} %param.5) | copy-start | bytes 786436
  0.6 17.2 %copy-start.9 = (s32[64,32]{0,1:T(8,128)S(1)}, s32[64,32]{0,1:T(8,128)}, u32[]{:S(2)}) copy-start(s32[64,32]{0,1:T(8,128)} %param.7) | copy-start | bytes 24580
  0.7 18.7 %copy-start.5 = (bf16[1,8,16,1024]{3,2,1,0:T(8,128)(2,1)S(1)}, bf16[1,8,16,1024]{3,2,1,0:T(8,128)(2,1)}, u32[]{:S(2)}) copy-start(bf16[1,8,16,1024]{3,2,1,0:T(8,128)(2,1)} %param.6) | copy-start | bytes 786436
  0.7 19.4 %copy-start.2 = (bf16[512,1024]{1,0:T(8,128)(2,1)S(1)}, bf16[512,1024]{1,0:T(8,128)(2,1)}, u32[]{:S(2)}) copy-start(bf16[512,1024]{1,0:T(8,128)(2,1)} %param.9) | copy-start | bytes 3145732
  2.0 18.2 %collective-permute-start = (bf16[6,12,1024]{2,1,0:T(8,128)(2,1)S(1)}, bf16[6,12,1024]{2,1,0:T(8,128)(2,1)S(1)}, u32[]{:S(2)}, u32[]{:S(2)}) collective-permute-start(bf16[6,12,1024]{2,1,0:T(8,128)(2,1)S(1)} %pad_maximum_fusion.10), channel_id=1, source_target_pairs={{0,3},{1,2},{2,5},{3,4},{4,7},{5,6},{6,9},{7,8},{8,11},{9,10},{10,... | collective-permute-start | bytes 442376 | tf_op jit(solution)/shard_map/ppermute | solution.py:198
  7.9 13.9 %collective-permute-start.3 = (bf16[6,12,1024]{2,1,0:T(8,128)(2,1)S(1)}, bf16[6,12,1024]{2,1,0:T(8,128)(2,1)}, u32[]{:S(2)}, u32[]{:S(2)}) collective-permute-start(bf16[6,12,1024]{2,1,0:T(8,128)(2,1)S(1)} %pad_maximum_fusion.11), channel_id=1, source_target_pairs={{2,1},{3,0},{4,3},{5,2},{6,5},{7,4},{8,7},{9,6},{10,9},{11,8},{12,... | collective-permute-start | bytes 442376 | tf_op jit(solution)/shard_map/ppermute | solution.py:198
  10.3 12.9 %collective-permute-start.2 = (bf16[8,12,1024]{2,1,0:T(8,128)(2,1)S(1)}, bf16[8,12,1024]{2,1,0:T(8,128)(2,1)S(1)}, u32[]{:S(2)}, u32[]{:S(2)}) collective-permute-start(bf16[8,12,1024]{2,1,0:T(8,128)(2,1)S(1)} %pad_maximum_fusion.7), channel_id=1, source_target_pairs={{0,1},{1,0},{2,3},{3,2},{4,5},{5,4},{6,7},{7,6},{8,9},{9,8},{10,11... | collective-permute-start | bytes 589832 | tf_op jit(solution)/shard_map/ppermute | solution.py:198
  10.9 22.7 %collective-permute-start.5 = (bf16[512,3072]{1,0:T(8,128)(2,1)}, bf16[512,3072]{1,0:T(8,128)(2,1)}, u32[]{:S(2)}, u32[]{:S(2)}) collective-permute-start(bf16[512,3072]{1,0:T(8,128)(2,1)} %param.8), channel_id=1, source_target_pairs={{0,16},{16,0},{1,17},{17,1},{2,18},{18,2},{3,19},{19,3},{4,20},{20... | collective-permute-start | bytes 9437192 | tf_op jit(solution)/shard_map/ppermute | solution.py:314
  11.7 11.6 %collective-permute-start.1 = (bf16[6,16,1024]{2,1,0:T(8,128)(2,1)}, bf16[6,16,1024]{2,1,0:T(8,128)(2,1)}, u32[]{:S(2)}, u32[]{:S(2)}) collective-permute-start(bf16[6,16,1024]{2,1,0:T(8,128)(2,1)} %get-tuple-element.34), channel_id=1, source_target_pairs={{0,2},{1,3},{2,4},{3,5},{4,6},{5,7},{6,8},{7,9},{8,10},{9,11},{10,... | collective-permute-start | bytes 589832 | tf_op jit(solution)/shard_map/ppermute | solution.py:198
  20.2 11.1 %copy-start.3 = (bf16[512,3072]{1,0:T(8,128)(2,1)S(1)}, bf16[512,3072]{1,0:T(8,128)(2,1)}, u32[]{:S(2)}) copy-start(bf16[512,3072]{1,0:T(8,128)(2,1)} %param.8) | copy-start | bytes 9437188
  20.2 9.4 %collective-permute-start.4 = (bf16[6,16,1024]{2,1,0:T(8,128)(2,1)}, bf16[6,16,1024]{2,1,0:T(8,128)(2,1)S(1)}, u32[]{:S(2)}, u32[]{:S(2)}) collective-permute-start(bf16[6,16,1024]{2,1,0:T(8,128)(2,1)} %get-tuple-element.35), channel_id=1, source_target_pairs={{2,0},{3,1},{4,2},{5,3},{6,4},{7,5},{8,6},{9,7},{10,8},{11,9},{12,... | collective-permute-start | bytes 589832 | tf_op jit(solution)/shard_map/ppermute | solution.py:198
  21.8 11.7 %collective-permute-start.8 = (bf16[640,1024]{1,0:T(8,128)(2,1)S(1)}, bf16[640,1024]{1,0:T(8,128)(2,1)S(1)}, u32[]{:S(2)}, u32[]{:S(2)}) collective-permute-start(bf16[640,1024]{1,0:T(8,128)(2,1)S(1)} %pad_maximum_fusion), channel_id=1, source_target_pairs={{0,16},{16,0},{1,17},{17,1},{2,18},{18,2},{3,19},{19,3},{4,20},{20... | collective-permute-start | bytes 3932168 | tf_op jit(solution)/shard_map/ppermute | solution.py:314
  33.5 4.7 %copy-start.6 = (bf16[640,1024]{1,0:T(8,128)(2,1)}, bf16[640,1024]{1,0:T(8,128)(2,1)S(1)}, u32[]{:S(2)}) copy-start(bf16[640,1024]{1,0:T(8,128)(2,1)S(1)} %collective-permute-done.8) | copy-start | bytes 3932164
  38.2 1.9 %copy-start = (bf16[640,3072]{1,0:T(8,128)(2,1)}, bf16[640,3072]{1,0:T(8,128)(2,1)S(1)}, u32[]{:S(2)}) copy-start(bf16[640,3072]{1,0:T(8,128)(2,1)S(1)} %add_convert_fusion.k_ref.v_ref) | copy-start | bytes 11796484
  40.9 9.6 %slice-start = ((bf16[640,1024]{1,0:T(8,128)(2,1)}), bf16[128,1024]{1,0:T(8,128)(2,1)S(1)}, s32[]{:S(2)}) async-start(bf16[640,1024]{1,0:T(8,128)(2,1)} %copy-done.6), calls=%async_computation.1 | async-start | bytes 524288 | tf_op jit(solution)/shard_map/slice | solution.py:392
  41.0 24.1 %copy-start.8 = (bf16[128,512]{1,0:T(8,128)(2,1)S(1)}, bf16[128,512]{1,0:T(8,128)(2,1)}, u32[]{:S(2)}) copy-start(bf16[128,512]{1,0:T(8,128)(2,1)} %get-tuple-element.28) | copy-start | bytes 393220
  50.5 1.4 collective-permute-start.6
  50.6 9.2 %collective-permute-start.9 = (bf16[256,512]{1,0:T(8,128)(2,1)S(1)}, bf16[256,512]{1,0:T(8,128)(2,1)S(1)}, u32[]{:S(2)}, u32[]{:S(2)}) collective-permute-start(bf16[256,512]{1,0:T(8,128)(2,1)S(1)} %pad_maximum_fusion.9), channel_id=1, source_target_pairs={{0,1},{1,0},{2,3},{3,2},{4,5},{5,4},{6,7},{7,6},{8,9},{9,8},{10,11... | collective-permute-start | bytes 786440 | tf_op jit(solution)/shard_map/ppermute | solution.py:314
  51.9 13.1 %collective-permute-start.7 = (bf16[256,512]{1,0:T(8,128)(2,1)S(1)}, bf16[256,512]{1,0:T(8,128)(2,1)S(1)}, u32[]{:S(2)}, u32[]{:S(2)}) collective-permute-start(bf16[256,512]{1,0:T(8,128)(2,1)S(1)} %pad_maximum_fusion.8), channel_id=1, source_target_pairs={{0,1},{1,0},{2,3},{3,2},{4,5},{5,4},{6,7},{7,6},{8,9},{9,8},{10,11... | collective-permute-start | bytes 786440 | tf_op jit(solution)/shard_map/ppermute | solution.py:314
  65.0 7.7 %copy-start.7 = (bf16[640,1024]{1,0:T(8,128)(2,1)S(1)}, bf16[640,1024]{1,0:T(8,128)(2,1)}, u32[]{:S(2)}) copy-start(bf16[640,1024]{1,0:T(8,128)(2,1)} %copy-done.6) | copy-start | bytes 3932164
  66.3 20.3 %all-to-all-start = ((bf16[8,64,512]{2,1,0:T(8,128)(2,1)}), bf16[8,64,512]{2,1,0:T(8,128)(2,1)S(1)}, u32[]{:S(2)}, u32[]{:S(2)}) async-start(bf16[8,64,512]{2,1,0:T(8,128)(2,1)} %bitcast.43), calls=%async_computation | async-start | bytes 1048576 | tf_op jit(solution)/shard_map/all_to_all | solution.py:497
  101.4 16.4 %collective-permute-start.10 = (bf16[2,6,12,1024]{3,2,1,0:T(8,128)(2,1)S(1)}, bf16[2,6,12,1024]{3,2,1,0:T(8,128)(2,1)S(1)}, u32[]{:S(2)}, u32[]{:S(2)}) collective-permute-start(bf16[2,6,12,1024]{3,2,1,0:T(8,128)(2,1)S(1)} %pad_maximum_fusion.3), channel_id=1, source_target_pairs={{2,1},{3,0},{4,3},{5,2},{6,5},{7,4},{8,7},{9,6},{10,9},{11,8},{12,... | collective-permute-start | bytes 884744 | tf_op jit(solution)/shard_map/ppermute | solution.py:198
  102.9 28.3 %collective-permute-start.12 = (bf16[2,8,12,1024]{3,2,1,0:T(8,128)(2,1)S(1)}, bf16[2,8,12,1024]{3,2,1,0:T(8,128)(2,1)S(1)}, u32[]{:S(2)}, u32[]{:S(2)}) collective-permute-start(bf16[2,8,12,1024]{3,2,1,0:T(8,128)(2,1)S(1)} %pad_maximum_fusion.2), channel_id=1, source_target_pairs={{0,1},{1,0},{2,3},{3,2},{4,5},{5,4},{6,7},{7,6},{8,9},{9,8},{10,11... | collective-permute-start | bytes 1179656 | tf_op jit(solution)/shard_map/ppermute | solution.py:198
  103.6 27.5 %collective-permute-start.13 = (bf16[2,6,12,1024]{3,2,1,0:T(8,128)(2,1)S(1)}, bf16[2,6,12,1024]{3,2,1,0:T(8,128)(2,1)S(1)}, u32[]{:S(2)}, u32[]{:S(2)}) collective-permute-start(bf16[2,6,12,1024]{3,2,1,0:T(8,128)(2,1)S(1)} %pad_maximum_fusion.4), channel_id=1, source_target_pairs={{0,3},{1,2},{2,5},{3,4},{4,7},{5,6},{6,9},{7,8},{8,11},{9,10},{10,... | collective-permute-start | bytes 884744 | tf_op jit(solution)/shard_map/ppermute | solution.py:198
  110.7 20.6 %collective-permute-start.11 = (bf16[2,6,16,1024]{3,2,1,0:T(8,128)(2,1)S(1)}, bf16[2,6,16,1024]{3,2,1,0:T(8,128)(2,1)S(1)}, u32[]{:S(2)}, u32[]{:S(2)}) collective-permute-start(bf16[2,6,16,1024]{3,2,1,0:T(8,128)(2,1)S(1)} %get-tuple-element.12), channel_id=1, source_target_pairs={{2,0},{3,1},{4,2},{5,3},{6,4},{7,5},{8,6},{9,7},{10,8},{11,9},{12,... | collective-permute-start | bytes 1179656 | tf_op jit(solution)/shard_map/ppermute | solution.py:198
  112.0 27.5 %collective-permute-start.14 = (bf16[2,6,16,1024]{3,2,1,0:T(8,128)(2,1)S(1)}, bf16[2,6,16,1024]{3,2,1,0:T(8,128)(2,1)S(1)}, u32[]{:S(2)}, u32[]{:S(2)}) collective-permute-start(bf16[2,6,16,1024]{3,2,1,0:T(8,128)(2,1)S(1)} %get-tuple-element.13), channel_id=1, source_target_pairs={{0,2},{1,3},{2,4},{3,5},{4,6},{5,7},{6,8},{7,9},{8,10},{9,11},{10,... | collective-permute-start | bytes 1179656 | tf_op jit(solution)/shard_map/ppermute | solution.py:198
  131.3 10.4 %copy-start.4 = (bf16[512,3072]{1,0:T(8,128)(2,1)S(1)}, bf16[512,3072]{1,0:T(8,128)(2,1)}, u32[]{:S(2)}) copy-start(bf16[512,3072]{1,0:T(8,128)(2,1)} %param.8) | copy-start | bytes 9437188
  131.3 10.4 %copy-start.10 = (bf16[128,1024]{1,0:T(8,128)(2,1)S(1)}, bf16[128,1024]{1,0:T(8,128)(2,1)}, u32[]{:S(2)}) copy-start(bf16[128,1024]{1,0:T(8,128)(2,1)} %get-tuple-element.8) | copy-start | bytes 786436

commit v13 on v11

--- a/solution.py
+++ b/solution.py
@@ -342,12 +342,11 @@
             [columns(flat_grad, 1 - lon_index, cols_block), columns(cot_dp, 1 - lon_index, cols_block)],
             axis=0,
         )
-        cot_lon = swap(cot_send, "lon")
+        cot_later = cot_send
         cot_group = jnp.concatenate(
             [
                 columns(flat_grad, lon_index, cols_block),
                 columns(cot_dp, lon_index, cols_block),
-                cot_lon,
             ],
             axis=0,
         )
@@ -456,6 +455,10 @@
             att_group = gather_members(att_dp, "lon")
             att_group = att_group.transpose(1, 0, 2, 3).reshape(-1, rows_half)
 
+    if fast:
+        cot_later, _ = lax.optimization_barrier((cot_later, attended))
+        cot_group = jnp.concatenate([cot_group, swap(cot_later, "lon")], axis=0)
+
     device_count = dp_count * lat_count * lon_count
     partial = lax.dot_general(
         att_group, cot_group, (((0,), (0,)), ((), ())), preferred_element_type=jnp.float32

time: 123 us -> 125 us (1.016)
  waiting for transfers between devices: 29.7 us -> 33.3 us
  starting transfers between devices: 37.9 us -> 35.8 us
    ppermute x4, waiting for transfers between devices: 0.01 us -> 5.39 us  [swap(): return lax.ppermute(value, axis, [(0, 1), (1, 0)])]
    all_to_all x1, starting transfers between devices: 6.33 us -> 4.17 us  [shards(): lax.all_to_all(partial.astype(jnp.bfloat16), 'lat', 0, 0, tiled=True)]
    ppermute x10, waiting for transfers between devices: 23.1 us -> 21.3 us  [sent_to(): return lax.ppermute(value, ('lat', 'lon'), grid_pairs(delta_lat, delta_lon))]
  transfers between devices with their start and end apart: 15 -> 15, of which waited for: 5 -> 6; matrix products, arithmetic and copies ran while one was open for 30% -> 24% of each run, Pallas kernels for 10% -> 0%
where the time goes in v13:
time: 125 us; the launch traced here: 124 us
  starting transfers between devices  35.8 us (29%)
  waiting for transfers between devices  33.3 us (27%)
  local copies, waits for them, and re-layouts  19 us (15%)
  matrix products  14.1 us (11%)
  Pallas kernels  12 us (10%)
  other arithmetic  8.53 us (7%)
    ppermute x10, starting transfers between devices, sent_to(): return lax.ppermute(value, ('lat', 'lon'), grid_pairs(delta_lat, delta_lon))  29.4 us
    ppermute x10, waiting for transfers between devices, sent_to(): return lax.ppermute(value, ('lat', 'lon'), grid_pairs(delta_lat, delta_lon))  21.3 us
    pallas_call x1, Pallas kernels, block_attention(): pl.pallas_call(kernel, grid=(pairs,), in_specs=[pl.BlockSpec((queries, la...  12 us
    all_to_all x1, waiting for transfers between devices, shards(): lax.all_to_all(partial.astype(jnp.bfloat16), 'lat', 0, 0, tiled=True)  6.58 us
    ppermute x4, waiting for transfers between devices, swap(): return lax.ppermute(value, axis, [(0, 1), (1, 0)])  5.39 us
    unnamed x31, local copies, waits for them, and re-layouts  4.56 us
    slice x3, local copies, waits for them, and re-layouts, halo_return(): pieces.append((da, db, ext_low[:, row_slices[da], col_slices[db]]))  4.34 us
    dot_general x1, matrix products, project(): jnp.dot(columns(rows, 1 - dp_index, rows_half), qkv_other, preferred_elem...  4.19 us
  transfers between devices with their start and end apart: 15, of which 6 were waited for; matrix products, arithmetic and copies ran while one was open for 24% of the time, Pallas kernels for 0%

profile of v13, /device:TPU:0, one launch (start us, length us, event | category | flops | bytes accessed | tf_op | source)
XLA Modules:
  0.0 123.8 jit_solution(2312381314189934001)
XLA Ops:
  0.7 1.1 fusion.71
  1.8 0.1 pad_maximum_fusion.7
  1.9 3.0 %collective-permute-start.2 = (bf16[8,12,1024]{2,1,0:T(8,128)(2,1)S(1)}, bf16[8,12,1024]{2,1,0:T(8,128)(2,1)S(1)}, u32[]{:S(2)}, u32[]{:S(2)}) collective-permute-start(bf16[8,12,1024]{2,1,0:T(8,128)(2,1)S(1)} %pad_maximum_fusion.7), channel_id=1, source_target_pairs={{0,1},{1,0},{2,3},{3,2},{4,5},{5,4},{6,7},{7,6},{8,9},{9,8},{10,11... | collective-permute-start | bytes 589832 | tf_op jit(solution)/shard_map/ppermute | solution.py:146
  4.9 1.1 fusion.70
  6.1 1.3 %collective-permute-start.3 = (bf16[6,12,1024]{2,1,0:T(8,128)(2,1)S(1)}, bf16[6,12,1024]{2,1,0:T(8,128)(2,1)S(1)}, u32[]{:S(2)}, u32[]{:S(2)}) collective-permute-start(bf16[6,12,1024]{2,1,0:T(8,128)(2,1)S(1)} %pad_maximum_fusion.11), channel_id=1, source_target_pairs={{2,1},{3,0},{4,3},{5,2},{6,5},{7,4},{8,7},{9,6},{10,9},{11,8},{12,... | collective-permute-start | bytes 442376 | tf_op jit(solution)/shard_map/ppermute | solution.py:146
  7.4 5.5 %collective-permute-start = (bf16[6,12,1024]{2,1,0:T(8,128)(2,1)S(1)}, bf16[6,12,1024]{2,1,0:T(8,128)(2,1)S(1)}, u32[]{:S(2)}, u32[]{:S(2)}) collective-permute-start(bf16[6,12,1024]{2,1,0:T(8,128)(2,1)S(1)} %pad_maximum_fusion.10), channel_id=1, source_target_pairs={{0,3},{1,2},{2,5},{3,4},{4,7},{5,6},{6,9},{7,8},{8,11},{9,10},{10,... | collective-permute-start | bytes 442376 | tf_op jit(solution)/shard_map/ppermute | solution.py:146
  12.9 0.7 slice_bitcast_fusion.1
  13.6 4.3 %collective-permute-start.1 = (bf16[6,16,1024]{2,1,0:T(8,128)(2,1)}, bf16[6,16,1024]{2,1,0:T(8,128)(2,1)S(1)}, u32[]{:S(2)}, u32[]{:S(2)}) collective-permute-start(bf16[6,16,1024]{2,1,0:T(8,128)(2,1)} %get-tuple-element.34), channel_id=1, source_target_pairs={{0,2},{1,3},{2,4},{3,5},{4,6},{5,7},{6,8},{7,9},{8,10},{9,11},{10,... | collective-permute-start | bytes 589832 | tf_op jit(solution)/shard_map/ppermute | solution.py:146
  18.2 0.1 copy.40
  18.3 0.1 copy.42
  18.6 0.1 eq.28
  18.6 1.0 fusion.45.bias_ref
  19.7 0.5 convolution_convert_fusion.1
  20.2 0.7 constant_dynamic-slice_fusion.3
  20.8 0.1 pad_maximum_fusion
  21.0 1.6 %collective-permute-start.4 = (bf16[6,16,1024]{2,1,0:T(8,128)(2,1)S(1)}, bf16[6,16,1024]{2,1,0:T(8,128)(2,1)S(1)}, u32[]{:S(2)}, u32[]{:S(2)}) collective-permute-start(bf16[6,16,1024]{2,1,0:T(8,128)(2,1)S(1)} %get-tuple-element.35), channel_id=1, source_target_pairs={{2,0},{3,1},{4,2},{5,3},{6,4},{7,5},{8,6},{9,7},{10,8},{11,9},{12,... | collective-permute-start | bytes 589832 | tf_op jit(solution)/shard_map/ppermute | solution.py:146
  22.6 0.5 collective-permute-start.6
  23.2 0.5 collective-permute-done.1
  23.7 6.7 %collective-permute-done.4 = bf16[6,16,1024]{2,1,0:T(8,128)(2,1)S(1)} collective-permute-done((bf16[6,16,1024]{2,1,0:T(8,128)(2,1)S(1)}, bf16[6,16,1024]{2,1,0:T(8,128)(2,1)S(1)}, u32[]{:S(2)}, u32[]{:S(2)}) %collective-permute-start.4) | collective-permute-done | bytes 196640 | tf_op jit(solution)/shard_map/ppermute | solution.py:146
  30.4 0.7 fusion.12
  31.1 2.2 %fusion.29 = f32[640,3072]{1,0:T(8,128)S(1)} fusion(bf16[512,3072]{1,0:T(8,128)(2,1)S(1)} %copy-done.3, bf16[640,1024]{1,0:T(8,128)(2,1)S(1)} %bitcast.31, s32[]{:T(128)S(6)} %select_n.95), kind=kOutput, calls=%fused_computation.41 | convolution fusion | flops 2013265920 | bytes 11665412 | tf_op jit(solution)/shard_map/dot_general | solution.py:366
  33.4 0.7 constant_dynamic-slice_fusion.2
  34.1 0.7 pad_maximum_fusion.9
  34.8 0.5 fusion.18
  35.3 0.8 maximum_select_fusion.g_ref
  36.1 4.2 %add_convert_fusion.k_ref.v_ref = bf16[640,3072]{1,0:T(8,128)(2,1)S(1)} fusion(f32[640,3072]{1,0:T(8,128)S(1)} %fusion.29, bf16[512,3072]{1,0:T(8,128)(2,1)} %collective-permute-done.5, bf16[640,1024]{1,0:T(8,128)(2,1)S(1)} %bitcast.32, s32[]{:T(128)S(6)} %select_n.96), kind=kOutput, calls=%fused_computation | convolution fusion | flops 2017198080 | bytes 15597572 | tf_op jit(solution)/shard_map/dot_general | solution.py:369
  40.3 1.9 %copy-done = bf16[640,3072]{1,0:T(8,128)(2,1)} copy-done((bf16[640,3072]{1,0:T(8,128)(2,1)}, bf16[640,3072]{1,0:T(8,128)(2,1)S(1)}, u32[]{:S(2)}) %copy-start) | copy-done | bytes 3932184
  42.3 0.8 slice.181
  43.1 12.0 %block_attention.1 = (bf16[128,1024]{1,0:T(8,128)(2,1)}, bf16[128,1024]{1,0:T(8,128)(2,1)}, f32[2,640,1024]{2,1,0:T(8,128)}, bf16[2,640,1024]{2,1,0:T(8,128)(2,1)}) custom-call(bf16[128,1024]{1,0:T(8,128)(2,1)} %bitcast.40, bf16[640,3072]{1,0:T(8,128)(2,1)} %copy-done, bf16[640,3072]{1,0:T(8,128)(2,1)} %copy-done, ...), custom_call_target="tpu_custom_call" | custom-call | flops 2013265920 | bytes 9240576 | tf_op jit(solution)/shard_map/block_attention/pallas_call | solution.py:106
  55.0 1.3 %fusion.64 = (bf16[2,8,6,1024]{3,2,1,0:T(8,128)(2,1)S(1)}, bf16[2,8,6,1024]{3,2,1,0:T(8,128)(2,1)S(1)}) fusion(bf16[2,20,32,1024]{3,2,1,0:T(8,128)(2,1)} %bitcast.37), kind=kLoop, calls=%fused_computation.109 | loop fusion | bytes 786432 | tf_op jit(solution)/shard_map/slice | solution.py:201
  56.3 1.5 %fusion.63 = (bf16[2,6,6,1024]{3,2,1,0:T(8,128)(2,1)S(1)}, bf16[2,6,6,1024]{3,2,1,0:T(8,128)(2,1)S(1)}, bf16[2,6,6,1024]{3,2,1,0:T(8,128)(2,1)S(1)}, bf16[2,6,6,1024]{3,2,1,0:T(8,128)(2,1)S(1)}) fusion(bf16[2,20,32,1024]{3,2,1,0:T(8,128)(2,1)} %bitcast.38), kind=kLoop, calls=%fused_computation.108 | loop fusion | bytes 1179648 | tf_op jit(solution)/shard_map/slice | solution.py:201
  58.2 0.1 copy.61
  58.3 0.1 copy.62
  58.6 1.3 %collective-permute-start.7 = (bf16[2,6,12,1024]{3,1,2,0:T(8,128)(2,1)S(1)}, bf16[2,6,12,1024]{3,1,2,0:T(8,128)(2,1)}, u32[]{:S(2)}, u32[]{:S(2)}) collective-permute-start(bf16[2,6,12,1024]{3,1,2,0:T(8,128)(2,1)S(1)} %pad_maximum_fusion.3), channel_id=1, source_target_pairs={{2,1},{3,0},{4,3},{5,2},{6,5},{7,4},{8,7},{9,6},{10,9},{11,8},{12,... | collective-permute-start | bytes 884744 | tf_op jit(solution)/shard_map/ppermute | solution.py:146
  59.9 0.8 pad_maximum_fusion.4
  60.7 6.2 %collective-permute-start.11 = (bf16[2,6,12,1024]{3,1,2,0:T(8,128)(2,1)}, bf16[2,6,12,1024]{3,1,2,0:T(8,128)(2,1)}, u32[]{:S(2)}, u32[]{:S(2)}) collective-permute-start(bf16[2,6,12,1024]{3,1,2,0:T(8,128)(2,1)} %pad_maximum_fusion.4), channel_id=1, source_target_pairs={{0,3},{1,2},{2,5},{3,4},{4,7},{5,6},{6,9},{7,8},{8,11},{9,10},{10,... | collective-permute-start | bytes 884744 | tf_op jit(solution)/shard_map/ppermute | solution.py:146
  67.0 0.7 copy-done.8
  67.6 0.1 reshape.154
  67.7 0.2 copy.49
  68.0 0.6 collective-permute-start.10
  68.6 1.6 %fusion.62 = (bf16[2,6,16,1024]{3,2,1,0:T(8,128)(2,1)S(1)}, bf16[2,6,16,1024]{3,2,1,0:T(8,128)(2,1)S(1)}) fusion(bf16[2,20,32,1024]{3,2,1,0:T(8,128)(2,1)} %bitcast.39), kind=kLoop, calls=%fused_computation.107 | loop fusion | bytes 1572864 | tf_op jit(solution)/shard_map/slice | solution.py:201
  70.2 1.5 %slice.183 = f32[2,8,16,1024]{3,2,1,0:T(8,128)S(1)} slice(f32[2,20,32,1024]{3,2,1,0:T(8,128)} %bitcast.46), slice={[0:2], [6:14], [6:22], [0:1024]} | slice | bytes 2097152 | tf_op jit(solution)/shard_map/slice | solution.py:193
  71.7 1.6 %collective-permute-start.13 = (bf16[256,512]{1,0:T(8,128)(2,1)}, bf16[256,512]{1,0:T(8,128)(2,1)}, u32[]{:S(2)}, u32[]{:S(2)}) collective-permute-start(bf16[256,512]{1,0:T(8,128)(2,1)} %pad_maximum_fusion.9), channel_id=1, source_target_pairs={{0,1},{1,0},{2,3},{3,2},{4,5},{5,4},{6,7},{7,6},{8,9},{9,8},{10,11... | collective-permute-start | bytes 786440 | tf_op jit(solution)/shard_map/ppermute | solution.py:262
  73.3 0.2 copy.60
  73.5 1.0 copy.65
  74.5 4.4 %collective-permute-start.12 = (bf16[2,6,16,1024]{3,1,2,0:T(8,128)(2,1)}, bf16[2,6,16,1024]{3,1,2,0:T(8,128)(2,1)}, u32[]{:S(2)}, u32[]{:S(2)}) collective-permute-start(bf16[2,6,16,1024]{3,1,2,0:T(8,128)(2,1)} %copy.65), channel_id=1, source_target_pairs={{0,2},{1,3},{2,4},{3,5},{4,6},{5,7},{6,8},{7,9},{8,10},{9,11},{10,... | collective-permute-start | bytes 1179656 | tf_op jit(solution)/shard_map/ppermute | solution.py:146
  78.9 1.3 %collective-permute-start.8 = (bf16[2,6,16,1024]{3,1,2,0:T(8,128)(2,1)S(1)}, bf16[2,6,16,1024]{3,1,2,0:T(8,128)(2,1)}, u32[]{:S(2)}, u32[]{:S(2)}) collective-permute-start(bf16[2,6,16,1024]{3,1,2,0:T(8,128)(2,1)S(1)} %copy.60), channel_id=1, source_target_pairs={{2,0},{3,1},{4,2},{5,3},{6,4},{7,5},{8,6},{9,7},{10,8},{11,9},{12,... | collective-permute-start | bytes 1179656 | tf_op jit(solution)/shard_map/ppermute | solution.py:146
  80.2 1.1 fusion.67
  81.3 0.6 collective-permute-done.11
  81.8 1.0 fusion.68
  82.9 13.6 %collective-permute-done.10 = bf16[2,8,20,1024]{3,1,2,0:T(8,128)(2,1)S(1)} collective-permute-done((bf16[2,8,20,1024]{3,1,2,0:T(8,128)(2,1)S(1)}, bf16[2,8,20,1024]{3,1,2,0:T(8,128)(2,1)S(1)}, u32[]{:S(2)}, u32[]{:S(2)}) %collective-permute-start.10) | collective-permute-done | bytes 655392 | tf_op jit(solution)/shard_map/ppermute | solution.py:146
  96.5 0.2 copy.55
  96.6 0.1 reshape.155
  96.7 5.4 %collective-permute-done.13 = bf16[256,512]{1,0:T(8,128)(2,1)} collective-permute-done((bf16[256,512]{1,0:T(8,128)(2,1)}, bf16[256,512]{1,0:T(8,128)(2,1)}, u32[]{:S(2)}, u32[]{:S(2)}) %collective-permute-start.13) | collective-permute-done | bytes 262176 | tf_op jit(solution)/shard_map/ppermute | solution.py:262
  102.1 2.4 %fusion.17 = bf16[512,512]{1,0:T(8,128)(2,1)} fusion(bf16[256,512]{1,0:T(8,128)(2,1)S(1)} %reshape.155, bf16[128,512]{1,0:T(8,128)(2,1)} %copy-done.8, bf16[128,512]{1,0:T(8,128)(2,1)} %copy-done.6, bf16[256,512]{1,0:T(8,128)(2,1)} %collective-permute-done.13, bf16[128,512]{1,0:T(8,128)(2,1)} %get-tuple-element.30, bf16[128,512]{1,0:T(8,128)(2,1)} %get-tuple-element.28), kind=kOutput, calls=%fused_computation.21 | convolution fusion | flops 272105472 | bytes 1572864 | tf_op jit(solution)/shard_map/dot_general | solution.py:463
  104.5 4.2 %all-to-all-start = ((bf16[8,64,512]{2,1,0:T(8,128)(2,1)}), bf16[8,64,512]{2,1,0:T(8,128)(2,1)S(1)}, u32[]{:S(2)}, u32[]{:S(2)}) async-start(bf16[8,64,512]{2,1,0:T(8,128)(2,1)} %bitcast.41), calls=%async_computation | async-start | bytes 1048576 | tf_op jit(solution)/shard_map/all_to_all | solution.py:466
  108.8 2.3 %fusion.27 = bf16[2,8,16,1024]{3,1,2,0:T(8,128)(2,1)S(1)} fusion(f32[2,8,16,1024]{3,2,1,0:T(8,128)S(1)} %slice.183, bf16[2,6,6,1024]{3,1,2,0:T(8,128)(2,1)S(1)} %get-tuple-element.27, bf16[2,6,16,1024]{3,1,2,0:T(8,128)(2,1)} %collective-permute-done.12, bf16[2,6,6,1024]{3,1,2,0:T(8,128)(2,1)S(1)} %get-tuple-element.26, ...), kind=kLoop, calls=%fused_computation.36 | loop fusion | flops 4456448 | bytes 3342336 | tf_op jit(solution)/shard_map/convert_element_type | solution.py:469
  111.1 0.2 copy.53
  111.3 0.2 copy.54
  111.5 1.2 convolution_convert_fusion.3
  112.7 3.1 %convolution_convert_fusion.2 = bf16[128,512]{1,0:T(8,128)(2,1)S(1)} fusion(bf16[512,3072]{1,0:T(8,128)(2,1)} %collective-permute-done.5, bf16[128,1024]{1,0:T(8,128)(2,1)S(1)} %bitcast.45, bf16[128,1024]{1,0:T(8,128)(2,1)S(1)} %bitcast.43, bf16[128,1024]{1,0:T(8,128)(2,1)S(1)} %copy-done.10), kind=kOutput, calls=%fused_computation.24 | convolution fusion | flops 405078016 | bytes 4063232 | tf_op jit(solution)/shard_map/dot_general | solution.py:376
  115.7 0.8 maximum_select_fusion.1
  116.5 6.6 %all-to-all-done = bf16[8,64,512]{2,1,0:T(8,128)(2,1)S(1)} async-done(((bf16[8,64,512]{2,1,0:T(8,128)(2,1)}), bf16[8,64,512]{2,1,0:T(8,128)(2,1)S(1)}, u32[]{:S(2)}, u32[]{:S(2)}) %all-to-all-start) | async-done | bytes 524320 | tf_op jit(solution)/shard_map/all_to_all | solution.py:466
  123.1 0.7 convert_reduce_fusion
  (55 shorter events, 1.4 us)
Async XLA Ops:
  0.6 12.3 %copy-start.1 = (bf16[1,8,16,1024]{3,2,1,0:T(8,128)(2,1)S(1)}, bf16[1,8,16,1024]{3,2,1,0:T(8,128)(2,1)}, u32[]{:S(2)}) copy-start(bf16[1,8,16,1024]{3,2,1,0:T(8,128)(2,1)} %param.5) | copy-start | bytes 786436
  0.6 17.4 %copy-start.9 = (s32[64,32]{0,1:T(8,128)S(1)}, s32[64,32]{0,1:T(8,128)}, u32[]{:S(2)}) copy-start(s32[64,32]{0,1:T(8,128)} %param.7) | copy-start | bytes 24580
  0.7 19.0 %copy-start.2 = (bf16[512,1024]{1,0:T(8,128)(2,1)S(1)}, bf16[512,1024]{1,0:T(8,128)(2,1)}, u32[]{:S(2)}) copy-start(bf16[512,1024]{1,0:T(8,128)(2,1)} %param.9) | copy-start | bytes 3145732
  0.7 19.0 %copy-start.5 = (bf16[1,8,16,1024]{3,2,1,0:T(8,128)(2,1)S(1)}, bf16[1,8,16,1024]{3,2,1,0:T(8,128)(2,1)}, u32[]{:S(2)}) copy-start(bf16[1,8,16,1024]{3,2,1,0:T(8,128)(2,1)} %param.6) | copy-start | bytes 786436
  1.9 21.3 %collective-permute-start.2 = (bf16[8,12,1024]{2,1,0:T(8,128)(2,1)S(1)}, bf16[8,12,1024]{2,1,0:T(8,128)(2,1)S(1)}, u32[]{:S(2)}, u32[]{:S(2)}) collective-permute-start(bf16[8,12,1024]{2,1,0:T(8,128)(2,1)S(1)} %pad_maximum_fusion.7), channel_id=1, source_target_pairs={{0,1},{1,0},{2,3},{3,2},{4,5},{5,4},{6,7},{7,6},{8,9},{9,8},{10,11... | collective-permute-start | bytes 589832 | tf_op jit(solution)/shard_map/ppermute | solution.py:146
  6.1 14.9 %collective-permute-start.3 = (bf16[6,12,1024]{2,1,0:T(8,128)(2,1)S(1)}, bf16[6,12,1024]{2,1,0:T(8,128)(2,1)S(1)}, u32[]{:S(2)}, u32[]{:S(2)}) collective-permute-start(bf16[6,12,1024]{2,1,0:T(8,128)(2,1)S(1)} %pad_maximum_fusion.11), channel_id=1, source_target_pairs={{2,1},{3,0},{4,3},{5,2},{6,5},{7,4},{8,7},{9,6},{10,9},{11,8},{12,... | collective-permute-start | bytes 442376 | tf_op jit(solution)/shard_map/ppermute | solution.py:146
  7.4 15.1 %collective-permute-start = (bf16[6,12,1024]{2,1,0:T(8,128)(2,1)S(1)}, bf16[6,12,1024]{2,1,0:T(8,128)(2,1)S(1)}, u32[]{:S(2)}, u32[]{:S(2)}) collective-permute-start(bf16[6,12,1024]{2,1,0:T(8,128)(2,1)S(1)} %pad_maximum_fusion.10), channel_id=1, source_target_pairs={{0,3},{1,2},{2,5},{3,4},{4,7},{5,6},{6,9},{7,8},{8,11},{9,10},{10,... | collective-permute-start | bytes 442376 | tf_op jit(solution)/shard_map/ppermute | solution.py:146
  13.6 10.1 %collective-permute-start.1 = (bf16[6,16,1024]{2,1,0:T(8,128)(2,1)}, bf16[6,16,1024]{2,1,0:T(8,128)(2,1)S(1)}, u32[]{:S(2)}, u32[]{:S(2)}) collective-permute-start(bf16[6,16,1024]{2,1,0:T(8,128)(2,1)} %get-tuple-element.34), channel_id=1, source_target_pairs={{0,2},{1,3},{2,4},{3,5},{4,6},{5,7},{6,8},{7,9},{8,10},{9,11},{10,... | collective-permute-start | bytes 589832 | tf_op jit(solution)/shard_map/ppermute | solution.py:146
  18.0 18.2 %collective-permute-start.5 = (bf16[512,3072]{1,0:T(8,128)(2,1)}, bf16[512,3072]{1,0:T(8,128)(2,1)}, u32[]{:S(2)}, u32[]{:S(2)}) collective-permute-start(bf16[512,3072]{1,0:T(8,128)(2,1)} %param.8), channel_id=1, source_target_pairs={{0,16},{16,0},{1,17},{17,1},{2,18},{18,2},{3,19},{19,3},{4,20},{20... | collective-permute-start | bytes 9437192 | tf_op jit(solution)/shard_map/ppermute | solution.py:262
  20.9 10.2 %copy-start.3 = (bf16[512,3072]{1,0:T(8,128)(2,1)S(1)}, bf16[512,3072]{1,0:T(8,128)(2,1)}, u32[]{:S(2)}) copy-start(bf16[512,3072]{1,0:T(8,128)(2,1)} %param.8) | copy-start | bytes 9437188
  21.0 9.4 %collective-permute-start.4 = (bf16[6,16,1024]{2,1,0:T(8,128)(2,1)S(1)}, bf16[6,16,1024]{2,1,0:T(8,128)(2,1)S(1)}, u32[]{:S(2)}, u32[]{:S(2)}) collective-permute-start(bf16[6,16,1024]{2,1,0:T(8,128)(2,1)S(1)} %get-tuple-element.35), channel_id=1, source_target_pairs={{2,0},{3,1},{4,2},{5,3},{6,4},{7,5},{8,6},{9,7},{10,8},{11,9},{12,... | collective-permute-start | bytes 589832 | tf_op jit(solution)/shard_map/ppermute | solution.py:146
  22.6 10.8 %collective-permute-start.6 = (bf16[640,1024]{1,0:T(8,128)(2,1)S(1)}, bf16[640,1024]{1,0:T(8,128)(2,1)S(1)}, u32[]{:S(2)}, u32[]{:S(2)}) collective-permute-start(bf16[640,1024]{1,0:T(8,128)(2,1)S(1)} %pad_maximum_fusion), channel_id=1, source_target_pairs={{0,16},{16,0},{1,17},{17,1},{2,18},{18,2},{3,19},{19,3},{4,20},{20... | collective-permute-start | bytes 3932168 | tf_op jit(solution)/shard_map/ppermute | solution.py:262
  40.3 2.0 %copy-start = (bf16[640,3072]{1,0:T(8,128)(2,1)}, bf16[640,3072]{1,0:T(8,128)(2,1)S(1)}, u32[]{:S(2)}) copy-start(bf16[640,3072]{1,0:T(8,128)(2,1)S(1)} %add_convert_fusion.k_ref.v_ref) | copy-start | bytes 11796484
  55.0 2.7 %copy-start.7 = (bf16[128,1024]{1,0:T(8,128)(2,1)S(1)}, bf16[128,1024]{1,0:T(8,128)(2,1)}, u32[]{:S(2)}) copy-start(bf16[128,1024]{1,0:T(8,128)(2,1)} %get-tuple-element.10) | copy-start | bytes 786436
  57.8 9.2 %copy-start.6 = (bf16[128,512]{1,0:T(8,128)(2,1)}, bf16[128,512]{1,0:T(8,128)(2,1)S(1)}, u32[]{:S(2)}) copy-start(bf16[128,512]{1,0:T(8,128)(2,1)S(1)} %get-tuple-element.32) | copy-start | bytes 393220
  57.8 9.1 %collective-permute-start.9 = (bf16[128,512]{1,0:T(8,128)(2,1)S(1)}, bf16[128,512]{1,0:T(8,128)(2,1)S(1)}, u32[]{:S(2)}, u32[]{:S(2)}) collective-permute-start(bf16[128,512]{1,0:T(8,128)(2,1)S(1)} %get-tuple-element.33), channel_id=1, source_target_pairs={{0,16},{16,0},{1,17},{17,1},{2,18},{18,2},{3,19},{19,3},{4,20},{20... | collective-permute-start | bytes 393224 | tf_op jit(solution)/shard_map/ppermute | solution.py:262
  58.6 20.3 %collective-permute-start.7 = (bf16[2,6,12,1024]{3,1,2,0:T(8,128)(2,1)S(1)}, bf16[2,6,12,1024]{3,1,2,0:T(8,128)(2,1)}, u32[]{:S(2)}, u32[]{:S(2)}) collective-permute-start(bf16[2,6,12,1024]{3,1,2,0:T(8,128)(2,1)S(1)} %pad_maximum_fusion.3), channel_id=1, source_target_pairs={{2,1},{3,0},{4,3},{5,2},{6,5},{7,4},{8,7},{9,6},{10,9},{11,8},{12,... | collective-permute-start | bytes 884744 | tf_op jit(solution)/shard_map/ppermute | solution.py:146
  60.7 21.1 %collective-permute-start.11 = (bf16[2,6,12,1024]{3,1,2,0:T(8,128)(2,1)}, bf16[2,6,12,1024]{3,1,2,0:T(8,128)(2,1)}, u32[]{:S(2)}, u32[]{:S(2)}) collective-permute-start(bf16[2,6,12,1024]{3,1,2,0:T(8,128)(2,1)} %pad_maximum_fusion.4), channel_id=1, source_target_pairs={{0,3},{1,2},{2,5},{3,4},{4,7},{5,6},{6,9},{7,8},{8,11},{9,10},{10,... | collective-permute-start | bytes 884744 | tf_op jit(solution)/shard_map/ppermute | solution.py:146
  67.0 0.7 copy-start.8
  68.0 28.5 %collective-permute-start.10 = (bf16[2,8,20,1024]{3,1,2,0:T(8,128)(2,1)S(1)}, bf16[2,8,20,1024]{3,1,2,0:T(8,128)(2,1)S(1)}, u32[]{:S(2)}, u32[]{:S(2)}) collective-permute-start(bf16[2,8,20,1024]{3,1,2,0:T(8,128)(2,1)S(1)} %pad_maximum_fusion.2), channel_id=1, source_target_pairs={{0,1},{1,0},{2,3},{3,2},{4,5},{5,4},{6,7},{7,6},{8,9},{9,8},{10,11... | collective-permute-start | bytes 1966088 | tf_op jit(solution)/shard_map/ppermute | solution.py:146
  71.7 30.4 %collective-permute-start.13 = (bf16[256,512]{1,0:T(8,128)(2,1)}, bf16[256,512]{1,0:T(8,128)(2,1)}, u32[]{:S(2)}, u32[]{:S(2)}) collective-permute-start(bf16[256,512]{1,0:T(8,128)(2,1)} %pad_maximum_fusion.9), channel_id=1, source_target_pairs={{0,1},{1,0},{2,3},{3,2},{4,5},{5,4},{6,7},{7,6},{8,9},{9,8},{10,11... | collective-permute-start | bytes 786440 | tf_op jit(solution)/shard_map/ppermute | solution.py:262
  74.5 34.2 %collective-permute-start.12 = (bf16[2,6,16,1024]{3,1,2,0:T(8,128)(2,1)}, bf16[2,6,16,1024]{3,1,2,0:T(8,128)(2,1)}, u32[]{:S(2)}, u32[]{:S(2)}) collective-permute-start(bf16[2,6,16,1024]{3,1,2,0:T(8,128)(2,1)} %copy.65), channel_id=1, source_target_pairs={{0,2},{1,3},{2,4},{3,5},{4,6},{5,7},{6,8},{7,9},{8,10},{9,11},{10,... | collective-permute-start | bytes 1179656 | tf_op jit(solution)/shard_map/ppermute | solution.py:146
  78.9 29.8 %collective-permute-start.8 = (bf16[2,6,16,1024]{3,1,2,0:T(8,128)(2,1)S(1)}, bf16[2,6,16,1024]{3,1,2,0:T(8,128)(2,1)}, u32[]{:S(2)}, u32[]{:S(2)}) collective-permute-start(bf16[2,6,16,1024]{3,1,2,0:T(8,128)(2,1)S(1)} %copy.60), channel_id=1, source_target_pairs={{2,0},{3,1},{4,2},{5,3},{6,4},{7,5},{8,6},{9,7},{10,8},{11,9},{12,... | collective-permute-start | bytes 1179656 | tf_op jit(solution)/shard_map/ppermute | solution.py:146
  104.5 18.6 %all-to-all-start = ((bf16[8,64,512]{2,1,0:T(8,128)(2,1)}), bf16[8,64,512]{2,1,0:T(8,128)(2,1)S(1)}, u32[]{:S(2)}, u32[]{:S(2)}) async-start(bf16[8,64,512]{2,1,0:T(8,128)(2,1)} %bitcast.41), calls=%async_computation | async-start | bytes 1048576 | tf_op jit(solution)/shard_map/all_to_all | solution.py:466
  108.8 2.7 %copy-start.4 = (bf16[512,3072]{1,0:T(8,128)(2,1)S(1)}, bf16[512,3072]{1,0:T(8,128)(2,1)}, u32[]{:S(2)}) copy-start(bf16[512,3072]{1,0:T(8,128)(2,1)} %param.8) | copy-start | bytes 9437188
  108.8 2.7 %copy-start.10 = (bf16[128,1024]{1,0:T(8,128)(2,1)S(1)}, bf16[128,1024]{1,0:T(8,128)(2,1)}, u32[]{:S(2)}) copy-start(bf16[128,1024]{1,0:T(8,128)(2,1)} %get-tuple-element.7) | copy-start | bytes 786436

commit v14 on v11

--- a/solution.py
+++ b/solution.py
@@ -363,25 +363,20 @@
             jnp.concatenate([other_part, mine_part], axis=1),
         )
 
+        rows_first = jnp.concatenate([w_qkv, qkv_other], axis=0)
+
         def project(rows):
-            own = jnp.dot(
-                columns(rows, dp_index, rows_half), w_qkv, preferred_element_type=jnp.float32
+            ordered = jnp.concatenate(
+                [columns(rows, dp_index, rows_half), columns(rows, 1 - dp_index, rows_half)], axis=1
             )
-            other = jnp.dot(
-                columns(rows, 1 - dp_index, rows_half), qkv_other, preferred_element_type=jnp.float32
-            )
-            return (own + other).astype(jnp.bfloat16)
+            out = jnp.dot(ordered, rows_first, preferred_element_type=jnp.float32)
+            return out.astype(jnp.bfloat16)
 
         def back_project(grad_proj):
-            own = lax.dot_general(grad_proj, w_qkv, TRANS_B, preferred_element_type=jnp.float32)
-            other = lax.dot_general(grad_proj, qkv_other, TRANS_B, preferred_element_type=jnp.float32)
-            own = own.astype(jnp.bfloat16)
-            other = other.astype(jnp.bfloat16)
-            return jnp.where(
-                dp_index == 0,
-                jnp.concatenate([own, other], axis=1),
-                jnp.concatenate([other, own], axis=1),
-            )
+            out = lax.dot_general(grad_proj, rows_first, TRANS_B, preferred_element_type=jnp.float32)
+            out = out.astype(jnp.bfloat16)
+            swapped = jnp.concatenate([out[:, rows_half:], out[:, :rows_half]], axis=1)
+            return jnp.where(dp_index == 0, out, swapped)
     else:
         panels = lax.all_gather(w_qkv, "dp", axis=0, tiled=True)
         cot_blocks = flat_grad.reshape(token_count, lon_count, cols_block).transpose(1, 0, 2)

time: 123 us -> 125 us (1.016)
  local copies, waits for them, and re-layouts: 19 us -> 24.9 us
  waiting for transfers between devices: 29.7 us -> 28.1 us
  starting transfers between devices: 37.9 us -> 36.4 us
    unnamed x31 -> x34, local copies, waits for them, and re-layouts: 4.56 us -> 8.19 us
    concatenate x0 -> x1, local copies, waits for them, and re-layouts: none -> 2.09 us  [shards(): rows_first = jnp.concatenate([w_qkv, qkv_other], axis=0)]
    all_to_all x1, starting transfers between devices: 6.33 us -> 4.97 us  [shards(): lax.all_to_all(partial.astype(jnp.bfloat16), 'lat', 0, 0, tiled=True)]
    dot_general x4 -> x2, matrix products: 10.7 us -> 9.41 us  [the longest x1 4.98 us: back_project(): lax.dot_general(grad_proj, rows_first, TRANS_B, preferred_element_type=jn...]
  transfers between devices with their start and end apart: 15 -> 15, of which waited for: 5 -> 4; matrix products, arithmetic and copies ran while one was open for 30% -> 34% of each run, Pallas kernels for 10% -> 10%
where the time goes in v14:
time: 125 us; the launch traced here: 124 us
  starting transfers between devices  36.4 us (29%)
  waiting for transfers between devices  28.1 us (22%)
  local copies, waits for them, and re-layouts  24.9 us (20%)
  matrix products  12.9 us (10%)
  Pallas kernels  12 us (10%)
  other arithmetic  8.42 us (7%)
    ppermute x10, starting transfers between devices, sent_to(): return lax.ppermute(value, ('lat', 'lon'), grid_pairs(delta_lat, delta_lon))  30.2 us
    ppermute x10, waiting for transfers between devices, sent_to(): return lax.ppermute(value, ('lat', 'lon'), grid_pairs(delta_lat, delta_lon))  22.2 us
    pallas_call x1, Pallas kernels, block_attention(): pl.pallas_call(kernel, grid=(pairs,), in_specs=[pl.BlockSpec((queries, la...  12 us
    unnamed x34, local copies, waits for them, and re-layouts  8.19 us
    all_to_all x1, waiting for transfers between devices, shards(): lax.all_to_all(partial.astype(jnp.bfloat16), 'lat', 0, 0, tiled=True)  5.93 us
    dot_general x1, matrix products, back_project(): lax.dot_general(grad_proj, rows_first, TRANS_B, preferred_element_type=jn...  4.98 us
    all_to_all x1, starting transfers between devices, shards(): lax.all_to_all(partial.astype(jnp.bfloat16), 'lat', 0, 0, tiled=True)  4.97 us
    dot_general x1, matrix products, project(): out = jnp.dot(ordered, rows_first, preferred_element_type=jnp.float32)  4.43 us
  transfers between devices with their start and end apart: 15, of which 4 were waited for; matrix products, arithmetic and copies ran while one was open for 34% of the time, Pallas kernels for 10%

profile of v14, /device:TPU:0, one launch (start us, length us, event | category | flops | bytes accessed | tf_op | source)
XLA Modules:
  0.0 123.8 jit_solution(13771537455204438018)
XLA Ops:
  0.7 1.1 fusion.75
  1.8 0.1 pad_maximum_fusion.4
  1.9 3.0 %collective-permute-start.2 = (bf16[8,12,1024]{2,1,0:T(8,128)(2,1)S(1)}, bf16[8,12,1024]{2,1,0:T(8,128)(2,1)S(1)}, u32[]{:S(2)}, u32[]{:S(2)}) collective-permute-start(bf16[8,12,1024]{2,1,0:T(8,128)(2,1)S(1)} %pad_maximum_fusion.4), channel_id=1, source_target_pairs={{0,1},{1,0},{2,3},{3,2},{4,5},{5,4},{6,7},{7,6},{8,9},{9,8},{10,11... | collective-permute-start | bytes 589832 | tf_op jit(solution)/shard_map/ppermute | solution.py:146
  4.9 1.1 fusion.74
  6.1 1.3 %collective-permute-start.3 = (bf16[6,12,1024]{2,1,0:T(8,128)(2,1)S(1)}, bf16[6,12,1024]{2,1,0:T(8,128)(2,1)S(1)}, u32[]{:S(2)}, u32[]{:S(2)}) collective-permute-start(bf16[6,12,1024]{2,1,0:T(8,128)(2,1)S(1)} %pad_maximum_fusion.8), channel_id=1, source_target_pairs={{2,1},{3,0},{4,3},{5,2},{6,5},{7,4},{8,7},{9,6},{10,9},{11,8},{12,... | collective-permute-start | bytes 442376 | tf_op jit(solution)/shard_map/ppermute | solution.py:146
  7.4 5.5 %collective-permute-start = (bf16[6,12,1024]{2,1,0:T(8,128)(2,1)S(1)}, bf16[6,12,1024]{2,1,0:T(8,128)(2,1)S(1)}, u32[]{:S(2)}, u32[]{:S(2)}) collective-permute-start(bf16[6,12,1024]{2,1,0:T(8,128)(2,1)S(1)} %pad_maximum_fusion.7), channel_id=1, source_target_pairs={{0,3},{1,2},{2,5},{3,4},{4,7},{5,6},{6,9},{7,8},{8,11},{9,10},{10,... | collective-permute-start | bytes 442376 | tf_op jit(solution)/shard_map/ppermute | solution.py:146
  12.9 0.7 slice_bitcast_fusion.1
  13.6 4.3 %collective-permute-start.1 = (bf16[6,16,1024]{2,1,0:T(8,128)(2,1)}, bf16[6,16,1024]{2,1,0:T(8,128)(2,1)S(1)}, u32[]{:S(2)}, u32[]{:S(2)}) collective-permute-start(bf16[6,16,1024]{2,1,0:T(8,128)(2,1)} %get-tuple-element.36), channel_id=1, source_target_pairs={{0,2},{1,3},{2,4},{3,5},{4,6},{5,7},{6,8},{7,9},{8,10},{9,11},{10,... | collective-permute-start | bytes 589832 | tf_op jit(solution)/shard_map/ppermute | solution.py:146
  18.2 0.1 copy.40
  18.3 0.1 copy.42
  18.6 0.1 eq.28
  18.6 1.0 fusion.50.bias_ref
  19.7 0.5 convolution_convert_fusion.3
  20.2 3.7 %constant_dynamic-update-slice_fusion.1 = bf16[1024,3072]{1,0:T(8,128)(2,1)} fusion(bf16[512,3072]{1,0:T(8,128)(2,1)} %param.8), kind=kLoop, calls=%fused_computation.89 | loop fusion | bytes 6291456
  23.9 0.7 constant_dynamic-slice_fusion.3
  24.6 0.1 pad_maximum_fusion
  24.7 0.5 collective-permute-start.6
  25.3 1.4 %collective-permute-start.4 = (bf16[6,16,1024]{2,1,0:T(8,128)(2,1)S(1)}, bf16[6,16,1024]{2,1,0:T(8,128)(2,1)S(1)}, u32[]{:S(2)}, u32[]{:S(2)}) collective-permute-start(bf16[6,16,1024]{2,1,0:T(8,128)(2,1)S(1)} %get-tuple-element.37), channel_id=1, source_target_pairs={{2,0},{3,1},{4,2},{5,3},{6,4},{7,5},{8,6},{9,7},{10,8},{11,9},{12,... | collective-permute-start | bytes 589832 | tf_op jit(solution)/shard_map/ppermute | solution.py:146
  26.8 7.5 %collective-permute-done.4 = bf16[6,16,1024]{2,1,0:T(8,128)(2,1)S(1)} collective-permute-done((bf16[6,16,1024]{2,1,0:T(8,128)(2,1)S(1)}, bf16[6,16,1024]{2,1,0:T(8,128)(2,1)S(1)}, u32[]{:S(2)}, u32[]{:S(2)}) %collective-permute-start.4) | collective-permute-done | bytes 196640 | tf_op jit(solution)/shard_map/ppermute | solution.py:146
  34.3 0.7 fusion.12
  35.0 0.1 constant_dynamic-slice_fusion.7
  35.2 0.7 constant_dynamic-slice_fusion.2
  35.9 0.7 pad_maximum_fusion.6
  36.6 0.5 collective-permute-start.13
  37.1 0.5 fusion.21
  37.7 0.8 maximum_select_fusion.g_ref
  38.5 2.1 %constant_dynamic-update-slice_fusion = bf16[1024,3072]{1,0:T(8,128)(2,1)S(1)} fusion(bf16[1024,3072]{1,0:T(8,128)(2,1)S(1)} %bitcast.37, bf16[512,3072]{1,0:T(8,128)(2,1)} %collective-permute-done.5), kind=kLoop, calls=%fused_computation.88 | loop fusion | bytes 6291456 | tf_op jit(solution)/shard_map/concatenate | solution.py:366
  40.6 4.4 %convolution_convert_fusion.k_ref.v_ref = bf16[640,3072]{1,0:T(8,128)(2,1)S(1)} fusion(bf16[1024,3072]{1,0:T(8,128)(2,1)S(1)} %constant_dynamic-update-slice_fusion, bf16[640,512]{1,0:T(8,128)(2,1)S(1)} %get-tuple-element.19, bf16[640,512]{1,0:T(8,128)(2,1)S(1)} %get-tuple-element.18), kind=kOutput, calls=%fused_computation | convolution fusion | flops 4031119360 | bytes 11534336 | tf_op jit(solution)/shard_map/dot_general | solution.py:372
  45.0 1.9 %copy-done = bf16[640,3072]{1,0:T(8,128)(2,1)} copy-done((bf16[640,3072]{1,0:T(8,128)(2,1)}, bf16[640,3072]{1,0:T(8,128)(2,1)S(1)}, u32[]{:S(2)}) %copy-start) | copy-done | bytes 3932184
  46.9 0.8 slice.189
  47.7 12.0 %block_attention.1 = (bf16[128,1024]{1,0:T(8,128)(2,1)}, bf16[128,1024]{1,0:T(8,128)(2,1)}, f32[2,640,1024]{2,1,0:T(8,128)}, bf16[2,640,1024]{2,1,0:T(8,128)(2,1)}) custom-call(bf16[128,1024]{1,0:T(8,128)(2,1)} %bitcast.38, bf16[640,3072]{1,0:T(8,128)(2,1)} %copy-done, bf16[640,3072]{1,0:T(8,128)(2,1)} %copy-done, ...), custom_call_target="tpu_custom_call" | custom-call | flops 2013265920 | bytes 9240576 | tf_op jit(solution)/shard_map/block_attention/pallas_call | solution.py:106
  59.6 1.3 %fusion.67 = (bf16[2,8,6,1024]{3,2,1,0:T(8,128)(2,1)S(1)}, bf16[2,8,6,1024]{3,2,1,0:T(8,128)(2,1)S(1)}) fusion(bf16[2,20,32,1024]{3,2,1,0:T(8,128)(2,1)} %bitcast.33), kind=kLoop, calls=%fused_computation.114 | loop fusion | bytes 786432 | tf_op jit(solution)/shard_map/slice | solution.py:201
  60.9 1.5 %fusion.66 = (bf16[2,6,6,1024]{3,2,1,0:T(8,128)(2,1)S(1)}, bf16[2,6,6,1024]{3,2,1,0:T(8,128)(2,1)S(1)}, bf16[2,6,6,1024]{3,2,1,0:T(8,128)(2,1)S(1)}, bf16[2,6,6,1024]{3,2,1,0:T(8,128)(2,1)S(1)}) fusion(bf16[2,20,32,1024]{3,2,1,0:T(8,128)(2,1)} %bitcast.34), kind=kLoop, calls=%fused_computation.113 | loop fusion | bytes 1179648 | tf_op jit(solution)/shard_map/slice | solution.py:201
  62.8 0.1 copy.61
  62.9 0.1 copy.62
  63.0 0.1 copy.64
  63.2 1.3 %collective-permute-start.7 = (bf16[2,6,12,1024]{3,1,2,0:T(8,128)(2,1)S(1)}, bf16[2,6,12,1024]{3,1,2,0:T(8,128)(2,1)}, u32[]{:S(2)}, u32[]{:S(2)}) collective-permute-start(bf16[2,6,12,1024]{3,1,2,0:T(8,128)(2,1)S(1)} %pad_maximum_fusion.2), channel_id=1, source_target_pairs={{2,1},{3,0},{4,3},{5,2},{6,5},{7,4},{8,7},{9,6},{10,9},{11,8},{12,... | collective-permute-start | bytes 884744 | tf_op jit(solution)/shard_map/ppermute | solution.py:146
  64.5 0.8 pad_maximum_fusion.3
  65.4 6.2 %collective-permute-start.11 = (bf16[2,6,12,1024]{3,1,2,0:T(8,128)(2,1)}, bf16[2,6,12,1024]{3,1,2,0:T(8,128)(2,1)}, u32[]{:S(2)}, u32[]{:S(2)}) collective-permute-start(bf16[2,6,12,1024]{3,1,2,0:T(8,128)(2,1)} %pad_maximum_fusion.3), channel_id=1, source_target_pairs={{0,3},{1,2},{2,5},{3,4},{4,7},{5,6},{6,9},{7,8},{8,11},{9,10},{10,... | collective-permute-start | bytes 884744 | tf_op jit(solution)/shard_map/ppermute | solution.py:146
  71.6 0.7 copy-done.7
  72.3 0.1 reshape.101
  72.3 0.2 copy.49
  72.6 1.6 %collective-permute-start.10 = (bf16[2,8,20,1024]{3,1,2,0:T(8,128)(2,1)S(1)}, bf16[2,8,20,1024]{3,1,2,0:T(8,128)(2,1)S(1)}, u32[]{:S(2)}, u32[]{:S(2)}) collective-permute-start(bf16[2,8,20,1024]{3,1,2,0:T(8,128)(2,1)S(1)} %pad_maximum_fusion.1), channel_id=1, source_target_pairs={{0,1},{1,0},{2,3},{3,2},{4,5},{5,4},{6,7},{7,6},{8,9},{9,8},{10,11... | collective-permute-start | bytes 1966088 | tf_op jit(solution)/shard_map/ppermute | solution.py:146
  74.1 1.6 %fusion.65 = (bf16[2,6,16,1024]{3,2,1,0:T(8,128)(2,1)S(1)}, bf16[2,6,16,1024]{3,2,1,0:T(8,128)(2,1)S(1)}) fusion(bf16[2,20,32,1024]{3,2,1,0:T(8,128)(2,1)} %bitcast.35), kind=kLoop, calls=%fused_computation.112 | loop fusion | bytes 1572864 | tf_op jit(solution)/shard_map/slice | solution.py:201
  75.8 1.5 %slice.191 = f32[2,8,16,1024]{3,2,1,0:T(8,128)S(1)} slice(f32[2,20,32,1024]{3,2,1,0:T(8,128)} %bitcast.43), slice={[0:2], [6:14], [6:22], [0:1024]} | slice | bytes 2097152 | tf_op jit(solution)/shard_map/slice | solution.py:193
  77.3 0.2 copy.60
  77.5 1.0 copy.65
  78.5 4.3 %collective-permute-start.12 = (bf16[2,6,16,1024]{3,1,2,0:T(8,128)(2,1)}, bf16[2,6,16,1024]{3,1,2,0:T(8,128)(2,1)}, u32[]{:S(2)}, u32[]{:S(2)}) collective-permute-start(bf16[2,6,16,1024]{3,1,2,0:T(8,128)(2,1)} %copy.65), channel_id=1, source_target_pairs={{0,2},{1,3},{2,4},{3,5},{4,6},{5,7},{6,8},{7,9},{8,10},{9,11},{10,... | collective-permute-start | bytes 1179656 | tf_op jit(solution)/shard_map/ppermute | solution.py:146
  82.9 1.3 %collective-permute-start.8 = (bf16[2,6,16,1024]{3,1,2,0:T(8,128)(2,1)S(1)}, bf16[2,6,16,1024]{3,1,2,0:T(8,128)(2,1)}, u32[]{:S(2)}, u32[]{:S(2)}) collective-permute-start(bf16[2,6,16,1024]{3,1,2,0:T(8,128)(2,1)S(1)} %copy.60), channel_id=1, source_target_pairs={{2,0},{3,1},{4,2},{5,3},{6,4},{7,5},{8,6},{9,7},{10,8},{11,9},{12,... | collective-permute-start | bytes 1179656 | tf_op jit(solution)/shard_map/ppermute | solution.py:146
  84.2 1.1 fusion.70
  85.2 0.9 collective-permute-done.11
  86.1 1.0 fusion.71
  87.2 13.8 %collective-permute-done.10 = bf16[2,8,20,1024]{3,1,2,0:T(8,128)(2,1)S(1)} collective-permute-done((bf16[2,8,20,1024]{3,1,2,0:T(8,128)(2,1)S(1)}, bf16[2,8,20,1024]{3,1,2,0:T(8,128)(2,1)S(1)}, u32[]{:S(2)}, u32[]{:S(2)}) %collective-permute-start.10) | collective-permute-done | bytes 655392 | tf_op jit(solution)/shard_map/ppermute | solution.py:146
  101.0 0.2 copy.55
  101.2 0.1 reshape.103
  101.3 2.5 %fusion.20 = bf16[512,512]{1,0:T(8,128)(2,1)} fusion(bf16[256,512]{1,0:T(8,128)(2,1)S(1)} %reshape.103, bf16[128,512]{1,0:T(8,128)(2,1)} %copy-done.7, bf16[128,512]{1,0:T(8,128)(2,1)} %copy-done.5, bf16[256,512]{1,0:T(8,128)(2,1)} %collective-permute-done.13, bf16[128,512]{1,0:T(8,128)(2,1)} %get-tuple-element.30, bf16[128,512]{1,0:T(8,128)(2,1)} %get-tuple-element.28), kind=kOutput, calls=%fused_computation.24 | convolution fusion | flops 272105472 | bytes 1572864 | tf_op jit(solution)/shard_map/dot_general | solution.py:455
  103.7 5.0 %all-to-all-start = ((bf16[8,64,512]{2,1,0:T(8,128)(2,1)}), bf16[8,64,512]{2,1,0:T(8,128)(2,1)S(1)}, u32[]{:S(2)}, u32[]{:S(2)}) async-start(bf16[8,64,512]{2,1,0:T(8,128)(2,1)} %bitcast.39), calls=%async_computation | async-start | bytes 1048576 | tf_op jit(solution)/shard_map/all_to_all | solution.py:458
  108.8 2.2 %fusion.30 = bf16[2,8,16,1024]{3,1,2,0:T(8,128)(2,1)S(1)} fusion(f32[2,8,16,1024]{3,2,1,0:T(8,128)S(1)} %slice.191, bf16[2,6,6,1024]{3,1,2,0:T(8,128)(2,1)S(1)} %get-tuple-element.27, bf16[2,6,16,1024]{3,1,2,0:T(8,128)(2,1)} %collective-permute-done.12, bf16[2,6,6,1024]{3,1,2,0:T(8,128)(2,1)S(1)} %get-tuple-element.26, ...), kind=kLoop, calls=%fused_computation.38 | loop fusion | flops 4456448 | bytes 3342336 | tf_op jit(solution)/shard_map/convert_element_type | solution.py:461
  111.0 0.2 copy.53
  111.2 0.2 copy.54
  111.4 5.0 %convolution_convert_fusion.1 = bf16[128,1024]{1,0:T(8,128)(2,1)S(1)} fusion(bf16[1024,3072]{1,0:T(8,128)(2,1)} %copy-done.4, bf16[128,1024]{1,0:T(8,128)(2,1)S(1)} %bitcast.41, bf16[128,1024]{1,0:T(8,128)(2,1)S(1)} %bitcast.40, bf16[128,1024]{1,0:T(8,128)(2,1)S(1)} %copy-done.9), kind=kOutput, calls=%fused_computation.25 | convolution fusion | flops 807796736 | bytes 7340032 | tf_op jit(solution)/shard_map/dot_general | solution.py:376
  116.4 0.8 maximum_select_fusion.1
  117.1 5.9 %all-to-all-done = bf16[8,64,512]{2,1,0:T(8,128)(2,1)S(1)} async-done(((bf16[8,64,512]{2,1,0:T(8,128)(2,1)}), bf16[8,64,512]{2,1,0:T(8,128)(2,1)S(1)}, u32[]{:S(2)}, u32[]{:S(2)}) %all-to-all-start) | async-done | bytes 524320 | tf_op jit(solution)/shard_map/all_to_all | solution.py:458
  123.1 0.7 convert_reduce_fusion
  (60 shorter events, 1.3 us)
Async XLA Ops:
  0.6 12.3 %copy-start.1 = (bf16[1,8,16,1024]{3,2,1,0:T(8,128)(2,1)S(1)}, bf16[1,8,16,1024]{3,2,1,0:T(8,128)(2,1)}, u32[]{:S(2)}) copy-start(bf16[1,8,16,1024]{3,2,1,0:T(8,128)(2,1)} %param.5) | copy-start | bytes 786436
  0.6 17.4 %copy-start.8 = (s32[64,32]{0,1:T(8,128)S(1)}, s32[64,32]{0,1:T(8,128)}, u32[]{:S(2)}) copy-start(s32[64,32]{0,1:T(8,128)} %param.7) | copy-start | bytes 24580
  0.7 19.0 %copy-start.2 = (bf16[512,1024]{1,0:T(8,128)(2,1)S(1)}, bf16[512,1024]{1,0:T(8,128)(2,1)}, u32[]{:S(2)}) copy-start(bf16[512,1024]{1,0:T(8,128)(2,1)} %param.9) | copy-start | bytes 3145732
  0.7 19.0 %copy-start.3 = (bf16[1,8,16,1024]{3,2,1,0:T(8,128)(2,1)S(1)}, bf16[1,8,16,1024]{3,2,1,0:T(8,128)(2,1)}, u32[]{:S(2)}) copy-start(bf16[1,8,16,1024]{3,2,1,0:T(8,128)(2,1)} %param.6) | copy-start | bytes 786436
  1.9 24.8 %collective-permute-start.2 = (bf16[8,12,1024]{2,1,0:T(8,128)(2,1)S(1)}, bf16[8,12,1024]{2,1,0:T(8,128)(2,1)S(1)}, u32[]{:S(2)}, u32[]{:S(2)}) collective-permute-start(bf16[8,12,1024]{2,1,0:T(8,128)(2,1)S(1)} %pad_maximum_fusion.4), channel_id=1, source_target_pairs={{0,1},{1,0},{2,3},{3,2},{4,5},{5,4},{6,7},{7,6},{8,9},{9,8},{10,11... | collective-permute-start | bytes 589832 | tf_op jit(solution)/shard_map/ppermute | solution.py:146
  6.1 18.6 %collective-permute-start.3 = (bf16[6,12,1024]{2,1,0:T(8,128)(2,1)S(1)}, bf16[6,12,1024]{2,1,0:T(8,128)(2,1)S(1)}, u32[]{:S(2)}, u32[]{:S(2)}) collective-permute-start(bf16[6,12,1024]{2,1,0:T(8,128)(2,1)S(1)} %pad_maximum_fusion.8), channel_id=1, source_target_pairs={{2,1},{3,0},{4,3},{5,2},{6,5},{7,4},{8,7},{9,6},{10,9},{11,8},{12,... | collective-permute-start | bytes 442376 | tf_op jit(solution)/shard_map/ppermute | solution.py:146
  7.4 17.8 %collective-permute-start = (bf16[6,12,1024]{2,1,0:T(8,128)(2,1)S(1)}, bf16[6,12,1024]{2,1,0:T(8,128)(2,1)S(1)}, u32[]{:S(2)}, u32[]{:S(2)}) collective-permute-start(bf16[6,12,1024]{2,1,0:T(8,128)(2,1)S(1)} %pad_maximum_fusion.7), channel_id=1, source_target_pairs={{0,3},{1,2},{2,5},{3,4},{4,7},{5,6},{6,9},{7,8},{8,11},{9,10},{10,... | collective-permute-start | bytes 442376 | tf_op jit(solution)/shard_map/ppermute | solution.py:146
  13.6 13.2 %collective-permute-start.1 = (bf16[6,16,1024]{2,1,0:T(8,128)(2,1)}, bf16[6,16,1024]{2,1,0:T(8,128)(2,1)S(1)}, u32[]{:S(2)}, u32[]{:S(2)}) collective-permute-start(bf16[6,16,1024]{2,1,0:T(8,128)(2,1)} %get-tuple-element.36), channel_id=1, source_target_pairs={{0,2},{1,3},{2,4},{3,5},{4,6},{5,7},{6,8},{7,9},{8,10},{9,11},{10,... | collective-permute-start | bytes 589832 | tf_op jit(solution)/shard_map/ppermute | solution.py:146
  18.0 20.5 %collective-permute-start.5 = (bf16[512,3072]{1,0:T(8,128)(2,1)}, bf16[512,3072]{1,0:T(8,128)(2,1)}, u32[]{:S(2)}, u32[]{:S(2)}) collective-permute-start(bf16[512,3072]{1,0:T(8,128)(2,1)} %param.8), channel_id=1, source_target_pairs={{0,16},{16,0},{1,17},{17,1},{2,18},{18,2},{3,19},{19,3},{4,20},{20... | collective-permute-start | bytes 9437192 | tf_op jit(solution)/shard_map/ppermute | solution.py:262
  24.6 13.9 %slice-start = ((s8[6291456]{0:T(1024)(128)(4,1)}), s8[4194304]{0:T(1024)(128)(4,1)S(1)}, s32[]{:S(2)}) async-start(s8[6291456]{0:T(1024)(128)(4,1)} %bitcast.36), calls=%async_computation.1 | async-start | bytes 8388608
  24.7 10.5 %collective-permute-start.6 = (bf16[640,1024]{1,0:T(8,128)(2,1)S(1)}, bf16[640,1024]{1,0:T(8,128)(2,1)S(1)}, u32[]{:S(2)}, u32[]{:S(2)}) collective-permute-start(bf16[640,1024]{1,0:T(8,128)(2,1)S(1)} %pad_maximum_fusion), channel_id=1, source_target_pairs={{0,16},{16,0},{1,17},{17,1},{2,18},{18,2},{3,19},{19,3},{4,20},{20... | collective-permute-start | bytes 3932168 | tf_op jit(solution)/shard_map/ppermute | solution.py:262
  25.3 9.0 %collective-permute-start.4 = (bf16[6,16,1024]{2,1,0:T(8,128)(2,1)S(1)}, bf16[6,16,1024]{2,1,0:T(8,128)(2,1)S(1)}, u32[]{:S(2)}, u32[]{:S(2)}) collective-permute-start(bf16[6,16,1024]{2,1,0:T(8,128)(2,1)S(1)} %get-tuple-element.37), channel_id=1, source_target_pairs={{2,0},{3,1},{4,2},{5,3},{6,4},{7,5},{8,6},{9,7},{10,8},{11,9},{12,... | collective-permute-start | bytes 589832 | tf_op jit(solution)/shard_map/ppermute | solution.py:146
  34.3 4.2 %slice-start.1 = ((s8[6291456]{0:T(1024)(128)(4,1)}), s8[2097152]{0:T(1024)(128)(4,1)S(1)}, s32[]{:S(2)}) async-start(s8[6291456]{0:T(1024)(128)(4,1)} %bitcast.36), calls=%async_computation.2 | async-start | bytes 4194304
  36.6 64.7 %collective-permute-start.13 = (bf16[256,512]{1,0:T(8,128)(2,1)}, bf16[256,512]{1,0:T(8,128)(2,1)}, u32[]{:S(2)}, u32[]{:S(2)}) collective-permute-start(bf16[256,512]{1,0:T(8,128)(2,1)} %pad_maximum_fusion.6), channel_id=1, source_target_pairs={{0,1},{1,0},{2,3},{3,2},{4,5},{5,4},{6,7},{7,6},{8,9},{9,8},{10,11... | collective-permute-start | bytes 786440 | tf_op jit(solution)/shard_map/ppermute | solution.py:262
  40.6 4.5 %copy-start.4 = (bf16[1024,3072]{1,0:T(8,128)(2,1)}, bf16[1024,3072]{1,0:T(8,128)(2,1)S(1)}, u32[]{:S(2)}) copy-start(bf16[1024,3072]{1,0:T(8,128)(2,1)S(1)} %constant_dynamic-update-slice_fusion) | copy-start | bytes 18874372
  45.0 1.9 %copy-start = (bf16[640,3072]{1,0:T(8,128)(2,1)}, bf16[640,3072]{1,0:T(8,128)(2,1)S(1)}, u32[]{:S(2)}) copy-start(bf16[640,3072]{1,0:T(8,128)(2,1)S(1)} %convolution_convert_fusion.k_ref.v_ref) | copy-start | bytes 11796484
  59.6 2.7 %copy-start.6 = (bf16[128,1024]{1,0:T(8,128)(2,1)S(1)}, bf16[128,1024]{1,0:T(8,128)(2,1)}, u32[]{:S(2)}) copy-start(bf16[128,1024]{1,0:T(8,128)(2,1)} %get-tuple-element.9) | copy-start | bytes 786436
  62.4 9.2 %copy-start.5 = (bf16[128,512]{1,0:T(8,128)(2,1)}, bf16[128,512]{1,0:T(8,128)(2,1)S(1)}, u32[]{:S(2)}) copy-start(bf16[128,512]{1,0:T(8,128)(2,1)S(1)} %get-tuple-element.34) | copy-start | bytes 393220
  62.4 9.1 %collective-permute-start.9 = (bf16[128,512]{1,0:T(8,128)(2,1)S(1)}, bf16[128,512]{1,0:T(8,128)(2,1)S(1)}, u32[]{:S(2)}, u32[]{:S(2)}) collective-permute-start(bf16[128,512]{1,0:T(8,128)(2,1)S(1)} %get-tuple-element.35), channel_id=1, source_target_pairs={{0,16},{16,0},{1,17},{17,1},{2,18},{18,2},{3,19},{19,3},{4,20},{20... | collective-permute-start | bytes 393224 | tf_op jit(solution)/shard_map/ppermute | solution.py:262
  63.2 19.7 %collective-permute-start.7 = (bf16[2,6,12,1024]{3,1,2,0:T(8,128)(2,1)S(1)}, bf16[2,6,12,1024]{3,1,2,0:T(8,128)(2,1)}, u32[]{:S(2)}, u32[]{:S(2)}) collective-permute-start(bf16[2,6,12,1024]{3,1,2,0:T(8,128)(2,1)S(1)} %pad_maximum_fusion.2), channel_id=1, source_target_pairs={{2,1},{3,0},{4,3},{5,2},{6,5},{7,4},{8,7},{9,6},{10,9},{11,8},{12,... | collective-permute-start | bytes 884744 | tf_op jit(solution)/shard_map/ppermute | solution.py:146
  65.4 20.8 %collective-permute-start.11 = (bf16[2,6,12,1024]{3,1,2,0:T(8,128)(2,1)}, bf16[2,6,12,1024]{3,1,2,0:T(8,128)(2,1)}, u32[]{:S(2)}, u32[]{:S(2)}) collective-permute-start(bf16[2,6,12,1024]{3,1,2,0:T(8,128)(2,1)} %pad_maximum_fusion.3), channel_id=1, source_target_pairs={{0,3},{1,2},{2,5},{3,4},{4,7},{5,6},{6,9},{7,8},{8,11},{9,10},{10,... | collective-permute-start | bytes 884744 | tf_op jit(solution)/shard_map/ppermute | solution.py:146
  71.6 0.7 copy-start.7
  72.6 28.4 %collective-permute-start.10 = (bf16[2,8,20,1024]{3,1,2,0:T(8,128)(2,1)S(1)}, bf16[2,8,20,1024]{3,1,2,0:T(8,128)(2,1)S(1)}, u32[]{:S(2)}, u32[]{:S(2)}) collective-permute-start(bf16[2,8,20,1024]{3,1,2,0:T(8,128)(2,1)S(1)} %pad_maximum_fusion.1), channel_id=1, source_target_pairs={{0,1},{1,0},{2,3},{3,2},{4,5},{5,4},{6,7},{7,6},{8,9},{9,8},{10,11... | collective-permute-start | bytes 1966088 | tf_op jit(solution)/shard_map/ppermute | solution.py:146
  78.5 30.2 %collective-permute-start.12 = (bf16[2,6,16,1024]{3,1,2,0:T(8,128)(2,1)}, bf16[2,6,16,1024]{3,1,2,0:T(8,128)(2,1)}, u32[]{:S(2)}, u32[]{:S(2)}) collective-permute-start(bf16[2,6,16,1024]{3,1,2,0:T(8,128)(2,1)} %copy.65), channel_id=1, source_target_pairs={{0,2},{1,3},{2,4},{3,5},{4,6},{5,7},{6,8},{7,9},{8,10},{9,11},{10,... | collective-permute-start | bytes 1179656 | tf_op jit(solution)/shard_map/ppermute | solution.py:146
  82.9 25.9 %collective-permute-start.8 = (bf16[2,6,16,1024]{3,1,2,0:T(8,128)(2,1)S(1)}, bf16[2,6,16,1024]{3,1,2,0:T(8,128)(2,1)}, u32[]{:S(2)}, u32[]{:S(2)}) collective-permute-start(bf16[2,6,16,1024]{3,1,2,0:T(8,128)(2,1)S(1)} %copy.60), channel_id=1, source_target_pairs={{2,0},{3,1},{4,2},{5,3},{6,4},{7,5},{8,6},{9,7},{10,8},{11,9},{12,... | collective-permute-start | bytes 1179656 | tf_op jit(solution)/shard_map/ppermute | solution.py:146
  103.7 19.3 %all-to-all-start = ((bf16[8,64,512]{2,1,0:T(8,128)(2,1)}), bf16[8,64,512]{2,1,0:T(8,128)(2,1)S(1)}, u32[]{:S(2)}, u32[]{:S(2)}) async-start(bf16[8,64,512]{2,1,0:T(8,128)(2,1)} %bitcast.39), calls=%async_computation | async-start | bytes 1048576 | tf_op jit(solution)/shard_map/all_to_all | solution.py:458
  108.8 2.6 %copy-start.9 = (bf16[128,1024]{1,0:T(8,128)(2,1)S(1)}, bf16[128,1024]{1,0:T(8,128)(2,1)}, u32[]{:S(2)}) copy-start(bf16[128,1024]{1,0:T(8,128)(2,1)} %get-tuple-element.6) | copy-start | bytes 786436

commit v15 on v11

--- a/solution.py
+++ b/solution.py
@@ -4,6 +4,7 @@
 import jax.numpy as jnp
 from jax import lax
 from jax.experimental import pallas as pl
+from jax.experimental.pallas import tpu as pltpu
 from jax.sharding import PartitionSpec as P
 
 HEADS = 16
@@ -39,14 +40,16 @@
     return block
 
 
-def attention_kernel(q_ref, k_ref, v_ref, g_ref, bias_ref, att_ref, gq_ref, gkv_ref, gkv_low_ref,
+def attention_kernel(q_ref, proj_ref, g_ref, bias_ref, att_ref, gq_ref, gkv_ref, gkv_low_ref,
                      *, head_dim, scale):
     q = q_ref[...]
     g = g_ref[...]
-    k = k_ref[...]
-    v = v_ref[...]
+    lanes = q.shape[1]
+    width = proj_ref.shape[1] // 3
+    pair = pl.program_id(0)
+    k = proj_ref[:, pl.ds(pl.multiple_of(width + pair * lanes, lanes), lanes)]
+    v = proj_ref[:, pl.ds(pl.multiple_of(2 * width + pair * lanes, lanes), lanes)]
     bias = bias_ref[...]
-    lanes = q.shape[1]
     lane = lax.broadcasted_iota(jnp.int32, (1, lanes), 1)
     zero = jnp.zeros((), q.dtype)
     sels = [(lane >= j * head_dim) & (lane < (j + 1) * head_dim) for j in range(lanes // head_dim)]
@@ -108,8 +111,7 @@
         grid=(pairs,),
         in_specs=[
             pl.BlockSpec((queries, lanes), lambda h: (0, h)),
-            pl.BlockSpec((keys, lanes), lambda h: (0, h + pairs)),
-            pl.BlockSpec((keys, lanes), lambda h: (0, h + 2 * pairs)),
+            pl.BlockSpec(memory_space=pltpu.VMEM),
             pl.BlockSpec((queries, lanes), lambda h: (0, h)),
             pl.BlockSpec((queries, keys), lambda h: (0, 0)),
         ],
@@ -127,7 +129,7 @@
         ],
         cost_estimate=cost,
         name="block_attention",
-    )(query, projected, projected, grad_attn, bias)
+    )(query, projected, grad_attn, bias)
 
 
 def grid_pairs(delta_lat, delta_lon):

time: 123 us -> 124 us (level)
  no operation moved by 1% of the time
where the time goes in v15:
time: 124 us; the launch traced here: 123 us
  starting transfers between devices  37.9 us (31%)
  waiting for transfers between devices  29.7 us (24%)
  local copies, waits for them, and re-layouts  19 us (15%)
  matrix products  14.1 us (11%)
  Pallas kernels  12.5 us (10%)
  other arithmetic  8.53 us (7%)
    ppermute x10, starting transfers between devices, sent_to(): return lax.ppermute(value, ('lat', 'lon'), grid_pairs(delta_lat, delta_lon))  30.3 us
    ppermute x10, waiting for transfers between devices, sent_to(): return lax.ppermute(value, ('lat', 'lon'), grid_pairs(delta_lat, delta_lon))  23.1 us
    pallas_call x1, Pallas kernels, block_attention(): pl.pallas_call(kernel, grid=(pairs,), in_specs=[pl.BlockSpec((queries, la...  12.5 us
    all_to_all x1, waiting for transfers between devices, shards(): lax.all_to_all(partial.astype(jnp.bfloat16), 'lat', 0, 0, tiled=True)  6.54 us
    all_to_all x1, starting transfers between devices, shards(): lax.all_to_all(partial.astype(jnp.bfloat16), 'lat', 0, 0, tiled=True)  6.33 us
    unnamed x31, local copies, waits for them, and re-layouts  4.56 us
    slice x3, local copies, waits for them, and re-layouts, halo_return(): pieces.append((da, db, ext_low[:, row_slices[da], col_slices[db]]))  4.33 us
    dot_general x1, matrix products, project(): jnp.dot(columns(rows, 1 - dp_index, rows_half), qkv_other, preferred_elem...  4.19 us
  transfers between devices with their start and end apart: 15, of which 5 were waited for; matrix products, arithmetic and copies ran while one was open for 30% of the time, Pallas kernels for 10%

profile of v15, /device:TPU:0, one launch (start us, length us, event | category | flops | bytes accessed | tf_op | source)
XLA Modules:
  0.0 122.9 jit_solution(17301219051082547467)
XLA Ops:
  0.7 1.1 fusion.71
  1.8 0.1 pad_maximum_fusion.7
  1.9 3.0 %collective-permute-start.2 = (bf16[8,12,1024]{2,1,0:T(8,128)(2,1)S(1)}, bf16[8,12,1024]{2,1,0:T(8,128)(2,1)S(1)}, u32[]{:S(2)}, u32[]{:S(2)}) collective-permute-start(bf16[8,12,1024]{2,1,0:T(8,128)(2,1)S(1)} %pad_maximum_fusion.7), channel_id=1, source_target_pairs={{0,1},{1,0},{2,3},{3,2},{4,5},{5,4},{6,7},{7,6},{8,9},{9,8},{10,11... | collective-permute-start | bytes 589832 | tf_op jit(solution)/shard_map/ppermute | solution.py:148
  4.9 1.1 fusion.70
  6.1 1.3 %collective-permute-start.3 = (bf16[6,12,1024]{2,1,0:T(8,128)(2,1)S(1)}, bf16[6,12,1024]{2,1,0:T(8,128)(2,1)S(1)}, u32[]{:S(2)}, u32[]{:S(2)}) collective-permute-start(bf16[6,12,1024]{2,1,0:T(8,128)(2,1)S(1)} %pad_maximum_fusion.11), channel_id=1, source_target_pairs={{2,1},{3,0},{4,3},{5,2},{6,5},{7,4},{8,7},{9,6},{10,9},{11,8},{12,... | collective-permute-start | bytes 442376 | tf_op jit(solution)/shard_map/ppermute | solution.py:148
  7.4 5.5 %collective-permute-start = (bf16[6,12,1024]{2,1,0:T(8,128)(2,1)S(1)}, bf16[6,12,1024]{2,1,0:T(8,128)(2,1)S(1)}, u32[]{:S(2)}, u32[]{:S(2)}) collective-permute-start(bf16[6,12,1024]{2,1,0:T(8,128)(2,1)S(1)} %pad_maximum_fusion.10), channel_id=1, source_target_pairs={{0,3},{1,2},{2,5},{3,4},{4,7},{5,6},{6,9},{7,8},{8,11},{9,10},{10,... | collective-permute-start | bytes 442376 | tf_op jit(solution)/shard_map/ppermute | solution.py:148
  12.9 0.7 slice_bitcast_fusion.1
  13.6 4.3 %collective-permute-start.1 = (bf16[6,16,1024]{2,1,0:T(8,128)(2,1)}, bf16[6,16,1024]{2,1,0:T(8,128)(2,1)S(1)}, u32[]{:S(2)}, u32[]{:S(2)}) collective-permute-start(bf16[6,16,1024]{2,1,0:T(8,128)(2,1)} %get-tuple-element.32), channel_id=1, source_target_pairs={{0,2},{1,3},{2,4},{3,5},{4,6},{5,7},{6,8},{7,9},{8,10},{9,11},{10,... | collective-permute-start | bytes 589832 | tf_op jit(solution)/shard_map/ppermute | solution.py:148
  18.2 0.1 copy.40
  18.3 0.1 copy.42
  18.6 0.1 eq.28
  18.6 1.0 fusion.45.bias_ref
  19.7 0.5 convolution_convert_fusion.1
  20.2 0.7 constant_dynamic-slice_fusion.3
  20.9 0.1 pad_maximum_fusion
  21.0 1.6 %collective-permute-start.4 = (bf16[6,16,1024]{2,1,0:T(8,128)(2,1)S(1)}, bf16[6,16,1024]{2,1,0:T(8,128)(2,1)S(1)}, u32[]{:S(2)}, u32[]{:S(2)}) collective-permute-start(bf16[6,16,1024]{2,1,0:T(8,128)(2,1)S(1)} %get-tuple-element.33), channel_id=1, source_target_pairs={{2,0},{3,1},{4,2},{5,3},{6,4},{7,5},{8,6},{9,7},{10,8},{11,9},{12,... | collective-permute-start | bytes 589832 | tf_op jit(solution)/shard_map/ppermute | solution.py:148
  22.6 0.5 collective-permute-start.6
  23.2 0.5 collective-permute-done.1
  23.7 6.7 %collective-permute-done.4 = bf16[6,16,1024]{2,1,0:T(8,128)(2,1)S(1)} collective-permute-done((bf16[6,16,1024]{2,1,0:T(8,128)(2,1)S(1)}, bf16[6,16,1024]{2,1,0:T(8,128)(2,1)S(1)}, u32[]{:S(2)}, u32[]{:S(2)}) %collective-permute-start.4) | collective-permute-done | bytes 196640 | tf_op jit(solution)/shard_map/ppermute | solution.py:148
  30.4 0.7 fusion.12
  31.2 2.2 %fusion.29 = f32[640,3072]{1,0:T(8,128)S(1)} fusion(bf16[512,3072]{1,0:T(8,128)(2,1)S(1)} %copy-done.2, bf16[640,1024]{1,0:T(8,128)(2,1)S(1)} %bitcast.30, s32[]{:T(128)S(6)} %select_n.95), kind=kOutput, calls=%fused_computation.41 | convolution fusion | flops 2013265920 | bytes 11665412 | tf_op jit(solution)/shard_map/dot_general | solution.py:369
  33.4 0.7 constant_dynamic-slice_fusion.2
  34.1 0.7 pad_maximum_fusion.9
  34.9 0.5 collective-permute-start.13
  35.4 0.5 fusion.18
  35.9 0.8 maximum_select_fusion.g_ref
  36.7 4.2 %add_convert_fusion.proj_ref = bf16[640,3072]{1,0:T(8,128)(2,1)S(1)} fusion(f32[640,3072]{1,0:T(8,128)S(1)} %fusion.29, bf16[512,3072]{1,0:T(8,128)(2,1)} %collective-permute-done.5, bf16[640,1024]{1,0:T(8,128)(2,1)S(1)} %bitcast.31, s32[]{:T(128)S(6)} %select_n.96), kind=kOutput, calls=%fused_computation | convolution fusion | flops 2017198080 | bytes 15597572 | tf_op jit(solution)/shard_map/dot_general | solution.py:372
  40.9 1.9 %copy-done.9 = bf16[640,3072]{1,0:T(8,128)(2,1)} copy-done((bf16[640,3072]{1,0:T(8,128)(2,1)}, bf16[640,3072]{1,0:T(8,128)(2,1)S(1)}, u32[]{:S(2)}) %copy-start.9) | copy-done | bytes 3932184
  42.8 0.8 slice.181
  43.6 12.5 %block_attention.1 = (bf16[128,1024]{1,0:T(8,128)(2,1)}, bf16[128,1024]{1,0:T(8,128)(2,1)}, f32[2,640,1024]{2,1,0:T(8,128)}, bf16[2,640,1024]{2,1,0:T(8,128)(2,1)}) custom-call(bf16[128,1024]{1,0:T(8,128)(2,1)} %bitcast.42, bf16[640,3072]{1,0:T(8,128)(2,1)} %copy-done.9, bf16[128,1024]{1,0:T(8,128)(2,1)} %maximum_select_fusion.g_ref, f32[128,640]{1,0:T(8,128)} %fusion.45.bias_ref), custom_call_target="tpu_custom_call" | custom-call | flops 2013265920 | bytes 9240576 | tf_op jit(solution)/shard_map/block_attention/pallas_call | solution.py:109
  56.1 1.3 %fusion.64 = (bf16[2,8,6,1024]{3,2,1,0:T(8,128)(2,1)S(1)}, bf16[2,8,6,1024]{3,2,1,0:T(8,128)(2,1)S(1)}) fusion(bf16[2,20,32,1024]{3,2,1,0:T(8,128)(2,1)} %bitcast.36), kind=kLoop, calls=%fused_computation.109 | loop fusion | bytes 786432 | tf_op jit(solution)/shard_map/slice | solution.py:203
  57.4 1.5 %fusion.63 = (bf16[2,6,6,1024]{3,2,1,0:T(8,128)(2,1)S(1)}, bf16[2,6,6,1024]{3,2,1,0:T(8,128)(2,1)S(1)}, bf16[2,6,6,1024]{3,2,1,0:T(8,128)(2,1)S(1)}, bf16[2,6,6,1024]{3,2,1,0:T(8,128)(2,1)S(1)}) fusion(bf16[2,20,32,1024]{3,2,1,0:T(8,128)(2,1)} %bitcast.37), kind=kLoop, calls=%fused_computation.108 | loop fusion | bytes 1179648 | tf_op jit(solution)/shard_map/slice | solution.py:203
  59.0 0.1 copy.58
  59.3 0.1 copy.61
  59.4 0.1 copy.62
  59.7 1.3 %collective-permute-start.7 = (bf16[2,6,12,1024]{3,1,2,0:T(8,128)(2,1)S(1)}, bf16[2,6,12,1024]{3,1,2,0:T(8,128)(2,1)}, u32[]{:S(2)}, u32[]{:S(2)}) collective-permute-start(bf16[2,6,12,1024]{3,1,2,0:T(8,128)(2,1)S(1)} %pad_maximum_fusion.3), channel_id=1, source_target_pairs={{2,1},{3,0},{4,3},{5,2},{6,5},{7,4},{8,7},{9,6},{10,9},{11,8},{12,... | collective-permute-start | bytes 884744 | tf_op jit(solution)/shard_map/ppermute | solution.py:148
  61.0 0.8 pad_maximum_fusion.4
  61.8 6.2 %collective-permute-start.11 = (bf16[2,6,12,1024]{3,1,2,0:T(8,128)(2,1)}, bf16[2,6,12,1024]{3,1,2,0:T(8,128)(2,1)}, u32[]{:S(2)}, u32[]{:S(2)}) collective-permute-start(bf16[2,6,12,1024]{3,1,2,0:T(8,128)(2,1)} %pad_maximum_fusion.4), channel_id=1, source_target_pairs={{0,3},{1,2},{2,5},{3,4},{4,7},{5,6},{6,9},{7,8},{8,11},{9,10},{10,... | collective-permute-start | bytes 884744 | tf_op jit(solution)/shard_map/ppermute | solution.py:148
  68.0 0.7 copy-done.7
  68.7 0.1 reshape.154
  68.8 0.2 copy.49
  69.0 1.6 %collective-permute-start.10 = (bf16[2,8,20,1024]{3,1,2,0:T(8,128)(2,1)S(1)}, bf16[2,8,20,1024]{3,1,2,0:T(8,128)(2,1)S(1)}, u32[]{:S(2)}, u32[]{:S(2)}) collective-permute-start(bf16[2,8,20,1024]{3,1,2,0:T(8,128)(2,1)S(1)} %pad_maximum_fusion.2), channel_id=1, source_target_pairs={{0,1},{1,0},{2,3},{3,2},{4,5},{5,4},{6,7},{7,6},{8,9},{9,8},{10,11... | collective-permute-start | bytes 1966088 | tf_op jit(solution)/shard_map/ppermute | solution.py:148
  70.6 1.6 %fusion.62 = (bf16[2,6,16,1024]{3,2,1,0:T(8,128)(2,1)S(1)}, bf16[2,6,16,1024]{3,2,1,0:T(8,128)(2,1)S(1)}) fusion(bf16[2,20,32,1024]{3,2,1,0:T(8,128)(2,1)} %bitcast.38), kind=kLoop, calls=%fused_computation.107 | loop fusion | bytes 1572864 | tf_op jit(solution)/shard_map/slice | solution.py:203
  72.2 1.5 %slice.183 = f32[2,8,16,1024]{3,2,1,0:T(8,128)S(1)} slice(f32[2,20,32,1024]{3,2,1,0:T(8,128)} %bitcast.45), slice={[0:2], [6:14], [6:22], [0:1024]} | slice | bytes 2097152 | tf_op jit(solution)/shard_map/slice | solution.py:195
  73.7 0.2 copy.60
  74.0 1.0 copy.65
  75.0 4.4 %collective-permute-start.12 = (bf16[2,6,16,1024]{3,1,2,0:T(8,128)(2,1)}, bf16[2,6,16,1024]{3,1,2,0:T(8,128)(2,1)}, u32[]{:S(2)}, u32[]{:S(2)}) collective-permute-start(bf16[2,6,16,1024]{3,1,2,0:T(8,128)(2,1)} %copy.65), channel_id=1, source_target_pairs={{0,2},{1,3},{2,4},{3,5},{4,6},{5,7},{6,8},{7,9},{8,10},{9,11},{10,... | collective-permute-start | bytes 1179656 | tf_op jit(solution)/shard_map/ppermute | solution.py:148
  79.4 1.3 %collective-permute-start.8 = (bf16[2,6,16,1024]{3,1,2,0:T(8,128)(2,1)S(1)}, bf16[2,6,16,1024]{3,1,2,0:T(8,128)(2,1)}, u32[]{:S(2)}, u32[]{:S(2)}) collective-permute-start(bf16[2,6,16,1024]{3,1,2,0:T(8,128)(2,1)S(1)} %copy.60), channel_id=1, source_target_pairs={{2,0},{3,1},{4,2},{5,3},{6,4},{7,5},{8,6},{9,7},{10,8},{11,9},{12,... | collective-permute-start | bytes 1179656 | tf_op jit(solution)/shard_map/ppermute | solution.py:148
  80.7 1.1 fusion.67
  81.7 0.9 collective-permute-done.11
  82.6 1.0 fusion.68
  83.6 15.1 %collective-permute-done.10 = bf16[2,8,20,1024]{3,1,2,0:T(8,128)(2,1)S(1)} collective-permute-done((bf16[2,8,20,1024]{3,1,2,0:T(8,128)(2,1)S(1)}, bf16[2,8,20,1024]{3,1,2,0:T(8,128)(2,1)S(1)}, u32[]{:S(2)}, u32[]{:S(2)}) %collective-permute-start.10) | collective-permute-done | bytes 655392 | tf_op jit(solution)/shard_map/ppermute | solution.py:148
  98.8 0.2 copy.55
  98.9 0.1 reshape.155
  99.0 2.4 %fusion.17 = bf16[512,512]{1,0:T(8,128)(2,1)} fusion(bf16[256,512]{1,0:T(8,128)(2,1)S(1)} %reshape.155, bf16[128,512]{1,0:T(8,128)(2,1)} %copy-done.7, bf16[128,512]{1,0:T(8,128)(2,1)} %copy-done.5, bf16[256,512]{1,0:T(8,128)(2,1)} %collective-permute-done.13, bf16[128,512]{1,0:T(8,128)(2,1)} %get-tuple-element.28, bf16[128,512]{1,0:T(8,128)(2,1)} %get-tuple-element.26), kind=kOutput, calls=%fused_computation.21 | convolution fusion | flops 272105472 | bytes 1572864 | tf_op jit(solution)/shard_map/dot_general | solution.py:462
  101.5 6.3 %all-to-all-start = ((bf16[8,64,512]{2,1,0:T(8,128)(2,1)}), bf16[8,64,512]{2,1,0:T(8,128)(2,1)S(1)}, u32[]{:S(2)}, u32[]{:S(2)}) async-start(bf16[8,64,512]{2,1,0:T(8,128)(2,1)} %bitcast.39), calls=%async_computation | async-start | bytes 1048576 | tf_op jit(solution)/shard_map/all_to_all | solution.py:465
  107.9 2.3 %fusion.27 = bf16[2,8,16,1024]{3,1,2,0:T(8,128)(2,1)S(1)} fusion(f32[2,8,16,1024]{3,2,1,0:T(8,128)S(1)} %slice.183, bf16[2,6,6,1024]{3,1,2,0:T(8,128)(2,1)S(1)} %get-tuple-element.25, bf16[2,6,16,1024]{3,1,2,0:T(8,128)(2,1)} %collective-permute-done.12, bf16[2,6,6,1024]{3,1,2,0:T(8,128)(2,1)S(1)} %get-tuple-element.24, ...), kind=kLoop, calls=%fused_computation.36 | loop fusion | flops 4456448 | bytes 3342336 | tf_op jit(solution)/shard_map/convert_element_type | solution.py:468
  110.2 0.2 copy.53
  110.4 0.2 copy.54
  110.6 1.2 convolution_convert_fusion.3
  111.8 3.1 %convolution_convert_fusion.2 = bf16[128,512]{1,0:T(8,128)(2,1)S(1)} fusion(bf16[512,3072]{1,0:T(8,128)(2,1)} %collective-permute-done.5, bf16[128,1024]{1,0:T(8,128)(2,1)S(1)} %bitcast.44, bf16[128,1024]{1,0:T(8,128)(2,1)S(1)} %bitcast.41, bf16[128,1024]{1,0:T(8,128)(2,1)S(1)} %copy-done.10), kind=kOutput, calls=%fused_computation.24 | convolution fusion | flops 405078016 | bytes 4063232 | tf_op jit(solution)/shard_map/dot_general | solution.py:379
  114.8 0.8 maximum_select_fusion.1
  115.6 6.5 %all-to-all-done = bf16[8,64,512]{2,1,0:T(8,128)(2,1)S(1)} async-done(((bf16[8,64,512]{2,1,0:T(8,128)(2,1)}), bf16[8,64,512]{2,1,0:T(8,128)(2,1)S(1)}, u32[]{:S(2)}, u32[]{:S(2)}) %all-to-all-start) | async-done | bytes 524320 | tf_op jit(solution)/shard_map/all_to_all | solution.py:465
  122.2 0.7 convert_reduce_fusion
  (55 shorter events, 1.3 us)
Async XLA Ops:
  0.6 12.3 %copy-start = (bf16[1,8,16,1024]{3,2,1,0:T(8,128)(2,1)S(1)}, bf16[1,8,16,1024]{3,2,1,0:T(8,128)(2,1)}, u32[]{:S(2)}) copy-start(bf16[1,8,16,1024]{3,2,1,0:T(8,128)(2,1)} %param.5) | copy-start | bytes 786436
  0.6 17.4 %copy-start.8 = (s32[64,32]{0,1:T(8,128)S(1)}, s32[64,32]{0,1:T(8,128)}, u32[]{:S(2)}) copy-start(s32[64,32]{0,1:T(8,128)} %param.7) | copy-start | bytes 24580
  0.7 19.0 %copy-start.1 = (bf16[512,1024]{1,0:T(8,128)(2,1)S(1)}, bf16[512,1024]{1,0:T(8,128)(2,1)}, u32[]{:S(2)}) copy-start(bf16[512,1024]{1,0:T(8,128)(2,1)} %param.9) | copy-start | bytes 3145732
  0.7 19.0 %copy-start.4 = (bf16[1,8,16,1024]{3,2,1,0:T(8,128)(2,1)S(1)}, bf16[1,8,16,1024]{3,2,1,0:T(8,128)(2,1)}, u32[]{:S(2)}) copy-start(bf16[1,8,16,1024]{3,2,1,0:T(8,128)(2,1)} %param.6) | copy-start | bytes 786436
  1.9 21.3 %collective-permute-start.2 = (bf16[8,12,1024]{2,1,0:T(8,128)(2,1)S(1)}, bf16[8,12,1024]{2,1,0:T(8,128)(2,1)S(1)}, u32[]{:S(2)}, u32[]{:S(2)}) collective-permute-start(bf16[8,12,1024]{2,1,0:T(8,128)(2,1)S(1)} %pad_maximum_fusion.7), channel_id=1, source_target_pairs={{0,1},{1,0},{2,3},{3,2},{4,5},{5,4},{6,7},{7,6},{8,9},{9,8},{10,11... | collective-permute-start | bytes 589832 | tf_op jit(solution)/shard_map/ppermute | solution.py:148
  6.1 14.9 %collective-permute-start.3 = (bf16[6,12,1024]{2,1,0:T(8,128)(2,1)S(1)}, bf16[6,12,1024]{2,1,0:T(8,128)(2,1)S(1)}, u32[]{:S(2)}, u32[]{:S(2)}) collective-permute-start(bf16[6,12,1024]{2,1,0:T(8,128)(2,1)S(1)} %pad_maximum_fusion.11), channel_id=1, source_target_pairs={{2,1},{3,0},{4,3},{5,2},{6,5},{7,4},{8,7},{9,6},{10,9},{11,8},{12,... | collective-permute-start | bytes 442376 | tf_op jit(solution)/shard_map/ppermute | solution.py:148
  7.4 15.1 %collective-permute-start = (bf16[6,12,1024]{2,1,0:T(8,128)(2,1)S(1)}, bf16[6,12,1024]{2,1,0:T(8,128)(2,1)S(1)}, u32[]{:S(2)}, u32[]{:S(2)}) collective-permute-start(bf16[6,12,1024]{2,1,0:T(8,128)(2,1)S(1)} %pad_maximum_fusion.10), channel_id=1, source_target_pairs={{0,3},{1,2},{2,5},{3,4},{4,7},{5,6},{6,9},{7,8},{8,11},{9,10},{10,... | collective-permute-start | bytes 442376 | tf_op jit(solution)/shard_map/ppermute | solution.py:148
  13.6 10.1 %collective-permute-start.1 = (bf16[6,16,1024]{2,1,0:T(8,128)(2,1)}, bf16[6,16,1024]{2,1,0:T(8,128)(2,1)S(1)}, u32[]{:S(2)}, u32[]{:S(2)}) collective-permute-start(bf16[6,16,1024]{2,1,0:T(8,128)(2,1)} %get-tuple-element.32), channel_id=1, source_target_pairs={{0,2},{1,3},{2,4},{3,5},{4,6},{5,7},{6,8},{7,9},{8,10},{9,11},{10,... | collective-permute-start | bytes 589832 | tf_op jit(solution)/shard_map/ppermute | solution.py:148
  18.0 18.7 %collective-permute-start.5 = (bf16[512,3072]{1,0:T(8,128)(2,1)}, bf16[512,3072]{1,0:T(8,128)(2,1)}, u32[]{:S(2)}, u32[]{:S(2)}) collective-permute-start(bf16[512,3072]{1,0:T(8,128)(2,1)} %param.8), channel_id=1, source_target_pairs={{0,16},{16,0},{1,17},{17,1},{2,18},{18,2},{3,19},{19,3},{4,20},{20... | collective-permute-start | bytes 9437192 | tf_op jit(solution)/shard_map/ppermute | solution.py:264
  20.9 10.2 %copy-start.2 = (bf16[512,3072]{1,0:T(8,128)(2,1)S(1)}, bf16[512,3072]{1,0:T(8,128)(2,1)}, u32[]{:S(2)}) copy-start(bf16[512,3072]{1,0:T(8,128)(2,1)} %param.8) | copy-start | bytes 9437188
  21.0 9.4 %collective-permute-start.4 = (bf16[6,16,1024]{2,1,0:T(8,128)(2,1)S(1)}, bf16[6,16,1024]{2,1,0:T(8,128)(2,1)S(1)}, u32[]{:S(2)}, u32[]{:S(2)}) collective-permute-start(bf16[6,16,1024]{2,1,0:T(8,128)(2,1)S(1)} %get-tuple-element.33), channel_id=1, source_target_pairs={{2,0},{3,1},{4,2},{5,3},{6,4},{7,5},{8,6},{9,7},{10,8},{11,9},{12,... | collective-permute-start | bytes 589832 | tf_op jit(solution)/shard_map/ppermute | solution.py:148
  22.6 10.8 %collective-permute-start.6 = (bf16[640,1024]{1,0:T(8,128)(2,1)S(1)}, bf16[640,1024]{1,0:T(8,128)(2,1)S(1)}, u32[]{:S(2)}, u32[]{:S(2)}) collective-permute-start(bf16[640,1024]{1,0:T(8,128)(2,1)S(1)} %pad_maximum_fusion), channel_id=1, source_target_pairs={{0,16},{16,0},{1,17},{17,1},{2,18},{18,2},{3,19},{19,3},{4,20},{20... | collective-permute-start | bytes 3932168 | tf_op jit(solution)/shard_map/ppermute | solution.py:264
  34.9 64.2 %collective-permute-start.13 = (bf16[256,512]{1,0:T(8,128)(2,1)}, bf16[256,512]{1,0:T(8,128)(2,1)}, u32[]{:S(2)}, u32[]{:S(2)}) collective-permute-start(bf16[256,512]{1,0:T(8,128)(2,1)} %pad_maximum_fusion.9), channel_id=1, source_target_pairs={{0,1},{1,0},{2,3},{3,2},{4,5},{5,4},{6,7},{7,6},{8,9},{9,8},{10,11... | collective-permute-start | bytes 786440 | tf_op jit(solution)/shard_map/ppermute | solution.py:264
  40.9 2.0 %copy-start.9 = (bf16[640,3072]{1,0:T(8,128)(2,1)}, bf16[640,3072]{1,0:T(8,128)(2,1)S(1)}, u32[]{:S(2)}) copy-start(bf16[640,3072]{1,0:T(8,128)(2,1)S(1)} %add_convert_fusion.proj_ref) | copy-start | bytes 11796484
  56.1 2.7 %copy-start.6 = (bf16[128,1024]{1,0:T(8,128)(2,1)S(1)}, bf16[128,1024]{1,0:T(8,128)(2,1)}, u32[]{:S(2)}) copy-start(bf16[128,1024]{1,0:T(8,128)(2,1)} %get-tuple-element.9) | copy-start | bytes 786436
  58.9 9.1 %copy-start.5 = (bf16[128,512]{1,0:T(8,128)(2,1)}, bf16[128,512]{1,0:T(8,128)(2,1)S(1)}, u32[]{:S(2)}) copy-start(bf16[128,512]{1,0:T(8,128)(2,1)S(1)} %get-tuple-element.30) | copy-start | bytes 393220
  58.9 9.1 %collective-permute-start.9 = (bf16[128,512]{1,0:T(8,128)(2,1)S(1)}, bf16[128,512]{1,0:T(8,128)(2,1)S(1)}, u32[]{:S(2)}, u32[]{:S(2)}) collective-permute-start(bf16[128,512]{1,0:T(8,128)(2,1)S(1)} %get-tuple-element.31), channel_id=1, source_target_pairs={{0,16},{16,0},{1,17},{17,1},{2,18},{18,2},{3,19},{19,3},{4,20},{20... | collective-permute-start | bytes 393224 | tf_op jit(solution)/shard_map/ppermute | solution.py:264
  59.7 19.7 %collective-permute-start.7 = (bf16[2,6,12,1024]{3,1,2,0:T(8,128)(2,1)S(1)}, bf16[2,6,12,1024]{3,1,2,0:T(8,128)(2,1)}, u32[]{:S(2)}, u32[]{:S(2)}) collective-permute-start(bf16[2,6,12,1024]{3,1,2,0:T(8,128)(2,1)S(1)} %pad_maximum_fusion.3), channel_id=1, source_target_pairs={{2,1},{3,0},{4,3},{5,2},{6,5},{7,4},{8,7},{9,6},{10,9},{11,8},{12,... | collective-permute-start | bytes 884744 | tf_op jit(solution)/shard_map/ppermute | solution.py:148
  61.8 20.8 %collective-permute-start.11 = (bf16[2,6,12,1024]{3,1,2,0:T(8,128)(2,1)}, bf16[2,6,12,1024]{3,1,2,0:T(8,128)(2,1)}, u32[]{:S(2)}, u32[]{:S(2)}) collective-permute-start(bf16[2,6,12,1024]{3,1,2,0:T(8,128)(2,1)} %pad_maximum_fusion.4), channel_id=1, source_target_pairs={{0,3},{1,2},{2,5},{3,4},{4,7},{5,6},{6,9},{7,8},{8,11},{9,10},{10,... | collective-permute-start | bytes 884744 | tf_op jit(solution)/shard_map/ppermute | solution.py:148
  68.0 0.7 copy-start.7
  69.0 29.7 %collective-permute-start.10 = (bf16[2,8,20,1024]{3,1,2,0:T(8,128)(2,1)S(1)}, bf16[2,8,20,1024]{3,1,2,0:T(8,128)(2,1)S(1)}, u32[]{:S(2)}, u32[]{:S(2)}) collective-permute-start(bf16[2,8,20,1024]{3,1,2,0:T(8,128)(2,1)S(1)} %pad_maximum_fusion.2), channel_id=1, source_target_pairs={{0,1},{1,0},{2,3},{3,2},{4,5},{5,4},{6,7},{7,6},{8,9},{9,8},{10,11... | collective-permute-start | bytes 1966088 | tf_op jit(solution)/shard_map/ppermute | solution.py:148
  75.0 32.8 %collective-permute-start.12 = (bf16[2,6,16,1024]{3,1,2,0:T(8,128)(2,1)}, bf16[2,6,16,1024]{3,1,2,0:T(8,128)(2,1)}, u32[]{:S(2)}, u32[]{:S(2)}) collective-permute-start(bf16[2,6,16,1024]{3,1,2,0:T(8,128)(2,1)} %copy.65), channel_id=1, source_target_pairs={{0,2},{1,3},{2,4},{3,5},{4,6},{5,7},{6,8},{7,9},{8,10},{9,11},{10,... | collective-permute-start | bytes 1179656 | tf_op jit(solution)/shard_map/ppermute | solution.py:148
  79.4 28.4 %collective-permute-start.8 = (bf16[2,6,16,1024]{3,1,2,0:T(8,128)(2,1)S(1)}, bf16[2,6,16,1024]{3,1,2,0:T(8,128)(2,1)}, u32[]{:S(2)}, u32[]{:S(2)}) collective-permute-start(bf16[2,6,16,1024]{3,1,2,0:T(8,128)(2,1)S(1)} %copy.60), channel_id=1, source_target_pairs={{2,0},{3,1},{4,2},{5,3},{6,4},{7,5},{8,6},{9,7},{10,8},{11,9},{12,... | collective-permute-start | bytes 1179656 | tf_op jit(solution)/shard_map/ppermute | solution.py:148
  101.5 20.7 %all-to-all-start = ((bf16[8,64,512]{2,1,0:T(8,128)(2,1)}), bf16[8,64,512]{2,1,0:T(8,128)(2,1)S(1)}, u32[]{:S(2)}, u32[]{:S(2)}) async-start(bf16[8,64,512]{2,1,0:T(8,128)(2,1)} %bitcast.39), calls=%async_computation | async-start | bytes 1048576 | tf_op jit(solution)/shard_map/all_to_all | solution.py:465
  107.8 2.7 %copy-start.3 = (bf16[512,3072]{1,0:T(8,128)(2,1)S(1)}, bf16[512,3072]{1,0:T(8,128)(2,1)}, u32[]{:S(2)}) copy-start(bf16[512,3072]{1,0:T(8,128)(2,1)} %param.8) | copy-start | bytes 9437188
  107.9 2.7 %copy-start.10 = (bf16[128,1024]{1,0:T(8,128)(2,1)S(1)}, bf16[128,1024]{1,0:T(8,128)(2,1)}, u32[]{:S(2)}) copy-start(bf16[128,1024]{1,0:T(8,128)(2,1)} %get-tuple-element.6) | copy-start | bytes 786436

commit v16 on v11

--- a/solution.py
+++ b/solution.py
@@ -335,7 +335,8 @@
 
     if fast:
         qkv_other = swap(w_qkv, "dp")
-        dp_got = swap(jnp.concatenate([w_out, flat_grad], axis=0), "dp")
+        dp_all = lax.all_gather(jnp.concatenate([w_out, flat_grad], axis=0), "dp", axis=0)
+        dp_got = lax.dynamic_index_in_dim(dp_all, 1 - dp_index, 0, keepdims=False)
         w_out_other = dp_got[: w_out.shape[0]]
         cot_dp = dp_got[w_out.shape[0] :]
         cot_send = jnp.concatenate(

time: 123 us -> 144 us (1.17)
  between operations: 1.2 us -> 14.6 us
  matrix products: 14.1 us -> 20.5 us
    dot_general x1, matrix products: 2.23 us -> 5.29 us  [project(): jnp.dot(columns(rows, dp_index, rows_half), w_qkv, preferred_element_type...]
    dot_general x1, matrix products: 4.19 us -> 6.41 us  [project(): jnp.dot(columns(rows, 1 - dp_index, rows_half), qkv_other, preferred_elem...]
    unnamed x31 -> x29, local copies, waits for them, and re-layouts: 4.56 us -> 4.7 us
  transfers between devices with their start and end apart: 15 -> 15, of which waited for: 5 -> 4; matrix products, arithmetic and copies ran while one was open for 30% -> 31% of each run, Pallas kernels for 10% -> 8%
where the time goes in v16:
time: 144 us; the launch traced here: 143 us
  starting transfers between devices  37.8 us (26%)
  waiting for transfers between devices  30.1 us (21%)
  matrix products  20.5 us (14%)
  local copies, waits for them, and re-layouts  19 us (13%)
  between operations  14.6 us (10%)
  Pallas kernels  12 us (8%)
  other arithmetic  8.97 us (6%)
    ppermute x10, starting transfers between devices, sent_to(): return lax.ppermute(value, ('lat', 'lon'), grid_pairs(delta_lat, delta_lon))  30.2 us
    ppermute x10, waiting for transfers between devices, sent_to(): return lax.ppermute(value, ('lat', 'lon'), grid_pairs(delta_lat, delta_lon))  23.5 us
    pallas_call x1, Pallas kernels, block_attention(): pl.pallas_call(kernel, grid=(pairs,), in_specs=[pl.BlockSpec((queries, la...  12 us
    all_to_all x1, starting transfers between devices, shards(): lax.all_to_all(partial.astype(jnp.bfloat16), 'lat', 0, 0, tiled=True)  6.81 us
    all_to_all x1, waiting for transfers between devices, shards(): lax.all_to_all(partial.astype(jnp.bfloat16), 'lat', 0, 0, tiled=True)  6.54 us
    dot_general x1, matrix products, project(): jnp.dot(columns(rows, 1 - dp_index, rows_half), qkv_other, preferred_elem...  6.41 us
    dot_general x1, matrix products, project(): jnp.dot(columns(rows, dp_index, rows_half), w_qkv, preferred_element_type...  5.29 us
    unnamed x29, local copies, waits for them, and re-layouts  4.7 us
  transfers between devices with their start and end apart: 15, of which 4 were waited for; matrix products, arithmetic and copies ran while one was open for 31% of the time, Pallas kernels for 8%

profile of v16, /device:TPU:0, one launch (start us, length us, event | category | flops | bytes accessed | tf_op | source)
XLA Modules:
  0.0 142.9 jit_solution(17430502890682802115)
XLA Ops:
  7.2 1.1 fusion.71
  8.4 0.1 pad_maximum_fusion.7
  8.5 3.0 %collective-permute-start.2 = (bf16[8,12,1024]{2,1,0:T(8,128)(2,1)S(1)}, bf16[8,12,1024]{2,1,0:T(8,128)(2,1)S(1)}, u32[]{:S(2)}, u32[]{:S(2)}) collective-permute-start(bf16[8,12,1024]{2,1,0:T(8,128)(2,1)S(1)} %pad_maximum_fusion.7), channel_id=1, source_target_pairs={{0,1},{1,0},{2,3},{3,2},{4,5},{5,4},{6,7},{7,6},{8,9},{9,8},{10,11... | collective-permute-start | bytes 589832 | tf_op jit(solution)/shard_map/ppermute | solution.py:146
  11.5 1.1 fusion.70
  12.6 1.3 collective-permute-start.3
  14.0 5.5 %collective-permute-start = (bf16[6,12,1024]{2,1,0:T(8,128)(2,1)S(1)}, bf16[6,12,1024]{2,1,0:T(8,128)(2,1)S(1)}, u32[]{:S(2)}, u32[]{:S(2)}) collective-permute-start(bf16[6,12,1024]{2,1,0:T(8,128)(2,1)S(1)} %pad_maximum_fusion.10), channel_id=1, source_target_pairs={{0,3},{1,2},{2,5},{3,4},{4,7},{5,6},{6,9},{7,8},{8,11},{9,10},{10,... | collective-permute-start | bytes 442376 | tf_op jit(solution)/shard_map/ppermute | solution.py:146
  19.5 0.7 slice_bitcast_fusion.1
  20.2 4.3 %collective-permute-start.1 = (bf16[6,16,1024]{2,1,0:T(8,128)(2,1)}, bf16[6,16,1024]{2,1,0:T(8,128)(2,1)S(1)}, u32[]{:S(2)}, u32[]{:S(2)}) collective-permute-start(bf16[6,16,1024]{2,1,0:T(8,128)(2,1)} %get-tuple-element.32), channel_id=1, source_target_pairs={{0,2},{1,3},{2,4},{3,5},{4,6},{5,7},{6,8},{7,9},{8,10},{9,11},{10,... | collective-permute-start | bytes 589832 | tf_op jit(solution)/shard_map/ppermute | solution.py:146
  24.6 1.2 pad_maximum_fusion
  26.0 0.1 copy.40
  26.1 0.1 copy.42
  26.2 0.1 pad_add_fusion
  26.3 0.1 pad_dynamic-slice_fusion
  26.4 0.1 eq.28
  26.5 0.5 convolution_convert_fusion.1
  27.0 1.0 fusion.44.bias_ref
  28.0 0.7 constant_dynamic-slice_fusion.1
  28.7 1.4 collective-permute-start.4
  30.3 7.7 %collective-permute-done.4 = bf16[6,16,1024]{2,1,0:T(8,128)(2,1)S(1)} collective-permute-done((bf16[6,16,1024]{2,1,0:T(8,128)(2,1)S(1)}, bf16[6,16,1024]{2,1,0:T(8,128)(2,1)S(1)}, u32[]{:S(2)}, u32[]{:S(2)}) %collective-permute-start.4) | collective-permute-done | bytes 196640 | tf_op jit(solution)/shard_map/ppermute | solution.py:146
  38.0 0.7 fusion.12
  38.7 5.3 %fusion.28 = f32[640,3072]{1,0:T(8,128)} fusion(bf16[512,3072]{1,0:T(8,128)(2,1)S(1)} %copy-done.4, bf16[640,1024]{1,0:T(8,128)(2,1)S(1)} %bitcast.43, s32[]{:T(128)S(6)} %select_n.99), kind=kOutput, calls=%fused_computation.41 | convolution fusion | flops 2013265920 | bytes 11665412 | tf_op jit(solution)/shard_map/dot_general | solution.py:368
  44.0 1.6 %dynamic-slice_bitcast_fusion.3 = (bf16[128,512]{1,0:T(8,128)(2,1)}, bf16[128,512]{1,0:T(8,128)(2,1)S(1)}) fusion(bf16[2,640,1024]{2,1,0:T(8,128)(2,1)} %bitcast.49, s32[]{:T(128)S(6)} %select_n.102, s32[]{:T(128)S(6)} %add.142, s32[]{:T(128)S(6)} %select_n.112, s32[]{:T(128)S(6)} %select_n.113), kind=kLoop, calls=%fused_computation.76 | loop fusion | bytes 524304 | tf_op jit(solution)/shard_map/dynamic_slice | solution.py:266
  45.7 0.6 collective-permute-start.12
  46.3 1.7 %fusion.18 = bf16[128,512]{1,0:T(8,128)(2,1)S(1)} fusion(bf16[128,1024]{1,0:T(8,128)(2,1)S(1)} %bitcast.42, bf16[2,640,1024]{2,1,0:T(8,128)(2,1)} %bitcast.50, s32[]{:T(128)S(6)} %select_n.102), kind=kOutput, calls=%fused_computation.26 | convolution fusion | flops 134283264 | bytes 1441796 | tf_op jit(solution)/shard_map/dot_general | solution.py:356
  48.0 0.8 maximum_select_fusion.g_ref
  48.8 6.4 %add_convert_fusion.k_ref.v_ref = bf16[640,3072]{1,0:T(8,128)(2,1)S(1)} fusion(f32[640,3072]{1,0:T(8,128)} %fusion.28, bf16[512,3072]{1,0:T(8,128)(2,1)} %collective-permute-done.5, bf16[640,1024]{1,0:T(8,128)(2,1)S(1)} %bitcast.44, s32[]{:T(128)S(6)} %select_n.100), kind=kOutput, calls=%fused_computation | convolution fusion | flops 2017198080 | bytes 15597572 | tf_op jit(solution)/shard_map/dot_general | solution.py:371
  55.2 1.9 %copy-done = bf16[640,3072]{1,0:T(8,128)(2,1)} copy-done((bf16[640,3072]{1,0:T(8,128)(2,1)}, bf16[640,3072]{1,0:T(8,128)(2,1)S(1)}, u32[]{:S(2)}) %copy-start) | copy-done | bytes 3932184
  57.2 0.8 slice.186
  58.0 12.0 %block_attention.1 = (bf16[128,1024]{1,0:T(8,128)(2,1)}, bf16[128,1024]{1,0:T(8,128)(2,1)}, f32[2,640,1024]{2,1,0:T(8,128)}, bf16[2,640,1024]{2,1,0:T(8,128)(2,1)}) custom-call(bf16[128,1024]{1,0:T(8,128)(2,1)} %bitcast.48, bf16[640,3072]{1,0:T(8,128)(2,1)} %copy-done, bf16[640,3072]{1,0:T(8,128)(2,1)} %copy-done, ...), custom_call_target="tpu_custom_call" | custom-call | flops 2013265920 | bytes 9240576 | tf_op jit(solution)/shard_map/block_attention/pallas_call | solution.py:106
  69.9 1.3 fusion.64
  71.2 1.5 %fusion.63 = (bf16[2,6,6,1024]{3,2,1,0:T(8,128)(2,1)S(1)}, bf16[2,6,6,1024]{3,2,1,0:T(8,128)(2,1)S(1)}, bf16[2,6,6,1024]{3,2,1,0:T(8,128)(2,1)S(1)}, bf16[2,6,6,1024]{3,2,1,0:T(8,128)(2,1)S(1)}) fusion(bf16[2,20,32,1024]{3,2,1,0:T(8,128)(2,1)} %bitcast.46), kind=kLoop, calls=%fused_computation.109 | loop fusion | bytes 1179648 | tf_op jit(solution)/shard_map/slice | solution.py:201
  72.8 0.1 copy.58
  72.9 0.1 copy.59
  73.1 0.1 copy.61
  73.2 0.1 copy.62
  73.3 0.1 copy.64
  73.4 0.1 copy.63
  73.5 1.3 collective-permute-start.6
  74.8 0.8 pad_maximum_fusion.4
  75.6 6.2 %collective-permute-start.10 = (bf16[2,6,12,1024]{3,1,2,0:T(8,128)(2,1)}, bf16[2,6,12,1024]{3,1,2,0:T(8,128)(2,1)}, u32[]{:S(2)}, u32[]{:S(2)}) collective-permute-start(bf16[2,6,12,1024]{3,1,2,0:T(8,128)(2,1)} %pad_maximum_fusion.4), channel_id=1, source_target_pairs={{0,3},{1,2},{2,5},{3,4},{4,7},{5,6},{6,9},{7,8},{8,11},{9,10},{10,... | collective-permute-start | bytes 884744 | tf_op jit(solution)/shard_map/ppermute | solution.py:146
  81.8 0.1 reshape.158
  81.9 0.2 copy.49
  82.2 1.5 %collective-permute-start.9 = (bf16[2,8,20,1024]{3,1,2,0:T(8,128)(2,1)S(1)}, bf16[2,8,20,1024]{3,1,2,0:T(8,128)(2,1)S(1)}, u32[]{:S(2)}, u32[]{:S(2)}) collective-permute-start(bf16[2,8,20,1024]{3,1,2,0:T(8,128)(2,1)S(1)} %pad_maximum_fusion.2), channel_id=1, source_target_pairs={{0,1},{1,0},{2,3},{3,2},{4,5},{5,4},{6,7},{7,6},{8,9},{9,8},{10,11... | collective-permute-start | bytes 1966088 | tf_op jit(solution)/shard_map/ppermute | solution.py:146
  83.7 1.6 %fusion.62 = (bf16[2,6,16,1024]{3,2,1,0:T(8,128)(2,1)S(1)}, bf16[2,6,16,1024]{3,2,1,0:T(8,128)(2,1)S(1)}) fusion(bf16[2,20,32,1024]{3,2,1,0:T(8,128)(2,1)} %bitcast.47), kind=kLoop, calls=%fused_computation.108 | loop fusion | bytes 1572864 | tf_op jit(solution)/shard_map/slice | solution.py:201
  85.3 1.5 %slice.187 = f32[2,8,16,1024]{3,2,1,0:T(8,128)S(1)} slice(f32[2,20,32,1024]{3,2,1,0:T(8,128)} %bitcast.56), slice={[0:2], [6:14], [6:22], [0:1024]} | slice | bytes 2097152 | tf_op jit(solution)/shard_map/slice | solution.py:193
  86.9 1.0 copy.60
  87.9 1.0 copy.65
  88.9 4.4 %collective-permute-start.11 = (bf16[2,6,16,1024]{3,1,2,0:T(8,128)(2,1)}, bf16[2,6,16,1024]{3,1,2,0:T(8,128)(2,1)}, u32[]{:S(2)}, u32[]{:S(2)}) collective-permute-start(bf16[2,6,16,1024]{3,1,2,0:T(8,128)(2,1)} %copy.65), channel_id=1, source_target_pairs={{0,2},{1,3},{2,4},{3,5},{4,6},{5,7},{6,8},{7,9},{8,10},{9,11},{10,... | collective-permute-start | bytes 1179656 | tf_op jit(solution)/shard_map/ppermute | solution.py:146
  93.4 1.3 collective-permute-start.7
  94.7 1.7 %collective-permute-done.10 = bf16[2,6,12,1024]{3,1,2,0:T(8,128)(2,1)} collective-permute-done((bf16[2,6,12,1024]{3,1,2,0:T(8,128)(2,1)}, bf16[2,6,12,1024]{3,1,2,0:T(8,128)(2,1)}, u32[]{:S(2)}, u32[]{:S(2)}) %collective-permute-start.10) | collective-permute-done | bytes 294944 | tf_op jit(solution)/shard_map/ppermute | solution.py:146
  96.4 1.0 fusion.68
  97.4 14.1 %collective-permute-done.9 = bf16[2,8,20,1024]{3,1,2,0:T(8,128)(2,1)S(1)} collective-permute-done((bf16[2,8,20,1024]{3,1,2,0:T(8,128)(2,1)S(1)}, bf16[2,8,20,1024]{3,1,2,0:T(8,128)(2,1)S(1)}, u32[]{:S(2)}, u32[]{:S(2)}) %collective-permute-start.9) | collective-permute-done | bytes 655392 | tf_op jit(solution)/shard_map/ppermute | solution.py:146
  111.5 0.2 copy.55
  111.7 0.1 reshape.159
  111.8 2.4 %fusion.17 = bf16[512,512]{1,0:T(8,128)(2,1)} fusion(bf16[256,512]{1,0:T(8,128)(2,1)S(1)} %reshape.159, bf16[128,512]{1,0:T(8,128)(2,1)} %copy-done.7, bf16[128,512]{1,0:T(8,128)(2,1)S(1)} %get-tuple-element.30, bf16[256,512]{1,0:T(8,128)(2,1)} %collective-permute-done.12, bf16[128,512]{1,0:T(8,128)(2,1)} %get-tuple-element.10, ...), kind=kOutput, calls=%fused_computation.21 | convolution fusion | flops 272105472 | bytes 1572864 | tf_op jit(solution)/shard_map/dot_general | solution.py:461
  114.2 6.8 %all-to-all-start = ((bf16[8,64,512]{2,1,0:T(8,128)(2,1)}), bf16[8,64,512]{2,1,0:T(8,128)(2,1)S(1)}, u32[]{:S(2)}, u32[]{:S(2)}) async-start(bf16[8,64,512]{2,1,0:T(8,128)(2,1)} %bitcast.51), calls=%async_computation | async-start | bytes 1048576 | tf_op jit(solution)/shard_map/all_to_all | solution.py:464
  121.1 2.3 %fusion.26 = bf16[2,8,16,1024]{3,1,2,0:T(8,128)(2,1)S(1)} fusion(f32[2,8,16,1024]{3,2,1,0:T(8,128)S(1)} %slice.187, bf16[2,6,6,1024]{3,1,2,0:T(8,128)(2,1)S(1)} %get-tuple-element.27, bf16[2,6,16,1024]{3,1,2,0:T(8,128)(2,1)} %collective-permute-done.11, bf16[2,6,6,1024]{3,1,2,0:T(8,128)(2,1)S(1)} %get-tuple-element.26, ...), kind=kLoop, calls=%fused_computation.36 | loop fusion | flops 4456448 | bytes 3342336 | tf_op jit(solution)/shard_map/convert_element_type | solution.py:467
  123.4 0.2 copy.53
  123.6 0.2 copy.54
  123.8 1.2 convolution_convert_fusion.3
  125.0 3.1 %convolution_convert_fusion.2 = bf16[128,512]{1,0:T(8,128)(2,1)S(1)} fusion(bf16[512,3072]{1,0:T(8,128)(2,1)} %collective-permute-done.5, bf16[128,1024]{1,0:T(8,128)(2,1)S(1)} %bitcast.55, bf16[128,1024]{1,0:T(8,128)(2,1)S(1)} %bitcast.53, bf16[128,1024]{1,0:T(8,128)(2,1)S(1)} %copy-done.9), kind=kOutput, calls=%fused_computation.24 | convolution fusion | flops 405078016 | bytes 4063232 | tf_op jit(solution)/shard_map/dot_general | solution.py:378
  128.0 0.8 maximum_select_fusion.1
  128.8 6.5 %all-to-all-done = bf16[8,64,512]{2,1,0:T(8,128)(2,1)S(1)} async-done(((bf16[8,64,512]{2,1,0:T(8,128)(2,1)}), bf16[8,64,512]{2,1,0:T(8,128)(2,1)S(1)}, u32[]{:S(2)}, u32[]{:S(2)}) %all-to-all-start) | async-done | bytes 524320 | tf_op jit(solution)/shard_map/all_to_all | solution.py:464
  135.4 0.7 convert_reduce_fusion
  (53 shorter events, 1.0 us)
Async XLA Ops:
  7.2 12.3 %copy-start.1 = (bf16[1,8,16,1024]{3,2,1,0:T(8,128)(2,1)S(1)}, bf16[1,8,16,1024]{3,2,1,0:T(8,128)(2,1)}, u32[]{:S(2)}) copy-start(bf16[1,8,16,1024]{3,2,1,0:T(8,128)(2,1)} %param.5) | copy-start | bytes 786436
  7.2 17.4 %copy-start.2 = (bf16[512,1024]{1,0:T(8,128)(2,1)S(1)}, bf16[512,1024]{1,0:T(8,128)(2,1)}, u32[]{:S(2)}) copy-start(bf16[512,1024]{1,0:T(8,128)(2,1)} %param.9) | copy-start | bytes 3145732
  7.2 17.4 %copy-start.3 = (bf16[1,8,16,1024]{3,2,1,0:T(8,128)(2,1)S(1)}, bf16[1,8,16,1024]{3,2,1,0:T(8,128)(2,1)}, u32[]{:S(2)}) copy-start(bf16[1,8,16,1024]{3,2,1,0:T(8,128)(2,1)} %param.6) | copy-start | bytes 786436
  7.2 36.8 %all-gather.3.cloned.1.call-start = ((), (), s32[]{:S(2)}) async-start(), calls=%async_computation.1 | async-start | bytes 3932160 | tf_op jit(solution)/shard_map/all_gather | solution.py:338
  8.5 21.8 %collective-permute-start.2 = (bf16[8,12,1024]{2,1,0:T(8,128)(2,1)S(1)}, bf16[8,12,1024]{2,1,0:T(8,128)(2,1)S(1)}, u32[]{:S(2)}, u32[]{:S(2)}) collective-permute-start(bf16[8,12,1024]{2,1,0:T(8,128)(2,1)S(1)} %pad_maximum_fusion.7), channel_id=1, source_target_pairs={{0,1},{1,0},{2,3},{3,2},{4,5},{5,4},{6,7},{7,6},{8,9},{9,8},{10,11... | collective-permute-start | bytes 589832 | tf_op jit(solution)/shard_map/ppermute | solution.py:146
  12.6 13.3 %copy-start.8 = (s32[64,32]{0,1:T(8,128)S(1)}, s32[64,32]{0,1:T(8,128)}, u32[]{:S(2)}) copy-start(s32[64,32]{0,1:T(8,128)} %param.7) | copy-start | bytes 24580
  12.6 16.0 %collective-permute-start.3 = (bf16[6,12,1024]{2,1,0:T(8,128)(2,1)S(1)}, bf16[6,12,1024]{2,1,0:T(8,128)(2,1)S(1)}, u32[]{:S(2)}, u32[]{:S(2)}) collective-permute-start(bf16[6,12,1024]{2,1,0:T(8,128)(2,1)S(1)} %pad_maximum_fusion.11), channel_id=1, source_target_pairs={{2,1},{3,0},{4,3},{5,2},{6,5},{7,4},{8,7},{9,6},{10,9},{11,8},{12,... | collective-permute-start | bytes 442376 | tf_op jit(solution)/shard_map/ppermute | solution.py:146
  14.0 16.1 %collective-permute-start = (bf16[6,12,1024]{2,1,0:T(8,128)(2,1)S(1)}, bf16[6,12,1024]{2,1,0:T(8,128)(2,1)S(1)}, u32[]{:S(2)}, u32[]{:S(2)}) collective-permute-start(bf16[6,12,1024]{2,1,0:T(8,128)(2,1)S(1)} %pad_maximum_fusion.10), channel_id=1, source_target_pairs={{0,3},{1,2},{2,5},{3,4},{4,7},{5,6},{6,9},{7,8},{8,11},{9,10},{10,... | collective-permute-start | bytes 442376 | tf_op jit(solution)/shard_map/ppermute | solution.py:146
  20.2 10.1 %collective-permute-start.1 = (bf16[6,16,1024]{2,1,0:T(8,128)(2,1)}, bf16[6,16,1024]{2,1,0:T(8,128)(2,1)S(1)}, u32[]{:S(2)}, u32[]{:S(2)}) collective-permute-start(bf16[6,16,1024]{2,1,0:T(8,128)(2,1)} %get-tuple-element.32), channel_id=1, source_target_pairs={{0,2},{1,3},{2,4},{3,5},{4,6},{5,7},{6,8},{7,9},{8,10},{9,11},{10,... | collective-permute-start | bytes 589832 | tf_op jit(solution)/shard_map/ppermute | solution.py:146
  25.8 23.0 %collective-permute-start.5 = (bf16[512,3072]{1,0:T(8,128)(2,1)}, bf16[512,3072]{1,0:T(8,128)(2,1)}, u32[]{:S(2)}, u32[]{:S(2)}) collective-permute-start(bf16[512,3072]{1,0:T(8,128)(2,1)} %param.8), channel_id=1, source_target_pairs={{0,16},{16,0},{1,17},{17,1},{2,18},{18,2},{3,19},{19,3},{4,20},{20... | collective-permute-start | bytes 9437192 | tf_op jit(solution)/shard_map/ppermute | solution.py:262
  28.0 10.7 %copy-start.4 = (bf16[512,3072]{1,0:T(8,128)(2,1)S(1)}, bf16[512,3072]{1,0:T(8,128)(2,1)}, u32[]{:S(2)}) copy-start(bf16[512,3072]{1,0:T(8,128)(2,1)} %param.8) | copy-start | bytes 9437188
  28.7 9.3 %collective-permute-start.4 = (bf16[6,16,1024]{2,1,0:T(8,128)(2,1)S(1)}, bf16[6,16,1024]{2,1,0:T(8,128)(2,1)S(1)}, u32[]{:S(2)}, u32[]{:S(2)}) collective-permute-start(bf16[6,16,1024]{2,1,0:T(8,128)(2,1)S(1)} %get-tuple-element.33), channel_id=1, source_target_pairs={{2,0},{3,1},{4,2},{5,3},{6,4},{7,5},{8,6},{9,7},{10,8},{11,9},{12,... | collective-permute-start | bytes 589832 | tf_op jit(solution)/shard_map/ppermute | solution.py:146
  45.7 66.1 %collective-permute-start.12 = (bf16[256,512]{1,0:T(8,128)(2,1)S(1)}, bf16[256,512]{1,0:T(8,128)(2,1)}, u32[]{:S(2)}, u32[]{:S(2)}) collective-permute-start(bf16[256,512]{1,0:T(8,128)(2,1)S(1)} %pad_maximum_fusion.9), channel_id=1, source_target_pairs={{0,1},{1,0},{2,3},{3,2},{4,5},{5,4},{6,7},{7,6},{8,9},{9,8},{10,11... | collective-permute-start | bytes 786440 | tf_op jit(solution)/shard_map/ppermute | solution.py:262
  55.2 2.0 %copy-start = (bf16[640,3072]{1,0:T(8,128)(2,1)}, bf16[640,3072]{1,0:T(8,128)(2,1)S(1)}, u32[]{:S(2)}) copy-start(bf16[640,3072]{1,0:T(8,128)(2,1)S(1)} %add_convert_fusion.k_ref.v_ref) | copy-start | bytes 11796484
  69.9 2.7 %copy-start.6 = (bf16[128,1024]{1,0:T(8,128)(2,1)S(1)}, bf16[128,1024]{1,0:T(8,128)(2,1)}, u32[]{:S(2)}) copy-start(bf16[128,1024]{1,0:T(8,128)(2,1)} %get-tuple-element.9) | copy-start | bytes 786436
  72.7 9.1 %collective-permute-start.8 = (bf16[128,512]{1,0:T(8,128)(2,1)S(1)}, bf16[128,512]{1,0:T(8,128)(2,1)S(1)}, u32[]{:S(2)}, u32[]{:S(2)}) collective-permute-start(bf16[128,512]{1,0:T(8,128)(2,1)S(1)} %get-tuple-element.31), channel_id=1, source_target_pairs={{0,16},{16,0},{1,17},{17,1},{2,18},{18,2},{3,19},{19,3},{4,20},{20... | collective-permute-start | bytes 393224 | tf_op jit(solution)/shard_map/ppermute | solution.py:262
  73.5 19.9 %collective-permute-start.6 = (bf16[2,6,12,1024]{3,1,2,0:T(8,128)(2,1)S(1)}, bf16[2,6,12,1024]{3,1,2,0:T(8,128)(2,1)S(1)}, u32[]{:S(2)}, u32[]{:S(2)}) collective-permute-start(bf16[2,6,12,1024]{3,1,2,0:T(8,128)(2,1)S(1)} %pad_maximum_fusion.3), channel_id=1, source_target_pairs={{2,1},{3,0},{4,3},{5,2},{6,5},{7,4},{8,7},{9,6},{10,9},{11,8},{12,... | collective-permute-start | bytes 884744 | tf_op jit(solution)/shard_map/ppermute | solution.py:146
  75.6 20.8 %collective-permute-start.10 = (bf16[2,6,12,1024]{3,1,2,0:T(8,128)(2,1)}, bf16[2,6,12,1024]{3,1,2,0:T(8,128)(2,1)}, u32[]{:S(2)}, u32[]{:S(2)}) collective-permute-start(bf16[2,6,12,1024]{3,1,2,0:T(8,128)(2,1)} %pad_maximum_fusion.4), channel_id=1, source_target_pairs={{0,3},{1,2},{2,5},{3,4},{4,7},{5,6},{6,9},{7,8},{8,11},{9,10},{10,... | collective-permute-start | bytes 884744 | tf_op jit(solution)/shard_map/ppermute | solution.py:146
  81.8 5.1 %copy-start.7 = (bf16[128,512]{1,0:T(8,128)(2,1)}, bf16[128,512]{1,0:T(8,128)(2,1)S(1)}, u32[]{:S(2)}) copy-start(bf16[128,512]{1,0:T(8,128)(2,1)S(1)} %collective-permute-done.8) | copy-start | bytes 393220
  82.2 29.4 %collective-permute-start.9 = (bf16[2,8,20,1024]{3,1,2,0:T(8,128)(2,1)S(1)}, bf16[2,8,20,1024]{3,1,2,0:T(8,128)(2,1)S(1)}, u32[]{:S(2)}, u32[]{:S(2)}) collective-permute-start(bf16[2,8,20,1024]{3,1,2,0:T(8,128)(2,1)S(1)} %pad_maximum_fusion.2), channel_id=1, source_target_pairs={{0,1},{1,0},{2,3},{3,2},{4,5},{5,4},{6,7},{7,6},{8,9},{9,8},{10,11... | collective-permute-start | bytes 1966088 | tf_op jit(solution)/shard_map/ppermute | solution.py:146
  88.9 32.1 %collective-permute-start.11 = (bf16[2,6,16,1024]{3,1,2,0:T(8,128)(2,1)}, bf16[2,6,16,1024]{3,1,2,0:T(8,128)(2,1)}, u32[]{:S(2)}, u32[]{:S(2)}) collective-permute-start(bf16[2,6,16,1024]{3,1,2,0:T(8,128)(2,1)} %copy.65), channel_id=1, source_target_pairs={{0,2},{1,3},{2,4},{3,5},{4,6},{5,7},{6,8},{7,9},{8,10},{9,11},{10,... | collective-permute-start | bytes 1179656 | tf_op jit(solution)/shard_map/ppermute | solution.py:146
  93.4 27.7 %collective-permute-start.7 = (bf16[2,6,16,1024]{3,1,2,0:T(8,128)(2,1)}, bf16[2,6,16,1024]{3,1,2,0:T(8,128)(2,1)}, u32[]{:S(2)}, u32[]{:S(2)}) collective-permute-start(bf16[2,6,16,1024]{3,1,2,0:T(8,128)(2,1)} %copy.60), channel_id=1, source_target_pairs={{2,0},{3,1},{4,2},{5,3},{6,4},{7,5},{8,6},{9,7},{10,8},{11,9},{12,... | collective-permute-start | bytes 1179656 | tf_op jit(solution)/shard_map/ppermute | solution.py:146
  114.2 21.2 %all-to-all-start = ((bf16[8,64,512]{2,1,0:T(8,128)(2,1)}), bf16[8,64,512]{2,1,0:T(8,128)(2,1)S(1)}, u32[]{:S(2)}, u32[]{:S(2)}) async-start(bf16[8,64,512]{2,1,0:T(8,128)(2,1)} %bitcast.51), calls=%async_computation | async-start | bytes 1048576 | tf_op jit(solution)/shard_map/all_to_all | solution.py:464
  121.0 2.7 %copy-start.5 = (bf16[512,3072]{1,0:T(8,128)(2,1)S(1)}, bf16[512,3072]{1,0:T(8,128)(2,1)}, u32[]{:S(2)}) copy-start(bf16[512,3072]{1,0:T(8,128)(2,1)} %param.8) | copy-start | bytes 9437188
  121.1 2.7 %copy-start.9 = (bf16[128,1024]{1,0:T(8,128)(2,1)S(1)}, bf16[128,1024]{1,0:T(8,128)(2,1)}, u32[]{:S(2)}) copy-start(bf16[128,1024]{1,0:T(8,128)(2,1)} %get-tuple-element.6) | copy-start | bytes 786436
Sparse Core Ops, SparseCore 0:
  25.9 9.7 all-gather.2

commit v17 on v11

--- a/solution.py
+++ b/solution.py
@@ -39,13 +39,7 @@
     return block
 
 
-def attention_kernel(q_ref, k_ref, v_ref, g_ref, bias_ref, att_ref, gq_ref, gkv_ref, gkv_low_ref,
-                     *, head_dim, scale):
-    q = q_ref[...]
-    g = g_ref[...]
-    k = k_ref[...]
-    v = v_ref[...]
-    bias = bias_ref[...]
+def pair_terms(q, k, v, g, bias, head_dim, scale):
     lanes = q.shape[1]
     lane = lax.broadcasted_iota(jnp.int32, (1, lanes), 1)
     zero = jnp.zeros((), q.dtype)
@@ -79,23 +73,36 @@
     probs_t = jnp.concatenate(
         [x.astype(jnp.float32).T.astype(jnp.bfloat16) for x in probs_list], axis=1
     )
-    att_ref[...] = att.astype(att_ref.dtype)
-    gq_ref[...] = gq.astype(gq_ref.dtype)
     grad_k = jnp.dot(grads_t, q_sel, preferred_element_type=jnp.float32)
     grad_v = jnp.dot(probs_t, g_sel, preferred_element_type=jnp.float32)
-    gkv_ref[0] = grad_k
-    gkv_ref[1] = grad_v
-    gkv_low_ref[0] = grad_k.astype(gkv_low_ref.dtype)
-    gkv_low_ref[1] = grad_v.astype(gkv_low_ref.dtype)
+    return att, gq, grad_k, grad_v
+
+
+def attention_kernel(q_ref, k_ref, v_ref, g_ref, bias_ref, att_ref, gq_ref, gkv_ref, gkv_low_ref,
+                     *, head_dim, scale, lanes):
+    bias = bias_ref[...]
+    for sub in range(q_ref.shape[1] // lanes):
+        cols = slice(sub * lanes, (sub + 1) * lanes)
+        att, gq, grad_k, grad_v = pair_terms(
+            q_ref[:, cols], k_ref[:, cols], v_ref[:, cols], g_ref[:, cols], bias, head_dim, scale
+        )
+        att_ref[:, cols] = att.astype(att_ref.dtype)
+        gq_ref[:, cols] = gq.astype(gq_ref.dtype)
+        gkv_ref[0, :, cols] = grad_k
+        gkv_ref[1, :, cols] = grad_v
+        gkv_low_ref[0, :, cols] = grad_k.astype(gkv_low_ref.dtype)
+        gkv_low_ref[1, :, cols] = grad_v.astype(gkv_low_ref.dtype)
 
 
 def block_attention(query, projected, grad_attn, bias, heads):
     queries, width = query.shape
     keys = projected.shape[0]
     head_dim = width // heads
-    lanes = 128
+    lanes = 256
     pairs = width // lanes
-    kernel = functools.partial(attention_kernel, head_dim=head_dim, scale=head_dim ** (-0.5))
+    kernel = functools.partial(
+        attention_kernel, head_dim=head_dim, scale=head_dim ** (-0.5), lanes=128
+    )
     flops = 2 * queries * keys * width * 2 * 6
     cost = pl.CostEstimate(
         flops=flops,

time: 123 us -> 122 us (level)
  Pallas kernels: 12 us -> 10.7 us
    pallas_call x1, Pallas kernels: 12 us -> 10.7 us  [block_attention(): pl.pallas_call(kernel, grid=(pairs,), in_specs=[pl.BlockSpec((queries, la...]
  transfers between devices with their start and end apart: 15 -> 15, of which waited for: 5 -> 5; matrix products, arithmetic and copies ran while one was open for 30% -> 31% of each run, Pallas kernels for 10% -> 9%
where the time goes in v17:
time: 122 us; the launch traced here: 121 us
  starting transfers between devices  38.1 us (31%)
  waiting for transfers between devices  29.5 us (24%)
  local copies, waits for them, and re-layouts  19 us (16%)
  matrix products  14.1 us (12%)
  Pallas kernels  10.7 us (9%)
  other arithmetic  8.53 us (7%)
    ppermute x10, starting transfers between devices, sent_to(): return lax.ppermute(value, ('lat', 'lon'), grid_pairs(delta_lat, delta_lon))  30.5 us
    ppermute x10, waiting for transfers between devices, sent_to(): return lax.ppermute(value, ('lat', 'lon'), grid_pairs(delta_lat, delta_lon))  23 us
    pallas_call x1, Pallas kernels, block_attention(): pl.pallas_call(kernel, grid=(pairs,), in_specs=[pl.BlockSpec((queries, la...  10.7 us
    all_to_all x1, waiting for transfers between devices, shards(): lax.all_to_all(partial.astype(jnp.bfloat16), 'lat', 0, 0, tiled=True)  6.54 us
    all_to_all x1, starting transfers between devices, shards(): lax.all_to_all(partial.astype(jnp.bfloat16), 'lat', 0, 0, tiled=True)  6.33 us
    unnamed x31, local copies, waits for them, and re-layouts  4.56 us
    slice x3, local copies, waits for them, and re-layouts, halo_return(): pieces.append((da, db, ext_low[:, row_slices[da], col_slices[db]]))  4.34 us
    dot_general x1, matrix products, project(): jnp.dot(columns(rows, 1 - dp_index, rows_half), qkv_other, preferred_elem...  4.19 us
  transfers between devices with their start and end apart: 15, of which 5 were waited for; matrix products, arithmetic and copies ran while one was open for 31% of the time, Pallas kernels for 9%

profile of v17, /device:TPU:0, one launch (start us, length us, event | category | flops | bytes accessed | tf_op | source)
XLA Modules:
  0.0 121.1 jit_solution(16609296040980651637)
XLA Ops:
  0.7 1.1 fusion.71
  1.8 0.1 pad_maximum_fusion.7
  1.9 3.0 %collective-permute-start.2 = (bf16[8,12,1024]{2,1,0:T(8,128)(2,1)S(1)}, bf16[8,12,1024]{2,1,0:T(8,128)(2,1)S(1)}, u32[]{:S(2)}, u32[]{:S(2)}) collective-permute-start(bf16[8,12,1024]{2,1,0:T(8,128)(2,1)S(1)} %pad_maximum_fusion.7), channel_id=1, source_target_pairs={{0,1},{1,0},{2,3},{3,2},{4,5},{5,4},{6,7},{7,6},{8,9},{9,8},{10,11... | collective-permute-start | bytes 589832 | tf_op jit(solution)/shard_map/ppermute | solution.py:153
  4.9 1.1 fusion.70
  6.1 1.3 %collective-permute-start.3 = (bf16[6,12,1024]{2,1,0:T(8,128)(2,1)S(1)}, bf16[6,12,1024]{2,1,0:T(8,128)(2,1)S(1)}, u32[]{:S(2)}, u32[]{:S(2)}) collective-permute-start(bf16[6,12,1024]{2,1,0:T(8,128)(2,1)S(1)} %pad_maximum_fusion.11), channel_id=1, source_target_pairs={{2,1},{3,0},{4,3},{5,2},{6,5},{7,4},{8,7},{9,6},{10,9},{11,8},{12,... | collective-permute-start | bytes 442376 | tf_op jit(solution)/shard_map/ppermute | solution.py:153
  7.4 5.5 %collective-permute-start = (bf16[6,12,1024]{2,1,0:T(8,128)(2,1)S(1)}, bf16[6,12,1024]{2,1,0:T(8,128)(2,1)S(1)}, u32[]{:S(2)}, u32[]{:S(2)}) collective-permute-start(bf16[6,12,1024]{2,1,0:T(8,128)(2,1)S(1)} %pad_maximum_fusion.10), channel_id=1, source_target_pairs={{0,3},{1,2},{2,5},{3,4},{4,7},{5,6},{6,9},{7,8},{8,11},{9,10},{10,... | collective-permute-start | bytes 442376 | tf_op jit(solution)/shard_map/ppermute | solution.py:153
  12.9 0.7 slice_bitcast_fusion.1
  13.6 4.3 %collective-permute-start.1 = (bf16[6,16,1024]{2,1,0:T(8,128)(2,1)}, bf16[6,16,1024]{2,1,0:T(8,128)(2,1)S(1)}, u32[]{:S(2)}, u32[]{:S(2)}) collective-permute-start(bf16[6,16,1024]{2,1,0:T(8,128)(2,1)} %get-tuple-element.32), channel_id=1, source_target_pairs={{0,2},{1,3},{2,4},{3,5},{4,6},{5,7},{6,8},{7,9},{8,10},{9,11},{10,... | collective-permute-start | bytes 589832 | tf_op jit(solution)/shard_map/ppermute | solution.py:153
  18.2 0.1 copy.40
  18.3 0.1 copy.42
  18.6 0.1 eq.28
  18.6 1.0 fusion.45.bias_ref
  19.7 0.5 convolution_convert_fusion.1
  20.2 0.7 constant_dynamic-slice_fusion.3
  20.9 0.1 pad_maximum_fusion
  21.0 1.6 %collective-permute-start.4 = (bf16[6,16,1024]{2,1,0:T(8,128)(2,1)S(1)}, bf16[6,16,1024]{2,1,0:T(8,128)(2,1)S(1)}, u32[]{:S(2)}, u32[]{:S(2)}) collective-permute-start(bf16[6,16,1024]{2,1,0:T(8,128)(2,1)S(1)} %get-tuple-element.33), channel_id=1, source_target_pairs={{2,0},{3,1},{4,2},{5,3},{6,4},{7,5},{8,6},{9,7},{10,8},{11,9},{12,... | collective-permute-start | bytes 589832 | tf_op jit(solution)/shard_map/ppermute | solution.py:153
  22.6 0.5 collective-permute-start.6
  23.2 0.5 collective-permute-done.1
  23.7 6.7 %collective-permute-done.4 = bf16[6,16,1024]{2,1,0:T(8,128)(2,1)S(1)} collective-permute-done((bf16[6,16,1024]{2,1,0:T(8,128)(2,1)S(1)}, bf16[6,16,1024]{2,1,0:T(8,128)(2,1)S(1)}, u32[]{:S(2)}, u32[]{:S(2)}) %collective-permute-start.4) | collective-permute-done | bytes 196640 | tf_op jit(solution)/shard_map/ppermute | solution.py:153
  30.4 0.7 fusion.12
  31.2 2.2 %fusion.29 = f32[640,3072]{1,0:T(8,128)S(1)} fusion(bf16[512,3072]{1,0:T(8,128)(2,1)S(1)} %copy-done.3, bf16[640,1024]{1,0:T(8,128)(2,1)S(1)} %bitcast.31, s32[]{:T(128)S(6)} %select_n.95), kind=kOutput, calls=%fused_computation.41 | convolution fusion | flops 2013265920 | bytes 11665412 | tf_op jit(solution)/shard_map/dot_general | solution.py:374
  33.4 0.7 constant_dynamic-slice_fusion.2
  34.1 0.7 pad_maximum_fusion.9
  34.9 0.5 collective-permute-start.13
  35.4 0.5 fusion.18
  35.9 0.8 maximum_select_fusion.g_ref
  36.7 4.2 %add_convert_fusion.k_ref.v_ref = bf16[640,3072]{1,0:T(8,128)(2,1)S(1)} fusion(f32[640,3072]{1,0:T(8,128)S(1)} %fusion.29, bf16[512,3072]{1,0:T(8,128)(2,1)} %collective-permute-done.5, bf16[640,1024]{1,0:T(8,128)(2,1)S(1)} %bitcast.32, s32[]{:T(128)S(6)} %select_n.96), kind=kOutput, calls=%fused_computation | convolution fusion | flops 2017198080 | bytes 15597572 | tf_op jit(solution)/shard_map/dot_general | solution.py:377
  40.9 1.9 %copy-done = bf16[640,3072]{1,0:T(8,128)(2,1)} copy-done((bf16[640,3072]{1,0:T(8,128)(2,1)}, bf16[640,3072]{1,0:T(8,128)(2,1)S(1)}, u32[]{:S(2)}) %copy-start) | copy-done | bytes 3932184
  42.8 0.8 slice.181
  43.6 10.7 %block_attention.1 = (bf16[128,1024]{1,0:T(8,128)(2,1)}, bf16[128,1024]{1,0:T(8,128)(2,1)}, f32[2,640,1024]{2,1,0:T(8,128)}, bf16[2,640,1024]{2,1,0:T(8,128)(2,1)}) custom-call(bf16[128,1024]{1,0:T(8,128)(2,1)} %bitcast.40, bf16[640,3072]{1,0:T(8,128)(2,1)} %copy-done, bf16[640,3072]{1,0:T(8,128)(2,1)} %copy-done, ...), custom_call_target="tpu_custom_call" | custom-call | flops 2013265920 | bytes 9240576 | tf_op jit(solution)/shard_map/block_attention/pallas_call | solution.py:113
  54.3 1.3 %fusion.64 = (bf16[2,8,6,1024]{3,2,1,0:T(8,128)(2,1)S(1)}, bf16[2,8,6,1024]{3,2,1,0:T(8,128)(2,1)S(1)}) fusion(bf16[2,20,32,1024]{3,2,1,0:T(8,128)(2,1)} %bitcast.37), kind=kLoop, calls=%fused_computation.109 | loop fusion | bytes 786432 | tf_op jit(solution)/shard_map/slice | solution.py:208
  55.6 1.5 %fusion.63 = (bf16[2,6,6,1024]{3,2,1,0:T(8,128)(2,1)S(1)}, bf16[2,6,6,1024]{3,2,1,0:T(8,128)(2,1)S(1)}, bf16[2,6,6,1024]{3,2,1,0:T(8,128)(2,1)S(1)}, bf16[2,6,6,1024]{3,2,1,0:T(8,128)(2,1)S(1)}) fusion(bf16[2,20,32,1024]{3,2,1,0:T(8,128)(2,1)} %bitcast.38), kind=kLoop, calls=%fused_computation.108 | loop fusion | bytes 1179648 | tf_op jit(solution)/shard_map/slice | solution.py:208
  57.5 0.1 copy.61
  57.6 0.1 copy.62
  57.7 0.1 copy.64
  57.9 1.3 %collective-permute-start.7 = (bf16[2,6,12,1024]{3,1,2,0:T(8,128)(2,1)S(1)}, bf16[2,6,12,1024]{3,1,2,0:T(8,128)(2,1)}, u32[]{:S(2)}, u32[]{:S(2)}) collective-permute-start(bf16[2,6,12,1024]{3,1,2,0:T(8,128)(2,1)S(1)} %pad_maximum_fusion.3), channel_id=1, source_target_pairs={{2,1},{3,0},{4,3},{5,2},{6,5},{7,4},{8,7},{9,6},{10,9},{11,8},{12,... | collective-permute-start | bytes 884744 | tf_op jit(solution)/shard_map/ppermute | solution.py:153
  59.2 0.8 pad_maximum_fusion.4
  60.0 6.2 %collective-permute-start.11 = (bf16[2,6,12,1024]{3,1,2,0:T(8,128)(2,1)}, bf16[2,6,12,1024]{3,1,2,0:T(8,128)(2,1)}, u32[]{:S(2)}, u32[]{:S(2)}) collective-permute-start(bf16[2,6,12,1024]{3,1,2,0:T(8,128)(2,1)} %pad_maximum_fusion.4), channel_id=1, source_target_pairs={{0,3},{1,2},{2,5},{3,4},{4,7},{5,6},{6,9},{7,8},{8,11},{9,10},{10,... | collective-permute-start | bytes 884744 | tf_op jit(solution)/shard_map/ppermute | solution.py:153
  66.2 0.7 copy-done.8
  66.9 0.1 reshape.154
  67.0 0.2 copy.49
  67.3 1.6 %collective-permute-start.10 = (bf16[2,8,20,1024]{3,1,2,0:T(8,128)(2,1)S(1)}, bf16[2,8,20,1024]{3,1,2,0:T(8,128)(2,1)S(1)}, u32[]{:S(2)}, u32[]{:S(2)}) collective-permute-start(bf16[2,8,20,1024]{3,1,2,0:T(8,128)(2,1)S(1)} %pad_maximum_fusion.2), channel_id=1, source_target_pairs={{0,1},{1,0},{2,3},{3,2},{4,5},{5,4},{6,7},{7,6},{8,9},{9,8},{10,11... | collective-permute-start | bytes 1966088 | tf_op jit(solution)/shard_map/ppermute | solution.py:153
  68.8 1.6 %fusion.62 = (bf16[2,6,16,1024]{3,2,1,0:T(8,128)(2,1)S(1)}, bf16[2,6,16,1024]{3,2,1,0:T(8,128)(2,1)S(1)}) fusion(bf16[2,20,32,1024]{3,2,1,0:T(8,128)(2,1)} %bitcast.39), kind=kLoop, calls=%fused_computation.107 | loop fusion | bytes 1572864 | tf_op jit(solution)/shard_map/slice | solution.py:208
  70.5 1.5 %slice.183 = f32[2,8,16,1024]{3,2,1,0:T(8,128)S(1)} slice(f32[2,20,32,1024]{3,2,1,0:T(8,128)} %bitcast.46), slice={[0:2], [6:14], [6:22], [0:1024]} | slice | bytes 2097152 | tf_op jit(solution)/shard_map/slice | solution.py:200
  72.0 0.2 copy.60
  72.2 1.0 copy.65
  73.3 4.4 %collective-permute-start.12 = (bf16[2,6,16,1024]{3,1,2,0:T(8,128)(2,1)}, bf16[2,6,16,1024]{3,1,2,0:T(8,128)(2,1)}, u32[]{:S(2)}, u32[]{:S(2)}) collective-permute-start(bf16[2,6,16,1024]{3,1,2,0:T(8,128)(2,1)} %copy.65), channel_id=1, source_target_pairs={{0,2},{1,3},{2,4},{3,5},{4,6},{5,7},{6,8},{7,9},{8,10},{9,11},{10,... | collective-permute-start | bytes 1179656 | tf_op jit(solution)/shard_map/ppermute | solution.py:153
  77.6 1.5 %collective-permute-start.8 = (bf16[2,6,16,1024]{3,1,2,0:T(8,128)(2,1)S(1)}, bf16[2,6,16,1024]{3,1,2,0:T(8,128)(2,1)}, u32[]{:S(2)}, u32[]{:S(2)}) collective-permute-start(bf16[2,6,16,1024]{3,1,2,0:T(8,128)(2,1)S(1)} %copy.60), channel_id=1, source_target_pairs={{2,0},{3,1},{4,2},{5,3},{6,4},{7,5},{8,6},{9,7},{10,8},{11,9},{12,... | collective-permute-start | bytes 1179656 | tf_op jit(solution)/shard_map/ppermute | solution.py:153
  79.1 1.1 fusion.67
  80.2 0.7 collective-permute-done.11
  80.9 1.0 fusion.68
  81.9 15.1 %collective-permute-done.10 = bf16[2,8,20,1024]{3,1,2,0:T(8,128)(2,1)S(1)} collective-permute-done((bf16[2,8,20,1024]{3,1,2,0:T(8,128)(2,1)S(1)}, bf16[2,8,20,1024]{3,1,2,0:T(8,128)(2,1)S(1)}, u32[]{:S(2)}, u32[]{:S(2)}) %collective-permute-start.10) | collective-permute-done | bytes 655392 | tf_op jit(solution)/shard_map/ppermute | solution.py:153
  97.0 0.2 copy.55
  97.2 0.1 reshape.155
  97.3 2.4 %fusion.17 = bf16[512,512]{1,0:T(8,128)(2,1)} fusion(bf16[256,512]{1,0:T(8,128)(2,1)S(1)} %reshape.155, bf16[128,512]{1,0:T(8,128)(2,1)} %copy-done.8, bf16[128,512]{1,0:T(8,128)(2,1)} %copy-done.6, bf16[256,512]{1,0:T(8,128)(2,1)} %collective-permute-done.13, bf16[128,512]{1,0:T(8,128)(2,1)} %get-tuple-element.28, bf16[128,512]{1,0:T(8,128)(2,1)} %get-tuple-element.26), kind=kOutput, calls=%fused_computation.21 | convolution fusion | flops 272105472 | bytes 1572864 | tf_op jit(solution)/shard_map/dot_general | solution.py:467
  99.7 6.3 %all-to-all-start = ((bf16[8,64,512]{2,1,0:T(8,128)(2,1)}), bf16[8,64,512]{2,1,0:T(8,128)(2,1)S(1)}, u32[]{:S(2)}, u32[]{:S(2)}) async-start(bf16[8,64,512]{2,1,0:T(8,128)(2,1)} %bitcast.41), calls=%async_computation | async-start | bytes 1048576 | tf_op jit(solution)/shard_map/all_to_all | solution.py:470
  106.1 2.3 %fusion.27 = bf16[2,8,16,1024]{3,1,2,0:T(8,128)(2,1)S(1)} fusion(f32[2,8,16,1024]{3,2,1,0:T(8,128)S(1)} %slice.183, bf16[2,6,6,1024]{3,1,2,0:T(8,128)(2,1)S(1)} %get-tuple-element.25, bf16[2,6,16,1024]{3,1,2,0:T(8,128)(2,1)} %collective-permute-done.12, bf16[2,6,6,1024]{3,1,2,0:T(8,128)(2,1)S(1)} %get-tuple-element.24, ...), kind=kLoop, calls=%fused_computation.36 | loop fusion | flops 4456448 | bytes 3342336 | tf_op jit(solution)/shard_map/convert_element_type | solution.py:473
  108.5 0.2 copy.53
  108.6 0.2 copy.54
  108.8 1.2 convolution_convert_fusion.3
  110.0 3.1 %convolution_convert_fusion.2 = bf16[128,512]{1,0:T(8,128)(2,1)S(1)} fusion(bf16[512,3072]{1,0:T(8,128)(2,1)} %collective-permute-done.5, bf16[128,1024]{1,0:T(8,128)(2,1)S(1)} %bitcast.45, bf16[128,1024]{1,0:T(8,128)(2,1)S(1)} %bitcast.43, bf16[128,1024]{1,0:T(8,128)(2,1)S(1)} %copy-done.10), kind=kOutput, calls=%fused_computation.24 | convolution fusion | flops 405078016 | bytes 4063232 | tf_op jit(solution)/shard_map/dot_general | solution.py:384
  113.1 0.8 maximum_select_fusion.1
  113.9 6.5 %all-to-all-done = bf16[8,64,512]{2,1,0:T(8,128)(2,1)S(1)} async-done(((bf16[8,64,512]{2,1,0:T(8,128)(2,1)}), bf16[8,64,512]{2,1,0:T(8,128)(2,1)S(1)}, u32[]{:S(2)}, u32[]{:S(2)}) %all-to-all-start) | async-done | bytes 524320 | tf_op jit(solution)/shard_map/all_to_all | solution.py:470
  120.4 0.7 convert_reduce_fusion
  (55 shorter events, 1.3 us)
Async XLA Ops:
  0.6 12.3 %copy-start.1 = (bf16[1,8,16,1024]{3,2,1,0:T(8,128)(2,1)S(1)}, bf16[1,8,16,1024]{3,2,1,0:T(8,128)(2,1)}, u32[]{:S(2)}) copy-start(bf16[1,8,16,1024]{3,2,1,0:T(8,128)(2,1)} %param.5) | copy-start | bytes 786436
  0.6 17.4 %copy-start.9 = (s32[64,32]{0,1:T(8,128)S(1)}, s32[64,32]{0,1:T(8,128)}, u32[]{:S(2)}) copy-start(s32[64,32]{0,1:T(8,128)} %param.7) | copy-start | bytes 24580
  0.7 19.0 %copy-start.2 = (bf16[512,1024]{1,0:T(8,128)(2,1)S(1)}, bf16[512,1024]{1,0:T(8,128)(2,1)}, u32[]{:S(2)}) copy-start(bf16[512,1024]{1,0:T(8,128)(2,1)} %param.9) | copy-start | bytes 3145732
  0.7 19.0 %copy-start.5 = (bf16[1,8,16,1024]{3,2,1,0:T(8,128)(2,1)S(1)}, bf16[1,8,16,1024]{3,2,1,0:T(8,128)(2,1)}, u32[]{:S(2)}) copy-start(bf16[1,8,16,1024]{3,2,1,0:T(8,128)(2,1)} %param.6) | copy-start | bytes 786436
  1.9 21.3 %collective-permute-start.2 = (bf16[8,12,1024]{2,1,0:T(8,128)(2,1)S(1)}, bf16[8,12,1024]{2,1,0:T(8,128)(2,1)S(1)}, u32[]{:S(2)}, u32[]{:S(2)}) collective-permute-start(bf16[8,12,1024]{2,1,0:T(8,128)(2,1)S(1)} %pad_maximum_fusion.7), channel_id=1, source_target_pairs={{0,1},{1,0},{2,3},{3,2},{4,5},{5,4},{6,7},{7,6},{8,9},{9,8},{10,11... | collective-permute-start | bytes 589832 | tf_op jit(solution)/shard_map/ppermute | solution.py:153
  6.1 14.9 %collective-permute-start.3 = (bf16[6,12,1024]{2,1,0:T(8,128)(2,1)S(1)}, bf16[6,12,1024]{2,1,0:T(8,128)(2,1)S(1)}, u32[]{:S(2)}, u32[]{:S(2)}) collective-permute-start(bf16[6,12,1024]{2,1,0:T(8,128)(2,1)S(1)} %pad_maximum_fusion.11), channel_id=1, source_target_pairs={{2,1},{3,0},{4,3},{5,2},{6,5},{7,4},{8,7},{9,6},{10,9},{11,8},{12,... | collective-permute-start | bytes 442376 | tf_op jit(solution)/shard_map/ppermute | solution.py:153
  7.4 15.1 %collective-permute-start = (bf16[6,12,1024]{2,1,0:T(8,128)(2,1)S(1)}, bf16[6,12,1024]{2,1,0:T(8,128)(2,1)S(1)}, u32[]{:S(2)}, u32[]{:S(2)}) collective-permute-start(bf16[6,12,1024]{2,1,0:T(8,128)(2,1)S(1)} %pad_maximum_fusion.10), channel_id=1, source_target_pairs={{0,3},{1,2},{2,5},{3,4},{4,7},{5,6},{6,9},{7,8},{8,11},{9,10},{10,... | collective-permute-start | bytes 442376 | tf_op jit(solution)/shard_map/ppermute | solution.py:153
  13.6 10.1 %collective-permute-start.1 = (bf16[6,16,1024]{2,1,0:T(8,128)(2,1)}, bf16[6,16,1024]{2,1,0:T(8,128)(2,1)S(1)}, u32[]{:S(2)}, u32[]{:S(2)}) collective-permute-start(bf16[6,16,1024]{2,1,0:T(8,128)(2,1)} %get-tuple-element.32), channel_id=1, source_target_pairs={{0,2},{1,3},{2,4},{3,5},{4,6},{5,7},{6,8},{7,9},{8,10},{9,11},{10,... | collective-permute-start | bytes 589832 | tf_op jit(solution)/shard_map/ppermute | solution.py:153
  18.0 18.7 %collective-permute-start.5 = (bf16[512,3072]{1,0:T(8,128)(2,1)}, bf16[512,3072]{1,0:T(8,128)(2,1)}, u32[]{:S(2)}, u32[]{:S(2)}) collective-permute-start(bf16[512,3072]{1,0:T(8,128)(2,1)} %param.8), channel_id=1, source_target_pairs={{0,16},{16,0},{1,17},{17,1},{2,18},{18,2},{3,19},{19,3},{4,20},{20... | collective-permute-start | bytes 9437192 | tf_op jit(solution)/shard_map/ppermute | solution.py:269
  20.9 10.2 %copy-start.3 = (bf16[512,3072]{1,0:T(8,128)(2,1)S(1)}, bf16[512,3072]{1,0:T(8,128)(2,1)}, u32[]{:S(2)}) copy-start(bf16[512,3072]{1,0:T(8,128)(2,1)} %param.8) | copy-start | bytes 9437188
  21.0 9.4 %collective-permute-start.4 = (bf16[6,16,1024]{2,1,0:T(8,128)(2,1)S(1)}, bf16[6,16,1024]{2,1,0:T(8,128)(2,1)S(1)}, u32[]{:S(2)}, u32[]{:S(2)}) collective-permute-start(bf16[6,16,1024]{2,1,0:T(8,128)(2,1)S(1)} %get-tuple-element.33), channel_id=1, source_target_pairs={{2,0},{3,1},{4,2},{5,3},{6,4},{7,5},{8,6},{9,7},{10,8},{11,9},{12,... | collective-permute-start | bytes 589832 | tf_op jit(solution)/shard_map/ppermute | solution.py:153
  22.6 10.8 %collective-permute-start.6 = (bf16[640,1024]{1,0:T(8,128)(2,1)S(1)}, bf16[640,1024]{1,0:T(8,128)(2,1)S(1)}, u32[]{:S(2)}, u32[]{:S(2)}) collective-permute-start(bf16[640,1024]{1,0:T(8,128)(2,1)S(1)} %pad_maximum_fusion), channel_id=1, source_target_pairs={{0,16},{16,0},{1,17},{17,1},{2,18},{18,2},{3,19},{19,3},{4,20},{20... | collective-permute-start | bytes 3932168 | tf_op jit(solution)/shard_map/ppermute | solution.py:269
  34.9 62.4 %collective-permute-start.13 = (bf16[256,512]{1,0:T(8,128)(2,1)}, bf16[256,512]{1,0:T(8,128)(2,1)}, u32[]{:S(2)}, u32[]{:S(2)}) collective-permute-start(bf16[256,512]{1,0:T(8,128)(2,1)} %pad_maximum_fusion.9), channel_id=1, source_target_pairs={{0,1},{1,0},{2,3},{3,2},{4,5},{5,4},{6,7},{7,6},{8,9},{9,8},{10,11... | collective-permute-start | bytes 786440 | tf_op jit(solution)/shard_map/ppermute | solution.py:269
  40.9 2.0 %copy-start = (bf16[640,3072]{1,0:T(8,128)(2,1)}, bf16[640,3072]{1,0:T(8,128)(2,1)S(1)}, u32[]{:S(2)}) copy-start(bf16[640,3072]{1,0:T(8,128)(2,1)S(1)} %add_convert_fusion.k_ref.v_ref) | copy-start | bytes 11796484
  54.3 2.7 %copy-start.7 = (bf16[128,1024]{1,0:T(8,128)(2,1)S(1)}, bf16[128,1024]{1,0:T(8,128)(2,1)}, u32[]{:S(2)}) copy-start(bf16[128,1024]{1,0:T(8,128)(2,1)} %get-tuple-element.9) | copy-start | bytes 786436
  57.1 9.1 %copy-start.6 = (bf16[128,512]{1,0:T(8,128)(2,1)}, bf16[128,512]{1,0:T(8,128)(2,1)S(1)}, u32[]{:S(2)}) copy-start(bf16[128,512]{1,0:T(8,128)(2,1)S(1)} %get-tuple-element.30) | copy-start | bytes 393220
  57.1 9.1 %collective-permute-start.9 = (bf16[128,512]{1,0:T(8,128)(2,1)S(1)}, bf16[128,512]{1,0:T(8,128)(2,1)S(1)}, u32[]{:S(2)}, u32[]{:S(2)}) collective-permute-start(bf16[128,512]{1,0:T(8,128)(2,1)S(1)} %get-tuple-element.31), channel_id=1, source_target_pairs={{0,16},{16,0},{1,17},{17,1},{2,18},{18,2},{3,19},{19,3},{4,20},{20... | collective-permute-start | bytes 393224 | tf_op jit(solution)/shard_map/ppermute | solution.py:269
  57.9 19.7 %collective-permute-start.7 = (bf16[2,6,12,1024]{3,1,2,0:T(8,128)(2,1)S(1)}, bf16[2,6,12,1024]{3,1,2,0:T(8,128)(2,1)}, u32[]{:S(2)}, u32[]{:S(2)}) collective-permute-start(bf16[2,6,12,1024]{3,1,2,0:T(8,128)(2,1)S(1)} %pad_maximum_fusion.3), channel_id=1, source_target_pairs={{2,1},{3,0},{4,3},{5,2},{6,5},{7,4},{8,7},{9,6},{10,9},{11,8},{12,... | collective-permute-start | bytes 884744 | tf_op jit(solution)/shard_map/ppermute | solution.py:153
  60.0 20.8 %collective-permute-start.11 = (bf16[2,6,12,1024]{3,1,2,0:T(8,128)(2,1)}, bf16[2,6,12,1024]{3,1,2,0:T(8,128)(2,1)}, u32[]{:S(2)}, u32[]{:S(2)}) collective-permute-start(bf16[2,6,12,1024]{3,1,2,0:T(8,128)(2,1)} %pad_maximum_fusion.4), channel_id=1, source_target_pairs={{0,3},{1,2},{2,5},{3,4},{4,7},{5,6},{6,9},{7,8},{8,11},{9,10},{10,... | collective-permute-start | bytes 884744 | tf_op jit(solution)/shard_map/ppermute | solution.py:153
  66.2 0.7 copy-start.8
  67.3 29.7 %collective-permute-start.10 = (bf16[2,8,20,1024]{3,1,2,0:T(8,128)(2,1)S(1)}, bf16[2,8,20,1024]{3,1,2,0:T(8,128)(2,1)S(1)}, u32[]{:S(2)}, u32[]{:S(2)}) collective-permute-start(bf16[2,8,20,1024]{3,1,2,0:T(8,128)(2,1)S(1)} %pad_maximum_fusion.2), channel_id=1, source_target_pairs={{0,1},{1,0},{2,3},{3,2},{4,5},{5,4},{6,7},{7,6},{8,9},{9,8},{10,11... | collective-permute-start | bytes 1966088 | tf_op jit(solution)/shard_map/ppermute | solution.py:153
  73.3 32.8 %collective-permute-start.12 = (bf16[2,6,16,1024]{3,1,2,0:T(8,128)(2,1)}, bf16[2,6,16,1024]{3,1,2,0:T(8,128)(2,1)}, u32[]{:S(2)}, u32[]{:S(2)}) collective-permute-start(bf16[2,6,16,1024]{3,1,2,0:T(8,128)(2,1)} %copy.65), channel_id=1, source_target_pairs={{0,2},{1,3},{2,4},{3,5},{4,6},{5,7},{6,8},{7,9},{8,10},{9,11},{10,... | collective-permute-start | bytes 1179656 | tf_op jit(solution)/shard_map/ppermute | solution.py:153
  77.6 28.4 %collective-permute-start.8 = (bf16[2,6,16,1024]{3,1,2,0:T(8,128)(2,1)S(1)}, bf16[2,6,16,1024]{3,1,2,0:T(8,128)(2,1)}, u32[]{:S(2)}, u32[]{:S(2)}) collective-permute-start(bf16[2,6,16,1024]{3,1,2,0:T(8,128)(2,1)S(1)} %copy.60), channel_id=1, source_target_pairs={{2,0},{3,1},{4,2},{5,3},{6,4},{7,5},{8,6},{9,7},{10,8},{11,9},{12,... | collective-permute-start | bytes 1179656 | tf_op jit(solution)/shard_map/ppermute | solution.py:153
  99.7 20.7 %all-to-all-start = ((bf16[8,64,512]{2,1,0:T(8,128)(2,1)}), bf16[8,64,512]{2,1,0:T(8,128)(2,1)S(1)}, u32[]{:S(2)}, u32[]{:S(2)}) async-start(bf16[8,64,512]{2,1,0:T(8,128)(2,1)} %bitcast.41), calls=%async_computation | async-start | bytes 1048576 | tf_op jit(solution)/shard_map/all_to_all | solution.py:470
  106.1 2.7 %copy-start.4 = (bf16[512,3072]{1,0:T(8,128)(2,1)S(1)}, bf16[512,3072]{1,0:T(8,128)(2,1)}, u32[]{:S(2)}) copy-start(bf16[512,3072]{1,0:T(8,128)(2,1)} %param.8) | copy-start | bytes 9437188
  106.1 2.7 %copy-start.10 = (bf16[128,1024]{1,0:T(8,128)(2,1)S(1)}, bf16[128,1024]{1,0:T(8,128)(2,1)}, u32[]{:S(2)}) copy-start(bf16[128,1024]{1,0:T(8,128)(2,1)} %get-tuple-element.6) | copy-start | bytes 786436

commit v18 on v17

--- a/solution.py
+++ b/solution.py
@@ -98,7 +98,7 @@
     queries, width = query.shape
     keys = projected.shape[0]
     head_dim = width // heads
-    lanes = 256
+    lanes = 512
     pairs = width // lanes
     kernel = functools.partial(
         attention_kernel, head_dim=head_dim, scale=head_dim ** (-0.5), lanes=128

time: 122 us -> 122 us (level)
  no operation moved by 1% of the time
where the time goes in v18:
time: 122 us; the launch traced here: 121 us
  starting transfers between devices  37.9 us (31%)
  waiting for transfers between devices  29.5 us (24%)
  local copies, waits for them, and re-layouts  19 us (16%)
  matrix products  14.1 us (12%)
  Pallas kernels  11.2 us (9%)
  other arithmetic  8.53 us (7%)
    ppermute x10, starting transfers between devices, sent_to(): return lax.ppermute(value, ('lat', 'lon'), grid_pairs(delta_lat, delta_lon))  30.5 us
    ppermute x10, waiting for transfers between devices, sent_to(): return lax.ppermute(value, ('lat', 'lon'), grid_pairs(delta_lat, delta_lon))  23 us
    pallas_call x1, Pallas kernels, block_attention(): pl.pallas_call(kernel, grid=(pairs,), in_specs=[pl.BlockSpec((queries, la...  11.2 us
    all_to_all x1, waiting for transfers between devices, shards(): lax.all_to_all(partial.astype(jnp.bfloat16), 'lat', 0, 0, tiled=True)  6.54 us
    all_to_all x1, starting transfers between devices, shards(): lax.all_to_all(partial.astype(jnp.bfloat16), 'lat', 0, 0, tiled=True)  6.15 us
    unnamed x31, local copies, waits for them, and re-layouts  4.56 us
    slice x3, local copies, waits for them, and re-layouts, halo_return(): pieces.append((da, db, ext_low[:, row_slices[da], col_slices[db]]))  4.34 us
    dot_general x1, matrix products, project(): jnp.dot(columns(rows, 1 - dp_index, rows_half), qkv_other, preferred_elem...  4.19 us
  transfers between devices with their start and end apart: 15, of which 5 were waited for; matrix products, arithmetic and copies ran while one was open for 31% of the time, Pallas kernels for 9%

profile of v18, /device:TPU:0, one launch (start us, length us, event | category | flops | bytes accessed | tf_op | source)
XLA Modules:
  0.0 121.4 jit_solution(5353383785967636709)
XLA Ops:
  0.7 1.1 fusion.71
  1.8 0.1 pad_maximum_fusion.7
  1.9 3.0 %collective-permute-start.2 = (bf16[8,12,1024]{2,1,0:T(8,128)(2,1)S(1)}, bf16[8,12,1024]{2,1,0:T(8,128)(2,1)S(1)}, u32[]{:S(2)}, u32[]{:S(2)}) collective-permute-start(bf16[8,12,1024]{2,1,0:T(8,128)(2,1)S(1)} %pad_maximum_fusion.7), channel_id=1, source_target_pairs={{0,1},{1,0},{2,3},{3,2},{4,5},{5,4},{6,7},{7,6},{8,9},{9,8},{10,11... | collective-permute-start | bytes 589832 | tf_op jit(solution)/shard_map/ppermute | solution.py:153
  4.9 1.1 fusion.70
  6.1 1.3 %collective-permute-start.3 = (bf16[6,12,1024]{2,1,0:T(8,128)(2,1)S(1)}, bf16[6,12,1024]{2,1,0:T(8,128)(2,1)S(1)}, u32[]{:S(2)}, u32[]{:S(2)}) collective-permute-start(bf16[6,12,1024]{2,1,0:T(8,128)(2,1)S(1)} %pad_maximum_fusion.11), channel_id=1, source_target_pairs={{2,1},{3,0},{4,3},{5,2},{6,5},{7,4},{8,7},{9,6},{10,9},{11,8},{12,... | collective-permute-start | bytes 442376 | tf_op jit(solution)/shard_map/ppermute | solution.py:153
  7.4 5.5 %collective-permute-start = (bf16[6,12,1024]{2,1,0:T(8,128)(2,1)S(1)}, bf16[6,12,1024]{2,1,0:T(8,128)(2,1)S(1)}, u32[]{:S(2)}, u32[]{:S(2)}) collective-permute-start(bf16[6,12,1024]{2,1,0:T(8,128)(2,1)S(1)} %pad_maximum_fusion.10), channel_id=1, source_target_pairs={{0,3},{1,2},{2,5},{3,4},{4,7},{5,6},{6,9},{7,8},{8,11},{9,10},{10,... | collective-permute-start | bytes 442376 | tf_op jit(solution)/shard_map/ppermute | solution.py:153
  12.9 0.7 slice_bitcast_fusion.1
  13.6 4.3 %collective-permute-start.1 = (bf16[6,16,1024]{2,1,0:T(8,128)(2,1)}, bf16[6,16,1024]{2,1,0:T(8,128)(2,1)S(1)}, u32[]{:S(2)}, u32[]{:S(2)}) collective-permute-start(bf16[6,16,1024]{2,1,0:T(8,128)(2,1)} %get-tuple-element.32), channel_id=1, source_target_pairs={{0,2},{1,3},{2,4},{3,5},{4,6},{5,7},{6,8},{7,9},{8,10},{9,11},{10,... | collective-permute-start | bytes 589832 | tf_op jit(solution)/shard_map/ppermute | solution.py:153
  18.2 0.1 copy.40
  18.3 0.1 copy.42
  18.6 0.1 eq.28
  18.6 1.0 fusion.45.bias_ref
  19.7 0.5 convolution_convert_fusion.1
  20.2 0.7 constant_dynamic-slice_fusion.3
  20.9 0.1 pad_maximum_fusion
  21.0 1.6 %collective-permute-start.4 = (bf16[6,16,1024]{2,1,0:T(8,128)(2,1)S(1)}, bf16[6,16,1024]{2,1,0:T(8,128)(2,1)S(1)}, u32[]{:S(2)}, u32[]{:S(2)}) collective-permute-start(bf16[6,16,1024]{2,1,0:T(8,128)(2,1)S(1)} %get-tuple-element.33), channel_id=1, source_target_pairs={{2,0},{3,1},{4,2},{5,3},{6,4},{7,5},{8,6},{9,7},{10,8},{11,9},{12,... | collective-permute-start | bytes 589832 | tf_op jit(solution)/shard_map/ppermute | solution.py:153
  22.6 0.5 collective-permute-start.6
  23.2 0.5 collective-permute-done.1
  23.7 6.7 %collective-permute-done.4 = bf16[6,16,1024]{2,1,0:T(8,128)(2,1)S(1)} collective-permute-done((bf16[6,16,1024]{2,1,0:T(8,128)(2,1)S(1)}, bf16[6,16,1024]{2,1,0:T(8,128)(2,1)S(1)}, u32[]{:S(2)}, u32[]{:S(2)}) %collective-permute-start.4) | collective-permute-done | bytes 196640 | tf_op jit(solution)/shard_map/ppermute | solution.py:153
  30.4 0.7 fusion.12
  31.2 2.2 %fusion.29 = f32[640,3072]{1,0:T(8,128)S(1)} fusion(bf16[512,3072]{1,0:T(8,128)(2,1)S(1)} %copy-done.3, bf16[640,1024]{1,0:T(8,128)(2,1)S(1)} %bitcast.31, s32[]{:T(128)S(6)} %select_n.95), kind=kOutput, calls=%fused_computation.41 | convolution fusion | flops 2013265920 | bytes 11665412 | tf_op jit(solution)/shard_map/dot_general | solution.py:374
  33.4 0.7 constant_dynamic-slice_fusion.2
  34.1 0.7 pad_maximum_fusion.9
  34.9 0.5 collective-permute-start.13
  35.4 0.5 fusion.18
  35.9 0.8 maximum_select_fusion.g_ref
  36.7 4.2 %add_convert_fusion.k_ref.v_ref = bf16[640,3072]{1,0:T(8,128)(2,1)S(1)} fusion(f32[640,3072]{1,0:T(8,128)S(1)} %fusion.29, bf16[512,3072]{1,0:T(8,128)(2,1)} %collective-permute-done.5, bf16[640,1024]{1,0:T(8,128)(2,1)S(1)} %bitcast.32, s32[]{:T(128)S(6)} %select_n.96), kind=kOutput, calls=%fused_computation | convolution fusion | flops 2017198080 | bytes 15597572 | tf_op jit(solution)/shard_map/dot_general | solution.py:377
  40.9 1.9 %copy-done = bf16[640,3072]{1,0:T(8,128)(2,1)} copy-done((bf16[640,3072]{1,0:T(8,128)(2,1)}, bf16[640,3072]{1,0:T(8,128)(2,1)S(1)}, u32[]{:S(2)}) %copy-start) | copy-done | bytes 3932184
  42.8 0.8 slice.181
  43.6 11.2 %block_attention.1 = (bf16[128,1024]{1,0:T(8,128)(2,1)}, bf16[128,1024]{1,0:T(8,128)(2,1)}, f32[2,640,1024]{2,1,0:T(8,128)}, bf16[2,640,1024]{2,1,0:T(8,128)(2,1)}) custom-call(bf16[128,1024]{1,0:T(8,128)(2,1)} %bitcast.40, bf16[640,3072]{1,0:T(8,128)(2,1)} %copy-done, bf16[640,3072]{1,0:T(8,128)(2,1)} %copy-done, ...), custom_call_target="tpu_custom_call" | custom-call | flops 2013265920 | bytes 9240576 | tf_op jit(solution)/shard_map/block_attention/pallas_call | solution.py:113
  54.8 1.3 %fusion.64 = (bf16[2,8,6,1024]{3,2,1,0:T(8,128)(2,1)S(1)}, bf16[2,8,6,1024]{3,2,1,0:T(8,128)(2,1)S(1)}) fusion(bf16[2,20,32,1024]{3,2,1,0:T(8,128)(2,1)} %bitcast.37), kind=kLoop, calls=%fused_computation.109 | loop fusion | bytes 786432 | tf_op jit(solution)/shard_map/slice | solution.py:208
  56.1 1.5 %fusion.63 = (bf16[2,6,6,1024]{3,2,1,0:T(8,128)(2,1)S(1)}, bf16[2,6,6,1024]{3,2,1,0:T(8,128)(2,1)S(1)}, bf16[2,6,6,1024]{3,2,1,0:T(8,128)(2,1)S(1)}, bf16[2,6,6,1024]{3,2,1,0:T(8,128)(2,1)S(1)}) fusion(bf16[2,20,32,1024]{3,2,1,0:T(8,128)(2,1)} %bitcast.38), kind=kLoop, calls=%fused_computation.108 | loop fusion | bytes 1179648 | tf_op jit(solution)/shard_map/slice | solution.py:208
  57.8 0.1 copy.59
  58.0 0.1 copy.61
  58.1 0.1 copy.62
  58.4 1.3 %collective-permute-start.7 = (bf16[2,6,12,1024]{3,1,2,0:T(8,128)(2,1)S(1)}, bf16[2,6,12,1024]{3,1,2,0:T(8,128)(2,1)}, u32[]{:S(2)}, u32[]{:S(2)}) collective-permute-start(bf16[2,6,12,1024]{3,1,2,0:T(8,128)(2,1)S(1)} %pad_maximum_fusion.3), channel_id=1, source_target_pairs={{2,1},{3,0},{4,3},{5,2},{6,5},{7,4},{8,7},{9,6},{10,9},{11,8},{12,... | collective-permute-start | bytes 884744 | tf_op jit(solution)/shard_map/ppermute | solution.py:153
  59.7 0.8 pad_maximum_fusion.4
  60.5 6.2 %collective-permute-start.11 = (bf16[2,6,12,1024]{3,1,2,0:T(8,128)(2,1)}, bf16[2,6,12,1024]{3,1,2,0:T(8,128)(2,1)}, u32[]{:S(2)}, u32[]{:S(2)}) collective-permute-start(bf16[2,6,12,1024]{3,1,2,0:T(8,128)(2,1)} %pad_maximum_fusion.4), channel_id=1, source_target_pairs={{0,3},{1,2},{2,5},{3,4},{4,7},{5,6},{6,9},{7,8},{8,11},{9,10},{10,... | collective-permute-start | bytes 884744 | tf_op jit(solution)/shard_map/ppermute | solution.py:153
  66.7 0.7 copy-done.8
  67.4 0.1 reshape.154
  67.5 0.2 copy.49
  67.7 1.6 %collective-permute-start.10 = (bf16[2,8,20,1024]{3,1,2,0:T(8,128)(2,1)S(1)}, bf16[2,8,20,1024]{3,1,2,0:T(8,128)(2,1)S(1)}, u32[]{:S(2)}, u32[]{:S(2)}) collective-permute-start(bf16[2,8,20,1024]{3,1,2,0:T(8,128)(2,1)S(1)} %pad_maximum_fusion.2), channel_id=1, source_target_pairs={{0,1},{1,0},{2,3},{3,2},{4,5},{5,4},{6,7},{7,6},{8,9},{9,8},{10,11... | collective-permute-start | bytes 1966088 | tf_op jit(solution)/shard_map/ppermute | solution.py:153
  69.3 1.6 %fusion.62 = (bf16[2,6,16,1024]{3,2,1,0:T(8,128)(2,1)S(1)}, bf16[2,6,16,1024]{3,2,1,0:T(8,128)(2,1)S(1)}) fusion(bf16[2,20,32,1024]{3,2,1,0:T(8,128)(2,1)} %bitcast.39), kind=kLoop, calls=%fused_computation.107 | loop fusion | bytes 1572864 | tf_op jit(solution)/shard_map/slice | solution.py:208
  70.9 1.5 %slice.183 = f32[2,8,16,1024]{3,2,1,0:T(8,128)S(1)} slice(f32[2,20,32,1024]{3,2,1,0:T(8,128)} %bitcast.46), slice={[0:2], [6:14], [6:22], [0:1024]} | slice | bytes 2097152 | tf_op jit(solution)/shard_map/slice | solution.py:200
  72.5 0.2 copy.60
  72.7 1.0 copy.65
  73.7 4.6 %collective-permute-start.12 = (bf16[2,6,16,1024]{3,1,2,0:T(8,128)(2,1)}, bf16[2,6,16,1024]{3,1,2,0:T(8,128)(2,1)}, u32[]{:S(2)}, u32[]{:S(2)}) collective-permute-start(bf16[2,6,16,1024]{3,1,2,0:T(8,128)(2,1)} %copy.65), channel_id=1, source_target_pairs={{0,2},{1,3},{2,4},{3,5},{4,6},{5,7},{6,8},{7,9},{8,10},{9,11},{10,... | collective-permute-start | bytes 1179656 | tf_op jit(solution)/shard_map/ppermute | solution.py:153
  78.3 1.3 %collective-permute-start.8 = (bf16[2,6,16,1024]{3,1,2,0:T(8,128)(2,1)S(1)}, bf16[2,6,16,1024]{3,1,2,0:T(8,128)(2,1)}, u32[]{:S(2)}, u32[]{:S(2)}) collective-permute-start(bf16[2,6,16,1024]{3,1,2,0:T(8,128)(2,1)S(1)} %copy.60), channel_id=1, source_target_pairs={{2,0},{3,1},{4,2},{5,3},{6,4},{7,5},{8,6},{9,7},{10,8},{11,9},{12,... | collective-permute-start | bytes 1179656 | tf_op jit(solution)/shard_map/ppermute | solution.py:153
  79.6 1.1 fusion.67
  80.6 0.7 collective-permute-done.11
  81.3 1.0 fusion.68
  82.4 15.1 %collective-permute-done.10 = bf16[2,8,20,1024]{3,1,2,0:T(8,128)(2,1)S(1)} collective-permute-done((bf16[2,8,20,1024]{3,1,2,0:T(8,128)(2,1)S(1)}, bf16[2,8,20,1024]{3,1,2,0:T(8,128)(2,1)S(1)}, u32[]{:S(2)}, u32[]{:S(2)}) %collective-permute-start.10) | collective-permute-done | bytes 655392 | tf_op jit(solution)/shard_map/ppermute | solution.py:153
  97.5 0.2 copy.55
  97.6 0.1 reshape.155
  97.7 2.4 %fusion.17 = bf16[512,512]{1,0:T(8,128)(2,1)} fusion(bf16[256,512]{1,0:T(8,128)(2,1)S(1)} %reshape.155, bf16[128,512]{1,0:T(8,128)(2,1)} %copy-done.8, bf16[128,512]{1,0:T(8,128)(2,1)} %copy-done.6, bf16[256,512]{1,0:T(8,128)(2,1)} %collective-permute-done.13, bf16[128,512]{1,0:T(8,128)(2,1)} %get-tuple-element.28, bf16[128,512]{1,0:T(8,128)(2,1)} %get-tuple-element.26), kind=kOutput, calls=%fused_computation.21 | convolution fusion | flops 272105472 | bytes 1572864 | tf_op jit(solution)/shard_map/dot_general | solution.py:467
  100.2 6.2 %all-to-all-start = ((bf16[8,64,512]{2,1,0:T(8,128)(2,1)}), bf16[8,64,512]{2,1,0:T(8,128)(2,1)S(1)}, u32[]{:S(2)}, u32[]{:S(2)}) async-start(bf16[8,64,512]{2,1,0:T(8,128)(2,1)} %bitcast.41), calls=%async_computation | async-start | bytes 1048576 | tf_op jit(solution)/shard_map/all_to_all | solution.py:470
  106.4 2.3 %fusion.27 = bf16[2,8,16,1024]{3,1,2,0:T(8,128)(2,1)S(1)} fusion(f32[2,8,16,1024]{3,2,1,0:T(8,128)S(1)} %slice.183, bf16[2,6,6,1024]{3,1,2,0:T(8,128)(2,1)S(1)} %get-tuple-element.25, bf16[2,6,16,1024]{3,1,2,0:T(8,128)(2,1)} %collective-permute-done.12, bf16[2,6,6,1024]{3,1,2,0:T(8,128)(2,1)S(1)} %get-tuple-element.24, ...), kind=kLoop, calls=%fused_computation.36 | loop fusion | flops 4456448 | bytes 3342336 | tf_op jit(solution)/shard_map/convert_element_type | solution.py:473
  108.8 0.2 copy.53
  108.9 0.2 copy.54
  109.1 1.2 convolution_convert_fusion.3
  110.3 3.1 %convolution_convert_fusion.2 = bf16[128,512]{1,0:T(8,128)(2,1)S(1)} fusion(bf16[512,3072]{1,0:T(8,128)(2,1)} %collective-permute-done.5, bf16[128,1024]{1,0:T(8,128)(2,1)S(1)} %bitcast.45, bf16[128,1024]{1,0:T(8,128)(2,1)S(1)} %bitcast.43, bf16[128,1024]{1,0:T(8,128)(2,1)S(1)} %copy-done.10), kind=kOutput, calls=%fused_computation.24 | convolution fusion | flops 405078016 | bytes 4063232 | tf_op jit(solution)/shard_map/dot_general | solution.py:384
  113.4 0.8 maximum_select_fusion.1
  114.1 6.5 %all-to-all-done = bf16[8,64,512]{2,1,0:T(8,128)(2,1)S(1)} async-done(((bf16[8,64,512]{2,1,0:T(8,128)(2,1)}), bf16[8,64,512]{2,1,0:T(8,128)(2,1)S(1)}, u32[]{:S(2)}, u32[]{:S(2)}) %all-to-all-start) | async-done | bytes 524320 | tf_op jit(solution)/shard_map/all_to_all | solution.py:470
  120.7 0.7 convert_reduce_fusion
  (55 shorter events, 1.3 us)
Async XLA Ops:
  0.6 12.3 %copy-start.1 = (bf16[1,8,16,1024]{3,2,1,0:T(8,128)(2,1)S(1)}, bf16[1,8,16,1024]{3,2,1,0:T(8,128)(2,1)}, u32[]{:S(2)}) copy-start(bf16[1,8,16,1024]{3,2,1,0:T(8,128)(2,1)} %param.5) | copy-start | bytes 786436
  0.6 17.4 %copy-start.9 = (s32[64,32]{0,1:T(8,128)S(1)}, s32[64,32]{0,1:T(8,128)}, u32[]{:S(2)}) copy-start(s32[64,32]{0,1:T(8,128)} %param.7) | copy-start | bytes 24580
  0.7 19.0 %copy-start.2 = (bf16[512,1024]{1,0:T(8,128)(2,1)S(1)}, bf16[512,1024]{1,0:T(8,128)(2,1)}, u32[]{:S(2)}) copy-start(bf16[512,1024]{1,0:T(8,128)(2,1)} %param.9) | copy-start | bytes 3145732
  0.7 19.0 %copy-start.5 = (bf16[1,8,16,1024]{3,2,1,0:T(8,128)(2,1)S(1)}, bf16[1,8,16,1024]{3,2,1,0:T(8,128)(2,1)}, u32[]{:S(2)}) copy-start(bf16[1,8,16,1024]{3,2,1,0:T(8,128)(2,1)} %param.6) | copy-start | bytes 786436
  1.9 21.3 %collective-permute-start.2 = (bf16[8,12,1024]{2,1,0:T(8,128)(2,1)S(1)}, bf16[8,12,1024]{2,1,0:T(8,128)(2,1)S(1)}, u32[]{:S(2)}, u32[]{:S(2)}) collective-permute-start(bf16[8,12,1024]{2,1,0:T(8,128)(2,1)S(1)} %pad_maximum_fusion.7), channel_id=1, source_target_pairs={{0,1},{1,0},{2,3},{3,2},{4,5},{5,4},{6,7},{7,6},{8,9},{9,8},{10,11... | collective-permute-start | bytes 589832 | tf_op jit(solution)/shard_map/ppermute | solution.py:153
  6.1 14.9 %collective-permute-start.3 = (bf16[6,12,1024]{2,1,0:T(8,128)(2,1)S(1)}, bf16[6,12,1024]{2,1,0:T(8,128)(2,1)S(1)}, u32[]{:S(2)}, u32[]{:S(2)}) collective-permute-start(bf16[6,12,1024]{2,1,0:T(8,128)(2,1)S(1)} %pad_maximum_fusion.11), channel_id=1, source_target_pairs={{2,1},{3,0},{4,3},{5,2},{6,5},{7,4},{8,7},{9,6},{10,9},{11,8},{12,... | collective-permute-start | bytes 442376 | tf_op jit(solution)/shard_map/ppermute | solution.py:153
  7.4 15.1 %collective-permute-start = (bf16[6,12,1024]{2,1,0:T(8,128)(2,1)S(1)}, bf16[6,12,1024]{2,1,0:T(8,128)(2,1)S(1)}, u32[]{:S(2)}, u32[]{:S(2)}) collective-permute-start(bf16[6,12,1024]{2,1,0:T(8,128)(2,1)S(1)} %pad_maximum_fusion.10), channel_id=1, source_target_pairs={{0,3},{1,2},{2,5},{3,4},{4,7},{5,6},{6,9},{7,8},{8,11},{9,10},{10,... | collective-permute-start | bytes 442376 | tf_op jit(solution)/shard_map/ppermute | solution.py:153
  13.6 10.1 %collective-permute-start.1 = (bf16[6,16,1024]{2,1,0:T(8,128)(2,1)}, bf16[6,16,1024]{2,1,0:T(8,128)(2,1)S(1)}, u32[]{:S(2)}, u32[]{:S(2)}) collective-permute-start(bf16[6,16,1024]{2,1,0:T(8,128)(2,1)} %get-tuple-element.32), channel_id=1, source_target_pairs={{0,2},{1,3},{2,4},{3,5},{4,6},{5,7},{6,8},{7,9},{8,10},{9,11},{10,... | collective-permute-start | bytes 589832 | tf_op jit(solution)/shard_map/ppermute | solution.py:153
  18.0 18.7 %collective-permute-start.5 = (bf16[512,3072]{1,0:T(8,128)(2,1)}, bf16[512,3072]{1,0:T(8,128)(2,1)}, u32[]{:S(2)}, u32[]{:S(2)}) collective-permute-start(bf16[512,3072]{1,0:T(8,128)(2,1)} %param.8), channel_id=1, source_target_pairs={{0,16},{16,0},{1,17},{17,1},{2,18},{18,2},{3,19},{19,3},{4,20},{20... | collective-permute-start | bytes 9437192 | tf_op jit(solution)/shard_map/ppermute | solution.py:269
  20.9 10.2 %copy-start.3 = (bf16[512,3072]{1,0:T(8,128)(2,1)S(1)}, bf16[512,3072]{1,0:T(8,128)(2,1)}, u32[]{:S(2)}) copy-start(bf16[512,3072]{1,0:T(8,128)(2,1)} %param.8) | copy-start | bytes 9437188
  21.0 9.4 %collective-permute-start.4 = (bf16[6,16,1024]{2,1,0:T(8,128)(2,1)S(1)}, bf16[6,16,1024]{2,1,0:T(8,128)(2,1)S(1)}, u32[]{:S(2)}, u32[]{:S(2)}) collective-permute-start(bf16[6,16,1024]{2,1,0:T(8,128)(2,1)S(1)} %get-tuple-element.33), channel_id=1, source_target_pairs={{2,0},{3,1},{4,2},{5,3},{6,4},{7,5},{8,6},{9,7},{10,8},{11,9},{12,... | collective-permute-start | bytes 589832 | tf_op jit(solution)/shard_map/ppermute | solution.py:153
  22.6 10.8 %collective-permute-start.6 = (bf16[640,1024]{1,0:T(8,128)(2,1)S(1)}, bf16[640,1024]{1,0:T(8,128)(2,1)S(1)}, u32[]{:S(2)}, u32[]{:S(2)}) collective-permute-start(bf16[640,1024]{1,0:T(8,128)(2,1)S(1)} %pad_maximum_fusion), channel_id=1, source_target_pairs={{0,16},{16,0},{1,17},{17,1},{2,18},{18,2},{3,19},{19,3},{4,20},{20... | collective-permute-start | bytes 3932168 | tf_op jit(solution)/shard_map/ppermute | solution.py:269
  34.9 62.9 %collective-permute-start.13 = (bf16[256,512]{1,0:T(8,128)(2,1)}, bf16[256,512]{1,0:T(8,128)(2,1)}, u32[]{:S(2)}, u32[]{:S(2)}) collective-permute-start(bf16[256,512]{1,0:T(8,128)(2,1)} %pad_maximum_fusion.9), channel_id=1, source_target_pairs={{0,1},{1,0},{2,3},{3,2},{4,5},{5,4},{6,7},{7,6},{8,9},{9,8},{10,11... | collective-permute-start | bytes 786440 | tf_op jit(solution)/shard_map/ppermute | solution.py:269
  40.9 2.0 %copy-start = (bf16[640,3072]{1,0:T(8,128)(2,1)}, bf16[640,3072]{1,0:T(8,128)(2,1)S(1)}, u32[]{:S(2)}) copy-start(bf16[640,3072]{1,0:T(8,128)(2,1)S(1)} %add_convert_fusion.k_ref.v_ref) | copy-start | bytes 11796484
  54.8 2.7 %copy-start.7 = (bf16[128,1024]{1,0:T(8,128)(2,1)S(1)}, bf16[128,1024]{1,0:T(8,128)(2,1)}, u32[]{:S(2)}) copy-start(bf16[128,1024]{1,0:T(8,128)(2,1)} %get-tuple-element.9) | copy-start | bytes 786436
  57.6 9.1 %copy-start.6 = (bf16[128,512]{1,0:T(8,128)(2,1)}, bf16[128,512]{1,0:T(8,128)(2,1)S(1)}, u32[]{:S(2)}) copy-start(bf16[128,512]{1,0:T(8,128)(2,1)S(1)} %get-tuple-element.30) | copy-start | bytes 393220
  57.6 9.1 %collective-permute-start.9 = (bf16[128,512]{1,0:T(8,128)(2,1)S(1)}, bf16[128,512]{1,0:T(8,128)(2,1)S(1)}, u32[]{:S(2)}, u32[]{:S(2)}) collective-permute-start(bf16[128,512]{1,0:T(8,128)(2,1)S(1)} %get-tuple-element.31), channel_id=1, source_target_pairs={{0,16},{16,0},{1,17},{17,1},{2,18},{18,2},{3,19},{19,3},{4,20},{20... | collective-permute-start | bytes 393224 | tf_op jit(solution)/shard_map/ppermute | solution.py:269
  58.4 19.9 %collective-permute-start.7 = (bf16[2,6,12,1024]{3,1,2,0:T(8,128)(2,1)S(1)}, bf16[2,6,12,1024]{3,1,2,0:T(8,128)(2,1)}, u32[]{:S(2)}, u32[]{:S(2)}) collective-permute-start(bf16[2,6,12,1024]{3,1,2,0:T(8,128)(2,1)S(1)} %pad_maximum_fusion.3), channel_id=1, source_target_pairs={{2,1},{3,0},{4,3},{5,2},{6,5},{7,4},{8,7},{9,6},{10,9},{11,8},{12,... | collective-permute-start | bytes 884744 | tf_op jit(solution)/shard_map/ppermute | solution.py:153
  60.5 20.8 %collective-permute-start.11 = (bf16[2,6,12,1024]{3,1,2,0:T(8,128)(2,1)}, bf16[2,6,12,1024]{3,1,2,0:T(8,128)(2,1)}, u32[]{:S(2)}, u32[]{:S(2)}) collective-permute-start(bf16[2,6,12,1024]{3,1,2,0:T(8,128)(2,1)} %pad_maximum_fusion.4), channel_id=1, source_target_pairs={{0,3},{1,2},{2,5},{3,4},{4,7},{5,6},{6,9},{7,8},{8,11},{9,10},{10,... | collective-permute-start | bytes 884744 | tf_op jit(solution)/shard_map/ppermute | solution.py:153
  66.7 0.7 copy-start.8
  67.7 29.7 %collective-permute-start.10 = (bf16[2,8,20,1024]{3,1,2,0:T(8,128)(2,1)S(1)}, bf16[2,8,20,1024]{3,1,2,0:T(8,128)(2,1)S(1)}, u32[]{:S(2)}, u32[]{:S(2)}) collective-permute-start(bf16[2,8,20,1024]{3,1,2,0:T(8,128)(2,1)S(1)} %pad_maximum_fusion.2), channel_id=1, source_target_pairs={{0,1},{1,0},{2,3},{3,2},{4,5},{5,4},{6,7},{7,6},{8,9},{9,8},{10,11... | collective-permute-start | bytes 1966088 | tf_op jit(solution)/shard_map/ppermute | solution.py:153
  73.7 32.6 %collective-permute-start.12 = (bf16[2,6,16,1024]{3,1,2,0:T(8,128)(2,1)}, bf16[2,6,16,1024]{3,1,2,0:T(8,128)(2,1)}, u32[]{:S(2)}, u32[]{:S(2)}) collective-permute-start(bf16[2,6,16,1024]{3,1,2,0:T(8,128)(2,1)} %copy.65), channel_id=1, source_target_pairs={{0,2},{1,3},{2,4},{3,5},{4,6},{5,7},{6,8},{7,9},{8,10},{9,11},{10,... | collective-permute-start | bytes 1179656 | tf_op jit(solution)/shard_map/ppermute | solution.py:153
  78.3 28.1 %collective-permute-start.8 = (bf16[2,6,16,1024]{3,1,2,0:T(8,128)(2,1)S(1)}, bf16[2,6,16,1024]{3,1,2,0:T(8,128)(2,1)}, u32[]{:S(2)}, u32[]{:S(2)}) collective-permute-start(bf16[2,6,16,1024]{3,1,2,0:T(8,128)(2,1)S(1)} %copy.60), channel_id=1, source_target_pairs={{2,0},{3,1},{4,2},{5,3},{6,4},{7,5},{8,6},{9,7},{10,8},{11,9},{12,... | collective-permute-start | bytes 1179656 | tf_op jit(solution)/shard_map/ppermute | solution.py:153
  100.2 20.5 %all-to-all-start = ((bf16[8,64,512]{2,1,0:T(8,128)(2,1)}), bf16[8,64,512]{2,1,0:T(8,128)(2,1)S(1)}, u32[]{:S(2)}, u32[]{:S(2)}) async-start(bf16[8,64,512]{2,1,0:T(8,128)(2,1)} %bitcast.41), calls=%async_computation | async-start | bytes 1048576 | tf_op jit(solution)/shard_map/all_to_all | solution.py:470
  106.4 2.7 %copy-start.4 = (bf16[512,3072]{1,0:T(8,128)(2,1)S(1)}, bf16[512,3072]{1,0:T(8,128)(2,1)}, u32[]{:S(2)}) copy-start(bf16[512,3072]{1,0:T(8,128)(2,1)} %param.8) | copy-start | bytes 9437188
  106.4 2.7 %copy-start.10 = (bf16[128,1024]{1,0:T(8,128)(2,1)S(1)}, bf16[128,1024]{1,0:T(8,128)(2,1)}, u32[]{:S(2)}) copy-start(bf16[128,1024]{1,0:T(8,128)(2,1)} %get-tuple-element.6) | copy-start | bytes 786436

commit v19 on v17

--- a/solution.py
+++ b/solution.py
@@ -80,7 +80,7 @@
 
 def attention_kernel(q_ref, k_ref, v_ref, g_ref, bias_ref, att_ref, gq_ref, gkv_ref, gkv_low_ref,
                      *, head_dim, scale, lanes):
-    bias = bias_ref[...]
+    bias = bias_ref[...].astype(jnp.float32)
     for sub in range(q_ref.shape[1] // lanes):
         cols = slice(sub * lanes, (sub + 1) * lanes)
         att, gq, grad_k, grad_v = pair_terms(
@@ -431,7 +431,7 @@
     inside = (jnp.abs(delta_row) <= radius) & (jnp.abs(delta_col) <= radius)
     itself = (delta_row == 0) & (delta_col == 0)
     allowed = inside & ((valid_ext == 1) | itself)
-    bias = jnp.where(allowed, 0.0, -jnp.inf).astype(jnp.float32)
+    bias = jnp.where(allowed, 0.0, -jnp.inf).astype(jnp.bfloat16)
 
     attended, grad_query, grad_kv, grad_kv_low = block_attention(
         query, projected, grad_attn, bias, HEADS

time: 122 us -> 122 us (level)
  transfers between devices with their start and end apart: 15 -> 15, of which waited for: 5 -> 5; matrix products, arithmetic and copies ran while one was open for 31% -> 30% of each run, Pallas kernels for 9% -> 9%
where the time goes in v19:
time: 122 us
  starting transfers between devices  38.6 us (32%)
  waiting for transfers between devices  30.1 us (25%)
  local copies, waits for them, and re-layouts  18.4 us (15%)
  matrix products  14.1 us (12%)
  Pallas kernels  10.7 us (9%)
  other arithmetic  8.51 us (7%)
    ppermute x10, starting transfers between devices, sent_to(): return lax.ppermute(value, ('lat', 'lon'), grid_pairs(delta_lat, delta_lon))  30.5 us
    ppermute x10, waiting for transfers between devices, sent_to(): return lax.ppermute(value, ('lat', 'lon'), grid_pairs(delta_lat, delta_lon))  23.6 us
    pallas_call x1, Pallas kernels, block_attention(): pl.pallas_call(kernel, grid=(pairs,), in_specs=[pl.BlockSpec((queries, la...  10.7 us
    all_to_all x1, starting transfers between devices, shards(): lax.all_to_all(partial.astype(jnp.bfloat16), 'lat', 0, 0, tiled=True)  6.87 us
    all_to_all x1, waiting for transfers between devices, shards(): lax.all_to_all(partial.astype(jnp.bfloat16), 'lat', 0, 0, tiled=True)  6.53 us
    slice x3, local copies, waits for them, and re-layouts, halo_return(): pieces.append((da, db, ext_low[:, row_slices[da], col_slices[db]]))  4.34 us
    dot_general x1, matrix products, project(): jnp.dot(columns(rows, 1 - dp_index, rows_half), qkv_other, preferred_elem...  4.19 us
    unnamed x31, local copies, waits for them, and re-layouts  3.91 us
  transfers between devices with their start and end apart: 15, of which 5 were waited for; matrix products, arithmetic and copies ran while one was open for 30% of the time, Pallas kernels for 9%

profile of v19, /device:TPU:0, one launch (start us, length us, event | category | flops | bytes accessed | tf_op | source)
XLA Modules:
  0.0 121.6 jit_solution(7146225191383963681)
XLA Ops:
  0.7 1.1 fusion.70
  1.8 0.1 pad_maximum_fusion.7
  1.9 3.0 %collective-permute-start.2 = (bf16[8,12,1024]{2,1,0:T(8,128)(2,1)S(1)}, bf16[8,12,1024]{2,1,0:T(8,128)(2,1)S(1)}, u32[]{:S(2)}, u32[]{:S(2)}) collective-permute-start(bf16[8,12,1024]{2,1,0:T(8,128)(2,1)S(1)} %pad_maximum_fusion.7), channel_id=1, source_target_pairs={{0,1},{1,0},{2,3},{3,2},{4,5},{5,4},{6,7},{7,6},{8,9},{9,8},{10,11... | collective-permute-start | bytes 589832 | tf_op jit(solution)/shard_map/ppermute | solution.py:153
  4.9 1.1 fusion.69
  6.1 1.3 %collective-permute-start.3 = (bf16[6,12,1024]{2,1,0:T(8,128)(2,1)S(1)}, bf16[6,12,1024]{2,1,0:T(8,128)(2,1)S(1)}, u32[]{:S(2)}, u32[]{:S(2)}) collective-permute-start(bf16[6,12,1024]{2,1,0:T(8,128)(2,1)S(1)} %pad_maximum_fusion.11), channel_id=1, source_target_pairs={{2,1},{3,0},{4,3},{5,2},{6,5},{7,4},{8,7},{9,6},{10,9},{11,8},{12,... | collective-permute-start | bytes 442376 | tf_op jit(solution)/shard_map/ppermute | solution.py:153
  7.4 5.5 %collective-permute-start = (bf16[6,12,1024]{2,1,0:T(8,128)(2,1)S(1)}, bf16[6,12,1024]{2,1,0:T(8,128)(2,1)S(1)}, u32[]{:S(2)}, u32[]{:S(2)}) collective-permute-start(bf16[6,12,1024]{2,1,0:T(8,128)(2,1)S(1)} %pad_maximum_fusion.10), channel_id=1, source_target_pairs={{0,3},{1,2},{2,5},{3,4},{4,7},{5,6},{6,9},{7,8},{8,11},{9,10},{10,... | collective-permute-start | bytes 442376 | tf_op jit(solution)/shard_map/ppermute | solution.py:153
  12.9 0.7 slice_bitcast_fusion.1
  13.6 4.3 %collective-permute-start.1 = (bf16[6,16,1024]{2,1,0:T(8,128)(2,1)}, bf16[6,16,1024]{2,1,0:T(8,128)(2,1)S(1)}, u32[]{:S(2)}, u32[]{:S(2)}) collective-permute-start(bf16[6,16,1024]{2,1,0:T(8,128)(2,1)} %get-tuple-element.32), channel_id=1, source_target_pairs={{0,2},{1,3},{2,4},{3,5},{4,6},{5,7},{6,8},{7,9},{8,10},{9,11},{10,... | collective-permute-start | bytes 589832 | tf_op jit(solution)/shard_map/ppermute | solution.py:153
  18.2 0.1 copy.40
  18.3 0.1 copy.42
  18.5 0.1 pad_dynamic-slice_fusion
  18.6 1.0 select_convert_fusion.bias_ref
  19.6 0.5 convolution_convert_fusion.1
  20.1 0.7 constant_dynamic-slice_fusion.3
  20.8 0.1 pad_maximum_fusion
  20.9 1.6 %collective-permute-start.4 = (bf16[6,16,1024]{2,1,0:T(8,128)(2,1)S(1)}, bf16[6,16,1024]{2,1,0:T(8,128)(2,1)S(1)}, u32[]{:S(2)}, u32[]{:S(2)}) collective-permute-start(bf16[6,16,1024]{2,1,0:T(8,128)(2,1)S(1)} %get-tuple-element.33), channel_id=1, source_target_pairs={{2,0},{3,1},{4,2},{5,3},{6,4},{7,5},{8,6},{9,7},{10,8},{11,9},{12,... | collective-permute-start | bytes 589832 | tf_op jit(solution)/shard_map/ppermute | solution.py:153
  22.5 0.5 collective-permute-start.6
  23.2 0.5 collective-permute-done.1
  23.7 6.7 %collective-permute-done.4 = bf16[6,16,1024]{2,1,0:T(8,128)(2,1)S(1)} collective-permute-done((bf16[6,16,1024]{2,1,0:T(8,128)(2,1)S(1)}, bf16[6,16,1024]{2,1,0:T(8,128)(2,1)S(1)}, u32[]{:S(2)}, u32[]{:S(2)}) %collective-permute-start.4) | collective-permute-done | bytes 196640 | tf_op jit(solution)/shard_map/ppermute | solution.py:153
  30.4 0.7 fusion.12
  31.1 2.2 %fusion.29 = f32[640,3072]{1,0:T(8,128)S(1)} fusion(bf16[512,3072]{1,0:T(8,128)(2,1)S(1)} %copy-done.3, bf16[640,1024]{1,0:T(8,128)(2,1)S(1)} %bitcast.31, s32[]{:T(128)S(6)} %select_n.95), kind=kOutput, calls=%fused_computation.41 | convolution fusion | flops 2013265920 | bytes 11665412 | tf_op jit(solution)/shard_map/dot_general | solution.py:374
  33.4 0.7 constant_dynamic-slice_fusion.2
  34.0 0.8 pad_maximum_fusion.9
  34.8 0.5 collective-permute-start.13
  35.3 0.5 fusion.18
  35.8 0.8 maximum_select_fusion.g_ref
  36.6 4.2 %add_convert_fusion.k_ref.v_ref = bf16[640,3072]{1,0:T(8,128)(2,1)S(1)} fusion(f32[640,3072]{1,0:T(8,128)S(1)} %fusion.29, bf16[512,3072]{1,0:T(8,128)(2,1)} %collective-permute-done.5, bf16[640,1024]{1,0:T(8,128)(2,1)S(1)} %bitcast.32, s32[]{:T(128)S(6)} %select_n.96), kind=kOutput, calls=%fused_computation | convolution fusion | flops 2017198080 | bytes 15597572 | tf_op jit(solution)/shard_map/dot_general | solution.py:377
  40.8 1.9 %copy-done = bf16[640,3072]{1,0:T(8,128)(2,1)} copy-done((bf16[640,3072]{1,0:T(8,128)(2,1)}, bf16[640,3072]{1,0:T(8,128)(2,1)S(1)}, u32[]{:S(2)}) %copy-start) | copy-done | bytes 3932184
  42.8 0.8 slice.181
  43.6 10.7 %block_attention.1 = (bf16[128,1024]{1,0:T(8,128)(2,1)}, bf16[128,1024]{1,0:T(8,128)(2,1)}, f32[2,640,1024]{2,1,0:T(8,128)}, bf16[2,640,1024]{2,1,0:T(8,128)(2,1)}) custom-call(bf16[128,1024]{1,0:T(8,128)(2,1)} %bitcast.40, bf16[640,3072]{1,0:T(8,128)(2,1)} %copy-done, bf16[640,3072]{1,0:T(8,128)(2,1)} %copy-done, ...), custom_call_target="tpu_custom_call" | custom-call | flops 2013265920 | bytes 9240576 | tf_op jit(solution)/shard_map/block_attention/pallas_call | solution.py:113
  54.2 1.3 %fusion.63 = (bf16[2,8,6,1024]{3,2,1,0:T(8,128)(2,1)S(1)}, bf16[2,8,6,1024]{3,2,1,0:T(8,128)(2,1)S(1)}) fusion(bf16[2,20,32,1024]{3,2,1,0:T(8,128)(2,1)} %bitcast.37), kind=kLoop, calls=%fused_computation.109 | loop fusion | bytes 786432 | tf_op jit(solution)/shard_map/slice | solution.py:208
  55.5 1.5 %fusion.62 = (bf16[2,6,6,1024]{3,2,1,0:T(8,128)(2,1)S(1)}, bf16[2,6,6,1024]{3,2,1,0:T(8,128)(2,1)S(1)}, bf16[2,6,6,1024]{3,2,1,0:T(8,128)(2,1)S(1)}, bf16[2,6,6,1024]{3,2,1,0:T(8,128)(2,1)S(1)}) fusion(bf16[2,20,32,1024]{3,2,1,0:T(8,128)(2,1)} %bitcast.38), kind=kLoop, calls=%fused_computation.108 | loop fusion | bytes 1179648 | tf_op jit(solution)/shard_map/slice | solution.py:208
  57.1 0.1 copy.58
  57.2 0.1 copy.59
  57.4 0.1 copy.61
  57.5 0.1 copy.62
  57.8 1.3 %collective-permute-start.7 = (bf16[2,6,12,1024]{3,1,2,0:T(8,128)(2,1)S(1)}, bf16[2,6,12,1024]{3,1,2,0:T(8,128)(2,1)}, u32[]{:S(2)}, u32[]{:S(2)}) collective-permute-start(bf16[2,6,12,1024]{3,1,2,0:T(8,128)(2,1)S(1)} %pad_maximum_fusion.3), channel_id=1, source_target_pairs={{2,1},{3,0},{4,3},{5,2},{6,5},{7,4},{8,7},{9,6},{10,9},{11,8},{12,... | collective-permute-start | bytes 884744 | tf_op jit(solution)/shard_map/ppermute | solution.py:153
  59.1 0.8 pad_maximum_fusion.4
  59.9 6.2 %collective-permute-start.11 = (bf16[2,6,12,1024]{3,1,2,0:T(8,128)(2,1)}, bf16[2,6,12,1024]{3,1,2,0:T(8,128)(2,1)}, u32[]{:S(2)}, u32[]{:S(2)}) collective-permute-start(bf16[2,6,12,1024]{3,1,2,0:T(8,128)(2,1)} %pad_maximum_fusion.4), channel_id=1, source_target_pairs={{0,3},{1,2},{2,5},{3,4},{4,7},{5,6},{6,9},{7,8},{8,11},{9,10},{10,... | collective-permute-start | bytes 884744 | tf_op jit(solution)/shard_map/ppermute | solution.py:153
  66.2 0.1 reshape.154
  66.3 0.2 copy.49
  66.5 1.6 %collective-permute-start.10 = (bf16[2,8,20,1024]{3,1,2,0:T(8,128)(2,1)S(1)}, bf16[2,8,20,1024]{3,1,2,0:T(8,128)(2,1)S(1)}, u32[]{:S(2)}, u32[]{:S(2)}) collective-permute-start(bf16[2,8,20,1024]{3,1,2,0:T(8,128)(2,1)S(1)} %pad_maximum_fusion.2), channel_id=1, source_target_pairs={{0,1},{1,0},{2,3},{3,2},{4,5},{5,4},{6,7},{7,6},{8,9},{9,8},{10,11... | collective-permute-start | bytes 1966088 | tf_op jit(solution)/shard_map/ppermute | solution.py:153
  68.1 1.6 %fusion.61 = (bf16[2,6,16,1024]{3,2,1,0:T(8,128)(2,1)S(1)}, bf16[2,6,16,1024]{3,2,1,0:T(8,128)(2,1)S(1)}) fusion(bf16[2,20,32,1024]{3,2,1,0:T(8,128)(2,1)} %bitcast.39), kind=kLoop, calls=%fused_computation.107 | loop fusion | bytes 1572864 | tf_op jit(solution)/shard_map/slice | solution.py:208
  69.7 1.6 %slice.183 = f32[2,8,16,1024]{3,2,1,0:T(8,128)S(1)} slice(f32[2,20,32,1024]{3,2,1,0:T(8,128)} %bitcast.46), slice={[0:2], [6:14], [6:22], [0:1024]} | slice | bytes 2097152 | tf_op jit(solution)/shard_map/slice | solution.py:200
  71.3 0.2 copy.60
  71.5 1.0 copy.65
  72.6 4.4 %collective-permute-start.12 = (bf16[2,6,16,1024]{3,1,2,0:T(8,128)(2,1)}, bf16[2,6,16,1024]{3,1,2,0:T(8,128)(2,1)}, u32[]{:S(2)}, u32[]{:S(2)}) collective-permute-start(bf16[2,6,16,1024]{3,1,2,0:T(8,128)(2,1)} %copy.65), channel_id=1, source_target_pairs={{0,2},{1,3},{2,4},{3,5},{4,6},{5,7},{6,8},{7,9},{8,10},{9,11},{10,... | collective-permute-start | bytes 1179656 | tf_op jit(solution)/shard_map/ppermute | solution.py:153
  77.0 1.5 %collective-permute-start.8 = (bf16[2,6,16,1024]{3,1,2,0:T(8,128)(2,1)S(1)}, bf16[2,6,16,1024]{3,1,2,0:T(8,128)(2,1)}, u32[]{:S(2)}, u32[]{:S(2)}) collective-permute-start(bf16[2,6,16,1024]{3,1,2,0:T(8,128)(2,1)S(1)} %copy.60), channel_id=1, source_target_pairs={{2,0},{3,1},{4,2},{5,3},{6,4},{7,5},{8,6},{9,7},{10,8},{11,9},{12,... | collective-permute-start | bytes 1179656 | tf_op jit(solution)/shard_map/ppermute | solution.py:153
  78.4 1.1 fusion.66
  79.5 1.2 %collective-permute-done.11 = bf16[2,6,12,1024]{3,1,2,0:T(8,128)(2,1)} collective-permute-done((bf16[2,6,12,1024]{3,1,2,0:T(8,128)(2,1)}, bf16[2,6,12,1024]{3,1,2,0:T(8,128)(2,1)}, u32[]{:S(2)}, u32[]{:S(2)}) %collective-permute-start.11) | collective-permute-done | bytes 294944 | tf_op jit(solution)/shard_map/ppermute | solution.py:153
  80.7 1.0 fusion.67
  81.8 15.2 %collective-permute-done.10 = bf16[2,8,20,1024]{3,1,2,0:T(8,128)(2,1)S(1)} collective-permute-done((bf16[2,8,20,1024]{3,1,2,0:T(8,128)(2,1)S(1)}, bf16[2,8,20,1024]{3,1,2,0:T(8,128)(2,1)S(1)}, u32[]{:S(2)}, u32[]{:S(2)}) %collective-permute-start.10) | collective-permute-done | bytes 655392 | tf_op jit(solution)/shard_map/ppermute | solution.py:153
  96.9 0.2 copy.55
  97.1 0.1 reshape.155
  97.2 2.4 %fusion.17 = bf16[512,512]{1,0:T(8,128)(2,1)} fusion(bf16[256,512]{1,0:T(8,128)(2,1)S(1)} %reshape.155, bf16[128,512]{1,0:T(8,128)(2,1)} %copy-done.8, bf16[128,512]{1,0:T(8,128)(2,1)} %copy-done.6, bf16[256,512]{1,0:T(8,128)(2,1)} %collective-permute-done.13, bf16[128,512]{1,0:T(8,128)(2,1)} %get-tuple-element.28, bf16[128,512]{1,0:T(8,128)(2,1)} %get-tuple-element.26), kind=kOutput, calls=%fused_computation.21 | convolution fusion | flops 272105472 | bytes 1572864 | tf_op jit(solution)/shard_map/dot_general | solution.py:467
  99.7 6.9 %all-to-all-start = ((bf16[8,64,512]{2,1,0:T(8,128)(2,1)}), bf16[8,64,512]{2,1,0:T(8,128)(2,1)S(1)}, u32[]{:S(2)}, u32[]{:S(2)}) async-start(bf16[8,64,512]{2,1,0:T(8,128)(2,1)} %bitcast.41), calls=%async_computation | async-start | bytes 1048576 | tf_op jit(solution)/shard_map/all_to_all | solution.py:470
  106.6 2.3 %fusion.27 = bf16[2,8,16,1024]{3,1,2,0:T(8,128)(2,1)S(1)} fusion(f32[2,8,16,1024]{3,2,1,0:T(8,128)S(1)} %slice.183, bf16[2,6,6,1024]{3,1,2,0:T(8,128)(2,1)S(1)} %get-tuple-element.25, bf16[2,6,16,1024]{3,1,2,0:T(8,128)(2,1)} %collective-permute-done.12, bf16[2,6,6,1024]{3,1,2,0:T(8,128)(2,1)S(1)} %get-tuple-element.24, ...), kind=kLoop, calls=%fused_computation.36 | loop fusion | flops 4456448 | bytes 3342336 | tf_op jit(solution)/shard_map/convert_element_type | solution.py:473
  109.0 0.2 copy.53
  109.1 0.2 copy.54
  109.3 1.2 convolution_convert_fusion.3
  110.5 3.1 %convolution_convert_fusion.2 = bf16[128,512]{1,0:T(8,128)(2,1)S(1)} fusion(bf16[512,3072]{1,0:T(8,128)(2,1)} %collective-permute-done.5, bf16[128,1024]{1,0:T(8,128)(2,1)S(1)} %bitcast.45, bf16[128,1024]{1,0:T(8,128)(2,1)S(1)} %bitcast.43, bf16[128,1024]{1,0:T(8,128)(2,1)S(1)} %copy-done.10), kind=kOutput, calls=%fused_computation.24 | convolution fusion | flops 405078016 | bytes 4063232 | tf_op jit(solution)/shard_map/dot_general | solution.py:384
  113.6 0.8 maximum_select_fusion.1
  114.4 6.5 %all-to-all-done = bf16[8,64,512]{2,1,0:T(8,128)(2,1)S(1)} async-done(((bf16[8,64,512]{2,1,0:T(8,128)(2,1)}), bf16[8,64,512]{2,1,0:T(8,128)(2,1)S(1)}, u32[]{:S(2)}, u32[]{:S(2)}) %all-to-all-start) | async-done | bytes 524320 | tf_op jit(solution)/shard_map/all_to_all | solution.py:470
  120.9 0.7 convert_reduce_fusion
  (55 shorter events, 1.2 us)
Async XLA Ops:
  0.6 12.3 %copy-start.1 = (bf16[1,8,16,1024]{3,2,1,0:T(8,128)(2,1)S(1)}, bf16[1,8,16,1024]{3,2,1,0:T(8,128)(2,1)}, u32[]{:S(2)}) copy-start(bf16[1,8,16,1024]{3,2,1,0:T(8,128)(2,1)} %param.5) | copy-start | bytes 786436
  0.6 17.4 %copy-start.9 = (s32[64,32]{0,1:T(8,128)S(1)}, s32[64,32]{0,1:T(8,128)}, u32[]{:S(2)}) copy-start(s32[64,32]{0,1:T(8,128)} %param.7) | copy-start | bytes 24580
  0.7 19.0 %copy-start.2 = (bf16[512,1024]{1,0:T(8,128)(2,1)S(1)}, bf16[512,1024]{1,0:T(8,128)(2,1)}, u32[]{:S(2)}) copy-start(bf16[512,1024]{1,0:T(8,128)(2,1)} %param.9) | copy-start | bytes 3145732
  0.7 19.0 %copy-start.5 = (bf16[1,8,16,1024]{3,2,1,0:T(8,128)(2,1)S(1)}, bf16[1,8,16,1024]{3,2,1,0:T(8,128)(2,1)}, u32[]{:S(2)}) copy-start(bf16[1,8,16,1024]{3,2,1,0:T(8,128)(2,1)} %param.6) | copy-start | bytes 786436
  1.9 21.2 %collective-permute-start.2 = (bf16[8,12,1024]{2,1,0:T(8,128)(2,1)S(1)}, bf16[8,12,1024]{2,1,0:T(8,128)(2,1)S(1)}, u32[]{:S(2)}, u32[]{:S(2)}) collective-permute-start(bf16[8,12,1024]{2,1,0:T(8,128)(2,1)S(1)} %pad_maximum_fusion.7), channel_id=1, source_target_pairs={{0,1},{1,0},{2,3},{3,2},{4,5},{5,4},{6,7},{7,6},{8,9},{9,8},{10,11... | collective-permute-start | bytes 589832 | tf_op jit(solution)/shard_map/ppermute | solution.py:153
  6.1 14.8 %collective-permute-start.3 = (bf16[6,12,1024]{2,1,0:T(8,128)(2,1)S(1)}, bf16[6,12,1024]{2,1,0:T(8,128)(2,1)S(1)}, u32[]{:S(2)}, u32[]{:S(2)}) collective-permute-start(bf16[6,12,1024]{2,1,0:T(8,128)(2,1)S(1)} %pad_maximum_fusion.11), channel_id=1, source_target_pairs={{2,1},{3,0},{4,3},{5,2},{6,5},{7,4},{8,7},{9,6},{10,9},{11,8},{12,... | collective-permute-start | bytes 442376 | tf_op jit(solution)/shard_map/ppermute | solution.py:153
  7.4 15.1 %collective-permute-start = (bf16[6,12,1024]{2,1,0:T(8,128)(2,1)S(1)}, bf16[6,12,1024]{2,1,0:T(8,128)(2,1)S(1)}, u32[]{:S(2)}, u32[]{:S(2)}) collective-permute-start(bf16[6,12,1024]{2,1,0:T(8,128)(2,1)S(1)} %pad_maximum_fusion.10), channel_id=1, source_target_pairs={{0,3},{1,2},{2,5},{3,4},{4,7},{5,6},{6,9},{7,8},{8,11},{9,10},{10,... | collective-permute-start | bytes 442376 | tf_op jit(solution)/shard_map/ppermute | solution.py:153
  13.6 10.1 %collective-permute-start.1 = (bf16[6,16,1024]{2,1,0:T(8,128)(2,1)}, bf16[6,16,1024]{2,1,0:T(8,128)(2,1)S(1)}, u32[]{:S(2)}, u32[]{:S(2)}) collective-permute-start(bf16[6,16,1024]{2,1,0:T(8,128)(2,1)} %get-tuple-element.32), channel_id=1, source_target_pairs={{0,2},{1,3},{2,4},{3,5},{4,6},{5,7},{6,8},{7,9},{8,10},{9,11},{10,... | collective-permute-start | bytes 589832 | tf_op jit(solution)/shard_map/ppermute | solution.py:153
  18.0 18.7 %collective-permute-start.5 = (bf16[512,3072]{1,0:T(8,128)(2,1)}, bf16[512,3072]{1,0:T(8,128)(2,1)}, u32[]{:S(2)}, u32[]{:S(2)}) collective-permute-start(bf16[512,3072]{1,0:T(8,128)(2,1)} %param.8), channel_id=1, source_target_pairs={{0,16},{16,0},{1,17},{17,1},{2,18},{18,2},{3,19},{19,3},{4,20},{20... | collective-permute-start | bytes 9437192 | tf_op jit(solution)/shard_map/ppermute | solution.py:269
  20.9 10.2 %copy-start.3 = (bf16[512,3072]{1,0:T(8,128)(2,1)S(1)}, bf16[512,3072]{1,0:T(8,128)(2,1)}, u32[]{:S(2)}) copy-start(bf16[512,3072]{1,0:T(8,128)(2,1)} %param.8) | copy-start | bytes 9437188
  20.9 9.4 %collective-permute-start.4 = (bf16[6,16,1024]{2,1,0:T(8,128)(2,1)S(1)}, bf16[6,16,1024]{2,1,0:T(8,128)(2,1)S(1)}, u32[]{:S(2)}, u32[]{:S(2)}) collective-permute-start(bf16[6,16,1024]{2,1,0:T(8,128)(2,1)S(1)} %get-tuple-element.33), channel_id=1, source_target_pairs={{2,0},{3,1},{4,2},{5,3},{6,4},{7,5},{8,6},{9,7},{10,8},{11,9},{12,... | collective-permute-start | bytes 589832 | tf_op jit(solution)/shard_map/ppermute | solution.py:153
  22.5 10.8 %collective-permute-start.6 = (bf16[640,1024]{1,0:T(8,128)(2,1)S(1)}, bf16[640,1024]{1,0:T(8,128)(2,1)S(1)}, u32[]{:S(2)}, u32[]{:S(2)}) collective-permute-start(bf16[640,1024]{1,0:T(8,128)(2,1)S(1)} %pad_maximum_fusion), channel_id=1, source_target_pairs={{0,16},{16,0},{1,17},{17,1},{2,18},{18,2},{3,19},{19,3},{4,20},{20... | collective-permute-start | bytes 3932168 | tf_op jit(solution)/shard_map/ppermute | solution.py:269
  34.8 62.4 %collective-permute-start.13 = (bf16[256,512]{1,0:T(8,128)(2,1)}, bf16[256,512]{1,0:T(8,128)(2,1)}, u32[]{:S(2)}, u32[]{:S(2)}) collective-permute-start(bf16[256,512]{1,0:T(8,128)(2,1)} %pad_maximum_fusion.9), channel_id=1, source_target_pairs={{0,1},{1,0},{2,3},{3,2},{4,5},{5,4},{6,7},{7,6},{8,9},{9,8},{10,11... | collective-permute-start | bytes 786440 | tf_op jit(solution)/shard_map/ppermute | solution.py:269
  40.8 2.0 %copy-start = (bf16[640,3072]{1,0:T(8,128)(2,1)}, bf16[640,3072]{1,0:T(8,128)(2,1)S(1)}, u32[]{:S(2)}) copy-start(bf16[640,3072]{1,0:T(8,128)(2,1)S(1)} %add_convert_fusion.k_ref.v_ref) | copy-start | bytes 11796484
  54.2 2.7 %copy-start.7 = (bf16[128,1024]{1,0:T(8,128)(2,1)S(1)}, bf16[128,1024]{1,0:T(8,128)(2,1)}, u32[]{:S(2)}) copy-start(bf16[128,1024]{1,0:T(8,128)(2,1)} %get-tuple-element.9) | copy-start | bytes 786436
  57.0 9.1 %copy-start.6 = (bf16[128,512]{1,0:T(8,128)(2,1)}, bf16[128,512]{1,0:T(8,128)(2,1)S(1)}, u32[]{:S(2)}) copy-start(bf16[128,512]{1,0:T(8,128)(2,1)S(1)} %get-tuple-element.30) | copy-start | bytes 393220
  57.0 9.1 %collective-permute-start.9 = (bf16[128,512]{1,0:T(8,128)(2,1)S(1)}, bf16[128,512]{1,0:T(8,128)(2,1)S(1)}, u32[]{:S(2)}, u32[]{:S(2)}) collective-permute-start(bf16[128,512]{1,0:T(8,128)(2,1)S(1)} %get-tuple-element.31), channel_id=1, source_target_pairs={{0,16},{16,0},{1,17},{17,1},{2,18},{18,2},{3,19},{19,3},{4,20},{20... | collective-permute-start | bytes 393224 | tf_op jit(solution)/shard_map/ppermute | solution.py:269
  57.8 19.1 %collective-permute-start.7 = (bf16[2,6,12,1024]{3,1,2,0:T(8,128)(2,1)S(1)}, bf16[2,6,12,1024]{3,1,2,0:T(8,128)(2,1)}, u32[]{:S(2)}, u32[]{:S(2)}) collective-permute-start(bf16[2,6,12,1024]{3,1,2,0:T(8,128)(2,1)S(1)} %pad_maximum_fusion.3), channel_id=1, source_target_pairs={{2,1},{3,0},{4,3},{5,2},{6,5},{7,4},{8,7},{9,6},{10,9},{11,8},{12,... | collective-permute-start | bytes 884744 | tf_op jit(solution)/shard_map/ppermute | solution.py:153
  59.9 20.8 %collective-permute-start.11 = (bf16[2,6,12,1024]{3,1,2,0:T(8,128)(2,1)}, bf16[2,6,12,1024]{3,1,2,0:T(8,128)(2,1)}, u32[]{:S(2)}, u32[]{:S(2)}) collective-permute-start(bf16[2,6,12,1024]{3,1,2,0:T(8,128)(2,1)} %pad_maximum_fusion.4), channel_id=1, source_target_pairs={{0,3},{1,2},{2,5},{3,4},{4,7},{5,6},{6,9},{7,8},{8,11},{9,10},{10,... | collective-permute-start | bytes 884744 | tf_op jit(solution)/shard_map/ppermute | solution.py:153
  66.2 3.5 %copy-start.8 = (bf16[128,512]{1,0:T(8,128)(2,1)}, bf16[128,512]{1,0:T(8,128)(2,1)S(1)}, u32[]{:S(2)}) copy-start(bf16[128,512]{1,0:T(8,128)(2,1)S(1)} %collective-permute-done.9) | copy-start | bytes 393220
  66.5 30.4 %collective-permute-start.10 = (bf16[2,8,20,1024]{3,1,2,0:T(8,128)(2,1)S(1)}, bf16[2,8,20,1024]{3,1,2,0:T(8,128)(2,1)S(1)}, u32[]{:S(2)}, u32[]{:S(2)}) collective-permute-start(bf16[2,8,20,1024]{3,1,2,0:T(8,128)(2,1)S(1)} %pad_maximum_fusion.2), channel_id=1, source_target_pairs={{0,1},{1,0},{2,3},{3,2},{4,5},{5,4},{6,7},{7,6},{8,9},{9,8},{10,11... | collective-permute-start | bytes 1966088 | tf_op jit(solution)/shard_map/ppermute | solution.py:153
  72.6 34.0 %collective-permute-start.12 = (bf16[2,6,16,1024]{3,1,2,0:T(8,128)(2,1)}, bf16[2,6,16,1024]{3,1,2,0:T(8,128)(2,1)}, u32[]{:S(2)}, u32[]{:S(2)}) collective-permute-start(bf16[2,6,16,1024]{3,1,2,0:T(8,128)(2,1)} %copy.65), channel_id=1, source_target_pairs={{0,2},{1,3},{2,4},{3,5},{4,6},{5,7},{6,8},{7,9},{8,10},{9,11},{10,... | collective-permute-start | bytes 1179656 | tf_op jit(solution)/shard_map/ppermute | solution.py:153
  77.0 29.6 %collective-permute-start.8 = (bf16[2,6,16,1024]{3,1,2,0:T(8,128)(2,1)S(1)}, bf16[2,6,16,1024]{3,1,2,0:T(8,128)(2,1)}, u32[]{:S(2)}, u32[]{:S(2)}) collective-permute-start(bf16[2,6,16,1024]{3,1,2,0:T(8,128)(2,1)S(1)} %copy.60), channel_id=1, source_target_pairs={{2,0},{3,1},{4,2},{5,3},{6,4},{7,5},{8,6},{9,7},{10,8},{11,9},{12,... | collective-permute-start | bytes 1179656 | tf_op jit(solution)/shard_map/ppermute | solution.py:153
  99.7 21.2 %all-to-all-start = ((bf16[8,64,512]{2,1,0:T(8,128)(2,1)}), bf16[8,64,512]{2,1,0:T(8,128)(2,1)S(1)}, u32[]{:S(2)}, u32[]{:S(2)}) async-start(bf16[8,64,512]{2,1,0:T(8,128)(2,1)} %bitcast.41), calls=%async_computation | async-start | bytes 1048576 | tf_op jit(solution)/shard_map/all_to_all | solution.py:470
  106.6 2.7 %copy-start.4 = (bf16[512,3072]{1,0:T(8,128)(2,1)S(1)}, bf16[512,3072]{1,0:T(8,128)(2,1)}, u32[]{:S(2)}) copy-start(bf16[512,3072]{1,0:T(8,128)(2,1)} %param.8) | copy-start | bytes 9437188
  106.6 2.7 %copy-start.10 = (bf16[128,1024]{1,0:T(8,128)(2,1)S(1)}, bf16[128,1024]{1,0:T(8,128)(2,1)}, u32[]{:S(2)}) copy-start(bf16[128,1024]{1,0:T(8,128)(2,1)} %get-tuple-element.6) | copy-start | bytes 786436
